TPU v7x, 512 devices: a whole 4x4x16 slice. The times are simulated.
512 devices in a mesh: tm: 32 (over x, z_lo, core), height: 4 (over y), width: 4 (over z_hi).
Axes of the slice: x: 4, y: 4, z: 16 (z_hi: 4, z_lo: 4; z = z_hi * 4 + z_lo), core: 2. Of those that a mesh axis runs over, the one named last changes fastest.
Arguments:
- queries: bfloat16 [4, 4, 1024, 512], P('height', 'width'), may hold values from -40 to 40
- kv_blocks: bfloat16 [2, 64, 4, 4, 2, 64, 512], P(None, 'tm', 'height', 'width'), may hold values from -8 to 8
- block_list: int32 [4, 4, 8], P('height', 'width'), may hold values from 0 to 17, as said below
- block_valid: int32 [4, 4, 8], P('height', 'width'), may hold values from 0 to 1, as said below
- w_out: bfloat16 [512, 512], replicated, may hold values from -0.25 to 0.25
Outputs:
- joined: float32 [4, 4, 1024, 512], P('height', 'width', 'tm')
Inputs may be any that keep to these rules, and one draw needn't show every extreme that they name: `block_list`: the entries of one tile are distinct and each names a block of a tile inside the image. `block_valid`: in each tile the used entries come first, 4 to 8 of them.
All inputs are finite; a program needn't handle non-finite values.
Results may differ from a plain program's by a relative error of at most 0.0039.
Values may be sent and summed in bfloat16 or wider, within the bound.
No kernel may reach another device: no remote copies, remote signals or barrier semaphores. Data moves between devices by JAX's collectives and lax.ppermute only.
A program may use at most 192 MiB of HBM per device.

v0:
```python
import jax
import jax.numpy as jnp
from jax import lax
from jax.sharding import PartitionSpec as P

HEADS = 8
HD = 64


def padded(array, sides, width):
    for axis, dim in sides:
        size, length = (lax.axis_size(axis), array.shape[dim])
        up = [(i, (i + 1) % size) for i in range(size - 1)]
        down = [(j, i) for i, j in up]
        last = lax.slice_in_dim(array, length - width, length, axis=dim)
        first = lax.slice_in_dim(array, 0, width, axis=dim)
        before = lax.ppermute(last, axis, up)
        after = lax.ppermute(first, axis, down)
        array = jnp.concatenate([before, array, after], axis=dim)
    return array


def group_partial(query_rows, keys, values, keep):
    count = query_rows.shape[0]
    query_heads = query_rows.reshape(count, HEADS, HD)
    key_heads = keys.reshape(-1, HEADS, HD)
    value_heads = values.reshape(-1, HEADS, HD)
    scores = jnp.einsum("qhd,khd->hqk", query_heads, key_heads, preferred_element_type=jnp.float32)
    scores = scores / jnp.sqrt(jnp.float32(HD))
    scores = jnp.where(keep[None, None, :], scores, jnp.float32(-1e30))
    row_top = jnp.max(scores, axis=2)
    probs = jnp.where(keep[None, None, :], jnp.exp(scores - row_top[:, :, None]), jnp.float32(0.0))
    totals = jnp.sum(probs, axis=2)
    outputs = jnp.einsum(
        "hqk,khd->qhd", probs.astype(jnp.bfloat16), value_heads, preferred_element_type=jnp.float32
    )
    return (row_top.T, totals.T, outputs.reshape(count, HEADS * HD))


def local(queries, kv_blocks, block_list, block_valid, w_out):
    hood = padded(kv_blocks, (("height", 2), ("width", 3)), 1)
    frames = hood.shape[1]
    nblk = hood.shape[4]
    blk = hood.shape[5]
    width = hood.shape[6]
    hood = hood.reshape(2, frames, 9 * nblk, blk, width)
    listed = block_list[0, 0]
    nlist = listed.shape[0]
    chosen = jnp.take(hood, listed, axis=2)
    keep = jnp.broadcast_to((block_valid[0, 0] > 0)[None, :, None], (frames, nlist, blk)).reshape(
        -1
    )
    keys = chosen[0].reshape(-1, width)
    values = chosen[1].reshape(-1, width)
    query_rows = queries[0, 0]
    qtok = query_rows.shape[0]
    step_rows = min(512, qtok)

    def one_block(rows):
        return group_partial(rows, keys, values, keep)

    tops, totals, outputs = lax.map(
        one_block, query_rows.reshape(qtok // step_rows, step_rows, width)
    )
    tops = tops.reshape(qtok, HEADS)
    totals = totals.reshape(qtok, HEADS)
    outputs = outputs.reshape(qtok, width)
    groups = lax.axis_size("tm")
    own_rows = qtok // groups
    overall = lax.pmax(tops, "tm")
    factor = jnp.exp(tops - overall)
    summed, total = (
        lax.psum_scatter(
            outputs * jnp.repeat(factor, HD, axis=1), "tm", scatter_dimension=0, tiled=True
        ),
        lax.psum_scatter(totals * factor, "tm", scatter_dimension=0, tiled=True),
    )
    attended = summed / jnp.repeat(total, HD, axis=1)
    normed = attended * lax.rsqrt(jnp.mean(attended * attended, axis=1, keepdims=True) + 1e-06)
    normed = normed.astype(jnp.bfloat16)
    joined = jnp.dot(normed, w_out, preferred_element_type=jnp.float32)
    return joined.reshape(1, 1, own_rows, width)


def solution(mesh):
    in_specs = (
        P("height", "width", None, None),
        P(None, "tm", "height", "width", None, None, None),
        P("height", "width", None),
        P("height", "width", None),
        P(),
    )
    out_specs = P("height", "width", "tm", None)
    return jax.shard_map(local, mesh=mesh, in_specs=in_specs, out_specs=out_specs, check_vma=False)
```

profile of v0, /device:TPU:24, one launch (start us, length us, event | category | flops | bytes accessed | tf_op | source)
XLA Modules:
  0.0 686.1 jit_solution(10602972662053147666)
XLA Ops:
  6.5 1.4 collective-permute-start
  8.0 4.6 collective-permute-start.1
  12.6 9.9 %collective-permute-done = bf16[2,2,1,1,2,64,512]{6,5,4,3,2,1,0:T(8,128)(2,1)S(1)} collective-permute-done((bf16[2,2,1,1,2,64,512]{6,5,4,3,2,1,0:T(8,128)(2,1)}, bf16[2,2,1,1,2,64,512]{6,5,4,3,2,1,0:T(8,128)(2,1)S(1)}, u32[]{:S(2)}, u32[]{:S(2)}) %collective-permute-start) | collective-permute-done | bytes 524320 | tf_op jit(solution)/shard_map/ppermute | solution.py:17
  22.5 1.1 constant_dynamic-update-slice_fusion.2
  23.6 0.2 collective-permute-done.1
  23.8 10.2 %collective-permute-start.2 = (bf16[2,2,3,1,2,64,512]{6,5,4,3,2,1,0:T(8,128)(2,1)S(1)}, bf16[2,2,3,1,2,64,512]{6,5,4,3,2,1,0:T(8,128)(2,1)}, u32[]{:S(2)}, u32[]{:S(2)}) collective-permute-start(bf16[2,2,3,1,2,64,512]{6,5,4,3,2,1,0:T(8,128)(2,1)S(1)} %constant_dynamic-update-slice_fusion.1), channel_id=1, source_target_pairs={{0,1},{1,2},{2,3},{4,5},{5,6},{6,7},{8,9},{9,10},{10,11},{12,13},{... | collective-permute-start | bytes 4718600 | tf_op jit(solution)/shard_map/ppermute | solution.py:17
  34.0 1.3 collective-permute-start.3
  35.4 30.2 %collective-permute-done.2 = bf16[2,2,3,1,2,64,512]{6,5,4,3,2,1,0:T(8,128)(2,1)} collective-permute-done((bf16[2,2,3,1,2,64,512]{6,5,4,3,2,1,0:T(8,128)(2,1)S(1)}, bf16[2,2,3,1,2,64,512]{6,5,4,3,2,1,0:T(8,128)(2,1)}, u32[]{:S(2)}, u32[]{:S(2)}) %collective-permute-start.2) | collective-permute-done | bytes 1572896 | tf_op jit(solution)/shard_map/ppermute | solution.py:17
  65.6 110.7 %collective-permute-done.3 = bf16[2,2,3,1,2,64,512]{6,5,4,3,2,1,0:T(8,128)(2,1)} collective-permute-done((bf16[2,2,3,1,2,64,512]{6,5,4,3,2,1,0:T(8,128)(2,1)S(1)}, bf16[2,2,3,1,2,64,512]{6,5,4,3,2,1,0:T(8,128)(2,1)}, u32[]{:S(2)}, u32[]{:S(2)}) %collective-permute-start.3) | collective-permute-done | bytes 1572896 | tf_op jit(solution)/shard_map/ppermute | solution.py:18
  176.3 3.7 pad_maximum_fusion
  180.0 3.0 gather_fusion
  183.1 0.3 select_bitcast_fusion
  183.3 0.2 fusion.17
  183.5 1.1 copy.17
  184.6 1.1 copy.18
  185.7 55.6 %while.15 = (s32[]{:T(128)}, f32[2,512,8]{1,2,0:T(8,128)S(1)}, f32[2,512,8]{1,2,0:T(8,128)S(1)}, f32[2,512,512]{2,1,0:T(8,128)}, bf16[2,512,512]{2,1,0:T(8,128)(...) while((s32[]{:T(128)}, f32[2,512,8]{1,2,0:T(8,128)S(1)}, ...), condition=%wide.region_3.4_spmd.clone, body=%wide.region_0.3_spmd.clone.sunk | while | flops 1128259584 | bytes 131734152 | solution.py:62
  185.7 1.1 constant_dynamic-slice_fusion.2
  186.8 0.2 copy.40
  187.1 0.1 broadcast_in_dim.107
  187.2 2.8 reshape_reshape_squeeze.10
  190.0 3.8 fusion.29
  193.8 4.5 fusion.30
  198.3 1.2 copy-done.1
  199.5 2.8 reshape_reshape_squeeze.11
  202.3 8.6 %fusion.31 = f32[8,512,64]{1,2,0:T(8,128)} fusion(f32[8,512,1024]{2,1,0:T(8,128)} %copy-done.1, f32[8,512]{1,0:T(8,128)S(1)} %get-tuple-element.167, pred[1024]{0:T(1024)(128)(4,1)S(1)} %broadcast_in_dim.107, bf16[1024,8,64]{2,1,0:T(8,128)(2,1)S(1)} %reshape_reshape_squeeze.11), kind=kOutput, calls=%fused_computation.7.clone.1 | convolution fusion | flops 557842432 | bytes 18891776 | tf_op jit(solution)/shard_map/while/body/eval_jaxpr/hqk,khd->qhd/dot_general | solution.py:34
  210.9 1.6 copy.41
  212.4 1.1 constant_dynamic-update-slice_fusion.5
  213.5 1.1 constant_dynamic-slice_fusion.2
  214.6 0.2 copy.40
  215.0 2.8 reshape_reshape_squeeze.10
  217.7 3.8 fusion.29
  221.6 4.5 fusion.30
  226.0 1.2 copy-done.1
  227.3 2.8 reshape_reshape_squeeze.11
  230.1 8.6 %fusion.31 = f32[8,512,64]{1,2,0:T(8,128)} fusion(f32[8,512,1024]{2,1,0:T(8,128)} %copy-done.1, f32[8,512]{1,0:T(8,128)S(1)} %get-tuple-element.167, pred[1024]{0:T(1024)(128)(4,1)S(1)} %broadcast_in_dim.107, bf16[1024,8,64]{2,1,0:T(8,128)(2,1)S(1)} %reshape_reshape_squeeze.11), kind=kOutput, calls=%fused_computation.7.clone.1 | convolution fusion | flops 557842432 | bytes 18891776 | tf_op jit(solution)/shard_map/while/body/eval_jaxpr/hqk,khd->qhd/dot_general | solution.py:34
  238.7 1.6 copy.41
  240.2 1.1 constant_dynamic-update-slice_fusion.5
  241.3 133.2 %pmax.7 = f32[1024,8]{0,1:T(8,128)S(1)} all-reduce(f32[1024,8]{0,1:T(8,128)S(1)} %bitcast.51), channel_id=1, replica_groups=mesh['tm'=32,'height'=4,'width'=4] {'tm'}, use_global_device_ids=true, to_apply=%region_4.5 | all-reduce | flops 8192 | bytes 65536 | tf_op jit(solution)/shard_map/pmax | solution.py:70
  374.5 1.6 broadcast_in_dim.62
  376.1 1.9 copy.20
  378.1 1.0 copy.22
  379.1 3.4 bitcast_multiply_fusion
  382.6 142.9 %reduce-scatter.7.cloned.1.call-done = f32[32,8]{1,0:T(8,128)} async-done(((f32[1024,8]{1,0:T(8,128)}), f32[32,8]{1,0:T(8,128)}) %reduce-scatter.7.cloned.1.call-update) | async-done | bytes 1040 | tf_op jit(solution)/shard_map/reduce_scatter | solution.py:76
  525.5 0.8 broadcast_in_dim.63
  526.3 0.1 reshape.83
  526.4 151.0 %reduce-scatter.5.cloned.1.call-done = f32[32,512]{1,0:T(8,128)} async-done(((f32[1024,512]{1,0:T(8,128)}), f32[32,512]{1,0:T(8,128)}) %reduce-scatter.5.cloned.1.call-update) | async-done | bytes 65552 | tf_op jit(solution)/shard_map/reduce_scatter | solution.py:73
  677.4 1.0 multiply_reduce_fusion
  678.3 0.9 convolution_bitcast_fusion
  (28 shorter events, 0.5 us)
Async XLA Ops:
  6.5 671.8 %copy-start = (bf16[512,512]{1,0:T(8,128)(2,1)S(1)}, bf16[512,512]{1,0:T(8,128)(2,1)}, u32[]{:S(2)}) copy-start(bf16[512,512]{1,0:T(8,128)(2,1)} %param.11) | copy-start | bytes 1572868
  6.5 28.8 %copy-start.2 = (s32[1,1,8]{2,1,0:T(1,128)S(1)}, s32[1,1,8]{2,1,0:T(1,128)}, u32[]{:S(2)}) copy-start(s32[1,1,8]{2,1,0:T(1,128)} %param.9) | copy-start | bytes 100
  6.5 28.9 %copy-start.3 = (s32[1,1,8]{2,1,0:T(1,128)S(1)}, s32[1,1,8]{2,1,0:T(1,128)}, u32[]{:S(2)}) copy-start(s32[1,1,8]{2,1,0:T(1,128)} %param.10) | copy-start | bytes 100
  6.5 518.9 %reduce-scatter.7.cloned.1.call-start = ((), (), s32[]{:S(2)}) async-start(), calls=%async_computation.3 | async-start | bytes 540672 | tf_op jit(solution)/shard_map/reduce_scatter | solution.py:76
  6.5 15.9 %collective-permute-start = (bf16[2,2,1,1,2,64,512]{6,5,4,3,2,1,0:T(8,128)(2,1)}, bf16[2,2,1,1,2,64,512]{6,5,4,3,2,1,0:T(8,128)(2,1)S(1)}, u32[]{:S(2)}, u32[]{:S(2)}) collective-permute-start(bf16[2,2,1,1,2,64,512]{6,5,4,3,2,1,0:T(8,128)(2,1)} %param.8), channel_id=1, source_target_pairs={{0,4},{4,8},{8,12},{1,5},{5,9},{9,13},{2,6},{6,10},{10,14},{3,7},{... | collective-permute-start | bytes 1572872 | tf_op jit(solution)/shard_map/ppermute | solution.py:17
  8.0 15.8 %collective-permute-start.1 = (bf16[2,2,1,1,2,64,512]{6,5,4,3,2,1,0:T(8,128)(2,1)}, bf16[2,2,1,1,2,64,512]{6,5,4,3,2,1,0:T(8,128)(2,1)S(1)}, u32[]{:S(2)}, u32[]{:S(2)}) collective-permute-start(bf16[2,2,1,1,2,64,512]{6,5,4,3,2,1,0:T(8,128)(2,1)} %param.8), channel_id=1, source_target_pairs={{4,0},{8,4},{12,8},{5,1},{9,5},{13,9},{6,2},{10,6},{14,10},{7,3},{... | collective-permute-start | bytes 1572872 | tf_op jit(solution)/shard_map/ppermute | solution.py:18
  23.8 41.9 %collective-permute-start.2 = (bf16[2,2,3,1,2,64,512]{6,5,4,3,2,1,0:T(8,128)(2,1)S(1)}, bf16[2,2,3,1,2,64,512]{6,5,4,3,2,1,0:T(8,128)(2,1)}, u32[]{:S(2)}, u32[]{:S(2)}) collective-permute-start(bf16[2,2,3,1,2,64,512]{6,5,4,3,2,1,0:T(8,128)(2,1)S(1)} %constant_dynamic-update-slice_fusion.1), channel_id=1, source_target_pairs={{0,1},{1,2},{2,3},{4,5},{5,6},{6,7},{8,9},{9,10},{10,11},{12,13},{... | collective-permute-start | bytes 4718600 | tf_op jit(solution)/shard_map/ppermute | solution.py:17
  34.0 142.3 %collective-permute-start.3 = (bf16[2,2,3,1,2,64,512]{6,5,4,3,2,1,0:T(8,128)(2,1)S(1)}, bf16[2,2,3,1,2,64,512]{6,5,4,3,2,1,0:T(8,128)(2,1)}, u32[]{:S(2)}, u32[]{:S(2)}) collective-permute-start(bf16[2,2,3,1,2,64,512]{6,5,4,3,2,1,0:T(8,128)(2,1)S(1)} %constant_dynamic-update-slice_fusion.1), channel_id=1, source_target_pairs={{1,0},{2,1},{3,2},{5,4},{6,5},{7,6},{9,8},{10,9},{11,10},{13,12},{... | collective-permute-start | bytes 4718600 | tf_op jit(solution)/shard_map/ppermute | solution.py:18
  193.8 5.7 copy-start.1
  221.6 5.7 copy-start.1
  379.1 298.3 %reduce-scatter.5.cloned.1.call-start = ((), (), s32[]{:S(2)}) async-start(), calls=%async_computation.2 | async-start | bytes 2162688 | tf_op jit(solution)/shard_map/reduce_scatter | solution.py:73
Sparse Core Ops, SparseCore 0:
  379.2 146.2 reduce-scatter.6
  528.5 148.8 reduce-scatter.4
where the time goes:
time: 687 us; the launch traced here: 686 us
  waiting for transfers between devices  445 us (65%)
  blocking collectives  133 us (19%)
  local copies, waits for them, and re-layouts  33.7 us (5%)
  matrix products  25.6 us (4%)
  starting transfers between devices  17.6 us (3%)
  other arithmetic  17.4 us (3%)
  between operations  13.6 us (2%)
    reduce_scatter x1, waiting for transfers between devices, local(): lax.psum_scatter(outputs * jnp.repeat(factor, HD, axis=1), 'tm', scatter_...  151 us
    reduce_scatter x1, waiting for transfers between devices, local(): lax.psum_scatter(totals * factor, 'tm', scatter_dimension=0, tiled=True)  143 us
    pmax x1, blocking collectives, local(): overall = lax.pmax(tops, 'tm')  133 us
    ppermute x2, waiting for transfers between devices, padded(): after = lax.ppermute(first, axis, down)  111 us
    ppermute x2, waiting for transfers between devices, padded(): before = lax.ppermute(last, axis, up)  40.1 us
    dot_general x2, matrix products, group_partial(): jnp.einsum('hqk,khd->qhd', probs.astype(jnp.bfloat16), value_heads, prefe...  17.2 us
  transfers between devices with their start and end apart: 6, of which 6 were waited for; matrix products, arithmetic and copies ran while one was open for 1% of the time, Pallas kernels for 0%

commit v1 on v0

--- a/solution.py
+++ b/solution.py
@@ -7,17 +7,22 @@
 HD = 64
 
 
-def padded(array, sides, width):
-    for axis, dim in sides:
-        size, length = (lax.axis_size(axis), array.shape[dim])
-        up = [(i, (i + 1) % size) for i in range(size - 1)]
-        down = [(j, i) for i, j in up]
-        last = lax.slice_in_dim(array, length - width, length, axis=dim)
-        first = lax.slice_in_dim(array, 0, width, axis=dim)
-        before = lax.ppermute(last, axis, up)
-        after = lax.ppermute(first, axis, down)
-        array = jnp.concatenate([before, array, after], axis=dim)
-    return array
+def shifted(array, axis, forward):
+    size = lax.axis_size(axis)
+    if forward:
+        pairs = [(i, i + 1) for i in range(size - 1)]
+    else:
+        pairs = [(i + 1, i) for i in range(size - 1)]
+    return lax.ppermute(array, axis, pairs)
+
+
+def neighbourhood(kv_blocks):
+    left = shifted(kv_blocks, "width", True)
+    right = shifted(kv_blocks, "width", False)
+    row = jnp.concatenate([left, kv_blocks, right], axis=3)
+    up = shifted(row, "height", True)
+    down = shifted(row, "height", False)
+    return jnp.concatenate([up, row, down], axis=2)
 
 
 def group_partial(query_rows, keys, values, keep):
@@ -37,8 +42,49 @@
     return (row_top.T, totals.T, outputs.reshape(count, HEADS * HD))
 
 
+def merge(stats_a, out_a, stats_b, out_b):
+    heads = stats_a.shape[-1] // 2
+    top_a, tot_a = stats_a[..., :heads], stats_a[..., heads:]
+    top_b, tot_b = stats_b[..., :heads], stats_b[..., heads:]
+    top = jnp.maximum(top_a, top_b)
+    fa = jnp.exp(top_a - top)
+    fb = jnp.exp(top_b - top)
+    tot = tot_a * fa + tot_b * fb
+    shape = out_a.shape
+    out = (
+        out_a.reshape(shape[:-1] + (heads, -1)) * fa[..., None]
+        + out_b.reshape(shape[:-1] + (heads, -1)) * fb[..., None]
+    ).reshape(shape)
+    return jnp.concatenate([top, tot], axis=-1), out
+
+
+def tree_reduce(stats, out):
+    groups = lax.axis_size("tm")
+    nbits = groups.bit_length() - 1
+    me = lax.axis_index("tm")
+    rows = out.shape[0]
+    blk = rows // groups
+    stats = stats.reshape((2,) * nbits + (blk, stats.shape[-1]))
+    out = out.reshape((2,) * nbits + (blk, out.shape[-1]))
+    order = [0, 1, 3, 2, 4] if nbits == 5 else list(range(nbits))
+    remaining = list(range(nbits - 1, -1, -1))
+    for bit in order:
+        axis = remaining.index(bit)
+        remaining.remove(bit)
+        mine = (me >> bit) & 1
+        pairs = [(t, t ^ (1 << bit)) for t in range(groups)]
+        keep_s = lax.dynamic_index_in_dim(stats, mine, axis, keepdims=False)
+        keep_o = lax.dynamic_index_in_dim(out, mine, axis, keepdims=False)
+        send_s = lax.dynamic_index_in_dim(stats, 1 - mine, axis, keepdims=False)
+        send_o = lax.dynamic_index_in_dim(out, 1 - mine, axis, keepdims=False)
+        got_s = lax.ppermute(send_s, "tm", pairs)
+        got_o = lax.ppermute(send_o, "tm", pairs)
+        stats, out = merge(keep_s, keep_o, got_s, got_o)
+    return stats.reshape(blk, -1), out.reshape(blk, -1)
+
+
 def local(queries, kv_blocks, block_list, block_valid, w_out):
-    hood = padded(kv_blocks, (("height", 2), ("width", 3)), 1)
+    hood = neighbourhood(kv_blocks)
     frames = hood.shape[1]
     nblk = hood.shape[4]
     blk = hood.shape[5]
@@ -65,16 +111,10 @@
     tops = tops.reshape(qtok, HEADS)
     totals = totals.reshape(qtok, HEADS)
     outputs = outputs.reshape(qtok, width)
-    groups = lax.axis_size("tm")
-    own_rows = qtok // groups
-    overall = lax.pmax(tops, "tm")
-    factor = jnp.exp(tops - overall)
-    summed, total = (
-        lax.psum_scatter(
-            outputs * jnp.repeat(factor, HD, axis=1), "tm", scatter_dimension=0, tiled=True
-        ),
-        lax.psum_scatter(totals * factor, "tm", scatter_dimension=0, tiled=True),
-    )
+    stats = jnp.concatenate([tops, totals], axis=-1)
+    stats, summed = tree_reduce(stats, outputs)
+    total = stats[:, HEADS:]
+    own_rows = summed.shape[0]
     attended = summed / jnp.repeat(total, HD, axis=1)
     normed = attended * lax.rsqrt(jnp.mean(attended * attended, axis=1, keepdims=True) + 1e-06)
     normed = normed.astype(jnp.bfloat16)

time: 687 us -> 240 us (0.35)
  the two profiles are of different devices: /device:TPU:24 before, /device:TPU:6 now
where the time goes in v1:
time: 240 us; the launch traced here: 239 us
  waiting for transfers between devices  112 us (47%)
  starting transfers between devices  42.5 us (18%)
  local copies, waits for them, and re-layouts  40.8 us (17%)
  matrix products  25.6 us (11%)
  other arithmetic  17.5 us (7%)
    ppermute x4, waiting for transfers between devices, shifted(): return lax.ppermute(array, axis, pairs)  88.3 us
    dot_general x2, matrix products, group_partial(): jnp.einsum('hqk,khd->qhd', probs.astype(jnp.bfloat16), value_heads, prefe...  17.1 us
    ppermute x4, starting transfers between devices, shifted(): return lax.ppermute(array, axis, pairs)  16.5 us
    ppermute x5, starting transfers between devices, tree_reduce(): got_s = lax.ppermute(send_s, 'tm', pairs)  14.2 us
    ppermute x5, waiting for transfers between devices, tree_reduce(): got_s = lax.ppermute(send_s, 'tm', pairs)  12.6 us
    ppermute x5, starting transfers between devices, tree_reduce(): got_o = lax.ppermute(send_o, 'tm', pairs)  11.9 us
    ppermute x5, waiting for transfers between devices, tree_reduce(): got_o = lax.ppermute(send_o, 'tm', pairs)  10.9 us
    reduce_sum x2, other arithmetic, group_partial(): totals = jnp.sum(probs, axis=2)  8.95 us
  transfers between devices with their start and end apart: 14, of which 9 were waited for; matrix products, arithmetic and copies ran while one was open for 5% of the time, Pallas kernels for 0%

profile of v1, /device:TPU:6, one launch (start us, length us, event | category | flops | bytes accessed | tf_op | source)
XLA Modules:
  0.0 238.9 jit_solution(15638730324811432513)
XLA Ops:
  0.0 9.3 %collective-permute-start = (bf16[2,2,1,1,2,64,512]{6,5,4,3,2,1,0:T(8,128)(2,1)}, bf16[2,2,1,1,2,64,512]{6,5,4,3,2,1,0:T(8,128)(2,1)S(1)}, u32[]{:S(2)}, u32[]{:S(2)}) collective-permute-start(bf16[2,2,1,1,2,64,512]{6,5,4,3,2,1,0:T(8,128)(2,1)} %param.8), channel_id=1, source_target_pairs={{0,1},{1,2},{2,3},{4,5},{5,6},{6,7},{8,9},{9,10},{10,11},{12,13},{... | collective-permute-start | bytes 1572872 | tf_op jit(solution)/shard_map/ppermute | solution.py:16
  9.3 1.3 collective-permute-start.1
  10.6 10.3 %collective-permute-done = bf16[2,2,1,1,2,64,512]{6,5,4,3,2,1,0:T(8,128)(2,1)S(1)} collective-permute-done((bf16[2,2,1,1,2,64,512]{6,5,4,3,2,1,0:T(8,128)(2,1)}, bf16[2,2,1,1,2,64,512]{6,5,4,3,2,1,0:T(8,128)(2,1)S(1)}, u32[]{:S(2)}, u32[]{:S(2)}) %collective-permute-start) | collective-permute-done | bytes 524320 | tf_op jit(solution)/shard_map/ppermute | solution.py:16
  20.9 1.1 constant_dynamic-update-slice_fusion.2
  22.0 41.9 %collective-permute-done.1 = bf16[2,2,1,1,2,64,512]{6,5,4,3,2,1,0:T(8,128)(2,1)S(1)} collective-permute-done((bf16[2,2,1,1,2,64,512]{6,5,4,3,2,1,0:T(8,128)(2,1)}, bf16[2,2,1,1,2,64,512]{6,5,4,3,2,1,0:T(8,128)(2,1)S(1)}, u32[]{:S(2)}, u32[]{:S(2)}) %collective-permute-start.1) | collective-permute-done | bytes 524320 | tf_op jit(solution)/shard_map/ppermute | solution.py:16
  63.9 4.6 %collective-permute-start.2 = (bf16[2,2,1,3,2,64,512]{6,5,4,3,2,1,0:T(8,128)(2,1)S(1)}, bf16[2,2,1,3,2,64,512]{6,5,4,3,2,1,0:T(8,128)(2,1)}, u32[]{:S(2)}, u32[]{:S(2)}) collective-permute-start(bf16[2,2,1,3,2,64,512]{6,5,4,3,2,1,0:T(8,128)(2,1)S(1)} %constant_dynamic-update-slice_fusion.1), channel_id=1, source_target_pairs={{0,4},{4,8},{8,12},{1,5},{5,9},{9,13},{2,6},{6,10},{10,14},{3,7},{... | collective-permute-start | bytes 4718600 | tf_op jit(solution)/shard_map/ppermute | solution.py:16
  68.6 1.3 collective-permute-start.3
  70.0 30.8 %collective-permute-done.2 = bf16[2,2,1,3,2,64,512]{6,5,4,3,2,1,0:T(8,128)(2,1)} collective-permute-done((bf16[2,2,1,3,2,64,512]{6,5,4,3,2,1,0:T(8,128)(2,1)S(1)}, bf16[2,2,1,3,2,64,512]{6,5,4,3,2,1,0:T(8,128)(2,1)}, u32[]{:S(2)}, u32[]{:S(2)}) %collective-permute-start.2) | collective-permute-done | bytes 1572896 | tf_op jit(solution)/shard_map/ppermute | solution.py:16
  100.8 5.3 %collective-permute-done.3 = bf16[2,2,1,3,2,64,512]{6,5,4,3,2,1,0:T(8,128)(2,1)} collective-permute-done((bf16[2,2,1,3,2,64,512]{6,5,4,3,2,1,0:T(8,128)(2,1)S(1)}, bf16[2,2,1,3,2,64,512]{6,5,4,3,2,1,0:T(8,128)(2,1)}, u32[]{:S(2)}, u32[]{:S(2)}) %collective-permute-start.3) | collective-permute-done | bytes 1572896 | tf_op jit(solution)/shard_map/ppermute | solution.py:16
  106.1 3.8 %pad_maximum_fusion = bf16[2,2,3,3,2,64,512]{6,5,4,3,2,1,0:T(8,128)(2,1)} fusion(bf16[2,2,1,3,2,64,512]{6,5,4,3,2,1,0:T(8,128)(2,1)} %collective-permute-done.3, bf16[2,2,1,3,2,64,512]{6,5,4,3,2,1,0:T(8,128)(2,1)S(1)} %constant_dynamic-update-slice_fusion.1, bf16[2,2,1,3,2,64,512]{6,5,4,3,2,1,0:T(8,128)(2,1)} %collective-permute-done.2), kind=kLoop, calls=%fused_computation.19 | loop fusion | flops 4718592 | bytes 9437184 | tf_op jit(solution)/shard_map/concatenate | solution.py:25
  109.9 3.0 %gather_fusion = bf16[8,2,2,64,512]{4,3,2,1,0:T(8,128)(2,1)S(1)} fusion(bf16[2,2,18,64,512]{4,3,2,1,0:T(8,128)(2,1)} %bitcast.116, s32[1024]{0:T(1024)S(1)} %pad_clamp_fusion), kind=kCustom, calls=%fused_computation | custom fusion | bytes 4194336 | tf_op jit(solution)/shard_map/jit(_take)/gather | solution.py:95
  113.4 1.1 copy.90
  114.5 1.1 copy.91
  115.6 55.6 %while.15 = (s32[]{:T(128)}, f32[2,512,8]{1,2,0:T(8,128)S(1)}, f32[2,512,8]{1,2,0:T(8,128)S(1)}, f32[2,512,512]{2,1,0:T(8,128)}, bf16[2,512,512]{2,1,0:T(8,128)(...) while((s32[]{:T(128)}, f32[2,512,8]{1,2,0:T(8,128)S(1)}, ...), condition=%wide.region_3.4_spmd.clone, body=%wide.region_0.3_spmd.clone.sunk | while | flops 1128259584 | bytes 131734152 | solution.py:108
  115.6 1.1 constant_dynamic-slice_fusion.2
  117.0 2.8 %reshape_reshape_squeeze.10 = bf16[1024,8,64]{2,1,0:T(8,128)(2,1)S(1)} reshape(bf16[1,2,8,64,512]{4,3,2,1,0:T(8,128)(2,1)} %get-tuple-element.236) | data formatting | bytes 2097152 | tf_op jit(solution)/shard_map/while/body/eval_jaxpr/reshape;reshape;squeeze | solution.py:31
  119.8 3.8 %fusion.60 = (f32[8,512]{1,0:T(8,128)S(1)}, f32[8,512,1024]{2,1,0:T(8,128)S(1)}) fusion(pred[1024]{0:T(1024)(128)(4,1)S(1)} %broadcast_in_dim.113, bf16[512,8,64]{0,2,1:T(8,128)(2,1)S(1)} %bitcast.114, bf16[1024,8,64]{2,1,0:T(8,128)(2,1)S(1)} %reshape_reshape_squeeze.10), kind=kOutput, calls=%fused_computation.4.clone.1 | convolution fusion | flops 549449728 | bytes 18367488 | tf_op jit(solution)/shard_map/while/body/eval_jaxpr/qhd,khd->hqk/dot_general | solution.py:33
  123.6 4.5 %fusion.61 = f32[8,512]{1,0:T(8,128)S(1)} fusion(f32[8,512,1024]{2,1,0:T(8,128)S(1)} %get-tuple-element.209, f32[8,512]{1,0:T(8,128)S(1)} %get-tuple-element.210, pred[1024]{0:T(1024)(128)(4,1)S(1)} %broadcast_in_dim.113), kind=kLoop, calls=%fused_computation.6.clone.1 | loop fusion | flops 20967424 | bytes 16811008 | tf_op jit(solution)/shard_map/while/body/eval_jaxpr/reduce_sum | solution.py:38
  128.1 1.2 copy-done.1
  129.3 2.8 %reshape_reshape_squeeze.11 = bf16[1024,8,64]{2,1,0:T(8,128)(2,1)S(1)} reshape(bf16[1,2,8,64,512]{4,3,2,1,0:T(8,128)(2,1)} %get-tuple-element.237) | data formatting | bytes 2097152 | tf_op jit(solution)/shard_map/while/body/eval_jaxpr/reshape;reshape;squeeze | solution.py:32
  132.1 8.6 %fusion.62 = f32[8,512,64]{1,2,0:T(8,128)} fusion(f32[8,512,1024]{2,1,0:T(8,128)} %copy-done.1, f32[8,512]{1,0:T(8,128)S(1)} %get-tuple-element.210, pred[1024]{0:T(1024)(128)(4,1)S(1)} %broadcast_in_dim.113, bf16[1024,8,64]{2,1,0:T(8,128)(2,1)S(1)} %reshape_reshape_squeeze.11), kind=kOutput, calls=%fused_computation.7.clone.1 | convolution fusion | flops 557842432 | bytes 18891776 | tf_op jit(solution)/shard_map/while/body/eval_jaxpr/hqk,khd->qhd/dot_general | solution.py:39
  140.7 1.6 copy.125
  144.8 2.8 %reshape_reshape_squeeze.10 = bf16[1024,8,64]{2,1,0:T(8,128)(2,1)S(1)} reshape(bf16[1,2,8,64,512]{4,3,2,1,0:T(8,128)(2,1)} %get-tuple-element.236) | data formatting | bytes 2097152 | tf_op jit(solution)/shard_map/while/body/eval_jaxpr/reshape;reshape;squeeze | solution.py:31
  147.6 3.8 %fusion.60 = (f32[8,512]{1,0:T(8,128)S(1)}, f32[8,512,1024]{2,1,0:T(8,128)S(1)}) fusion(pred[1024]{0:T(1024)(128)(4,1)S(1)} %broadcast_in_dim.113, bf16[512,8,64]{0,2,1:T(8,128)(2,1)S(1)} %bitcast.114, bf16[1024,8,64]{2,1,0:T(8,128)(2,1)S(1)} %reshape_reshape_squeeze.10), kind=kOutput, calls=%fused_computation.4.clone.1 | convolution fusion | flops 549449728 | bytes 18367488 | tf_op jit(solution)/shard_map/while/body/eval_jaxpr/qhd,khd->hqk/dot_general | solution.py:33
  151.4 4.5 %fusion.61 = f32[8,512]{1,0:T(8,128)S(1)} fusion(f32[8,512,1024]{2,1,0:T(8,128)S(1)} %get-tuple-element.209, f32[8,512]{1,0:T(8,128)S(1)} %get-tuple-element.210, pred[1024]{0:T(1024)(128)(4,1)S(1)} %broadcast_in_dim.113), kind=kLoop, calls=%fused_computation.6.clone.1 | loop fusion | flops 20967424 | bytes 16811008 | tf_op jit(solution)/shard_map/while/body/eval_jaxpr/reduce_sum | solution.py:38
  155.9 1.2 copy-done.1
  157.1 2.8 %reshape_reshape_squeeze.11 = bf16[1024,8,64]{2,1,0:T(8,128)(2,1)S(1)} reshape(bf16[1,2,8,64,512]{4,3,2,1,0:T(8,128)(2,1)} %get-tuple-element.237) | data formatting | bytes 2097152 | tf_op jit(solution)/shard_map/while/body/eval_jaxpr/reshape;reshape;squeeze | solution.py:32
  159.9 8.6 %fusion.62 = f32[8,512,64]{1,2,0:T(8,128)} fusion(f32[8,512,1024]{2,1,0:T(8,128)} %copy-done.1, f32[8,512]{1,0:T(8,128)S(1)} %get-tuple-element.210, pred[1024]{0:T(1024)(128)(4,1)S(1)} %broadcast_in_dim.113, bf16[1024,8,64]{2,1,0:T(8,128)(2,1)S(1)} %reshape_reshape_squeeze.11), kind=kOutput, calls=%fused_computation.7.clone.1 | convolution fusion | flops 557842432 | bytes 18891776 | tf_op jit(solution)/shard_map/while/body/eval_jaxpr/hqk,khd->qhd/dot_general | solution.py:39
  168.5 1.6 copy.125
  171.1 2.3 dynamic-slice_bitcast_fusion
  173.4 1.9 collective-permute-start.5
  175.8 2.6 %collective-permute-start.4 = (f32[2,2,2,2,32,16]{4,5,3,2,1,0:T(8,128)S(1)}, f32[2,2,2,2,32,16]{4,5,3,2,1,0:T(8,128)S(1)}, u32[]{:S(2)}, u32[]{:S(2)}) collective-permute-start(f32[2,2,2,2,32,16]{4,5,3,2,1,0:T(8,128)S(1)} %get-tuple-element.147), channel_id=1, source_target_pairs={{0,16},{16,0},{32,48},{48,32},{64,80},{80,64},{96,112},{112,96},{1... | collective-permute-start | bytes 98312 | tf_op jit(solution)/shard_map/ppermute | solution.py:80
  179.9 1.5 mul.152
  182.1 1.5 mul.155
  183.6 2.7 %fusion.14 = f32[2,2,2,2,32,512]{5,4,3,2,1,0:T(8,128)S(1)} fusion(f32[2,2,2,2,32,512]{5,4,3,2,1,0:T(8,128)} %mul.152, f32[2,2,2,2,32,512]{5,4,3,2,1,0:T(8,128)} %collective-permute-done.5, f32[2,2,2,2,32,512]{5,4,3,2,1,0:T(8,128)} %mul.155, f32[2,2,2,2,2,32,512]{6,5,4,3,2,1,0:T(8,128)} %bitcast.119, s32[]{:T(128)S(6)} %select_n.80), kind=kLoop, calls=%fused_computation.23 | loop fusion | flops 786432 | bytes 5242884 | tf_op jit(solution)/shard_map/add | solution.py:55
  187.2 1.9 collective-permute-start.7
  189.1 3.9 %collective-permute-start.6 = (f32[2,2,2,32,16]{3,4,2,1,0:T(8,128)S(1)}, f32[2,2,2,32,16]{3,4,2,1,0:T(8,128)S(1)}, u32[]{:S(2)}, u32[]{:S(2)}) collective-permute-start(f32[2,2,2,32,16]{3,4,2,1,0:T(8,128)S(1)} %get-tuple-element.149), channel_id=1, source_target_pairs={{0,32},{16,48},{32,0},{48,16},{64,96},{80,112},{96,64},{112,80},{1... | collective-permute-start | bytes 49160 | tf_op jit(solution)/shard_map/ppermute | solution.py:80
  193.1 11.8 %collective-permute-done.6 = f32[2,2,2,32,16]{3,4,2,1,0:T(8,128)S(1)} collective-permute-done((f32[2,2,2,32,16]{3,4,2,1,0:T(8,128)S(1)}, f32[2,2,2,32,16]{3,4,2,1,0:T(8,128)S(1)}, u32[]{:S(2)}, u32[]{:S(2)}) %collective-permute-start.6) | collective-permute-done | bytes 16416 | tf_op jit(solution)/shard_map/ppermute | solution.py:80
  207.1 2.7 %collective-permute-start.8 = (f32[2,2,32,16]{2,3,1,0:T(8,128)S(1)}, f32[2,2,32,16]{2,3,1,0:T(8,128)S(1)}, u32[]{:S(2)}, u32[]{:S(2)}) collective-permute-start(f32[2,2,32,16]{2,3,1,0:T(8,128)S(1)} %get-tuple-element.151), channel_id=1, source_target_pairs={{0,128},{16,144},{32,160},{48,176},{64,192},{80,208},{96,224},{112... | collective-permute-start | bytes 24584 | tf_op jit(solution)/shard_map/ppermute | solution.py:80
  209.9 1.4 fusion.15
  211.3 3.1 %collective-permute-start.9 = (f32[2,2,32,512]{3,2,1,0:T(8,128)S(1)}, f32[2,2,32,512]{3,2,1,0:T(8,128)S(1)}, u32[]{:S(2)}, u32[]{:S(2)}) collective-permute-start(f32[2,2,32,512]{3,2,1,0:T(8,128)S(1)} %dynamic-slice_bitcast_fusion.2), channel_id=1, source_target_pairs={{0,128},{16,144},{32,160},{48,176},{64,192},{80,208},{96,224},{112... | collective-permute-start | bytes 786440 | tf_op jit(solution)/shard_map/ppermute | solution.py:81
  215.4 1.9 collective-permute-start.10
  217.3 3.4 %collective-permute-done.9 = f32[2,2,32,512]{3,2,1,0:T(8,128)S(1)} collective-permute-done((f32[2,2,32,512]{3,2,1,0:T(8,128)S(1)}, f32[2,2,32,512]{3,2,1,0:T(8,128)S(1)}, u32[]{:S(2)}, u32[]{:S(2)}) %collective-permute-start.9) | collective-permute-done | bytes 262176 | tf_op jit(solution)/shard_map/ppermute | solution.py:81
  220.8 1.9 collective-permute-start.11
  223.5 3.0 %collective-permute-start.12 = (f32[32,16]{0,1:T(8,128)S(1)}, f32[32,16]{0,1:T(8,128)S(1)}, u32[]{:S(2)}, u32[]{:S(2)}) collective-permute-start(f32[32,16]{0,1:T(8,128)S(1)} %get-tuple-element.155), channel_id=1, source_target_pairs={{0,256},{16,272},{32,288},{48,304},{64,320},{80,336},{96,352},{112... | collective-permute-start | bytes 6152 | tf_op jit(solution)/shard_map/ppermute | solution.py:80
  226.5 3.7 %collective-permute-done.11 = f32[2,32,512]{2,1,0:T(8,128)S(1)} collective-permute-done((f32[2,32,512]{2,1,0:T(8,128)S(1)}, f32[2,32,512]{2,1,0:T(8,128)S(1)}, u32[]{:S(2)}, u32[]{:S(2)}) %collective-permute-start.11) | collective-permute-done | bytes 131104 | tf_op jit(solution)/shard_map/ppermute | solution.py:81
  230.2 3.0 %collective-permute-start.13 = (f32[32,512]{1,0:T(8,128)S(1)}, f32[32,512]{1,0:T(8,128)S(1)}, u32[]{:S(2)}, u32[]{:S(2)}) collective-permute-start(f32[32,512]{1,0:T(8,128)S(1)} %dynamic-slice_bitcast_fusion.6), channel_id=1, source_target_pairs={{0,256},{16,272},{32,288},{48,304},{64,320},{80,336},{96,352},{112... | collective-permute-start | bytes 196616 | tf_op jit(solution)/shard_map/ppermute | solution.py:81
  234.1 3.8 %collective-permute-done.13 = f32[32,512]{1,0:T(8,128)S(1)} collective-permute-done((f32[32,512]{1,0:T(8,128)S(1)}, f32[32,512]{1,0:T(8,128)S(1)}, u32[]{:S(2)}, u32[]{:S(2)}) %collective-permute-start.13) | collective-permute-done | bytes 65568 | tf_op jit(solution)/shard_map/ppermute | solution.py:81
  (90 shorter events, 13.8 us)
Async XLA Ops:
  0.0 238.0 %copy-start = (bf16[512,512]{1,0:T(8,128)(2,1)S(1)}, bf16[512,512]{1,0:T(8,128)(2,1)}, u32[]{:S(2)}) copy-start(bf16[512,512]{1,0:T(8,128)(2,1)} %param.11) | copy-start | bytes 1572868
  0.0 69.9 %copy-start.2 = (s32[1,1,8]{2,1,0:T(1,128)S(1)}, s32[1,1,8]{2,1,0:T(1,128)}, u32[]{:S(2)}) copy-start(s32[1,1,8]{2,1,0:T(1,128)} %param.9) | copy-start | bytes 100
  0.0 69.9 %copy-start.3 = (s32[1,1,8]{2,1,0:T(1,128)S(1)}, s32[1,1,8]{2,1,0:T(1,128)}, u32[]{:S(2)}) copy-start(s32[1,1,8]{2,1,0:T(1,128)} %param.10) | copy-start | bytes 100
  0.0 20.8 %collective-permute-start = (bf16[2,2,1,1,2,64,512]{6,5,4,3,2,1,0:T(8,128)(2,1)}, bf16[2,2,1,1,2,64,512]{6,5,4,3,2,1,0:T(8,128)(2,1)S(1)}, u32[]{:S(2)}, u32[]{:S(2)}) collective-permute-start(bf16[2,2,1,1,2,64,512]{6,5,4,3,2,1,0:T(8,128)(2,1)} %param.8), channel_id=1, source_target_pairs={{0,1},{1,2},{2,3},{4,5},{5,6},{6,7},{8,9},{9,10},{10,11},{12,13},{... | collective-permute-start | bytes 1572872 | tf_op jit(solution)/shard_map/ppermute | solution.py:16
  9.3 54.6 %collective-permute-start.1 = (bf16[2,2,1,1,2,64,512]{6,5,4,3,2,1,0:T(8,128)(2,1)}, bf16[2,2,1,1,2,64,512]{6,5,4,3,2,1,0:T(8,128)(2,1)S(1)}, u32[]{:S(2)}, u32[]{:S(2)}) collective-permute-start(bf16[2,2,1,1,2,64,512]{6,5,4,3,2,1,0:T(8,128)(2,1)} %param.8), channel_id=1, source_target_pairs={{1,0},{2,1},{3,2},{5,4},{6,5},{7,6},{9,8},{10,9},{11,10},{13,12},{... | collective-permute-start | bytes 1572872 | tf_op jit(solution)/shard_map/ppermute | solution.py:16
  63.9 36.8 %collective-permute-start.2 = (bf16[2,2,1,3,2,64,512]{6,5,4,3,2,1,0:T(8,128)(2,1)S(1)}, bf16[2,2,1,3,2,64,512]{6,5,4,3,2,1,0:T(8,128)(2,1)}, u32[]{:S(2)}, u32[]{:S(2)}) collective-permute-start(bf16[2,2,1,3,2,64,512]{6,5,4,3,2,1,0:T(8,128)(2,1)S(1)} %constant_dynamic-update-slice_fusion.1), channel_id=1, source_target_pairs={{0,4},{4,8},{8,12},{1,5},{5,9},{9,13},{2,6},{6,10},{10,14},{3,7},{... | collective-permute-start | bytes 4718600 | tf_op jit(solution)/shard_map/ppermute | solution.py:16
  68.6 37.6 %collective-permute-start.3 = (bf16[2,2,1,3,2,64,512]{6,5,4,3,2,1,0:T(8,128)(2,1)S(1)}, bf16[2,2,1,3,2,64,512]{6,5,4,3,2,1,0:T(8,128)(2,1)}, u32[]{:S(2)}, u32[]{:S(2)}) collective-permute-start(bf16[2,2,1,3,2,64,512]{6,5,4,3,2,1,0:T(8,128)(2,1)S(1)} %constant_dynamic-update-slice_fusion.1), channel_id=1, source_target_pairs={{4,0},{8,4},{12,8},{5,1},{9,5},{13,9},{6,2},{10,6},{14,10},{7,3},{... | collective-permute-start | bytes 4718600 | tf_op jit(solution)/shard_map/ppermute | solution.py:16
  123.6 5.7 %copy-start.1 = (f32[8,512,1024]{2,1,0:T(8,128)}, f32[8,512,1024]{2,1,0:T(8,128)S(1)}, u32[]{:S(2)}) copy-start(f32[8,512,1024]{2,1,0:T(8,128)S(1)} %get-tuple-element.209) | copy-start | bytes 50331652 | tf_op jit(solution)/shard_map/while
  151.4 5.7 %copy-start.1 = (f32[8,512,1024]{2,1,0:T(8,128)}, f32[8,512,1024]{2,1,0:T(8,128)S(1)}, u32[]{:S(2)}) copy-start(f32[8,512,1024]{2,1,0:T(8,128)S(1)} %get-tuple-element.209) | copy-start | bytes 50331652 | tf_op jit(solution)/shard_map/while
  173.4 10.2 %collective-permute-start.5 = (f32[2,2,2,2,32,512]{5,4,3,2,1,0:T(8,128)}, f32[2,2,2,2,32,512]{5,4,3,2,1,0:T(8,128)}, u32[]{:S(2)}, u32[]{:S(2)}) collective-permute-start(f32[2,2,2,2,32,512]{5,4,3,2,1,0:T(8,128)} %dynamic-slice_bitcast_fusion), channel_id=1, source_target_pairs={{0,16},{16,0},{32,48},{48,32},{64,80},{80,64},{96,112},{112,96},{1... | collective-permute-start | bytes 3145736 | tf_op jit(solution)/shard_map/ppermute | solution.py:81
  175.8 3.4 %collective-permute-start.4 = (f32[2,2,2,2,32,16]{4,5,3,2,1,0:T(8,128)S(1)}, f32[2,2,2,2,32,16]{4,5,3,2,1,0:T(8,128)S(1)}, u32[]{:S(2)}, u32[]{:S(2)}) collective-permute-start(f32[2,2,2,2,32,16]{4,5,3,2,1,0:T(8,128)S(1)} %get-tuple-element.147), channel_id=1, source_target_pairs={{0,16},{16,0},{32,48},{48,32},{64,80},{80,64},{96,112},{112,96},{1... | collective-permute-start | bytes 98312 | tf_op jit(solution)/shard_map/ppermute | solution.py:80
  187.2 22.7 %collective-permute-start.7 = (f32[2,2,2,32,512]{4,3,2,1,0:T(8,128)}, f32[2,2,2,32,512]{4,3,2,1,0:T(8,128)}, u32[]{:S(2)}, u32[]{:S(2)}) collective-permute-start(f32[2,2,2,32,512]{4,3,2,1,0:T(8,128)} %dynamic-slice_bitcast_fusion.1), channel_id=1, source_target_pairs={{0,32},{16,48},{32,0},{48,16},{64,96},{80,112},{96,64},{112,80},{1... | collective-permute-start | bytes 1572872 | tf_op jit(solution)/shard_map/ppermute | solution.py:81
  189.1 15.7 %collective-permute-start.6 = (f32[2,2,2,32,16]{3,4,2,1,0:T(8,128)S(1)}, f32[2,2,2,32,16]{3,4,2,1,0:T(8,128)S(1)}, u32[]{:S(2)}, u32[]{:S(2)}) collective-permute-start(f32[2,2,2,32,16]{3,4,2,1,0:T(8,128)S(1)} %get-tuple-element.149), channel_id=1, source_target_pairs={{0,32},{16,48},{32,0},{48,16},{64,96},{80,112},{96,64},{112,80},{1... | collective-permute-start | bytes 49160 | tf_op jit(solution)/shard_map/ppermute | solution.py:80
  207.1 7.3 %collective-permute-start.8 = (f32[2,2,32,16]{2,3,1,0:T(8,128)S(1)}, f32[2,2,32,16]{2,3,1,0:T(8,128)S(1)}, u32[]{:S(2)}, u32[]{:S(2)}) collective-permute-start(f32[2,2,32,16]{2,3,1,0:T(8,128)S(1)} %get-tuple-element.151), channel_id=1, source_target_pairs={{0,128},{16,144},{32,160},{48,176},{64,192},{80,208},{96,224},{112... | collective-permute-start | bytes 24584 | tf_op jit(solution)/shard_map/ppermute | solution.py:80
  211.3 9.4 %collective-permute-start.9 = (f32[2,2,32,512]{3,2,1,0:T(8,128)S(1)}, f32[2,2,32,512]{3,2,1,0:T(8,128)S(1)}, u32[]{:S(2)}, u32[]{:S(2)}) collective-permute-start(f32[2,2,32,512]{3,2,1,0:T(8,128)S(1)} %dynamic-slice_bitcast_fusion.2), channel_id=1, source_target_pairs={{0,128},{16,144},{32,160},{48,176},{64,192},{80,208},{96,224},{112... | collective-permute-start | bytes 786440 | tf_op jit(solution)/shard_map/ppermute | solution.py:81
  215.4 7.4 %collective-permute-start.10 = (f32[2,32,16]{1,2,0:T(8,128)S(1)}, f32[2,32,16]{1,2,0:T(8,128)S(1)}, u32[]{:S(2)}, u32[]{:S(2)}) collective-permute-start(f32[2,32,16]{1,2,0:T(8,128)S(1)} %get-tuple-element.153), channel_id=1, source_target_pairs={{0,64},{16,80},{32,96},{48,112},{64,0},{80,16},{96,32},{112,48},{1... | collective-permute-start | bytes 12296 | tf_op jit(solution)/shard_map/ppermute | solution.py:80
  220.8 9.3 %collective-permute-start.11 = (f32[2,32,512]{2,1,0:T(8,128)S(1)}, f32[2,32,512]{2,1,0:T(8,128)S(1)}, u32[]{:S(2)}, u32[]{:S(2)}) collective-permute-start(f32[2,32,512]{2,1,0:T(8,128)S(1)} %dynamic-slice_bitcast_fusion.3), channel_id=1, source_target_pairs={{0,64},{16,80},{32,96},{48,112},{64,0},{80,16},{96,32},{112,48},{1... | collective-permute-start | bytes 393224 | tf_op jit(solution)/shard_map/ppermute | solution.py:81
  223.5 9.8 %collective-permute-start.12 = (f32[32,16]{0,1:T(8,128)S(1)}, f32[32,16]{0,1:T(8,128)S(1)}, u32[]{:S(2)}, u32[]{:S(2)}) collective-permute-start(f32[32,16]{0,1:T(8,128)S(1)} %get-tuple-element.155), channel_id=1, source_target_pairs={{0,256},{16,272},{32,288},{48,304},{64,320},{80,336},{96,352},{112... | collective-permute-start | bytes 6152 | tf_op jit(solution)/shard_map/ppermute | solution.py:80
  230.2 7.7 %collective-permute-start.13 = (f32[32,512]{1,0:T(8,128)S(1)}, f32[32,512]{1,0:T(8,128)S(1)}, u32[]{:S(2)}, u32[]{:S(2)}) collective-permute-start(f32[32,512]{1,0:T(8,128)S(1)} %dynamic-slice_bitcast_fusion.6), channel_id=1, source_target_pairs={{0,256},{16,272},{32,288},{48,304},{64,320},{80,336},{96,352},{112... | collective-permute-start | bytes 196616 | tf_op jit(solution)/shard_map/ppermute | solution.py:81

commit v2 on v1

v2 whole, which is shorter than its diff:
```python
import functools

import jax
import jax.numpy as jnp
from jax import lax
from jax.sharding import PartitionSpec as P

HEADS = 8
HD = 64


def shifted(array, axis, forward):
    size = lax.axis_size(axis)
    if forward:
        pairs = [(i, i + 1) for i in range(size - 1)]
    else:
        pairs = [(i + 1, i) for i in range(size - 1)]
    return lax.ppermute(array, axis, pairs)


def neighbourhood(kv_blocks):
    left = shifted(kv_blocks, "width", True)
    right = shifted(kv_blocks, "width", False)
    up_mid = shifted(kv_blocks, "height", True)
    down_mid = shifted(kv_blocks, "height", False)
    sides = jnp.concatenate([left, right], axis=3)
    up_sides = shifted(sides, "height", True)
    down_sides = shifted(sides, "height", False)
    row = jnp.concatenate([left, kv_blocks, right], axis=3)
    up = jnp.concatenate([up_sides[:, :, :, :1], up_mid, up_sides[:, :, :, 1:]], axis=3)
    down = jnp.concatenate([down_sides[:, :, :, :1], down_mid, down_sides[:, :, :, 1:]], axis=3)
    return jnp.concatenate([up, row, down], axis=2)


def attend(q, kv, keep, count):
    heads, qtok, hd = q.shape
    halves = q.reshape(heads, 2, qtok // 2, hd).transpose(1, 0, 2, 3)
    stats, out = lax.map(lambda part: attend_rows(part, kv, keep, count), halves)
    stats = stats.transpose(1, 2, 0, 3).reshape(2, heads, qtok)
    out = out.transpose(1, 0, 2, 3).reshape(heads, qtok, hd)
    return stats, out


def attend_rows(q, kv, keep, count):
    keys = kv[0, :, :count]
    values = kv[1, :, :count]
    keep = keep[:count]
    scores = jnp.einsum("hqd,hkd->hqk", q, keys, preferred_element_type=jnp.float32)
    scores = scores / jnp.sqrt(jnp.float32(HD))
    scores = jnp.where(keep[None, None, :], scores, jnp.float32(-1e30))
    top = jnp.max(scores, axis=2)
    probs = jnp.where(keep[None, None, :], jnp.exp(scores - top[:, :, None]), jnp.float32(0.0))
    total = jnp.sum(probs, axis=2)
    out = jnp.einsum(
        "hqk,hkd->hqd", probs.astype(jnp.bfloat16), values, preferred_element_type=jnp.float32
    )
    return jnp.stack([top, total]), out


def merge(stats_a, out_a, stats_b, out_b):
    top = jnp.maximum(stats_a[0], stats_b[0])
    fa = jnp.exp(stats_a[0] - top)
    fb = jnp.exp(stats_b[0] - top)
    tot = stats_a[1] * fa + stats_b[1] * fb
    out = out_a * fa[..., None] + out_b * fb[..., None]
    return jnp.stack([top, tot]), out


def tree_reduce(stats, out):
    groups = lax.axis_size("tm")
    nbits = groups.bit_length() - 1
    me = lax.axis_index("tm")
    rows = out.shape[1]
    blk = rows // groups
    heads = out.shape[0]
    stats = stats.reshape((2, heads) + (2,) * nbits + (blk,))
    out = out.reshape((heads,) + (2,) * nbits + (blk, out.shape[-1]))
    order = [0, 1, 3, 2, 4] if nbits == 5 else list(range(nbits))
    remaining = list(range(nbits - 1, -1, -1))
    for bit in order:
        axis = remaining.index(bit)
        remaining.remove(bit)
        mine = (me >> bit) & 1
        pairs = [(t, t ^ (1 << bit)) for t in range(groups)]
        keep_s = lax.dynamic_index_in_dim(stats, mine, axis + 2, keepdims=False)
        keep_o = lax.dynamic_index_in_dim(out, mine, axis + 1, keepdims=False)
        send_s = lax.dynamic_index_in_dim(stats, 1 - mine, axis + 2, keepdims=False)
        send_o = lax.dynamic_index_in_dim(out, 1 - mine, axis + 1, keepdims=False)
        got_s = lax.ppermute(send_s, "tm", pairs)
        got_o = lax.ppermute(send_o, "tm", pairs)
        stats, out = merge(keep_s, keep_o, got_s, got_o)
    return stats, out


def local(queries, kv_blocks, block_list, block_valid, w_out):
    hood = neighbourhood(kv_blocks)
    frames = hood.shape[1]
    nblk = hood.shape[4]
    blk = hood.shape[5]
    width = hood.shape[6]
    hood = hood.reshape(2, frames, 9 * nblk, blk, width)
    listed = block_list[0, 0]
    nlist = listed.shape[0]
    chosen = jnp.take(hood, listed, axis=2)
    kv = chosen.transpose(0, 2, 1, 3, 4).reshape(2, nlist * frames * blk, HEADS, HD)
    kv = kv.transpose(0, 2, 1, 3)
    query_rows = queries[0, 0]
    qtok = query_rows.shape[0]
    q = query_rows.reshape(qtok, HEADS, HD).transpose(1, 0, 2)
    valid = block_valid[0, 0] > 0
    used = jnp.sum(valid.astype(jnp.int32))
    keep = jnp.broadcast_to(valid[:, None], (nlist, frames * blk)).reshape(-1)
    least = nlist // 2
    branches = [
        functools.partial(attend, count=c * frames * blk) for c in range(least, nlist + 1, 2)
    ]
    stats, out = lax.switch((used - least + 1) // 2, branches, q, kv, keep)
    stats, summed = tree_reduce(stats, out)
    total = stats[1]
    attended = summed / total[..., None]
    own_rows = attended.shape[1]
    attended = attended.transpose(1, 0, 2).reshape(own_rows, width)
    normed = attended * lax.rsqrt(jnp.mean(attended * attended, axis=1, keepdims=True) + 1e-06)
    normed = normed.astype(jnp.bfloat16)
    joined = jnp.dot(normed, w_out, preferred_element_type=jnp.float32)
    return joined.reshape(1, 1, own_rows, width)


def solution(mesh):
    in_specs = (
        P("height", "width", None, None),
        P(None, "tm", "height", "width", None, None, None),
        P("height", "width", None),
        P("height", "width", None),
        P(),
    )
    out_specs = P("height", "width", "tm", None)
    return jax.shard_map(local, mesh=mesh, in_specs=in_specs, out_specs=out_specs, check_vma=False)
```

time: 240 us -> 256 us (1.067)
  waiting for transfers between devices: 112 us -> 132 us
  matrix products: 25.6 us -> 15.2 us
  other arithmetic: 17.5 us -> 22.7 us
  local copies, waits for them, and re-layouts: 40.8 us -> 37.5 us
    ppermute x5, waiting for transfers between devices: 10.9 us -> 45.7 us  [tree_reduce(): got_o = lax.ppermute(send_o, 'tm', pairs)]
    dot_general x4, matrix products: 24.7 us -> 14.3 us  [the longest x2 7.41 us: attend_rows(): jnp.einsum('hqd,hkd->hqk', q, keys, preferred_element_type=jnp.float32)]
    ppermute x4 -> x6, waiting for transfers between devices: 88.3 us -> 80.6 us  [shifted(): return lax.ppermute(array, axis, pairs)]
    mul x20 -> x0, local copies, waits for them, and re-layouts: 7.72 us -> none  [the longest x10 4.26 us: merge(): out_b.reshape(shape[:-1] + (heads, -1)) * fb[..., None]]
    reshape x1 -> x4, local copies, waits for them, and re-layouts: 0.09 us -> 7.26 us  [the longest x1 6.15 us: local(): chosen.transpose(0, 2, 1, 3, 4).reshape(2, nlist * frames * blk, HEADS, HD)]
    ppermute x5, waiting for transfers between devices: 12.6 us -> 5.88 us  [tree_reduce(): got_s = lax.ppermute(send_s, 'tm', pairs)]
    another operation x4 -> x1, local copies, waits for them, and re-layouts: 11.1 us -> 4.46 us  [the longest x2 5.57 us: group_partial(): key_heads = keys.reshape(-1, HEADS, HD)]
    cond x0 -> x4, local copies, waits for them, and re-layouts: none -> 6.18 us  [the longest x3 4.97 us: local(): stats, out = lax.switch((used - least + 1) // 2, branches, q, kv, keep)]
  transfers between devices with their start and end apart: 14 -> 16, of which waited for: 9 -> 10; matrix products, arithmetic and copies ran while one was open for 5% -> 5% of each run, Pallas kernels for 0% -> 0%
where the time goes in v2:
time: 256 us; the launch traced here: 254 us
  waiting for transfers between devices  132 us (52%)
  starting transfers between devices  44.9 us (18%)
  local copies, waits for them, and re-layouts  37.5 us (15%)
  other arithmetic  22.7 us (9%)
  matrix products  15.2 us (6%)
    ppermute x6, waiting for transfers between devices, shifted(): return lax.ppermute(array, axis, pairs)  80.6 us
    ppermute x5, waiting for transfers between devices, tree_reduce(): got_o = lax.ppermute(send_o, 'tm', pairs)  45.7 us
    ppermute x6, starting transfers between devices, shifted(): return lax.ppermute(array, axis, pairs)  20.9 us
    ppermute x5, starting transfers between devices, tree_reduce(): got_o = lax.ppermute(send_o, 'tm', pairs)  12 us
    ppermute x5, starting transfers between devices, tree_reduce(): got_s = lax.ppermute(send_s, 'tm', pairs)  12 us
    reduce_sum x2, other arithmetic, attend_rows(): total = jnp.sum(probs, axis=2)  8.73 us
    dot_general x2, matrix products, attend_rows(): jnp.einsum('hqd,hkd->hqk', q, keys, preferred_element_type=jnp.float32)  7.41 us
    dot_general x2, matrix products, attend_rows(): jnp.einsum('hqk,hkd->hqd', probs.astype(jnp.bfloat16), values, preferred_...  6.91 us
  transfers between devices with their start and end apart: 16, of which 10 were waited for; matrix products, arithmetic and copies ran while one was open for 5% of the time, Pallas kernels for 0%

profile of v2, /device:TPU:6, one launch (start us, length us, event | category | flops | bytes accessed | tf_op | source)
XLA Modules:
  0.0 254.2 jit_solution(7460974631576255978)
XLA Ops:
  0.0 9.2 %collective-permute-start = (bf16[2,2,1,1,2,64,512]{6,5,4,3,2,1,0:T(8,128)(2,1)}, bf16[2,2,1,1,2,64,512]{6,5,4,3,2,1,0:T(8,128)(2,1)S(1)}, u32[]{:S(2)}, u32[]{:S(2)}) collective-permute-start(bf16[2,2,1,1,2,64,512]{6,5,4,3,2,1,0:T(8,128)(2,1)} %param.15), channel_id=1, source_target_pairs={{0,1},{1,2},{2,3},{4,5},{5,6},{6,7},{8,9},{9,10},{10,11},{12,13},{... | collective-permute-start | bytes 1572872 | tf_op jit(solution)/shard_map/ppermute | solution.py:18
  9.3 1.3 collective-permute-start.1
  10.6 10.3 %collective-permute-done = bf16[2,2,1,1,2,64,512]{6,5,4,3,2,1,0:T(8,128)(2,1)S(1)} collective-permute-done((bf16[2,2,1,1,2,64,512]{6,5,4,3,2,1,0:T(8,128)(2,1)}, bf16[2,2,1,1,2,64,512]{6,5,4,3,2,1,0:T(8,128)(2,1)S(1)}, u32[]{:S(2)}, u32[]{:S(2)}) %collective-permute-start) | collective-permute-done | bytes 524320 | tf_op jit(solution)/shard_map/ppermute | solution.py:18
  21.7 42.2 %collective-permute-done.1 = bf16[2,2,1,1,2,64,512]{6,5,4,3,2,1,0:T(8,128)(2,1)S(1)} collective-permute-done((bf16[2,2,1,1,2,64,512]{6,5,4,3,2,1,0:T(8,128)(2,1)}, bf16[2,2,1,1,2,64,512]{6,5,4,3,2,1,0:T(8,128)(2,1)S(1)}, u32[]{:S(2)}, u32[]{:S(2)}) %collective-permute-start.1) | collective-permute-done | bytes 524320 | tf_op jit(solution)/shard_map/ppermute | solution.py:18
  64.7 4.5 %collective-permute-start.2 = (bf16[2,2,1,2,2,64,512]{6,5,4,3,2,1,0:T(8,128)(2,1)}, bf16[2,2,1,2,2,64,512]{6,5,4,3,2,1,0:T(8,128)(2,1)}, u32[]{:S(2)}, u32[]{:S(2)}) collective-permute-start(bf16[2,2,1,2,2,64,512]{6,5,4,3,2,1,0:T(8,128)(2,1)} %constant_dynamic-update-slice_fusion), channel_id=1, source_target_pairs={{0,4},{4,8},{8,12},{1,5},{5,9},{9,13},{2,6},{6,10},{10,14},{3,7},{... | collective-permute-start | bytes 3145736 | tf_op jit(solution)/shard_map/ppermute | solution.py:18
  69.2 3.3 %collective-permute-start.3 = (bf16[2,2,1,1,2,64,512]{6,5,4,3,2,1,0:T(8,128)(2,1)}, bf16[2,2,1,1,2,64,512]{6,5,4,3,2,1,0:T(8,128)(2,1)}, u32[]{:S(2)}, u32[]{:S(2)}) collective-permute-start(bf16[2,2,1,1,2,64,512]{6,5,4,3,2,1,0:T(8,128)(2,1)} %param.15), channel_id=1, source_target_pairs={{0,4},{4,8},{8,12},{1,5},{5,9},{9,13},{2,6},{6,10},{10,14},{3,7},{... | collective-permute-start | bytes 1572872 | tf_op jit(solution)/shard_map/ppermute | solution.py:18
  72.5 1.3 collective-permute-start.5
  73.8 1.3 convert_reduce_fusion
  75.8 1.5 copy.133
  77.3 1.3 collective-permute-start.4
  80.6 11.5 %collective-permute-done.2 = bf16[2,2,1,2,2,64,512]{6,5,4,3,2,1,0:T(8,128)(2,1)} collective-permute-done((bf16[2,2,1,2,2,64,512]{6,5,4,3,2,1,0:T(8,128)(2,1)}, bf16[2,2,1,2,2,64,512]{6,5,4,3,2,1,0:T(8,128)(2,1)}, u32[]{:S(2)}, u32[]{:S(2)}) %collective-permute-start.2) | collective-permute-done | bytes 1048608 | tf_op jit(solution)/shard_map/ppermute | solution.py:18
  92.1 1.3 fusion.123
  93.4 16.6 %collective-permute-done.4 = bf16[2,2,1,2,2,64,512]{6,5,4,3,2,1,0:T(8,128)(2,1)} collective-permute-done((bf16[2,2,1,2,2,64,512]{6,5,4,3,2,1,0:T(8,128)(2,1)}, bf16[2,2,1,2,2,64,512]{6,5,4,3,2,1,0:T(8,128)(2,1)}, u32[]{:S(2)}, u32[]{:S(2)}) %collective-permute-start.4) | collective-permute-done | bytes 1048608 | tf_op jit(solution)/shard_map/ppermute | solution.py:18
  110.0 1.3 fusion.124
  111.3 4.3 %maximum_maximum_fusion = bf16[2,2,3,3,2,64,512]{6,5,4,3,2,1,0:T(8,128)(2,1)} fusion(bf16[2,2,1,1,2,64,512]{6,5,4,3,2,1,0:T(8,128)(2,1)S(1)} %get-tuple-element.351, bf16[2,2,1,1,2,64,512]{6,5,4,3,2,1,0:T(8,128)(2,1)} %collective-permute-done.5, bf16[2,2,1,1,2,64,512]{6,5,4,3,2,1,0:T(8,128)(2,1)S(1)} %get-tuple-element.350, ...), kind=kLoop, calls=%fused_computation.71 | loop fusion | flops 18874368 | bytes 9437184 | tf_op jit(solution)/shard_map/concatenate | solution.py:32
  115.6 4.4 %gather_fusion = bf16[8,2,2,64,512]{4,3,2,1,0:T(8,128)(2,1)} fusion(bf16[2,2,18,64,512]{4,3,2,1,0:T(8,128)(2,1)} %bitcast.346, s32[1024]{0:T(1024)S(1)} %pad_clamp_fusion), kind=kCustom, calls=%fused_computation | custom fusion | bytes 4194336 | tf_op jit(solution)/shard_map/jit(_take)/gather | solution.py:104
  120.0 1.9 select_bitcast_fusion
  121.9 1.6 copy.134
  123.4 6.2 %reshape.294 = bf16[2,1024,8,64]{3,2,1,0:T(8,128)(2,1)} reshape(bf16[2,8,2,64,512]{4,3,2,1,0:T(8,128)(2,1)} %copy.134) | data formatting | bytes 4194304 | tf_op jit(solution)/shard_map/reshape | solution.py:105
  129.6 39.0 %conditional.1 = (f32[2,8,2,2,2,2,2,32]{7,6,5,4,3,1,0,2:T(2,128)S(1)}, f32[8,2,2,2,2,2,32,64]{7,6,4,3,2,1,0,5:T(8,128)}) conditional(s32[]{:T(128)} %clamp.3, (bf16[8,1024,64]{1,2,0:T(8,128)(2,1)S(1)}, pred[8]{0:T(512)(128)(4,1)S(1)}, bf16[2,8,1024,64]{3,1,2,0:T(8,128)(2,1)}) %tuple.138, (bf16[8,1024,64]{1,2,0:T(8,128)(2,1)S(1)}, ...), branch_computations={%region_1.6_spmd, %region_6.11_spmd, %region_11.16_spmd} | conditional | flops 1128267776 | bytes 87823080 | solution.py:117
  131.6 4.5 %copy.137 = bf16[2,8,1024,64]{2,3,1,0:T(8,128)(2,1)S(1)} copy(bf16[2,8,1024,64]{3,1,2,0:T(8,128)(2,1)} %get-tuple-element.291) | data formatting | bytes 4194304 | tf_op jit(solution)/shard_map
  136.1 23.3 %while.36 = (s32[]{:T(128)}, f32[2,2,8,512]{3,2,1,0:T(8,128)S(1)}, f32[2,8,512,64]{2,3,1,0:T(8,128)}, bf16[2,8,512,64]{2,3,1,0:T(8,128)(2,1)}, bf16[2,8,1024,64]...) while((s32[]{:T(128)}, f32[2,2,8,512]{3,2,1,0:T(8,128)S(1)}, ...), condition=%wide.region_15.15_spmd.clone, body=%wide.region_12.14_spmd.clone.sunk | while | flops 1128267776 | bytes 70914712 | solution.py:38
  136.2 3.7 %fusion.146 = (f32[8,512]{1,0:T(8,128)S(1)}, f32[8,512,1024]{2,1,0:T(8,128)S(1)}) fusion(pred[1024]{0:T(1024)(128)(4,1)S(1)} %broadcast_bitcast_fusion.4, bf16[2,8,1024,64]{2,3,1,0:T(8,128)(2,1)S(1)} %get-tuple-element.511, bf16[2,8,512,64]{2,3,1,0:T(8,128)(2,1)} %get-tuple-element.510, s32[]{:T(128)} %get-tuple-element.500), kind=kOutput, calls=%fused_computation.50.clone.1 | convolution fusion | flops 549449728 | bytes 18368000 | tf_op jit(solution)/shard_map/cond/branch_2_fun/while/body/eval_jaxpr/hqd,hkd->hqk/dot_general | solution.py:48
  139.9 3.5 %fusion.149 = f32[2,8,512,64]{2,3,1,0:T(8,128)S(1)} fusion(f32[2,8,512,64]{2,3,1,0:T(8,128)S(1)} %copy-done.5, s32[]{:T(128)} %get-tuple-element.500, f32[8,512,1024]{2,1,0:T(8,128)S(1)} %get-tuple-element.475, f32[8,512]{1,0:T(8,128)S(1)} %get-tuple-element.476, pred[1024]{0:T(1024)(128)(4,1)S(1)} %broadcast_bitcast_fusion.4, ...), kind=kOutput, calls=%fused_computation.56.clone.1 | convolution fusion | flops 557842432 | bytes 18891780 | tf_op jit(solution)/shard_map/cond/branch_2_fun/while/body/eval_jaxpr/hqk,hkd->hqd/dot_general | solution.py:54
  143.3 4.4 %fusion.147 = f32[8,512]{1,0:T(8,128)S(1)} fusion(f32[8,512,1024]{2,1,0:T(8,128)S(1)} %get-tuple-element.475, f32[8,512]{1,0:T(8,128)S(1)} %get-tuple-element.476, pred[1024]{0:T(1024)(128)(4,1)S(1)} %broadcast_bitcast_fusion.4), kind=kLoop, calls=%fused_computation.52.clone.1 | loop fusion | flops 20967424 | bytes 16811008 | tf_op jit(solution)/shard_map/cond/branch_2_fun/while/body/eval_jaxpr/reduce_sum | solution.py:53
  147.8 3.7 %fusion.146 = (f32[8,512]{1,0:T(8,128)S(1)}, f32[8,512,1024]{2,1,0:T(8,128)S(1)}) fusion(pred[1024]{0:T(1024)(128)(4,1)S(1)} %broadcast_bitcast_fusion.4, bf16[2,8,1024,64]{2,3,1,0:T(8,128)(2,1)S(1)} %get-tuple-element.511, bf16[2,8,512,64]{2,3,1,0:T(8,128)(2,1)} %get-tuple-element.510, s32[]{:T(128)} %get-tuple-element.500), kind=kOutput, calls=%fused_computation.50.clone.1 | convolution fusion | flops 549449728 | bytes 18368000 | tf_op jit(solution)/shard_map/cond/branch_2_fun/while/body/eval_jaxpr/hqd,hkd->hqk/dot_general | solution.py:48
  151.5 3.5 %fusion.149 = f32[2,8,512,64]{2,3,1,0:T(8,128)S(1)} fusion(f32[2,8,512,64]{2,3,1,0:T(8,128)S(1)} %copy-done.5, s32[]{:T(128)} %get-tuple-element.500, f32[8,512,1024]{2,1,0:T(8,128)S(1)} %get-tuple-element.475, f32[8,512]{1,0:T(8,128)S(1)} %get-tuple-element.476, pred[1024]{0:T(1024)(128)(4,1)S(1)} %broadcast_bitcast_fusion.4, ...), kind=kOutput, calls=%fused_computation.56.clone.1 | convolution fusion | flops 557842432 | bytes 18891780 | tf_op jit(solution)/shard_map/cond/branch_2_fun/while/body/eval_jaxpr/hqk,hkd->hqd/dot_general | solution.py:54
  155.0 4.4 %fusion.147 = f32[8,512]{1,0:T(8,128)S(1)} fusion(f32[8,512,1024]{2,1,0:T(8,128)S(1)} %get-tuple-element.475, f32[8,512]{1,0:T(8,128)S(1)} %get-tuple-element.476, pred[1024]{0:T(1024)(128)(4,1)S(1)} %broadcast_bitcast_fusion.4), kind=kLoop, calls=%fused_computation.52.clone.1 | loop fusion | flops 20967424 | bytes 16811008 | tf_op jit(solution)/shard_map/cond/branch_2_fun/while/body/eval_jaxpr/reduce_sum | solution.py:53
  159.4 3.9 %copy.132 = f32[2,8,512,64]{3,2,0,1:T(8,128)} copy(f32[2,8,512,64]{2,3,1,0:T(8,128)} %get-tuple-element.137) | data formatting | bytes 4194304 | tf_op jit(solution)/shard_map/cond/branch_2_fun/while | solution.py:38
  163.3 4.8 %copy.161 = f32[8,2,2,2,2,2,32,64]{7,6,4,3,2,1,0,5:T(8,128)} copy(f32[8,2,2,2,2,2,32,64]{7,6,5,4,3,2,1,0:T(8,128)} %bitcast.342) | data formatting | bytes 4194304 | tf_op jit(solution)/shard_map/cond | solution.py:117
  168.7 3.2 %dynamic-slice_bitcast_fusion = f32[8,2,2,2,2,32,64]{6,5,4,3,2,1,0:T(8,128)} fusion(f32[8,2,2,2,2,2,32,64]{7,6,4,3,2,1,0,5:T(8,128)} %get-tuple-element.292, s32[]{:T(128)S(6)} %select_n.106), kind=kLoop, calls=%fused_computation.75 | loop fusion | bytes 2097156 | tf_op jit(solution)/shard_map/jit(dynamic_index_in_dim)/squeeze | solution.py:88
  171.9 1.9 collective-permute-start.7
  173.9 2.4 collective-permute-start.6
  176.4 1.8 collective-permute-done.6
  178.2 1.9 collective-permute-start.8
  180.3 4.1 %collective-permute-done.8 = f32[2,8,2,2,2,32]{5,1,4,3,2,0:T(8,128)S(1)} collective-permute-done((f32[2,8,2,2,2,32]{5,1,4,3,2,0:T(8,128)S(1)}, f32[2,8,2,2,2,32]{5,1,4,3,2,0:T(8,128)S(1)}, u32[]{:S(2)}, u32[]{:S(2)}) %collective-permute-start.8) | collective-permute-done | bytes 16416 | tf_op jit(solution)/shard_map/ppermute | solution.py:89
  184.4 2.7 %collective-permute-start.10 = (f32[2,8,2,2,32]{4,1,3,2,0:T(8,128)S(1)}, f32[2,8,2,2,32]{4,1,3,2,0:T(8,128)S(1)}, u32[]{:S(2)}, u32[]{:S(2)}) collective-permute-start(f32[2,8,2,2,32]{4,1,3,2,0:T(8,128)S(1)} %get-tuple-element.363), channel_id=1, source_target_pairs={{0,128},{16,144},{32,160},{48,176},{64,192},{80,208},{96,224},{112... | collective-permute-start | bytes 24584 | tf_op jit(solution)/shard_map/ppermute | solution.py:89
  187.2 2.5 fusion.74
  189.8 2.1 collective-permute-start.9
  192.0 1.9 collective-permute-start.12
  194.0 21.9 %collective-permute-done.9 = f32[8,2,2,2,32,64]{5,4,3,2,1,0:T(8,128)S(1)} collective-permute-done((f32[8,2,2,2,32,64]{5,4,3,2,1,0:T(8,128)S(1)}, f32[8,2,2,2,32,64]{5,4,3,2,1,0:T(8,128)S(1)}, u32[]{:S(2)}, u32[]{:S(2)}) %collective-permute-start.9) | collective-permute-done | bytes 524320 | tf_op jit(solution)/shard_map/ppermute | solution.py:90
  216.5 3.1 %collective-permute-start.11 = (f32[8,2,2,32,64]{4,3,2,1,0:T(8,128)S(1)}, f32[8,2,2,32,64]{4,3,2,1,0:T(8,128)S(1)}, u32[]{:S(2)}, u32[]{:S(2)}) collective-permute-start(f32[8,2,2,32,64]{4,3,2,1,0:T(8,128)S(1)} %dynamic-slice_bitcast_fusion.2), channel_id=1, source_target_pairs={{0,128},{16,144},{32,160},{48,176},{64,192},{80,208},{96,224},{112... | collective-permute-start | bytes 786440 | tf_op jit(solution)/shard_map/ppermute | solution.py:90
  219.7 10.3 %collective-permute-done.11 = f32[8,2,2,32,64]{4,3,2,1,0:T(8,128)S(1)} collective-permute-done((f32[8,2,2,32,64]{4,3,2,1,0:T(8,128)S(1)}, f32[8,2,2,32,64]{4,3,2,1,0:T(8,128)S(1)}, u32[]{:S(2)}, u32[]{:S(2)}) %collective-permute-start.11) | collective-permute-done | bytes 262176 | tf_op jit(solution)/shard_map/ppermute | solution.py:90
  230.4 1.9 collective-permute-start.13
  232.4 3.0 %collective-permute-start.14 = (f32[2,8,32]{2,1,0:T(8,128)S(1)}, f32[2,8,32]{2,1,0:T(8,128)S(1)}, u32[]{:S(2)}, u32[]{:S(2)}) collective-permute-start(f32[2,8,32]{2,1,0:T(8,128)S(1)} %get-tuple-element.369), channel_id=1, source_target_pairs={{0,256},{16,272},{32,288},{48,304},{64,320},{80,336},{96,352},{112... | collective-permute-start | bytes 6152 | tf_op jit(solution)/shard_map/ppermute | solution.py:89
  235.4 8.5 %collective-permute-done.13 = f32[8,2,32,64]{3,2,1,0:T(8,128)S(1)} collective-permute-done((f32[8,2,32,64]{3,2,1,0:T(8,128)S(1)}, f32[8,2,32,64]{3,2,1,0:T(8,128)S(1)}, u32[]{:S(2)}, u32[]{:S(2)}) %collective-permute-start.13) | collective-permute-done | bytes 131104 | tf_op jit(solution)/shard_map/ppermute | solution.py:90
  244.2 3.0 %collective-permute-start.15 = (f32[8,32,64]{2,0,1:T(8,128)S(1)}, f32[8,32,64]{2,0,1:T(8,128)S(1)}, u32[]{:S(2)}, u32[]{:S(2)}) collective-permute-start(f32[8,32,64]{2,0,1:T(8,128)S(1)} %bitcast.360), channel_id=1, source_target_pairs={{0,256},{16,272},{32,288},{48,304},{64,320},{80,336},{96,352},{112... | collective-permute-start | bytes 196616 | tf_op jit(solution)/shard_map/ppermute | solution.py:90
  247.5 5.1 %collective-permute-done.15 = f32[8,32,64]{2,0,1:T(8,128)S(1)} collective-permute-done((f32[8,32,64]{2,0,1:T(8,128)S(1)}, f32[8,32,64]{2,0,1:T(8,128)S(1)}, u32[]{:S(2)}, u32[]{:S(2)}) %collective-permute-start.15) | collective-permute-done | bytes 65568 | tf_op jit(solution)/shard_map/ppermute | solution.py:90
  (72 shorter events, 9.9 us)
Async XLA Ops:
  0.0 253.3 %copy-start = (bf16[512,512]{1,0:T(8,128)(2,1)S(1)}, bf16[512,512]{1,0:T(8,128)(2,1)}, u32[]{:S(2)}) copy-start(bf16[512,512]{1,0:T(8,128)(2,1)} %param.18) | copy-start | bytes 1572868
  0.0 111.3 %copy-start.7 = (bf16[2,2,1,1,2,64,512]{6,5,4,3,2,1,0:T(8,128)(2,1)S(1)}, bf16[2,2,1,1,2,64,512]{6,5,4,3,2,1,0:T(8,128)(2,1)}, u32[]{:S(2)}) copy-start(bf16[2,2,1,1,2,64,512]{6,5,4,3,2,1,0:T(8,128)(2,1)} %param.15) | copy-start | bytes 1572868
  0.0 20.8 %collective-permute-start = (bf16[2,2,1,1,2,64,512]{6,5,4,3,2,1,0:T(8,128)(2,1)}, bf16[2,2,1,1,2,64,512]{6,5,4,3,2,1,0:T(8,128)(2,1)S(1)}, u32[]{:S(2)}, u32[]{:S(2)}) collective-permute-start(bf16[2,2,1,1,2,64,512]{6,5,4,3,2,1,0:T(8,128)(2,1)} %param.15), channel_id=1, source_target_pairs={{0,1},{1,2},{2,3},{4,5},{5,6},{6,7},{8,9},{9,10},{10,11},{12,13},{... | collective-permute-start | bytes 1572872 | tf_op jit(solution)/shard_map/ppermute | solution.py:18
  9.3 54.6 %collective-permute-start.1 = (bf16[2,2,1,1,2,64,512]{6,5,4,3,2,1,0:T(8,128)(2,1)}, bf16[2,2,1,1,2,64,512]{6,5,4,3,2,1,0:T(8,128)(2,1)S(1)}, u32[]{:S(2)}, u32[]{:S(2)}) collective-permute-start(bf16[2,2,1,1,2,64,512]{6,5,4,3,2,1,0:T(8,128)(2,1)} %param.15), channel_id=1, source_target_pairs={{1,0},{2,1},{3,2},{5,4},{6,5},{7,6},{9,8},{10,9},{11,10},{13,12},{... | collective-permute-start | bytes 1572872 | tf_op jit(solution)/shard_map/ppermute | solution.py:18
  64.7 27.4 %collective-permute-start.2 = (bf16[2,2,1,2,2,64,512]{6,5,4,3,2,1,0:T(8,128)(2,1)}, bf16[2,2,1,2,2,64,512]{6,5,4,3,2,1,0:T(8,128)(2,1)}, u32[]{:S(2)}, u32[]{:S(2)}) collective-permute-start(bf16[2,2,1,2,2,64,512]{6,5,4,3,2,1,0:T(8,128)(2,1)} %constant_dynamic-update-slice_fusion), channel_id=1, source_target_pairs={{0,4},{4,8},{8,12},{1,5},{5,9},{9,13},{2,6},{6,10},{10,14},{3,7},{... | collective-permute-start | bytes 3145736 | tf_op jit(solution)/shard_map/ppermute | solution.py:18
  69.2 42.0 %collective-permute-start.3 = (bf16[2,2,1,1,2,64,512]{6,5,4,3,2,1,0:T(8,128)(2,1)}, bf16[2,2,1,1,2,64,512]{6,5,4,3,2,1,0:T(8,128)(2,1)}, u32[]{:S(2)}, u32[]{:S(2)}) collective-permute-start(bf16[2,2,1,1,2,64,512]{6,5,4,3,2,1,0:T(8,128)(2,1)} %param.15), channel_id=1, source_target_pairs={{0,4},{4,8},{8,12},{1,5},{5,9},{9,13},{2,6},{6,10},{10,14},{3,7},{... | collective-permute-start | bytes 1572872 | tf_op jit(solution)/shard_map/ppermute | solution.py:18
  72.5 38.8 %collective-permute-start.5 = (bf16[2,2,1,1,2,64,512]{6,5,4,3,2,1,0:T(8,128)(2,1)}, bf16[2,2,1,1,2,64,512]{6,5,4,3,2,1,0:T(8,128)(2,1)}, u32[]{:S(2)}, u32[]{:S(2)}) collective-permute-start(bf16[2,2,1,1,2,64,512]{6,5,4,3,2,1,0:T(8,128)(2,1)} %param.15), channel_id=1, source_target_pairs={{4,0},{8,4},{12,8},{5,1},{9,5},{13,9},{6,2},{10,6},{14,10},{7,3},{... | collective-permute-start | bytes 1572872 | tf_op jit(solution)/shard_map/ppermute | solution.py:18
  77.3 32.7 %collective-permute-start.4 = (bf16[2,2,1,2,2,64,512]{6,5,4,3,2,1,0:T(8,128)(2,1)}, bf16[2,2,1,2,2,64,512]{6,5,4,3,2,1,0:T(8,128)(2,1)}, u32[]{:S(2)}, u32[]{:S(2)}) collective-permute-start(bf16[2,2,1,2,2,64,512]{6,5,4,3,2,1,0:T(8,128)(2,1)} %constant_dynamic-update-slice_fusion), channel_id=1, source_target_pairs={{4,0},{8,4},{12,8},{5,1},{9,5},{13,9},{6,2},{10,6},{14,10},{7,3},{... | collective-permute-start | bytes 3145736 | tf_op jit(solution)/shard_map/ppermute | solution.py:18
  136.2 3.7 %copy-start.5 = (f32[2,8,512,64]{2,3,1,0:T(8,128)S(1)}, f32[2,8,512,64]{2,3,1,0:T(8,128)}, u32[]{:S(2)}) copy-start(f32[2,8,512,64]{2,3,1,0:T(8,128)} %get-tuple-element.502) | copy-start | bytes 6291460 | tf_op jit(solution)/shard_map/cond/branch_2_fun/while
  143.3 4.4 %copy-start.6 = (f32[2,8,512,64]{2,3,1,0:T(8,128)}, f32[2,8,512,64]{2,3,1,0:T(8,128)S(1)}, u32[]{:S(2)}) copy-start(f32[2,8,512,64]{2,3,1,0:T(8,128)S(1)} %fusion.149) | copy-start | bytes 6291460 | tf_op jit(solution)/shard_map/cond/branch_2_fun/while
  147.8 3.7 %copy-start.5 = (f32[2,8,512,64]{2,3,1,0:T(8,128)S(1)}, f32[2,8,512,64]{2,3,1,0:T(8,128)}, u32[]{:S(2)}) copy-start(f32[2,8,512,64]{2,3,1,0:T(8,128)} %get-tuple-element.502) | copy-start | bytes 6291460 | tf_op jit(solution)/shard_map/cond/branch_2_fun/while
  155.0 4.4 %copy-start.6 = (f32[2,8,512,64]{2,3,1,0:T(8,128)}, f32[2,8,512,64]{2,3,1,0:T(8,128)S(1)}, u32[]{:S(2)}) copy-start(f32[2,8,512,64]{2,3,1,0:T(8,128)S(1)} %fusion.149) | copy-start | bytes 6291460 | tf_op jit(solution)/shard_map/cond/branch_2_fun/while
  171.9 15.2 %collective-permute-start.7 = (f32[8,2,2,2,2,32,64]{6,5,4,3,2,1,0:T(8,128)}, f32[8,2,2,2,2,32,64]{6,5,4,3,2,1,0:T(8,128)S(1)}, u32[]{:S(2)}, u32[]{:S(2)}) collective-permute-start(f32[8,2,2,2,2,32,64]{6,5,4,3,2,1,0:T(8,128)} %dynamic-slice_bitcast_fusion), channel_id=1, source_target_pairs={{0,16},{16,0},{32,48},{48,32},{64,80},{80,64},{96,112},{112,96},{1... | collective-permute-start | bytes 3145736 | tf_op jit(solution)/shard_map/ppermute | solution.py:90
  173.9 4.3 %collective-permute-start.6 = (f32[2,8,2,2,2,2,32]{6,1,5,4,3,2,0:T(8,128)S(1)}, f32[2,8,2,2,2,2,32]{6,1,5,4,3,2,0:T(8,128)S(1)}, u32[]{:S(2)}, u32[]{:S(2)}) collective-permute-start(f32[2,8,2,2,2,2,32]{6,1,5,4,3,2,0:T(8,128)S(1)} %dynamic-slice_bitcast_fusion.4), channel_id=1, source_target_pairs={{0,16},{16,0},{32,48},{48,32},{64,80},{80,64},{96,112},{112,96},{1... | collective-permute-start | bytes 98312 | tf_op jit(solution)/shard_map/ppermute | solution.py:89
  178.2 6.2 %collective-permute-start.8 = (f32[2,8,2,2,2,32]{5,1,4,3,2,0:T(8,128)S(1)}, f32[2,8,2,2,2,32]{5,1,4,3,2,0:T(8,128)S(1)}, u32[]{:S(2)}, u32[]{:S(2)}) collective-permute-start(f32[2,8,2,2,2,32]{5,1,4,3,2,0:T(8,128)S(1)} %get-tuple-element.359), channel_id=1, source_target_pairs={{0,32},{16,48},{32,0},{48,16},{64,96},{80,112},{96,64},{112,80},{1... | collective-permute-start | bytes 49160 | tf_op jit(solution)/shard_map/ppermute | solution.py:89
  184.4 7.5 %collective-permute-start.10 = (f32[2,8,2,2,32]{4,1,3,2,0:T(8,128)S(1)}, f32[2,8,2,2,32]{4,1,3,2,0:T(8,128)S(1)}, u32[]{:S(2)}, u32[]{:S(2)}) collective-permute-start(f32[2,8,2,2,32]{4,1,3,2,0:T(8,128)S(1)} %get-tuple-element.363), channel_id=1, source_target_pairs={{0,128},{16,144},{32,160},{48,176},{64,192},{80,208},{96,224},{112... | collective-permute-start | bytes 24584 | tf_op jit(solution)/shard_map/ppermute | solution.py:89
  189.8 26.0 %collective-permute-start.9 = (f32[8,2,2,2,32,64]{5,4,3,2,1,0:T(8,128)S(1)}, f32[8,2,2,2,32,64]{5,4,3,2,1,0:T(8,128)S(1)}, u32[]{:S(2)}, u32[]{:S(2)}) collective-permute-start(f32[8,2,2,2,32,64]{5,4,3,2,1,0:T(8,128)S(1)} %dynamic-slice_bitcast_fusion.1), channel_id=1, source_target_pairs={{0,32},{16,48},{32,0},{48,16},{64,96},{80,112},{96,64},{112,80},{1... | collective-permute-start | bytes 1572872 | tf_op jit(solution)/shard_map/ppermute | solution.py:90
  192.0 27.7 %collective-permute-start.12 = (f32[2,8,2,32]{3,1,2,0:T(8,128)S(1)}, f32[2,8,2,32]{3,1,2,0:T(8,128)S(1)}, u32[]{:S(2)}, u32[]{:S(2)}) collective-permute-start(f32[2,8,2,32]{3,1,2,0:T(8,128)S(1)} %get-tuple-element.367), channel_id=1, source_target_pairs={{0,64},{16,80},{32,96},{48,112},{64,0},{80,16},{96,32},{112,48},{1... | collective-permute-start | bytes 12296 | tf_op jit(solution)/shard_map/ppermute | solution.py:89
  216.5 13.5 %collective-permute-start.11 = (f32[8,2,2,32,64]{4,3,2,1,0:T(8,128)S(1)}, f32[8,2,2,32,64]{4,3,2,1,0:T(8,128)S(1)}, u32[]{:S(2)}, u32[]{:S(2)}) collective-permute-start(f32[8,2,2,32,64]{4,3,2,1,0:T(8,128)S(1)} %dynamic-slice_bitcast_fusion.2), channel_id=1, source_target_pairs={{0,128},{16,144},{32,160},{48,176},{64,192},{80,208},{96,224},{112... | collective-permute-start | bytes 786440 | tf_op jit(solution)/shard_map/ppermute | solution.py:90
  230.4 13.5 %collective-permute-start.13 = (f32[8,2,32,64]{3,2,1,0:T(8,128)S(1)}, f32[8,2,32,64]{3,2,1,0:T(8,128)S(1)}, u32[]{:S(2)}, u32[]{:S(2)}) collective-permute-start(f32[8,2,32,64]{3,2,1,0:T(8,128)S(1)} %dynamic-slice_bitcast_fusion.3), channel_id=1, source_target_pairs={{0,64},{16,80},{32,96},{48,112},{64,0},{80,16},{96,32},{112,48},{1... | collective-permute-start | bytes 393224 | tf_op jit(solution)/shard_map/ppermute | solution.py:90
  232.4 14.8 %collective-permute-start.14 = (f32[2,8,32]{2,1,0:T(8,128)S(1)}, f32[2,8,32]{2,1,0:T(8,128)S(1)}, u32[]{:S(2)}, u32[]{:S(2)}) collective-permute-start(f32[2,8,32]{2,1,0:T(8,128)S(1)} %get-tuple-element.369), channel_id=1, source_target_pairs={{0,256},{16,272},{32,288},{48,304},{64,320},{80,336},{96,352},{112... | collective-permute-start | bytes 6152 | tf_op jit(solution)/shard_map/ppermute | solution.py:89
  244.2 8.4 %collective-permute-start.15 = (f32[8,32,64]{2,0,1:T(8,128)S(1)}, f32[8,32,64]{2,0,1:T(8,128)S(1)}, u32[]{:S(2)}, u32[]{:S(2)}) collective-permute-start(f32[8,32,64]{2,0,1:T(8,128)S(1)} %bitcast.360), channel_id=1, source_target_pairs={{0,256},{16,272},{32,288},{48,304},{64,320},{80,336},{96,352},{112... | collective-permute-start | bytes 196616 | tf_op jit(solution)/shard_map/ppermute | solution.py:90

commit v3 on v1

--- a/solution.py
+++ b/solution.py
@@ -1,10 +1,13 @@
 import jax
 import jax.numpy as jnp
 from jax import lax
+from jax.experimental import pallas as pl
+from jax.experimental.pallas import tpu as pltpu
 from jax.sharding import PartitionSpec as P
 
 HEADS = 8
 HD = 64
+TQ = 256
 
 
 def shifted(array, axis, forward):
@@ -19,27 +22,79 @@
 def neighbourhood(kv_blocks):
     left = shifted(kv_blocks, "width", True)
     right = shifted(kv_blocks, "width", False)
+    up_mid = shifted(kv_blocks, "height", True)
+    down_mid = shifted(kv_blocks, "height", False)
+    left, right, up_mid, down_mid = lax.optimization_barrier((left, right, up_mid, down_mid))
+    sides = jnp.concatenate([left, right], axis=3)
+    up_sides = shifted(sides, "height", True)
+    down_sides = shifted(sides, "height", False)
     row = jnp.concatenate([left, kv_blocks, right], axis=3)
-    up = shifted(row, "height", True)
-    down = shifted(row, "height", False)
+    up = jnp.concatenate([up_sides[:, :, :, :1], up_mid, up_sides[:, :, :, 1:]], axis=3)
+    down = jnp.concatenate([down_sides[:, :, :, :1], down_mid, down_sides[:, :, :, 1:]], axis=3)
     return jnp.concatenate([up, row, down], axis=2)
 
 
-def group_partial(query_rows, keys, values, keep):
-    count = query_rows.shape[0]
-    query_heads = query_rows.reshape(count, HEADS, HD)
-    key_heads = keys.reshape(-1, HEADS, HD)
-    value_heads = values.reshape(-1, HEADS, HD)
-    scores = jnp.einsum("qhd,khd->hqk", query_heads, key_heads, preferred_element_type=jnp.float32)
-    scores = scores / jnp.sqrt(jnp.float32(HD))
-    scores = jnp.where(keep[None, None, :], scores, jnp.float32(-1e30))
-    row_top = jnp.max(scores, axis=2)
-    probs = jnp.where(keep[None, None, :], jnp.exp(scores - row_top[:, :, None]), jnp.float32(0.0))
-    totals = jnp.sum(probs, axis=2)
-    outputs = jnp.einsum(
-        "hqk,khd->qhd", probs.astype(jnp.bfloat16), value_heads, preferred_element_type=jnp.float32
-    )
-    return (row_top.T, totals.T, outputs.reshape(count, HEADS * HD))
+def attention_kernel(q_ref, k_ref, v_ref, keep_ref, o_ref, st_ref):
+    rows = q_ref.shape[0]
+    keep = keep_ref[...] > 0
+    lane = lax.broadcasted_iota(jnp.int32, (1, 2 * HD), 1)
+    low = lane < HD
+    stat_lane = lax.broadcasted_iota(jnp.int32, (1, 2 * HEADS), 1)
+    stats = jnp.zeros((rows, 2 * HEADS), jnp.float32)
+    for pair in range(HEADS // 2):
+        cols = pl.ds(pair * 2 * HD, 2 * HD)
+        q2 = q_ref[:, cols]
+        k2 = k_ref[:, cols]
+        v2 = v_ref[:, cols]
+        outs = []
+        for half in range(2):
+            mine = low if half == 0 else jnp.logical_not(low)
+            qh = jnp.where(mine, q2, jnp.zeros_like(q2))
+            scores = lax.dot_general(
+                qh, k2, (((1,), (1,)), ((), ())), preferred_element_type=jnp.float32
+            )
+            scores = scores / jnp.float32(8.0)
+            scores = jnp.where(keep, scores, jnp.float32(-1e30))
+            top = jnp.max(scores, axis=1, keepdims=True)
+            probs = jnp.where(keep, jnp.exp(scores - top), jnp.float32(0.0))
+            total = jnp.sum(probs, axis=1, keepdims=True)
+            outs.append(
+                jnp.dot(probs.astype(jnp.bfloat16), v2, preferred_element_type=jnp.float32)
+            )
+            head = pair * 2 + half
+            stats = jnp.where(stat_lane == head, top, stats)
+            stats = jnp.where(stat_lane == HEADS + head, total, stats)
+        o_ref[:, cols] = jnp.where(low, outs[0], outs[1])
+    st_ref[...] = stats
+
+
+def attention(query_rows, keys, values, keep):
+    qtok, width = query_rows.shape
+    count = keys.shape[0]
+    flops = 2 * 2 * qtok * count * 2 * width
+    return pl.pallas_call(
+        attention_kernel,
+        grid=(qtok // TQ,),
+        in_specs=[
+            pl.BlockSpec((TQ, width), lambda i: (i, 0)),
+            pl.BlockSpec((count, width), lambda i: (0, 0)),
+            pl.BlockSpec((count, width), lambda i: (0, 0)),
+            pl.BlockSpec((1, count), lambda i: (0, 0)),
+        ],
+        out_specs=[
+            pl.BlockSpec((TQ, width), lambda i: (i, 0)),
+            pl.BlockSpec((TQ, 2 * HEADS), lambda i: (i, 0)),
+        ],
+        out_shape=[
+            jax.ShapeDtypeStruct((qtok, width), jnp.float32),
+            jax.ShapeDtypeStruct((qtok, 2 * HEADS), jnp.float32),
+        ],
+        cost_estimate=pl.CostEstimate(
+            flops=flops,
+            transcendentals=qtok * count * HEADS,
+            bytes_accessed=qtok * width * 6 + count * width * 4,
+        ),
+    )(query_rows, keys, values, keep)
 
 
 def merge(stats_a, out_a, stats_b, out_b):
@@ -93,25 +148,12 @@
     listed = block_list[0, 0]
     nlist = listed.shape[0]
     chosen = jnp.take(hood, listed, axis=2)
-    keep = jnp.broadcast_to((block_valid[0, 0] > 0)[None, :, None], (frames, nlist, blk)).reshape(
-        -1
-    )
+    keep = jnp.broadcast_to((block_valid[0, 0] > 0)[None, :, None], (frames, nlist, blk))
+    keep = keep.reshape(1, -1).astype(jnp.int32)
     keys = chosen[0].reshape(-1, width)
     values = chosen[1].reshape(-1, width)
     query_rows = queries[0, 0]
-    qtok = query_rows.shape[0]
-    step_rows = min(512, qtok)
-
-    def one_block(rows):
-        return group_partial(rows, keys, values, keep)
-
-    tops, totals, outputs = lax.map(
-        one_block, query_rows.reshape(qtok // step_rows, step_rows, width)
-    )
-    tops = tops.reshape(qtok, HEADS)
-    totals = totals.reshape(qtok, HEADS)
-    outputs = outputs.reshape(qtok, width)
-    stats = jnp.concatenate([tops, totals], axis=-1)
+    outputs, stats = attention(query_rows, keys, values, keep)
     stats, summed = tree_reduce(stats, outputs)
     total = stats[:, HEADS:]
     own_rows = summed.shape[0]

time: 240 us -> 197 us (0.82)
  matrix products: 25.6 us -> 0.87 us
  local copies, waits for them, and re-layouts: 40.8 us -> 21.5 us
  Pallas kernels: 0 us -> 18.7 us
  waiting for transfers between devices: 112 us -> 94.9 us
  other arithmetic: 17.5 us -> 11.9 us
  starting transfers between devices: 42.5 us -> 47 us
    dot_general x4 -> x0, matrix products: 24.7 us -> none  [the longest x2 17.1 us: group_partial(): jnp.einsum('hqk,khd->qhd', probs.astype(jnp.bfloat16), value_heads, prefe...]
    pallas_call x0 -> x1, Pallas kernels: none -> 18.7 us  [attention(): pl.pallas_call(attention_kernel, grid=(qtok // TQ,), in_specs=[pl.BlockSp...]
    ppermute x4 -> x6, waiting for transfers between devices: 88.3 us -> 69.6 us  [shifted(): return lax.ppermute(array, axis, pairs)]
    another operation x4 -> x0, local copies, waits for them, and re-layouts: 11.1 us -> none  [the longest x2 5.57 us: group_partial(): key_heads = keys.reshape(-1, HEADS, HD)]
    reduce_sum x2 -> x0, other arithmetic: 8.95 us -> none  [group_partial(): totals = jnp.sum(probs, axis=2)]
    dynamic_update_slice x6 -> x0, local copies, waits for them, and re-layouts: 5.24 us -> none  [local(): lax.map(one_block, query_rows.reshape(qtok // step_rows, step_rows, width))]
    ppermute x4 -> x6, starting transfers between devices: 16.5 us -> 21.1 us  [shifted(): return lax.ppermute(array, axis, pairs)]
    dynamic_slice x4 -> x0, local copies, waits for them, and re-layouts: 2.58 us -> none  [local(): lax.map(one_block, query_rows.reshape(qtok // step_rows, step_rows, width))]
  transfers between devices with their start and end apart: 14 -> 16, of which waited for: 9 -> 9; matrix products, arithmetic and copies ran while one was open for 5% -> 8% of each run, Pallas kernels for 0% -> 0%
where the time goes in v3:
time: 197 us; the launch traced here: 195 us
  waiting for transfers between devices  94.9 us (48%)
  starting transfers between devices  47 us (24%)
  local copies, waits for them, and re-layouts  21.5 us (11%)
  Pallas kernels  18.7 us (9%)
  other arithmetic  11.9 us (6%)
    ppermute x6, waiting for transfers between devices, shifted(): return lax.ppermute(array, axis, pairs)  69.6 us
    ppermute x6, starting transfers between devices, shifted(): return lax.ppermute(array, axis, pairs)  21.1 us
    pallas_call x1, Pallas kernels, attention(): pl.pallas_call(attention_kernel, grid=(qtok // TQ,), in_specs=[pl.BlockSp...  18.7 us
    ppermute x5, waiting for transfers between devices, tree_reduce(): got_s = lax.ppermute(send_s, 'tm', pairs)  14.2 us
    ppermute x5, starting transfers between devices, tree_reduce(): got_s = lax.ppermute(send_s, 'tm', pairs)  14 us
    ppermute x5, starting transfers between devices, tree_reduce(): got_o = lax.ppermute(send_o, 'tm', pairs)  11.9 us
    ppermute x5, waiting for transfers between devices, tree_reduce(): got_o = lax.ppermute(send_o, 'tm', pairs)  11.1 us
    concatenate x1, other arithmetic, neighbourhood(): return jnp.concatenate([up, row, down], axis=2)  4.29 us
  transfers between devices with their start and end apart: 16, of which 9 were waited for; matrix products, arithmetic and copies ran while one was open for 8% of the time, Pallas kernels for 0%

profile of v3, /device:TPU:6, one launch (start us, length us, event | category | flops | bytes accessed | tf_op | source)
XLA Modules:
  0.0 195.4 jit_solution(12668012563276983113)
XLA Ops:
  0.0 9.2 %collective-permute-start = (bf16[2,2,1,1,2,64,512]{6,5,4,3,2,1,0:T(8,128)(2,1)}, bf16[2,2,1,1,2,64,512]{6,5,4,3,2,1,0:T(8,128)(2,1)S(1)}, u32[]{:S(2)}, u32[]{:S(2)}) collective-permute-start(bf16[2,2,1,1,2,64,512]{6,5,4,3,2,1,0:T(8,128)(2,1)} %param.6), channel_id=1, source_target_pairs={{0,1},{1,2},{2,3},{4,5},{5,6},{6,7},{8,9},{9,10},{10,11},{12,13},{... | collective-permute-start | bytes 1572872 | tf_op jit(solution)/shard_map/ppermute | solution.py:19
  9.3 1.3 collective-permute-start.1
  10.6 3.5 %collective-permute-start.2 = (bf16[2,2,1,1,2,64,512]{6,5,4,3,2,1,0:T(8,128)(2,1)}, bf16[2,2,1,1,2,64,512]{6,5,4,3,2,1,0:T(8,128)(2,1)S(1)}, u32[]{:S(2)}, u32[]{:S(2)}) collective-permute-start(bf16[2,2,1,1,2,64,512]{6,5,4,3,2,1,0:T(8,128)(2,1)} %param.6), channel_id=1, source_target_pairs={{0,4},{4,8},{8,12},{1,5},{5,9},{9,13},{2,6},{6,10},{10,14},{3,7},{... | collective-permute-start | bytes 1572872 | tf_op jit(solution)/shard_map/ppermute | solution.py:19
  14.1 1.3 collective-permute-start.3
  15.4 5.5 %collective-permute-done = bf16[2,2,1,1,2,64,512]{6,5,4,3,2,1,0:T(8,128)(2,1)S(1)} collective-permute-done((bf16[2,2,1,1,2,64,512]{6,5,4,3,2,1,0:T(8,128)(2,1)}, bf16[2,2,1,1,2,64,512]{6,5,4,3,2,1,0:T(8,128)(2,1)S(1)}, u32[]{:S(2)}, u32[]{:S(2)}) %collective-permute-start) | collective-permute-done | bytes 524320 | tf_op jit(solution)/shard_map/ppermute | solution.py:19
  20.8 43.0 %collective-permute-done.1 = bf16[2,2,1,1,2,64,512]{6,5,4,3,2,1,0:T(8,128)(2,1)S(1)} collective-permute-done((bf16[2,2,1,1,2,64,512]{6,5,4,3,2,1,0:T(8,128)(2,1)}, bf16[2,2,1,1,2,64,512]{6,5,4,3,2,1,0:T(8,128)(2,1)S(1)}, u32[]{:S(2)}, u32[]{:S(2)}) %collective-permute-start.1) | collective-permute-done | bytes 524320 | tf_op jit(solution)/shard_map/ppermute | solution.py:19
  63.9 0.9 constant_dynamic-update-slice_fusion.1
  64.8 0.9 constant_dynamic-update-slice_fusion
  65.7 4.5 %collective-permute-start.4 = (bf16[2,2,1,2,2,64,512]{6,5,4,3,2,1,0:T(8,128)(2,1)}, bf16[2,2,1,2,2,64,512]{6,5,4,3,2,1,0:T(8,128)(2,1)}, u32[]{:S(2)}, u32[]{:S(2)}) collective-permute-start(bf16[2,2,1,2,2,64,512]{6,5,4,3,2,1,0:T(8,128)(2,1)} %constant_dynamic-update-slice_fusion), channel_id=1, source_target_pairs={{0,4},{4,8},{8,12},{1,5},{5,9},{9,13},{2,6},{6,10},{10,14},{3,7},{... | collective-permute-start | bytes 3145736 | tf_op jit(solution)/shard_map/ppermute | solution.py:19
  70.2 1.3 collective-permute-start.5
  71.4 0.7 fusion.30
  72.2 0.7 convert_element_type.12.keep_ref
  72.9 0.7 fusion.31
  73.5 0.7 compare_and_fusion
  74.2 17.4 %collective-permute-done.4 = bf16[2,2,1,2,2,64,512]{6,5,4,3,2,1,0:T(8,128)(2,1)} collective-permute-done((bf16[2,2,1,2,2,64,512]{6,5,4,3,2,1,0:T(8,128)(2,1)}, bf16[2,2,1,2,2,64,512]{6,5,4,3,2,1,0:T(8,128)(2,1)}, u32[]{:S(2)}, u32[]{:S(2)}) %collective-permute-start.4) | collective-permute-done | bytes 1048608 | tf_op jit(solution)/shard_map/ppermute | solution.py:19
  91.6 1.3 fusion.36
  92.9 3.7 %collective-permute-done.5 = bf16[2,2,1,2,2,64,512]{6,5,4,3,2,1,0:T(8,128)(2,1)S(1)} collective-permute-done((bf16[2,2,1,2,2,64,512]{6,5,4,3,2,1,0:T(8,128)(2,1)}, bf16[2,2,1,2,2,64,512]{6,5,4,3,2,1,0:T(8,128)(2,1)S(1)}, u32[]{:S(2)}, u32[]{:S(2)}) %collective-permute-start.5) | collective-permute-done | bytes 1048608 | tf_op jit(solution)/shard_map/ppermute | solution.py:19
  96.7 4.3 %maximum_maximum_fusion = bf16[2,2,3,3,2,64,512]{6,5,4,3,2,1,0:T(8,128)(2,1)} fusion(bf16[2,2,1,1,2,64,512]{6,5,4,3,2,1,0:T(8,128)(2,1)S(1)} %get-tuple-element.43, bf16[2,2,1,1,2,64,512]{6,5,4,3,2,1,0:T(8,128)(2,1)} %copy-done.3, bf16[2,2,1,1,2,64,512]{6,5,4,3,2,1,0:T(8,128)(2,1)S(1)} %get-tuple-element.42, ...), kind=kLoop, calls=%fused_computation.1 | loop fusion | flops 18874368 | bytes 9437184 | tf_op jit(solution)/shard_map/concatenate | solution.py:34
  101.0 3.0 %gather_fusion = bf16[8,2,2,64,512]{4,3,2,1,0:T(8,128)(2,1)S(1)} fusion(bf16[2,2,18,64,512]{4,3,2,1,0:T(8,128)(2,1)} %bitcast.88, s32[1024]{0:T(1024)S(1)} %pad_clamp_fusion), kind=kCustom, calls=%fused_computation | custom fusion | bytes 4194336 | tf_op jit(solution)/shard_map/jit(_take)/gather | solution.py:150
  104.5 1.1 copy.6
  105.6 1.1 copy.7
  106.6 18.7 %shard_map.55 = (f32[1024,512]{1,0:T(8,128)}, f32[1024,16]{1,0:T(8,128)}) custom-call(bf16[1024,512]{1,0:T(8,128)(2,1)} %bitcast.94, bf16[1024,512]{1,0:T(8,128)(2,1)} %bitcast.91, bf16[1024,512]{1,0:T(8,128)(2,1)} %bitcast.92, s32[1,1024]{1,0:T(1,128)} %convert_element_type.12.keep_ref), custom_call_target="tpu_custom_call" | custom-call | flops 4294967296 | bytes 5242880 | tf_op jit(solution)/shard_map/pallas_call | solution.py:75
  125.4 2.3 %dynamic-slice_bitcast_fusion = f32[2,2,2,2,32,512]{5,4,3,2,1,0:T(8,128)} fusion(f32[2,2,2,2,2,32,512]{6,5,4,3,2,1,0:T(8,128)} %bitcast.89, s32[]{:T(128)S(6)} %select_n.74), kind=kLoop, calls=%fused_computation.6 | loop fusion | bytes 2097156 | tf_op jit(solution)/shard_map/jit(dynamic_index_in_dim)/squeeze | solution.py:134
  127.7 1.9 collective-permute-start.7
  129.6 1.1 dynamic-slice_bitcast_fusion.4
  130.7 2.4 %collective-permute-start.6 = (f32[2,2,2,2,32,16]{5,4,3,2,1,0:T(8,128)S(1)}, f32[2,2,2,2,32,16]{5,4,3,2,1,0:T(8,128)S(1)}, u32[]{:S(2)}, u32[]{:S(2)}) collective-permute-start(f32[2,2,2,2,32,16]{5,4,3,2,1,0:T(8,128)S(1)} %get-tuple-element.47), channel_id=1, source_target_pairs={{0,16},{16,0},{32,48},{48,32},{64,80},{80,64},{96,112},{112,96},{1... | collective-permute-start | bytes 98312 | tf_op jit(solution)/shard_map/ppermute | solution.py:135
  133.1 1.1 collective-permute-done.6
  134.5 0.6 mul.151
  135.1 1.5 mul.152
  136.5 0.6 mul.154
  137.1 1.5 mul.155
  138.6 2.7 %fusion = f32[2,2,2,2,32,512]{5,4,3,2,1,0:T(8,128)S(1)} fusion(f32[2,2,2,2,32,512]{5,4,3,2,1,0:T(8,128)} %mul.152, f32[2,2,2,2,32,512]{5,4,3,2,1,0:T(8,128)} %collective-permute-done.7, f32[2,2,2,2,32,512]{5,4,3,2,1,0:T(8,128)} %mul.155, f32[2,2,2,2,2,32,512]{6,5,4,3,2,1,0:T(8,128)} %bitcast.90, s32[]{:T(128)S(6)} %select_n.73), kind=kLoop, calls=%fused_computation.5 | loop fusion | flops 786432 | bytes 5242884 | tf_op jit(solution)/shard_map/add | solution.py:110
  141.3 0.9 dynamic-slice_bitcast_fusion.1
  142.2 1.9 collective-permute-start.9
  144.2 3.9 %collective-permute-start.8 = (f32[2,2,2,32,16]{4,3,2,1,0:T(8,128)S(1)}, f32[2,2,2,32,16]{4,3,2,1,0:T(8,128)S(1)}, u32[]{:S(2)}, u32[]{:S(2)}) collective-permute-start(f32[2,2,2,32,16]{4,3,2,1,0:T(8,128)S(1)} %get-tuple-element.45), channel_id=1, source_target_pairs={{0,32},{16,48},{32,0},{48,16},{64,96},{80,112},{96,64},{112,80},{1... | collective-permute-start | bytes 49160 | tf_op jit(solution)/shard_map/ppermute | solution.py:135
  148.2 13.1 %collective-permute-done.8 = f32[2,2,2,32,16]{4,3,2,1,0:T(8,128)S(1)} collective-permute-done((f32[2,2,2,32,16]{4,3,2,1,0:T(8,128)S(1)}, f32[2,2,2,32,16]{4,3,2,1,0:T(8,128)S(1)}, u32[]{:S(2)}, u32[]{:S(2)}) %collective-permute-start.8) | collective-permute-done | bytes 16416 | tf_op jit(solution)/shard_map/ppermute | solution.py:135
  162.4 1.1 mul.163
  163.6 2.7 %collective-permute-start.10 = (f32[2,2,32,16]{3,2,1,0:T(8,128)S(1)}, f32[2,2,32,16]{3,2,1,0:T(8,128)S(1)}, u32[]{:S(2)}, u32[]{:S(2)}) collective-permute-start(f32[2,2,32,16]{3,2,1,0:T(8,128)S(1)} %get-tuple-element.49), channel_id=1, source_target_pairs={{0,128},{16,144},{32,160},{48,176},{64,192},{80,208},{96,224},{112... | collective-permute-start | bytes 24584 | tf_op jit(solution)/shard_map/ppermute | solution.py:135
  166.3 1.4 fusion.1
  167.8 3.1 %collective-permute-start.11 = (f32[2,2,32,512]{3,2,1,0:T(8,128)S(1)}, f32[2,2,32,512]{3,2,1,0:T(8,128)S(1)}, u32[]{:S(2)}, u32[]{:S(2)}) collective-permute-start(f32[2,2,32,512]{3,2,1,0:T(8,128)S(1)} %dynamic-slice_bitcast_fusion.2), channel_id=1, source_target_pairs={{0,128},{16,144},{32,160},{48,176},{64,192},{80,208},{96,224},{112... | collective-permute-start | bytes 786440 | tf_op jit(solution)/shard_map/ppermute | solution.py:136
  171.8 1.9 collective-permute-start.12
  173.7 3.4 %collective-permute-done.11 = f32[2,2,32,512]{3,2,1,0:T(8,128)S(1)} collective-permute-done((f32[2,2,32,512]{3,2,1,0:T(8,128)S(1)}, f32[2,2,32,512]{3,2,1,0:T(8,128)S(1)}, u32[]{:S(2)}, u32[]{:S(2)}) %collective-permute-start.11) | collective-permute-done | bytes 262176 | tf_op jit(solution)/shard_map/ppermute | solution.py:136
  177.3 1.9 collective-permute-start.13
  179.9 3.0 %collective-permute-start.14 = (f32[32,16]{1,0:T(8,128)S(1)}, f32[32,16]{1,0:T(8,128)S(1)}, u32[]{:S(2)}, u32[]{:S(2)}) collective-permute-start(f32[32,16]{1,0:T(8,128)S(1)} %get-tuple-element.53), channel_id=1, source_target_pairs={{0,256},{16,272},{32,288},{48,304},{64,320},{80,336},{96,352},{112... | collective-permute-start | bytes 6152 | tf_op jit(solution)/shard_map/ppermute | solution.py:135
  182.9 3.7 %collective-permute-done.13 = f32[2,32,512]{2,1,0:T(8,128)S(1)} collective-permute-done((f32[2,32,512]{2,1,0:T(8,128)S(1)}, f32[2,32,512]{2,1,0:T(8,128)S(1)}, u32[]{:S(2)}, u32[]{:S(2)}) %collective-permute-start.13) | collective-permute-done | bytes 131104 | tf_op jit(solution)/shard_map/ppermute | solution.py:136
  186.7 3.0 %collective-permute-start.15 = (f32[32,512]{1,0:T(8,128)S(1)}, f32[32,512]{1,0:T(8,128)S(1)}, u32[]{:S(2)}, u32[]{:S(2)}) collective-permute-start(f32[32,512]{1,0:T(8,128)S(1)} %dynamic-slice_bitcast_fusion.6), channel_id=1, source_target_pairs={{0,256},{16,272},{32,288},{48,304},{64,320},{80,336},{96,352},{112... | collective-permute-start | bytes 196616 | tf_op jit(solution)/shard_map/ppermute | solution.py:136
  190.4 3.9 %collective-permute-done.15 = f32[32,512]{1,0:T(8,128)S(1)} collective-permute-done((f32[32,512]{1,0:T(8,128)S(1)}, f32[32,512]{1,0:T(8,128)S(1)}, u32[]{:S(2)}, u32[]{:S(2)}) %collective-permute-start.15) | collective-permute-done | bytes 65568 | tf_op jit(solution)/shard_map/ppermute | solution.py:136
  194.5 0.9 convolution_bitcast_fusion
  (53 shorter events, 4.7 us)
Async XLA Ops:
  0.0 194.5 %copy-start = (bf16[512,512]{1,0:T(8,128)(2,1)S(1)}, bf16[512,512]{1,0:T(8,128)(2,1)}, u32[]{:S(2)}) copy-start(bf16[512,512]{1,0:T(8,128)(2,1)} %param.9) | copy-start | bytes 1572868
  0.0 96.7 %copy-start.1 = (bf16[2,2,1,1,2,64,512]{6,5,4,3,2,1,0:T(8,128)(2,1)S(1)}, bf16[2,2,1,1,2,64,512]{6,5,4,3,2,1,0:T(8,128)(2,1)}, u32[]{:S(2)}) copy-start(bf16[2,2,1,1,2,64,512]{6,5,4,3,2,1,0:T(8,128)(2,1)} %param.6) | copy-start | bytes 1572868
  0.0 20.8 %collective-permute-start = (bf16[2,2,1,1,2,64,512]{6,5,4,3,2,1,0:T(8,128)(2,1)}, bf16[2,2,1,1,2,64,512]{6,5,4,3,2,1,0:T(8,128)(2,1)S(1)}, u32[]{:S(2)}, u32[]{:S(2)}) collective-permute-start(bf16[2,2,1,1,2,64,512]{6,5,4,3,2,1,0:T(8,128)(2,1)} %param.6), channel_id=1, source_target_pairs={{0,1},{1,2},{2,3},{4,5},{5,6},{6,7},{8,9},{9,10},{10,11},{12,13},{... | collective-permute-start | bytes 1572872 | tf_op jit(solution)/shard_map/ppermute | solution.py:19
  9.3 54.6 %collective-permute-start.1 = (bf16[2,2,1,1,2,64,512]{6,5,4,3,2,1,0:T(8,128)(2,1)}, bf16[2,2,1,1,2,64,512]{6,5,4,3,2,1,0:T(8,128)(2,1)S(1)}, u32[]{:S(2)}, u32[]{:S(2)}) collective-permute-start(bf16[2,2,1,1,2,64,512]{6,5,4,3,2,1,0:T(8,128)(2,1)} %param.6), channel_id=1, source_target_pairs={{1,0},{2,1},{3,2},{5,4},{6,5},{7,6},{9,8},{10,9},{11,10},{13,12},{... | collective-permute-start | bytes 1572872 | tf_op jit(solution)/shard_map/ppermute | solution.py:19
  10.6 53.3 %collective-permute-start.2 = (bf16[2,2,1,1,2,64,512]{6,5,4,3,2,1,0:T(8,128)(2,1)}, bf16[2,2,1,1,2,64,512]{6,5,4,3,2,1,0:T(8,128)(2,1)S(1)}, u32[]{:S(2)}, u32[]{:S(2)}) collective-permute-start(bf16[2,2,1,1,2,64,512]{6,5,4,3,2,1,0:T(8,128)(2,1)} %param.6), channel_id=1, source_target_pairs={{0,4},{4,8},{8,12},{1,5},{5,9},{9,13},{2,6},{6,10},{10,14},{3,7},{... | collective-permute-start | bytes 1572872 | tf_op jit(solution)/shard_map/ppermute | solution.py:19
  14.1 49.8 %collective-permute-start.3 = (bf16[2,2,1,1,2,64,512]{6,5,4,3,2,1,0:T(8,128)(2,1)}, bf16[2,2,1,1,2,64,512]{6,5,4,3,2,1,0:T(8,128)(2,1)S(1)}, u32[]{:S(2)}, u32[]{:S(2)}) collective-permute-start(bf16[2,2,1,1,2,64,512]{6,5,4,3,2,1,0:T(8,128)(2,1)} %param.6), channel_id=1, source_target_pairs={{4,0},{8,4},{12,8},{5,1},{9,5},{13,9},{6,2},{10,6},{14,10},{7,3},{... | collective-permute-start | bytes 1572872 | tf_op jit(solution)/shard_map/ppermute | solution.py:19
  63.9 6.3 %copy-start.2 = (bf16[2,2,1,1,2,64,512]{6,5,4,3,2,1,0:T(8,128)(2,1)}, bf16[2,2,1,1,2,64,512]{6,5,4,3,2,1,0:T(8,128)(2,1)S(1)}, u32[]{:S(2)}) copy-start(bf16[2,2,1,1,2,64,512]{6,5,4,3,2,1,0:T(8,128)(2,1)S(1)} %collective-permute-done.2) | copy-start | bytes 1572868
  63.9 6.3 %copy-start.3 = (bf16[2,2,1,1,2,64,512]{6,5,4,3,2,1,0:T(8,128)(2,1)}, bf16[2,2,1,1,2,64,512]{6,5,4,3,2,1,0:T(8,128)(2,1)S(1)}, u32[]{:S(2)}) copy-start(bf16[2,2,1,1,2,64,512]{6,5,4,3,2,1,0:T(8,128)(2,1)S(1)} %collective-permute-done.3) | copy-start | bytes 1572868
  65.7 25.9 %collective-permute-start.4 = (bf16[2,2,1,2,2,64,512]{6,5,4,3,2,1,0:T(8,128)(2,1)}, bf16[2,2,1,2,2,64,512]{6,5,4,3,2,1,0:T(8,128)(2,1)}, u32[]{:S(2)}, u32[]{:S(2)}) collective-permute-start(bf16[2,2,1,2,2,64,512]{6,5,4,3,2,1,0:T(8,128)(2,1)} %constant_dynamic-update-slice_fusion), channel_id=1, source_target_pairs={{0,4},{4,8},{8,12},{1,5},{5,9},{9,13},{2,6},{6,10},{10,14},{3,7},{... | collective-permute-start | bytes 3145736 | tf_op jit(solution)/shard_map/ppermute | solution.py:19
  70.2 26.4 %collective-permute-start.5 = (bf16[2,2,1,2,2,64,512]{6,5,4,3,2,1,0:T(8,128)(2,1)}, bf16[2,2,1,2,2,64,512]{6,5,4,3,2,1,0:T(8,128)(2,1)S(1)}, u32[]{:S(2)}, u32[]{:S(2)}) collective-permute-start(bf16[2,2,1,2,2,64,512]{6,5,4,3,2,1,0:T(8,128)(2,1)} %constant_dynamic-update-slice_fusion), channel_id=1, source_target_pairs={{4,0},{8,4},{12,8},{5,1},{9,5},{13,9},{6,2},{10,6},{14,10},{7,3},{... | collective-permute-start | bytes 3145736 | tf_op jit(solution)/shard_map/ppermute | solution.py:19
  127.7 10.9 %collective-permute-start.7 = (f32[2,2,2,2,32,512]{5,4,3,2,1,0:T(8,128)}, f32[2,2,2,2,32,512]{5,4,3,2,1,0:T(8,128)}, u32[]{:S(2)}, u32[]{:S(2)}) collective-permute-start(f32[2,2,2,2,32,512]{5,4,3,2,1,0:T(8,128)} %dynamic-slice_bitcast_fusion), channel_id=1, source_target_pairs={{0,16},{16,0},{32,48},{48,32},{64,80},{80,64},{96,112},{112,96},{1... | collective-permute-start | bytes 3145736 | tf_op jit(solution)/shard_map/ppermute | solution.py:136
  130.7 3.6 %collective-permute-start.6 = (f32[2,2,2,2,32,16]{5,4,3,2,1,0:T(8,128)S(1)}, f32[2,2,2,2,32,16]{5,4,3,2,1,0:T(8,128)S(1)}, u32[]{:S(2)}, u32[]{:S(2)}) collective-permute-start(f32[2,2,2,2,32,16]{5,4,3,2,1,0:T(8,128)S(1)} %get-tuple-element.47), channel_id=1, source_target_pairs={{0,16},{16,0},{32,48},{48,32},{64,80},{80,64},{96,112},{112,96},{1... | collective-permute-start | bytes 98312 | tf_op jit(solution)/shard_map/ppermute | solution.py:135
  142.2 24.1 %collective-permute-start.9 = (f32[2,2,2,32,512]{4,3,2,1,0:T(8,128)}, f32[2,2,2,32,512]{4,3,2,1,0:T(8,128)}, u32[]{:S(2)}, u32[]{:S(2)}) collective-permute-start(f32[2,2,2,32,512]{4,3,2,1,0:T(8,128)} %dynamic-slice_bitcast_fusion.1), channel_id=1, source_target_pairs={{0,32},{16,48},{32,0},{48,16},{64,96},{80,112},{96,64},{112,80},{1... | collective-permute-start | bytes 1572872 | tf_op jit(solution)/shard_map/ppermute | solution.py:136
  144.2 17.0 %collective-permute-start.8 = (f32[2,2,2,32,16]{4,3,2,1,0:T(8,128)S(1)}, f32[2,2,2,32,16]{4,3,2,1,0:T(8,128)S(1)}, u32[]{:S(2)}, u32[]{:S(2)}) collective-permute-start(f32[2,2,2,32,16]{4,3,2,1,0:T(8,128)S(1)} %get-tuple-element.45), channel_id=1, source_target_pairs={{0,32},{16,48},{32,0},{48,16},{64,96},{80,112},{96,64},{112,80},{1... | collective-permute-start | bytes 49160 | tf_op jit(solution)/shard_map/ppermute | solution.py:135
  163.6 7.3 %collective-permute-start.10 = (f32[2,2,32,16]{3,2,1,0:T(8,128)S(1)}, f32[2,2,32,16]{3,2,1,0:T(8,128)S(1)}, u32[]{:S(2)}, u32[]{:S(2)}) collective-permute-start(f32[2,2,32,16]{3,2,1,0:T(8,128)S(1)} %get-tuple-element.49), channel_id=1, source_target_pairs={{0,128},{16,144},{32,160},{48,176},{64,192},{80,208},{96,224},{112... | collective-permute-start | bytes 24584 | tf_op jit(solution)/shard_map/ppermute | solution.py:135
  167.8 9.4 %collective-permute-start.11 = (f32[2,2,32,512]{3,2,1,0:T(8,128)S(1)}, f32[2,2,32,512]{3,2,1,0:T(8,128)S(1)}, u32[]{:S(2)}, u32[]{:S(2)}) collective-permute-start(f32[2,2,32,512]{3,2,1,0:T(8,128)S(1)} %dynamic-slice_bitcast_fusion.2), channel_id=1, source_target_pairs={{0,128},{16,144},{32,160},{48,176},{64,192},{80,208},{96,224},{112... | collective-permute-start | bytes 786440 | tf_op jit(solution)/shard_map/ppermute | solution.py:136
  171.8 7.4 %collective-permute-start.12 = (f32[2,32,16]{2,1,0:T(8,128)S(1)}, f32[2,32,16]{2,1,0:T(8,128)S(1)}, u32[]{:S(2)}, u32[]{:S(2)}) collective-permute-start(f32[2,32,16]{2,1,0:T(8,128)S(1)} %get-tuple-element.51), channel_id=1, source_target_pairs={{0,64},{16,80},{32,96},{48,112},{64,0},{80,16},{96,32},{112,48},{1... | collective-permute-start | bytes 12296 | tf_op jit(solution)/shard_map/ppermute | solution.py:135
  177.3 9.4 %collective-permute-start.13 = (f32[2,32,512]{2,1,0:T(8,128)S(1)}, f32[2,32,512]{2,1,0:T(8,128)S(1)}, u32[]{:S(2)}, u32[]{:S(2)}) collective-permute-start(f32[2,32,512]{2,1,0:T(8,128)S(1)} %dynamic-slice_bitcast_fusion.5), channel_id=1, source_target_pairs={{0,64},{16,80},{32,96},{48,112},{64,0},{80,16},{96,32},{112,48},{1... | collective-permute-start | bytes 393224 | tf_op jit(solution)/shard_map/ppermute | solution.py:136
  179.9 9.9 %collective-permute-start.14 = (f32[32,16]{1,0:T(8,128)S(1)}, f32[32,16]{1,0:T(8,128)S(1)}, u32[]{:S(2)}, u32[]{:S(2)}) collective-permute-start(f32[32,16]{1,0:T(8,128)S(1)} %get-tuple-element.53), channel_id=1, source_target_pairs={{0,256},{16,272},{32,288},{48,304},{64,320},{80,336},{96,352},{112... | collective-permute-start | bytes 6152 | tf_op jit(solution)/shard_map/ppermute | solution.py:135
  186.7 7.7 %collective-permute-start.15 = (f32[32,512]{1,0:T(8,128)S(1)}, f32[32,512]{1,0:T(8,128)S(1)}, u32[]{:S(2)}, u32[]{:S(2)}) collective-permute-start(f32[32,512]{1,0:T(8,128)S(1)} %dynamic-slice_bitcast_fusion.6), channel_id=1, source_target_pairs={{0,256},{16,272},{32,288},{48,304},{64,320},{80,336},{96,352},{112... | collective-permute-start | bytes 196616 | tf_op jit(solution)/shard_map/ppermute | solution.py:136

commit v4 on v3

v4 whole, which is shorter than its diff:
```python
import jax
import jax.numpy as jnp
from jax import lax
from jax.experimental import pallas as pl
from jax.experimental.pallas import tpu as pltpu
from jax.sharding import PartitionSpec as P

HEADS = 8
HD = 64
TQ = 256


def shifted(array, axis, forward):
    size = lax.axis_size(axis)
    if forward:
        pairs = [(i, i + 1) for i in range(size - 1)]
    else:
        pairs = [(i + 1, i) for i in range(size - 1)]
    return lax.ppermute(array, axis, pairs)


def neighbourhood(kv_blocks):
    up_mid = shifted(kv_blocks, "height", True)
    down_mid = shifted(kv_blocks, "height", False)
    frames = kv_blocks.shape[1]
    rows = []
    for f in range(frames):
        own = kv_blocks[:, f : f + 1]
        left = shifted(own, "width", True)
        right = shifted(own, "width", False)
        sides = jnp.concatenate([left, right], axis=3)
        up_sides = shifted(sides, "height", True)
        down_sides = shifted(sides, "height", False)
        row = jnp.concatenate([left, own, right], axis=3)
        rows.append((row, up_sides, down_sides))
    row = jnp.concatenate([r[0] for r in rows], axis=1)
    up_sides = jnp.concatenate([r[1] for r in rows], axis=1)
    down_sides = jnp.concatenate([r[2] for r in rows], axis=1)
    up = jnp.concatenate([up_sides[:, :, :, :1], up_mid, up_sides[:, :, :, 1:]], axis=3)
    down = jnp.concatenate([down_sides[:, :, :, :1], down_mid, down_sides[:, :, :, 1:]], axis=3)
    return jnp.concatenate([up, row, down], axis=2)


PACK = 128


def attention_kernel(q_ref, k_ref, v_ref, keep_ref, first_ref, second_ref):
    rows = q_ref.shape[0]
    step = pl.program_id(0)
    half = pl.num_programs(0) // 2
    keep = keep_ref[...] > 0
    lane = lax.broadcasted_iota(jnp.int32, (1, 2 * HD), 1)
    low = lane < HD
    stat_lane = lax.broadcasted_iota(jnp.int32, (1, PACK), 1)
    stats = jnp.zeros((rows, PACK), jnp.float32)
    blocks = []
    for pair in range(HEADS // 2):
        cols = pl.ds(pair * 2 * HD, 2 * HD)
        q2 = q_ref[:, cols]
        k2 = k_ref[:, cols]
        v2 = v_ref[:, cols]
        outs = []
        for part in range(2):
            mine = low if part == 0 else jnp.logical_not(low)
            qh = jnp.where(mine, q2, jnp.zeros_like(q2))
            scores = lax.dot_general(
                qh, k2, (((1,), (1,)), ((), ())), preferred_element_type=jnp.float32
            )
            scores = scores / jnp.float32(8.0)
            scores = jnp.where(keep, scores, jnp.float32(-1e30))
            top = jnp.max(scores, axis=1, keepdims=True)
            probs = jnp.where(keep, jnp.exp(scores - top), jnp.float32(0.0))
            total = jnp.sum(probs, axis=1, keepdims=True)
            outs.append(
                jnp.dot(probs.astype(jnp.bfloat16), v2, preferred_element_type=jnp.float32)
            )
            head = pair * 2 + part
            stats = jnp.where(stat_lane == head, top, stats)
            stats = jnp.where(stat_lane == HEADS + head, total, stats)
        blocks.append(jnp.where(low, outs[0], outs[1]))
    packed = jnp.concatenate(blocks + [stats], axis=1)

    @pl.when(step < half)
    def _():
        first_ref[...] = packed

    @pl.when(step >= half)
    def _():
        second_ref[...] = packed


def attention(query_rows, keys, values, keep):
    qtok, width = query_rows.shape
    count = keys.shape[0]
    tiles = qtok // TQ
    half = tiles // 2
    flops = 2 * 2 * qtok * count * 2 * width
    packed = jax.ShapeDtypeStruct((qtok // 2, width + PACK), jnp.float32)
    return pl.pallas_call(
        attention_kernel,
        grid=(tiles,),
        in_specs=[
            pl.BlockSpec((TQ, width), lambda i: (i, 0)),
            pl.BlockSpec((count, width), lambda i: (0, 0)),
            pl.BlockSpec((count, width), lambda i: (0, 0)),
            pl.BlockSpec((1, count), lambda i: (0, 0)),
        ],
        out_specs=[
            pl.BlockSpec((TQ, width + PACK), lambda i: (jnp.minimum(i, half - 1), 0)),
            pl.BlockSpec((TQ, width + PACK), lambda i: (jnp.maximum(i - half, 0), 0)),
        ],
        out_shape=[packed, packed],
        cost_estimate=pl.CostEstimate(
            flops=flops,
            transcendentals=qtok * count * HEADS,
            bytes_accessed=qtok * width * 6 + count * width * 4,
        ),
    )(query_rows, keys, values, keep)


def merge_kernel(a_ref, b_ref, *out_refs):
    width = a_ref.shape[1] - PACK
    sa = a_ref[:, pl.ds(width, PACK)]
    sb = b_ref[:, pl.ds(width, PACK)]
    stat_lane = lax.broadcasted_iota(jnp.int32, (1, PACK), 1)
    top = jnp.maximum(sa, sb)
    fa = jnp.exp(sa - top)
    fb = jnp.exp(sb - top)
    heads_a = [jnp.sum(jnp.where(stat_lane == h, fa, 0.0), axis=1, keepdims=True) for h in range(HEADS)]
    heads_b = [jnp.sum(jnp.where(stat_lane == h, fb, 0.0), axis=1, keepdims=True) for h in range(HEADS)]
    spread_a = jnp.zeros_like(sa)
    spread_b = jnp.zeros_like(sb)
    for h in range(HEADS):
        spread_a = jnp.where(stat_lane == HEADS + h, heads_a[h], spread_a)
        spread_b = jnp.where(stat_lane == HEADS + h, heads_b[h], spread_b)
    tot = sa * spread_a + sb * spread_b
    stats = jnp.where(
        stat_lane < HEADS, top, jnp.where(stat_lane < 2 * HEADS, tot, jnp.float32(0.0))
    )
    lane = lax.broadcasted_iota(jnp.int32, (1, 2 * HD), 1)
    low = lane < HD
    blocks = []
    for pair in range(HEADS // 2):
        cols = pl.ds(pair * 2 * HD, 2 * HD)
        f_a = jnp.where(low, heads_a[2 * pair], heads_a[2 * pair + 1])
        f_b = jnp.where(low, heads_b[2 * pair], heads_b[2 * pair + 1])
        blocks.append(a_ref[:, cols] * f_a + b_ref[:, cols] * f_b)
    merged = jnp.concatenate(blocks + [stats], axis=1)
    if len(out_refs) == 1:
        out_refs[0][...] = merged
    else:
        half = merged.shape[0] // 2
        out_refs[0][...] = merged[:half]
        out_refs[1][...] = merged[half:]


def merge(kept, got, split):
    rows, cols = kept.shape
    count = 2 if split else 1
    shape = jax.ShapeDtypeStruct((rows // count, cols), jnp.float32)
    return pl.pallas_call(
        merge_kernel,
        out_shape=[shape] * count,
        cost_estimate=pl.CostEstimate(
            flops=4 * rows * cols, transcendentals=2 * rows * PACK, bytes_accessed=12 * rows * cols
        ),
    )(kept, got)


def step_bits(nbits):
    return [0, 1, 3, 2, 4] if nbits == 5 else list(range(nbits))


def block_order(groups):
    nbits = groups.bit_length() - 1
    me = lax.axis_index("tm")
    order = step_bits(nbits)
    pos = jnp.arange(groups, dtype=jnp.int32)
    block = jnp.zeros_like(pos)
    for i, bit in enumerate(order):
        a = (pos >> (nbits - 1 - i)) & 1
        block = block + ((a ^ ((me >> bit) & 1)) << bit)
    return block


def tree_reduce(first, second):
    groups = lax.axis_size("tm")
    nbits = groups.bit_length() - 1
    order = step_bits(nbits)
    for i, bit in enumerate(order):
        pairs = [(t, t ^ (1 << bit)) for t in range(groups)]
        got = lax.ppermute(second, "tm", pairs)
        last = i == len(order) - 1
        outs = merge(first, got, not last)
        if last:
            return outs[0]
        first, second = outs


def local(queries, kv_blocks, block_list, block_valid, w_out):
    hood = neighbourhood(kv_blocks)
    frames = hood.shape[1]
    nblk = hood.shape[4]
    blk = hood.shape[5]
    width = hood.shape[6]
    hood = hood.reshape(2, frames, 9 * nblk, blk, width)
    listed = block_list[0, 0]
    nlist = listed.shape[0]
    chosen = jnp.take(hood, listed, axis=2)
    keep = jnp.broadcast_to((block_valid[0, 0] > 0)[None, :, None], (frames, nlist, blk))
    keep = keep.reshape(1, -1).astype(jnp.int32)
    keys = chosen[0].reshape(-1, width)
    values = chosen[1].reshape(-1, width)
    query_rows = queries[0, 0]
    qtok = query_rows.shape[0]
    groups = lax.axis_size("tm")
    order = block_order(groups)
    query_rows = jnp.take(query_rows.reshape(groups, qtok // groups, width), order, axis=0)
    query_rows = query_rows.reshape(qtok, width)
    first, second = attention(query_rows, keys, values, keep)
    final = tree_reduce(first, second)
    summed = final[:, :width]
    total = final[:, width + HEADS : width + 2 * HEADS]
    own_rows = summed.shape[0]
    attended = summed / jnp.repeat(total, HD, axis=1)
    normed = attended * lax.rsqrt(jnp.mean(attended * attended, axis=1, keepdims=True) + 1e-06)
    normed = normed.astype(jnp.bfloat16)
    joined = jnp.dot(normed, w_out, preferred_element_type=jnp.float32)
    return joined.reshape(1, 1, own_rows, width)


def solution(mesh):
    in_specs = (
        P("height", "width", None, None),
        P(None, "tm", "height", "width", None, None, None),
        P("height", "width", None),
        P("height", "width", None),
        P(),
    )
    out_specs = P("height", "width", "tm", None)
    return jax.shard_map(local, mesh=mesh, in_specs=in_specs, out_specs=out_specs, check_vma=False)
```

time: 197 us -> 206 us (1.046)
  Pallas kernels: 18.7 us -> 31.7 us
  other arithmetic: 11.9 us -> 6.82 us
  starting transfers between devices: 47 us -> 50.3 us
  local copies, waits for them, and re-layouts: 21.5 us -> 19.1 us
    ppermute x6 -> x10, starting transfers between devices: 21.1 us -> 38.4 us  [shifted(): return lax.ppermute(array, axis, pairs)]
    ppermute x10 -> x5, waiting for transfers between devices: 25.3 us -> 42.3 us  [tree_reduce(): got = lax.ppermute(second, 'tm', pairs)]
    ppermute x6 -> x10, waiting for transfers between devices: 69.6 us -> 53.3 us  [shifted(): return lax.ppermute(array, axis, pairs)]
    ppermute x10 -> x5, starting transfers between devices: 25.9 us -> 11.9 us  [tree_reduce(): got = lax.ppermute(second, 'tm', pairs)]
    pallas_call x1 -> x6, Pallas kernels: 18.7 us -> 31.7 us  [the longest x1 19.2 us: attention(): pl.pallas_call(attention_kernel, grid=(tiles,), in_specs=[pl.BlockSpec((T...]
    mul x20 -> x0, local copies, waits for them, and re-layouts: 7.66 us -> none  [the longest x10 4.24 us: merge(): out_b.reshape(shape[:-1] + (heads, -1)) * fb[..., None]]
    add x9 -> x0, other arithmetic: 4.85 us -> none  [the longest x4 4.23 us: merge(): out_a.reshape(shape[:-1] + (heads, -1)) * fa[..., None]]
    unnamed x9 -> x22, local copies, waits for them, and re-layouts: 0.96 us -> 5.48 us
  transfers between devices with their start and end apart: 16 -> 15, of which waited for: 9 -> 11; matrix products, arithmetic and copies ran while one was open for 8% -> 4% of each run, Pallas kernels for 0% -> 0%
where the time goes in v4:
time: 206 us; the launch traced here: 205 us
  waiting for transfers between devices  95.6 us (46%)
  starting transfers between devices  50.3 us (24%)
  Pallas kernels  31.7 us (15%)
  local copies, waits for them, and re-layouts  19.1 us (9%)
  other arithmetic  6.82 us (3%)
    ppermute x10, waiting for transfers between devices, shifted(): return lax.ppermute(array, axis, pairs)  53.3 us
    ppermute x5, waiting for transfers between devices, tree_reduce(): got = lax.ppermute(second, 'tm', pairs)  42.3 us
    ppermute x10, starting transfers between devices, shifted(): return lax.ppermute(array, axis, pairs)  38.4 us
    pallas_call x1, Pallas kernels, attention(): pl.pallas_call(attention_kernel, grid=(tiles,), in_specs=[pl.BlockSpec((T...  19.2 us
    pallas_call x5, Pallas kernels, merge(): pl.pallas_call(merge_kernel, out_shape=[shape] * count, cost_estimate=pl....  12.5 us
    ppermute x5, starting transfers between devices, tree_reduce(): got = lax.ppermute(second, 'tm', pairs)  11.9 us
    unnamed x22, local copies, waits for them, and re-layouts  5.48 us
    concatenate x1, other arithmetic, neighbourhood(): return jnp.concatenate([up, row, down], axis=2)  4.3 us
  transfers between devices with their start and end apart: 15, of which 11 were waited for; matrix products, arithmetic and copies ran while one was open for 4% of the time, Pallas kernels for 0%

profile of v4, /device:TPU:6, one launch (start us, length us, event | category | flops | bytes accessed | tf_op | source)
XLA Modules:
  0.0 205.4 jit_solution(7986457772304577795)
XLA Ops:
  0.0 1.9 fusion.7
  1.9 9.1 %collective-permute-start = (bf16[2,1,1,1,2,64,512]{6,5,4,3,2,1,0:T(8,128)(2,1)}, bf16[2,1,1,1,2,64,512]{6,5,4,3,2,1,0:T(8,128)(2,1)S(1)}, u32[]{:S(2)}, u32[]{:S(2)}) collective-permute-start(bf16[2,1,1,1,2,64,512]{6,5,4,3,2,1,0:T(8,128)(2,1)} %get-tuple-element.32), channel_id=1, source_target_pairs={{0,1},{1,2},{2,3},{4,5},{5,6},{6,7},{8,9},{9,10},{10,11},{12,13},{... | collective-permute-start | bytes 786440 | tf_op jit(solution)/shard_map/ppermute | solution.py:19
  11.0 1.3 collective-permute-start.1
  12.3 9.7 %collective-permute-start.3 = (bf16[2,1,1,1,2,64,512]{6,5,4,3,2,1,0:T(8,128)(2,1)S(1)}, bf16[2,1,1,1,2,64,512]{6,5,4,3,2,1,0:T(8,128)(2,1)S(1)}, u32[]{:S(2)}, u32[]{:S(2)}) collective-permute-start(bf16[2,1,1,1,2,64,512]{6,5,4,3,2,1,0:T(8,128)(2,1)S(1)} %get-tuple-element.31), channel_id=1, source_target_pairs={{0,1},{1,2},{2,3},{4,5},{5,6},{6,7},{8,9},{9,10},{10,11},{12,13},{... | collective-permute-start | bytes 786440 | tf_op jit(solution)/shard_map/ppermute | solution.py:19
  22.0 1.3 collective-permute-start.4
  23.3 4.3 %collective-permute-start.6 = (bf16[2,2,1,1,2,64,512]{6,5,4,3,2,1,0:T(8,128)(2,1)}, bf16[2,2,1,1,2,64,512]{6,5,4,3,2,1,0:T(8,128)(2,1)}, u32[]{:S(2)}, u32[]{:S(2)}) collective-permute-start(bf16[2,2,1,1,2,64,512]{6,5,4,3,2,1,0:T(8,128)(2,1)} %param.6), channel_id=1, source_target_pairs={{0,4},{4,8},{8,12},{1,5},{5,9},{9,13},{2,6},{6,10},{10,14},{3,7},{... | collective-permute-start | bytes 1572872 | tf_op jit(solution)/shard_map/ppermute | solution.py:19
  28.5 1.2 bitcast_select_fusion.q_ref
  30.4 30.1 %collective-permute-done.1 = bf16[2,1,1,1,2,64,512]{6,5,4,3,2,1,0:T(8,128)(2,1)S(1)} collective-permute-done((bf16[2,1,1,1,2,64,512]{6,5,4,3,2,1,0:T(8,128)(2,1)}, bf16[2,1,1,1,2,64,512]{6,5,4,3,2,1,0:T(8,128)(2,1)S(1)}, u32[]{:S(2)}, u32[]{:S(2)}) %collective-permute-start.1) | collective-permute-done | bytes 262176 | tf_op jit(solution)/shard_map/ppermute | solution.py:19
  60.6 0.8 constant_dynamic-update-slice_fusion
  61.3 3.5 %collective-permute-start.2 = (bf16[2,1,1,2,2,64,512]{6,5,4,3,2,1,0:T(8,128)(2,1)}, bf16[2,1,1,2,2,64,512]{6,5,4,3,2,1,0:T(8,128)(2,1)S(1)}, u32[]{:S(2)}, u32[]{:S(2)}) collective-permute-start(bf16[2,1,1,2,2,64,512]{6,5,4,3,2,1,0:T(8,128)(2,1)} %constant_dynamic-update-slice_fusion), channel_id=1, source_target_pairs={{0,4},{4,8},{8,12},{1,5},{5,9},{9,13},{2,6},{6,10},{10,14},{3,7},{... | collective-permute-start | bytes 1572872 | tf_op jit(solution)/shard_map/ppermute | solution.py:19
  64.8 1.3 collective-permute-start.7
  66.2 0.7 constant_dynamic-update-slice_fusion.3
  66.9 0.7 constant_dynamic-update-slice_fusion.2
  67.6 5.3 %collective-permute-start.5 = (bf16[2,1,1,2,2,64,512]{6,5,4,3,2,1,0:T(8,128)(2,1)}, bf16[2,1,1,2,2,64,512]{6,5,4,3,2,1,0:T(8,128)(2,1)}, u32[]{:S(2)}, u32[]{:S(2)}) collective-permute-start(bf16[2,1,1,2,2,64,512]{6,5,4,3,2,1,0:T(8,128)(2,1)} %constant_dynamic-update-slice_fusion.2), channel_id=1, source_target_pairs={{0,4},{4,8},{8,12},{1,5},{5,9},{9,13},{2,6},{6,10},{10,14},{3,7},{... | collective-permute-start | bytes 1572872 | tf_op jit(solution)/shard_map/ppermute | solution.py:19
  73.0 1.3 collective-permute-start.8
  75.1 2.4 %collective-permute-done.2 = bf16[2,1,1,2,2,64,512]{6,5,4,3,2,1,0:T(8,128)(2,1)S(1)} collective-permute-done((bf16[2,1,1,2,2,64,512]{6,5,4,3,2,1,0:T(8,128)(2,1)}, bf16[2,1,1,2,2,64,512]{6,5,4,3,2,1,0:T(8,128)(2,1)S(1)}, u32[]{:S(2)}, u32[]{:S(2)}) %collective-permute-start.2) | collective-permute-done | bytes 524320 | tf_op jit(solution)/shard_map/ppermute | solution.py:19
  77.5 1.3 collective-permute-start.9
  78.8 3.0 %collective-permute-done.7 = bf16[2,1,1,2,2,64,512]{6,5,4,3,2,1,0:T(8,128)(2,1)S(1)} collective-permute-done((bf16[2,1,1,2,2,64,512]{6,5,4,3,2,1,0:T(8,128)(2,1)}, bf16[2,1,1,2,2,64,512]{6,5,4,3,2,1,0:T(8,128)(2,1)S(1)}, u32[]{:S(2)}, u32[]{:S(2)}) %collective-permute-start.7) | collective-permute-done | bytes 524320 | tf_op jit(solution)/shard_map/ppermute | solution.py:19
  81.8 4.8 %collective-permute-done.5 = bf16[2,1,1,2,2,64,512]{6,5,4,3,2,1,0:T(8,128)(2,1)} collective-permute-done((bf16[2,1,1,2,2,64,512]{6,5,4,3,2,1,0:T(8,128)(2,1)}, bf16[2,1,1,2,2,64,512]{6,5,4,3,2,1,0:T(8,128)(2,1)}, u32[]{:S(2)}, u32[]{:S(2)}) %collective-permute-start.5) | collective-permute-done | bytes 524320 | tf_op jit(solution)/shard_map/ppermute | solution.py:19
  86.7 1.1 constant_dynamic-update-slice_fusion.4
  87.8 5.4 %collective-permute-done.8 = bf16[2,1,1,2,2,64,512]{6,5,4,3,2,1,0:T(8,128)(2,1)} collective-permute-done((bf16[2,1,1,2,2,64,512]{6,5,4,3,2,1,0:T(8,128)(2,1)}, bf16[2,1,1,2,2,64,512]{6,5,4,3,2,1,0:T(8,128)(2,1)}, u32[]{:S(2)}, u32[]{:S(2)}) %collective-permute-start.8) | collective-permute-done | bytes 524320 | tf_op jit(solution)/shard_map/ppermute | solution.py:19
  93.2 1.1 constant_dynamic-update-slice_fusion.6
  94.4 7.5 %collective-permute-done.9 = bf16[2,2,1,1,2,64,512]{6,5,4,3,2,1,0:T(8,128)(2,1)S(1)} collective-permute-done((bf16[2,2,1,1,2,64,512]{6,5,4,3,2,1,0:T(8,128)(2,1)}, bf16[2,2,1,1,2,64,512]{6,5,4,3,2,1,0:T(8,128)(2,1)S(1)}, u32[]{:S(2)}, u32[]{:S(2)}) %collective-permute-start.9) | collective-permute-done | bytes 524320 | tf_op jit(solution)/shard_map/ppermute | solution.py:19
  102.0 4.3 %maximum_maximum_fusion = bf16[2,2,3,3,2,64,512]{6,5,4,3,2,1,0:T(8,128)(2,1)} fusion(bf16[2,2,1,1,2,64,512]{6,5,4,3,2,1,0:T(8,128)(2,1)S(1)} %get-tuple-element.30, bf16[2,2,1,1,2,64,512]{6,5,4,3,2,1,0:T(8,128)(2,1)S(1)} %collective-permute-done.9, bf16[2,2,1,1,2,64,512]{6,5,4,3,2,1,0:T(8,128)(2,1)S(1)} %get-tuple-element.29, ...), kind=kLoop, calls=%fused_computation.2 | loop fusion | flops 25952256 | bytes 9437184 | tf_op jit(solution)/shard_map/concatenate | solution.py:41
  106.2 3.0 %gather_fusion.1 = bf16[8,2,2,64,512]{4,3,2,1,0:T(8,128)(2,1)S(1)} fusion(bf16[2,2,18,64,512]{4,3,2,1,0:T(8,128)(2,1)} %bitcast.22, s32[1024]{0:T(1024)S(1)} %pad_clamp_fusion), kind=kCustom, calls=%fused_computation.1 | custom fusion | bytes 4194336 | tf_op jit(solution)/shard_map/jit(_take)/gather | solution.py:209
  109.7 1.1 copy.6
  110.8 1.1 copy.7
  111.9 19.2 %shard_map.55 = (f32[512,640]{1,0:T(8,128)}, f32[512,640]{1,0:T(8,128)}) custom-call(bf16[1024,512]{1,0:T(8,128)(2,1)} %bitcast_select_fusion.q_ref, bf16[1024,512]{1,0:T(8,128)(2,1)} %bitcast.23, bf16[1024,512]{1,0:T(8,128)(2,1)} %bitcast.24, s32[1,1024]{1,0:T(1,128)} %convert_element_type.12.keep_ref), custom_call_target="tpu_custom_call" | custom-call | flops 4294967296 | bytes 5242880 | tf_op jit(solution)/shard_map/pallas_call | solution.py:99
  131.1 2.0 collective-permute-start.10
  133.1 3.2 %collective-permute-done.10.b_ref = f32[512,640]{1,0:T(8,128)S(1)} collective-permute-done((f32[512,640]{1,0:T(8,128)}, f32[512,640]{1,0:T(8,128)S(1)}, u32[]{:S(2)}, u32[]{:S(2)}) %collective-permute-start.10) | collective-permute-done | bytes 1310752 | tf_op jit(solution)/shard_map/ppermute | solution.py:192
  136.3 1.1 copy-done.1
  137.4 4.0 %shard_map.56 = (f32[256,640]{1,0:T(8,128)}, f32[256,640]{1,0:T(8,128)}) custom-call(f32[512,640]{1,0:T(8,128)} %get-tuple-element.15.a_ref, f32[512,640]{1,0:T(8,128)} %copy-done.1), custom_call_target="tpu_custom_call" | custom-call | flops 1310720 | bytes 3932160 | tf_op jit(solution)/shard_map/pallas_call | solution.py:161
  141.4 1.9 collective-permute-start.11
  143.3 16.9 %collective-permute-done.11.b_ref = f32[256,640]{1,0:T(8,128)S(1)} collective-permute-done((f32[256,640]{1,0:T(8,128)}, f32[256,640]{1,0:T(8,128)S(1)}, u32[]{:S(2)}, u32[]{:S(2)}) %collective-permute-start.11) | collective-permute-done | bytes 655392 | tf_op jit(solution)/shard_map/ppermute | solution.py:192
  160.2 0.8 copy-done.2
  161.1 2.8 %shard_map.57 = (f32[128,640]{1,0:T(8,128)}, f32[128,640]{1,0:T(8,128)}) custom-call(f32[256,640]{1,0:T(8,128)} %get-tuple-element.17.a_ref, f32[256,640]{1,0:T(8,128)} %copy-done.2), custom_call_target="tpu_custom_call" | custom-call | flops 655360 | bytes 1966080 | tf_op jit(solution)/shard_map/pallas_call | solution.py:161
  163.9 2.7 %collective-permute-start.12 = (f32[128,640]{1,0:T(8,128)}, f32[128,640]{1,0:T(8,128)S(1)}, u32[]{:S(2)}, u32[]{:S(2)}) collective-permute-start(f32[128,640]{1,0:T(8,128)} %get-tuple-element.20), channel_id=1, source_target_pairs={{0,128},{16,144},{32,160},{48,176},{64,192},{80,208},{96,224},{112... | collective-permute-start | bytes 983048 | tf_op jit(solution)/shard_map/ppermute | solution.py:192
  166.6 8.3 %collective-permute-done.12.b_ref = f32[128,640]{1,0:T(8,128)S(1)} collective-permute-done((f32[128,640]{1,0:T(8,128)}, f32[128,640]{1,0:T(8,128)S(1)}, u32[]{:S(2)}, u32[]{:S(2)}) %collective-permute-start.12) | collective-permute-done | bytes 327712 | tf_op jit(solution)/shard_map/ppermute | solution.py:192
  175.6 2.2 %shard_map.58 = (f32[64,640]{1,0:T(8,128)}, f32[64,640]{1,0:T(8,128)}) custom-call(f32[128,640]{1,0:T(8,128)} %get-tuple-element.19.a_ref, f32[128,640]{1,0:T(8,128)} %copy-done.4), custom_call_target="tpu_custom_call" | custom-call | flops 327680 | bytes 983040 | tf_op jit(solution)/shard_map/pallas_call | solution.py:161
  177.8 1.9 collective-permute-start.13
  179.7 9.1 %collective-permute-done.13.b_ref = f32[64,640]{1,0:T(8,128)S(1)} collective-permute-done((f32[64,640]{1,0:T(8,128)}, f32[64,640]{1,0:T(8,128)S(1)}, u32[]{:S(2)}, u32[]{:S(2)}) %collective-permute-start.13) | collective-permute-done | bytes 163872 | tf_op jit(solution)/shard_map/ppermute | solution.py:192
  189.5 1.9 shard_map.59
  191.3 3.3 %collective-permute-start.14 = (f32[32,640]{1,0:T(8,128)}, f32[32,640]{1,0:T(8,128)S(1)}, u32[]{:S(2)}, u32[]{:S(2)}) collective-permute-start(f32[32,640]{1,0:T(8,128)} %get-tuple-element.24), channel_id=1, source_target_pairs={{0,256},{16,272},{32,288},{48,304},{64,320},{80,336},{96,352},{112... | collective-permute-start | bytes 245768 | tf_op jit(solution)/shard_map/ppermute | solution.py:192
  194.6 4.7 %collective-permute-done.14.b_ref = f32[32,640]{1,0:T(8,128)S(1)} collective-permute-done((f32[32,640]{1,0:T(8,128)}, f32[32,640]{1,0:T(8,128)S(1)}, u32[]{:S(2)}, u32[]{:S(2)}) %collective-permute-start.14) | collective-permute-done | bytes 81952 | tf_op jit(solution)/shard_map/ppermute | solution.py:192
  200.0 1.7 shard_map.60
  201.7 0.8 slice.51
  202.7 1.0 multiply_reduce_fusion
  203.7 1.7 convolution_bitcast_fusion
  (42 shorter events, 5.2 us)
Async XLA Ops:
  0.0 27.8 %copy-start = (bf16[1,1,1024,512]{3,2,1,0:T(8,128)(2,1)S(1)}, bf16[1,1,1024,512]{3,2,1,0:T(8,128)(2,1)}, u32[]{:S(2)}) copy-start(bf16[1,1,1024,512]{3,2,1,0:T(8,128)(2,1)} %param.5) | copy-start | bytes 3145732
  0.0 29.7 %copy-start.7 = (s32[1,1,8]{2,1,0:T(1,128)S(1)}, s32[1,1,8]{2,1,0:T(1,128)}, u32[]{:S(2)}) copy-start(s32[1,1,8]{2,1,0:T(1,128)} %param.7) | copy-start | bytes 100
  0.0 74.3 %copy-start.8 = (s32[1,1,8]{2,1,0:T(1,128)S(1)}, s32[1,1,8]{2,1,0:T(1,128)}, u32[]{:S(2)}) copy-start(s32[1,1,8]{2,1,0:T(1,128)} %param.8) | copy-start | bytes 100
  1.9 27.8 %collective-permute-start = (bf16[2,1,1,1,2,64,512]{6,5,4,3,2,1,0:T(8,128)(2,1)}, bf16[2,1,1,1,2,64,512]{6,5,4,3,2,1,0:T(8,128)(2,1)S(1)}, u32[]{:S(2)}, u32[]{:S(2)}) collective-permute-start(bf16[2,1,1,1,2,64,512]{6,5,4,3,2,1,0:T(8,128)(2,1)} %get-tuple-element.32), channel_id=1, source_target_pairs={{0,1},{1,2},{2,3},{4,5},{5,6},{6,7},{8,9},{9,10},{10,11},{12,13},{... | collective-permute-start | bytes 786440 | tf_op jit(solution)/shard_map/ppermute | solution.py:19
  11.0 49.6 %collective-permute-start.1 = (bf16[2,1,1,1,2,64,512]{6,5,4,3,2,1,0:T(8,128)(2,1)}, bf16[2,1,1,1,2,64,512]{6,5,4,3,2,1,0:T(8,128)(2,1)S(1)}, u32[]{:S(2)}, u32[]{:S(2)}) collective-permute-start(bf16[2,1,1,1,2,64,512]{6,5,4,3,2,1,0:T(8,128)(2,1)} %get-tuple-element.32), channel_id=1, source_target_pairs={{1,0},{2,1},{3,2},{5,4},{6,5},{7,6},{9,8},{10,9},{11,10},{13,12},{... | collective-permute-start | bytes 786440 | tf_op jit(solution)/shard_map/ppermute | solution.py:19
  12.3 53.9 %collective-permute-start.3 = (bf16[2,1,1,1,2,64,512]{6,5,4,3,2,1,0:T(8,128)(2,1)S(1)}, bf16[2,1,1,1,2,64,512]{6,5,4,3,2,1,0:T(8,128)(2,1)S(1)}, u32[]{:S(2)}, u32[]{:S(2)}) collective-permute-start(bf16[2,1,1,1,2,64,512]{6,5,4,3,2,1,0:T(8,128)(2,1)S(1)} %get-tuple-element.31), channel_id=1, source_target_pairs={{0,1},{1,2},{2,3},{4,5},{5,6},{6,7},{8,9},{9,10},{10,11},{12,13},{... | collective-permute-start | bytes 786440 | tf_op jit(solution)/shard_map/ppermute | solution.py:19
  22.0 44.9 %collective-permute-start.4 = (bf16[2,1,1,1,2,64,512]{6,5,4,3,2,1,0:T(8,128)(2,1)S(1)}, bf16[2,1,1,1,2,64,512]{6,5,4,3,2,1,0:T(8,128)(2,1)S(1)}, u32[]{:S(2)}, u32[]{:S(2)}) collective-permute-start(bf16[2,1,1,1,2,64,512]{6,5,4,3,2,1,0:T(8,128)(2,1)S(1)} %get-tuple-element.31), channel_id=1, source_target_pairs={{1,0},{2,1},{3,2},{5,4},{6,5},{7,6},{9,8},{10,9},{11,10},{13,12},{... | collective-permute-start | bytes 786440 | tf_op jit(solution)/shard_map/ppermute | solution.py:19
  23.3 71.1 %collective-permute-start.6 = (bf16[2,2,1,1,2,64,512]{6,5,4,3,2,1,0:T(8,128)(2,1)}, bf16[2,2,1,1,2,64,512]{6,5,4,3,2,1,0:T(8,128)(2,1)}, u32[]{:S(2)}, u32[]{:S(2)}) collective-permute-start(bf16[2,2,1,1,2,64,512]{6,5,4,3,2,1,0:T(8,128)(2,1)} %param.6), channel_id=1, source_target_pairs={{0,4},{4,8},{8,12},{1,5},{5,9},{9,13},{2,6},{6,10},{10,14},{3,7},{... | collective-permute-start | bytes 1572872 | tf_op jit(solution)/shard_map/ppermute | solution.py:19
  61.3 16.2 %collective-permute-start.2 = (bf16[2,1,1,2,2,64,512]{6,5,4,3,2,1,0:T(8,128)(2,1)}, bf16[2,1,1,2,2,64,512]{6,5,4,3,2,1,0:T(8,128)(2,1)S(1)}, u32[]{:S(2)}, u32[]{:S(2)}) collective-permute-start(bf16[2,1,1,2,2,64,512]{6,5,4,3,2,1,0:T(8,128)(2,1)} %constant_dynamic-update-slice_fusion), channel_id=1, source_target_pairs={{0,4},{4,8},{8,12},{1,5},{5,9},{9,13},{2,6},{6,10},{10,14},{3,7},{... | collective-permute-start | bytes 1572872 | tf_op jit(solution)/shard_map/ppermute | solution.py:19
  64.8 17.0 %collective-permute-start.7 = (bf16[2,1,1,2,2,64,512]{6,5,4,3,2,1,0:T(8,128)(2,1)}, bf16[2,1,1,2,2,64,512]{6,5,4,3,2,1,0:T(8,128)(2,1)S(1)}, u32[]{:S(2)}, u32[]{:S(2)}) collective-permute-start(bf16[2,1,1,2,2,64,512]{6,5,4,3,2,1,0:T(8,128)(2,1)} %constant_dynamic-update-slice_fusion), channel_id=1, source_target_pairs={{4,0},{8,4},{12,8},{5,1},{9,5},{13,9},{6,2},{10,6},{14,10},{7,3},{... | collective-permute-start | bytes 1572872 | tf_op jit(solution)/shard_map/ppermute | solution.py:19
  67.6 19.0 %collective-permute-start.5 = (bf16[2,1,1,2,2,64,512]{6,5,4,3,2,1,0:T(8,128)(2,1)}, bf16[2,1,1,2,2,64,512]{6,5,4,3,2,1,0:T(8,128)(2,1)}, u32[]{:S(2)}, u32[]{:S(2)}) collective-permute-start(bf16[2,1,1,2,2,64,512]{6,5,4,3,2,1,0:T(8,128)(2,1)} %constant_dynamic-update-slice_fusion.2), channel_id=1, source_target_pairs={{0,4},{4,8},{8,12},{1,5},{5,9},{9,13},{2,6},{6,10},{10,14},{3,7},{... | collective-permute-start | bytes 1572872 | tf_op jit(solution)/shard_map/ppermute | solution.py:19
  73.0 20.2 %collective-permute-start.8 = (bf16[2,1,1,2,2,64,512]{6,5,4,3,2,1,0:T(8,128)(2,1)}, bf16[2,1,1,2,2,64,512]{6,5,4,3,2,1,0:T(8,128)(2,1)}, u32[]{:S(2)}, u32[]{:S(2)}) collective-permute-start(bf16[2,1,1,2,2,64,512]{6,5,4,3,2,1,0:T(8,128)(2,1)} %constant_dynamic-update-slice_fusion.2), channel_id=1, source_target_pairs={{4,0},{8,4},{12,8},{5,1},{9,5},{13,9},{6,2},{10,6},{14,10},{7,3},{... | collective-permute-start | bytes 1572872 | tf_op jit(solution)/shard_map/ppermute | solution.py:19
  77.5 24.5 %collective-permute-start.9 = (bf16[2,2,1,1,2,64,512]{6,5,4,3,2,1,0:T(8,128)(2,1)}, bf16[2,2,1,1,2,64,512]{6,5,4,3,2,1,0:T(8,128)(2,1)S(1)}, u32[]{:S(2)}, u32[]{:S(2)}) collective-permute-start(bf16[2,2,1,1,2,64,512]{6,5,4,3,2,1,0:T(8,128)(2,1)} %param.6), channel_id=1, source_target_pairs={{4,0},{8,4},{12,8},{5,1},{9,5},{13,9},{6,2},{10,6},{14,10},{7,3},{... | collective-permute-start | bytes 1572872 | tf_op jit(solution)/shard_map/ppermute | solution.py:19
  131.0 72.6 %copy-start.3 = (bf16[512,512]{1,0:T(8,128)(2,1)S(1)}, bf16[512,512]{1,0:T(8,128)(2,1)}, u32[]{:S(2)}) copy-start(bf16[512,512]{1,0:T(8,128)(2,1)} %param.9) | copy-start | bytes 1572868
  131.1 5.3 %collective-permute-start.10 = (f32[512,640]{1,0:T(8,128)}, f32[512,640]{1,0:T(8,128)S(1)}, u32[]{:S(2)}, u32[]{:S(2)}) collective-permute-start(f32[512,640]{1,0:T(8,128)} %get-tuple-element.16), channel_id=1, source_target_pairs={{0,16},{16,0},{32,48},{48,32},{64,80},{80,64},{96,112},{112,96},{1... | collective-permute-start | bytes 3932168 | tf_op jit(solution)/shard_map/ppermute | solution.py:192
  136.3 1.1 copy-start.1
  141.4 18.9 %collective-permute-start.11 = (f32[256,640]{1,0:T(8,128)}, f32[256,640]{1,0:T(8,128)S(1)}, u32[]{:S(2)}, u32[]{:S(2)}) collective-permute-start(f32[256,640]{1,0:T(8,128)} %get-tuple-element.18), channel_id=1, source_target_pairs={{0,32},{16,48},{32,0},{48,16},{64,96},{80,112},{96,64},{112,80},{1... | collective-permute-start | bytes 1966088 | tf_op jit(solution)/shard_map/ppermute | solution.py:192
  160.2 0.8 copy-start.2
  163.9 11.0 %collective-permute-start.12 = (f32[128,640]{1,0:T(8,128)}, f32[128,640]{1,0:T(8,128)S(1)}, u32[]{:S(2)}, u32[]{:S(2)}) collective-permute-start(f32[128,640]{1,0:T(8,128)} %get-tuple-element.20), channel_id=1, source_target_pairs={{0,128},{16,144},{32,160},{48,176},{64,192},{80,208},{96,224},{112... | collective-permute-start | bytes 983048 | tf_op jit(solution)/shard_map/ppermute | solution.py:192
  174.9 0.7 copy-start.4
  177.8 11.0 %collective-permute-start.13 = (f32[64,640]{1,0:T(8,128)}, f32[64,640]{1,0:T(8,128)S(1)}, u32[]{:S(2)}, u32[]{:S(2)}) collective-permute-start(f32[64,640]{1,0:T(8,128)} %get-tuple-element.22), channel_id=1, source_target_pairs={{0,64},{16,80},{32,96},{48,112},{64,0},{80,16},{96,32},{112,48},{1... | collective-permute-start | bytes 491528 | tf_op jit(solution)/shard_map/ppermute | solution.py:192
  188.8 0.7 copy-start.5
  191.3 8.0 %collective-permute-start.14 = (f32[32,640]{1,0:T(8,128)}, f32[32,640]{1,0:T(8,128)S(1)}, u32[]{:S(2)}, u32[]{:S(2)}) collective-permute-start(f32[32,640]{1,0:T(8,128)} %get-tuple-element.24), channel_id=1, source_target_pairs={{0,256},{16,272},{32,288},{48,304},{64,320},{80,336},{96,352},{112... | collective-permute-start | bytes 245768 | tf_op jit(solution)/shard_map/ppermute | solution.py:192
  199.4 0.6 copy-start.6

commit v5 on v4

--- a/solution.py
+++ b/solution.py
@@ -20,28 +20,48 @@
 
 
 def neighbourhood(kv_blocks):
+    left = shifted(kv_blocks, "width", True)
+    right = shifted(kv_blocks, "width", False)
     up_mid = shifted(kv_blocks, "height", True)
     down_mid = shifted(kv_blocks, "height", False)
-    frames = kv_blocks.shape[1]
-    rows = []
-    for f in range(frames):
-        own = kv_blocks[:, f : f + 1]
-        left = shifted(own, "width", True)
-        right = shifted(own, "width", False)
-        sides = jnp.concatenate([left, right], axis=3)
-        up_sides = shifted(sides, "height", True)
-        down_sides = shifted(sides, "height", False)
-        row = jnp.concatenate([left, own, right], axis=3)
-        rows.append((row, up_sides, down_sides))
-    row = jnp.concatenate([r[0] for r in rows], axis=1)
-    up_sides = jnp.concatenate([r[1] for r in rows], axis=1)
-    down_sides = jnp.concatenate([r[2] for r in rows], axis=1)
+    left, right, up_mid, down_mid = lax.optimization_barrier((left, right, up_mid, down_mid))
+    sides = jnp.concatenate([left, right], axis=3)
+    up_sides = shifted(sides, "height", True)
+    down_sides = shifted(sides, "height", False)
+    row = jnp.concatenate([left, kv_blocks, right], axis=3)
     up = jnp.concatenate([up_sides[:, :, :, :1], up_mid, up_sides[:, :, :, 1:]], axis=3)
     down = jnp.concatenate([down_sides[:, :, :, :1], down_mid, down_sides[:, :, :, 1:]], axis=3)
     return jnp.concatenate([up, row, down], axis=2)
 
 
 PACK = 128
+
+
+def encode_stats(stats):
+    lane = lax.broadcasted_iota(jnp.int32, (1, PACK), 1)
+    used = lane < 2 * HEADS
+    hi = stats.astype(jnp.bfloat16).astype(jnp.float32)
+    rest = stats - hi
+    mid = rest.astype(jnp.bfloat16).astype(jnp.float32)
+    lo = rest - mid
+    zero = jnp.float32(0.0)
+    coded = (
+        jnp.where(used, hi, zero)
+        + pltpu.roll(jnp.where(used, mid, zero), 2 * HEADS, 1)
+        + pltpu.roll(jnp.where(used, lo, zero), 4 * HEADS, 1)
+    )
+    return coded.astype(jnp.bfloat16)
+
+
+def decode_stats(coded):
+    lane = lax.broadcasted_iota(jnp.int32, (1, PACK), 1)
+    used = lane < 2 * HEADS
+    wide = coded.astype(jnp.float32)
+    zero = jnp.float32(0.0)
+    hi = jnp.where(used, wide, zero)
+    mid = jnp.where(used, pltpu.roll(wide, PACK - 2 * HEADS, 1), zero)
+    lo = jnp.where(used, pltpu.roll(wide, PACK - 4 * HEADS, 1), zero)
+    return (hi + mid) + lo
 
 
 def attention_kernel(q_ref, k_ref, v_ref, keep_ref, first_ref, second_ref):
@@ -78,15 +98,14 @@
             stats = jnp.where(stat_lane == head, top, stats)
             stats = jnp.where(stat_lane == HEADS + head, total, stats)
         blocks.append(jnp.where(low, outs[0], outs[1]))
-    packed = jnp.concatenate(blocks + [stats], axis=1)
-
     @pl.when(step < half)
     def _():
-        first_ref[...] = packed
+        first_ref[...] = jnp.concatenate(blocks + [stats], axis=1)
 
     @pl.when(step >= half)
     def _():
-        second_ref[...] = packed
+        sent = [b.astype(jnp.bfloat16) for b in blocks]
+        second_ref[...] = jnp.concatenate(sent + [encode_stats(stats)], axis=1)
 
 
 def attention(query_rows, keys, values, keep):
@@ -96,6 +115,7 @@
     half = tiles // 2
     flops = 2 * 2 * qtok * count * 2 * width
     packed = jax.ShapeDtypeStruct((qtok // 2, width + PACK), jnp.float32)
+    sent = jax.ShapeDtypeStruct((qtok // 2, width + PACK), jnp.bfloat16)
     return pl.pallas_call(
         attention_kernel,
         grid=(tiles,),
@@ -109,7 +129,7 @@
             pl.BlockSpec((TQ, width + PACK), lambda i: (jnp.minimum(i, half - 1), 0)),
             pl.BlockSpec((TQ, width + PACK), lambda i: (jnp.maximum(i - half, 0), 0)),
         ],
-        out_shape=[packed, packed],
+        out_shape=[packed, sent],
         cost_estimate=pl.CostEstimate(
             flops=flops,
             transcendentals=qtok * count * HEADS,
@@ -121,7 +141,7 @@
 def merge_kernel(a_ref, b_ref, *out_refs):
     width = a_ref.shape[1] - PACK
     sa = a_ref[:, pl.ds(width, PACK)]
-    sb = b_ref[:, pl.ds(width, PACK)]
+    sb = decode_stats(b_ref[:, pl.ds(width, PACK)])
     stat_lane = lax.broadcasted_iota(jnp.int32, (1, PACK), 1)
     top = jnp.maximum(sa, sb)
     fa = jnp.exp(sa - top)
@@ -144,23 +164,24 @@
         cols = pl.ds(pair * 2 * HD, 2 * HD)
         f_a = jnp.where(low, heads_a[2 * pair], heads_a[2 * pair + 1])
         f_b = jnp.where(low, heads_b[2 * pair], heads_b[2 * pair + 1])
-        blocks.append(a_ref[:, cols] * f_a + b_ref[:, cols] * f_b)
-    merged = jnp.concatenate(blocks + [stats], axis=1)
+        blocks.append(a_ref[:, cols] * f_a + b_ref[:, cols].astype(jnp.float32) * f_b)
     if len(out_refs) == 1:
-        out_refs[0][...] = merged
+        out_refs[0][...] = jnp.concatenate(blocks + [stats], axis=1)
     else:
-        half = merged.shape[0] // 2
-        out_refs[0][...] = merged[:half]
-        out_refs[1][...] = merged[half:]
+        half = stats.shape[0] // 2
+        out_refs[0][...] = jnp.concatenate([b[:half] for b in blocks] + [stats[:half]], axis=1)
+        sent = [b[half:].astype(jnp.bfloat16) for b in blocks]
+        out_refs[1][...] = jnp.concatenate(sent + [encode_stats(stats[half:])], axis=1)
 
 
 def merge(kept, got, split):
     rows, cols = kept.shape
     count = 2 if split else 1
     shape = jax.ShapeDtypeStruct((rows // count, cols), jnp.float32)
+    shapes = [shape, jax.ShapeDtypeStruct(shape.shape, jnp.bfloat16)] if split else [shape]
     return pl.pallas_call(
         merge_kernel,
-        out_shape=[shape] * count,
+        out_shape=shapes,
         cost_estimate=pl.CostEstimate(
             flops=4 * rows * cols, transcendentals=2 * rows * PACK, bytes_accessed=12 * rows * cols
         ),

time: 206 us -> 186 us (0.903)
  starting transfers between devices: 50.3 us -> 32.8 us
  local copies, waits for them, and re-layouts: 19.1 us -> 15.7 us
    ppermute x10 -> x6, starting transfers between devices: 38.4 us -> 21.1 us  [shifted(): return lax.ppermute(array, axis, pairs)]
    ppermute x10 -> x6, waiting for transfers between devices: 53.3 us -> 68.4 us  [shifted(): return lax.ppermute(array, axis, pairs)]
    ppermute x5, waiting for transfers between devices: 42.3 us -> 27.6 us  [tree_reduce(): got = lax.ppermute(second, 'tm', pairs)]
    concatenate x2 -> x0, local copies, waits for them, and re-layouts: 2.17 us -> none  [the longest x1 1.08 us: neighbourhood(): down_sides = jnp.concatenate([r[2] for r in rows], axis=1)]
    unnamed x22 -> x25, local copies, waits for them, and re-layouts: 5.48 us -> 4.47 us
  transfers between devices with their start and end apart: 15 -> 11, of which waited for: 11 -> 9; matrix products, arithmetic and copies ran while one was open for 4% -> 3% of each run, Pallas kernels for 0% -> 0%
where the time goes in v5:
time: 186 us
  waiting for transfers between devices  96.1 us (52%)
  starting transfers between devices  32.8 us (18%)
  Pallas kernels  31.6 us (17%)
  local copies, waits for them, and re-layouts  15.7 us (8%)
  other arithmetic  7.39 us (4%)
    ppermute x6, waiting for transfers between devices, shifted(): return lax.ppermute(array, axis, pairs)  68.4 us
    ppermute x5, waiting for transfers between devices, tree_reduce(): got = lax.ppermute(second, 'tm', pairs)  27.6 us
    ppermute x6, starting transfers between devices, shifted(): return lax.ppermute(array, axis, pairs)  21.1 us
    pallas_call x1, Pallas kernels, attention(): pl.pallas_call(attention_kernel, grid=(tiles,), in_specs=[pl.BlockSpec((T...  19.3 us
    pallas_call x5, Pallas kernels, merge(): pl.pallas_call(merge_kernel, out_shape=shapes, cost_estimate=pl.CostEstim...  12.4 us
    ppermute x5, starting transfers between devices, tree_reduce(): got = lax.ppermute(second, 'tm', pairs)  11.8 us
    unnamed x25, local copies, waits for them, and re-layouts  4.47 us
  transfers between devices with their start and end apart: 11, of which 9 were waited for; matrix products, arithmetic and copies ran while one was open for 3% of the time, Pallas kernels for 0%

profile of v5, /device:TPU:6, one launch (start us, length us, event | category | flops | bytes accessed | tf_op | source)
XLA Modules:
  0.0 185.6 jit_solution(14725880655495224155)
XLA Ops:
  0.0 9.2 %collective-permute-start = (bf16[2,2,1,1,2,64,512]{6,5,4,3,2,1,0:T(8,128)(2,1)}, bf16[2,2,1,1,2,64,512]{6,5,4,3,2,1,0:T(8,128)(2,1)S(1)}, u32[]{:S(2)}, u32[]{:S(2)}) collective-permute-start(bf16[2,2,1,1,2,64,512]{6,5,4,3,2,1,0:T(8,128)(2,1)} %param.6), channel_id=1, source_target_pairs={{0,1},{1,2},{2,3},{4,5},{5,6},{6,7},{8,9},{9,10},{10,11},{12,13},{... | collective-permute-start | bytes 1572872 | tf_op jit(solution)/shard_map/ppermute | solution.py:19
  9.3 1.3 collective-permute-start.1
  10.6 3.5 %collective-permute-start.2 = (bf16[2,2,1,1,2,64,512]{6,5,4,3,2,1,0:T(8,128)(2,1)}, bf16[2,2,1,1,2,64,512]{6,5,4,3,2,1,0:T(8,128)(2,1)S(1)}, u32[]{:S(2)}, u32[]{:S(2)}) collective-permute-start(bf16[2,2,1,1,2,64,512]{6,5,4,3,2,1,0:T(8,128)(2,1)} %param.6), channel_id=1, source_target_pairs={{0,4},{4,8},{8,12},{1,5},{5,9},{9,13},{2,6},{6,10},{10,14},{3,7},{... | collective-permute-start | bytes 1572872 | tf_op jit(solution)/shard_map/ppermute | solution.py:19
  14.1 1.3 collective-permute-start.3
  15.4 0.7 fusion.1
  16.1 4.8 %collective-permute-done = bf16[2,2,1,1,2,64,512]{6,5,4,3,2,1,0:T(8,128)(2,1)S(1)} collective-permute-done((bf16[2,2,1,1,2,64,512]{6,5,4,3,2,1,0:T(8,128)(2,1)}, bf16[2,2,1,1,2,64,512]{6,5,4,3,2,1,0:T(8,128)(2,1)S(1)}, u32[]{:S(2)}, u32[]{:S(2)}) %collective-permute-start) | collective-permute-done | bytes 524320 | tf_op jit(solution)/shard_map/ppermute | solution.py:19
  20.8 43.0 %collective-permute-done.1 = bf16[2,2,1,1,2,64,512]{6,5,4,3,2,1,0:T(8,128)(2,1)S(1)} collective-permute-done((bf16[2,2,1,1,2,64,512]{6,5,4,3,2,1,0:T(8,128)(2,1)}, bf16[2,2,1,1,2,64,512]{6,5,4,3,2,1,0:T(8,128)(2,1)S(1)}, u32[]{:S(2)}, u32[]{:S(2)}) %collective-permute-start.1) | collective-permute-done | bytes 524320 | tf_op jit(solution)/shard_map/ppermute | solution.py:19
  63.9 1.0 constant_dynamic-update-slice_fusion.1
  64.9 0.8 constant_dynamic-update-slice_fusion
  65.7 4.4 %collective-permute-start.4 = (bf16[2,2,1,2,2,64,512]{6,5,4,3,2,1,0:T(8,128)(2,1)}, bf16[2,2,1,2,2,64,512]{6,5,4,3,2,1,0:T(8,128)(2,1)}, u32[]{:S(2)}, u32[]{:S(2)}) collective-permute-start(bf16[2,2,1,2,2,64,512]{6,5,4,3,2,1,0:T(8,128)(2,1)} %constant_dynamic-update-slice_fusion), channel_id=1, source_target_pairs={{0,4},{4,8},{8,12},{1,5},{5,9},{9,13},{2,6},{6,10},{10,14},{3,7},{... | collective-permute-start | bytes 3145736 | tf_op jit(solution)/shard_map/ppermute | solution.py:19
  70.4 0.7 convert_element_type.12.keep_ref
  71.1 1.3 collective-permute-start.5
  72.4 0.7 fusion.3
  73.1 0.6 gather_fusion
  73.7 0.8 compare_and_fusion
  74.5 1.2 bitcast_select_fusion.q_ref
  75.7 15.9 %collective-permute-done.4 = bf16[2,2,1,2,2,64,512]{6,5,4,3,2,1,0:T(8,128)(2,1)} collective-permute-done((bf16[2,2,1,2,2,64,512]{6,5,4,3,2,1,0:T(8,128)(2,1)}, bf16[2,2,1,2,2,64,512]{6,5,4,3,2,1,0:T(8,128)(2,1)}, u32[]{:S(2)}, u32[]{:S(2)}) %collective-permute-start.4) | collective-permute-done | bytes 1048608 | tf_op jit(solution)/shard_map/ppermute | solution.py:19
  91.6 1.3 fusion.5
  92.9 4.7 %collective-permute-done.5 = bf16[2,2,1,2,2,64,512]{6,5,4,3,2,1,0:T(8,128)(2,1)} collective-permute-done((bf16[2,2,1,2,2,64,512]{6,5,4,3,2,1,0:T(8,128)(2,1)}, bf16[2,2,1,2,2,64,512]{6,5,4,3,2,1,0:T(8,128)(2,1)}, u32[]{:S(2)}, u32[]{:S(2)}) %collective-permute-start.5) | collective-permute-done | bytes 1048608 | tf_op jit(solution)/shard_map/ppermute | solution.py:19
  97.6 1.3 fusion.6
  98.9 2.8 %maximum_maximum_fusion = bf16[2,2,3,3,2,64,512]{6,5,4,3,2,1,0:T(8,128)(2,1)} fusion(bf16[2,2,1,1,2,64,512]{6,5,4,3,2,1,0:T(8,128)(2,1)S(1)} %get-tuple-element.38, bf16[2,2,1,1,2,64,512]{6,5,4,3,2,1,0:T(8,128)(2,1)S(1)} %copy-done.6, bf16[2,2,1,1,2,64,512]{6,5,4,3,2,1,0:T(8,128)(2,1)S(1)} %get-tuple-element.37, ...), kind=kLoop, calls=%fused_computation.2 | loop fusion | flops 18874368 | bytes 9437184 | tf_op jit(solution)/shard_map/concatenate | solution.py:34
  101.7 3.0 %gather_fusion.1 = bf16[8,2,2,64,512]{4,3,2,1,0:T(8,128)(2,1)S(1)} fusion(bf16[2,2,18,64,512]{4,3,2,1,0:T(8,128)(2,1)} %bitcast.22, s32[1024]{0:T(1024)S(1)} %get-tuple-element.39), kind=kCustom, calls=%fused_computation.1 | custom fusion | bytes 4194336 | tf_op jit(solution)/shard_map/jit(_take)/gather | solution.py:230
  105.2 1.1 copy.6
  106.3 1.1 copy.7
  107.4 19.3 %shard_map.55 = (f32[512,640]{1,0:T(8,128)}, bf16[512,640]{1,0:T(8,128)(2,1)}) custom-call(bf16[1024,512]{1,0:T(8,128)(2,1)} %bitcast_select_fusion.q_ref, bf16[1024,512]{1,0:T(8,128)(2,1)} %bitcast.23, bf16[1024,512]{1,0:T(8,128)(2,1)} %bitcast.24, s32[1,1024]{1,0:T(1,128)} %convert_element_type.12.keep_ref), custom_call_target="tpu_custom_call" | custom-call | flops 4294967296 | bytes 5242880 | tf_op jit(solution)/shard_map/pallas_call | solution.py:119
  126.7 1.9 %collective-permute-start.6 = (bf16[512,640]{1,0:T(8,128)(2,1)}, bf16[512,640]{1,0:T(8,128)(2,1)S(1)}, u32[]{:S(2)}, u32[]{:S(2)}) collective-permute-start(bf16[512,640]{1,0:T(8,128)(2,1)} %get-tuple-element.24), channel_id=1, source_target_pairs={{0,16},{16,0},{32,48},{48,32},{64,80},{80,64},{96,112},{112,96},{1... | collective-permute-start | bytes 1966088 | tf_op jit(solution)/shard_map/ppermute | solution.py:213
  128.6 2.3 %collective-permute-done.6.b_ref = bf16[512,640]{1,0:T(8,128)(2,1)S(1)} collective-permute-done((bf16[512,640]{1,0:T(8,128)(2,1)}, bf16[512,640]{1,0:T(8,128)(2,1)S(1)}, u32[]{:S(2)}, u32[]{:S(2)}) %collective-permute-start.6) | collective-permute-done | bytes 655392 | tf_op jit(solution)/shard_map/ppermute | solution.py:213
  130.9 0.8 copy-done.1
  131.7 3.8 %shard_map.56 = (f32[256,640]{1,0:T(8,128)}, bf16[256,640]{1,0:T(8,128)(2,1)}) custom-call(f32[512,640]{1,0:T(8,128)} %get-tuple-element.23.a_ref, bf16[512,640]{1,0:T(8,128)(2,1)} %copy-done.1), custom_call_target="tpu_custom_call" | custom-call | flops 1310720 | bytes 3932160 | tf_op jit(solution)/shard_map/pallas_call | solution.py:182
  135.5 1.9 %collective-permute-start.7 = (bf16[256,640]{1,0:T(8,128)(2,1)}, bf16[256,640]{1,0:T(8,128)(2,1)S(1)}, u32[]{:S(2)}, u32[]{:S(2)}) collective-permute-start(bf16[256,640]{1,0:T(8,128)(2,1)} %get-tuple-element.26), channel_id=1, source_target_pairs={{0,32},{16,48},{32,0},{48,16},{64,96},{80,112},{96,64},{112,80},{1... | collective-permute-start | bytes 983048 | tf_op jit(solution)/shard_map/ppermute | solution.py:213
  137.4 9.9 %collective-permute-done.7.b_ref = bf16[256,640]{1,0:T(8,128)(2,1)S(1)} collective-permute-done((bf16[256,640]{1,0:T(8,128)(2,1)}, bf16[256,640]{1,0:T(8,128)(2,1)S(1)}, u32[]{:S(2)}, u32[]{:S(2)}) %collective-permute-start.7) | collective-permute-done | bytes 327712 | tf_op jit(solution)/shard_map/ppermute | solution.py:213
  147.3 0.7 copy-done.8
  148.1 2.7 %shard_map.57 = (f32[128,640]{1,0:T(8,128)}, bf16[128,640]{1,0:T(8,128)(2,1)}) custom-call(f32[256,640]{1,0:T(8,128)} %get-tuple-element.25.a_ref, bf16[256,640]{1,0:T(8,128)(2,1)} %copy-done.8), custom_call_target="tpu_custom_call" | custom-call | flops 655360 | bytes 1966080 | tf_op jit(solution)/shard_map/pallas_call | solution.py:182
  150.8 2.7 %collective-permute-start.8 = (bf16[128,640]{1,0:T(8,128)(2,1)}, bf16[128,640]{1,0:T(8,128)(2,1)S(1)}, u32[]{:S(2)}, u32[]{:S(2)}) collective-permute-start(bf16[128,640]{1,0:T(8,128)(2,1)} %get-tuple-element.28), channel_id=1, source_target_pairs={{0,128},{16,144},{32,160},{48,176},{64,192},{80,208},{96,224},{112... | collective-permute-start | bytes 491528 | tf_op jit(solution)/shard_map/ppermute | solution.py:213
  153.5 4.8 %collective-permute-done.8.b_ref = bf16[128,640]{1,0:T(8,128)(2,1)S(1)} collective-permute-done((bf16[128,640]{1,0:T(8,128)(2,1)}, bf16[128,640]{1,0:T(8,128)(2,1)S(1)}, u32[]{:S(2)}, u32[]{:S(2)}) %collective-permute-start.8) | collective-permute-done | bytes 163872 | tf_op jit(solution)/shard_map/ppermute | solution.py:213
  158.3 0.7 copy-done.9
  159.0 2.2 %shard_map.58 = (f32[64,640]{1,0:T(8,128)}, bf16[64,640]{1,0:T(8,128)(2,1)}) custom-call(f32[128,640]{1,0:T(8,128)} %get-tuple-element.27.a_ref, bf16[128,640]{1,0:T(8,128)(2,1)} %copy-done.9), custom_call_target="tpu_custom_call" | custom-call | flops 327680 | bytes 983040 | tf_op jit(solution)/shard_map/pallas_call | solution.py:182
  161.1 1.9 %collective-permute-start.9 = (bf16[64,640]{1,0:T(8,128)(2,1)}, bf16[64,640]{1,0:T(8,128)(2,1)S(1)}, u32[]{:S(2)}, u32[]{:S(2)}) collective-permute-start(bf16[64,640]{1,0:T(8,128)(2,1)} %get-tuple-element.30), channel_id=1, source_target_pairs={{0,64},{16,80},{32,96},{48,112},{64,0},{80,16},{96,32},{112,48},{1... | collective-permute-start | bytes 245768 | tf_op jit(solution)/shard_map/ppermute | solution.py:213
  163.0 6.4 %collective-permute-done.9.b_ref = bf16[64,640]{1,0:T(8,128)(2,1)S(1)} collective-permute-done((bf16[64,640]{1,0:T(8,128)(2,1)}, bf16[64,640]{1,0:T(8,128)(2,1)S(1)}, u32[]{:S(2)}, u32[]{:S(2)}) %collective-permute-start.9) | collective-permute-done | bytes 81952 | tf_op jit(solution)/shard_map/ppermute | solution.py:213
  169.4 0.6 copy-done.10
  170.1 1.9 %shard_map.59 = (f32[32,640]{1,0:T(8,128)}, bf16[32,640]{1,0:T(8,128)(2,1)}) custom-call(f32[64,640]{1,0:T(8,128)} %get-tuple-element.29.a_ref, bf16[64,640]{1,0:T(8,128)(2,1)} %copy-done.10), custom_call_target="tpu_custom_call" | custom-call | flops 163840 | bytes 491520 | tf_op jit(solution)/shard_map/pallas_call | solution.py:182
  172.0 3.3 %collective-permute-start.10 = (bf16[32,640]{1,0:T(8,128)(2,1)}, bf16[32,640]{1,0:T(8,128)(2,1)S(1)}, u32[]{:S(2)}, u32[]{:S(2)}) collective-permute-start(bf16[32,640]{1,0:T(8,128)(2,1)} %get-tuple-element.32), channel_id=1, source_target_pairs={{0,256},{16,272},{32,288},{48,304},{64,320},{80,336},{96,352},{112... | collective-permute-start | bytes 122888 | tf_op jit(solution)/shard_map/ppermute | solution.py:213
  175.3 4.3 %collective-permute-done.10.b_ref = bf16[32,640]{1,0:T(8,128)(2,1)S(1)} collective-permute-done((bf16[32,640]{1,0:T(8,128)(2,1)}, bf16[32,640]{1,0:T(8,128)(2,1)S(1)}, u32[]{:S(2)}, u32[]{:S(2)}) %collective-permute-start.10) | collective-permute-done | bytes 40992 | tf_op jit(solution)/shard_map/ppermute | solution.py:213
  179.6 0.6 copy-done.11
  180.2 1.7 shard_map.60
  181.9 0.8 slice.43
  182.9 1.0 multiply_reduce_fusion
  183.9 1.7 convolution_bitcast_fusion
  (32 shorter events, 1.0 us)
Async XLA Ops:
  0.0 73.1 %copy-start = (bf16[1,1,1024,512]{3,2,1,0:T(8,128)(2,1)S(1)}, bf16[1,1,1024,512]{3,2,1,0:T(8,128)(2,1)}, u32[]{:S(2)}) copy-start(bf16[1,1,1024,512]{3,2,1,0:T(8,128)(2,1)} %param.5) | copy-start | bytes 3145732
  0.0 20.8 %collective-permute-start = (bf16[2,2,1,1,2,64,512]{6,5,4,3,2,1,0:T(8,128)(2,1)}, bf16[2,2,1,1,2,64,512]{6,5,4,3,2,1,0:T(8,128)(2,1)S(1)}, u32[]{:S(2)}, u32[]{:S(2)}) collective-permute-start(bf16[2,2,1,1,2,64,512]{6,5,4,3,2,1,0:T(8,128)(2,1)} %param.6), channel_id=1, source_target_pairs={{0,1},{1,2},{2,3},{4,5},{5,6},{6,7},{8,9},{9,10},{10,11},{12,13},{... | collective-permute-start | bytes 1572872 | tf_op jit(solution)/shard_map/ppermute | solution.py:19
  9.3 54.6 %collective-permute-start.1 = (bf16[2,2,1,1,2,64,512]{6,5,4,3,2,1,0:T(8,128)(2,1)}, bf16[2,2,1,1,2,64,512]{6,5,4,3,2,1,0:T(8,128)(2,1)S(1)}, u32[]{:S(2)}, u32[]{:S(2)}) collective-permute-start(bf16[2,2,1,1,2,64,512]{6,5,4,3,2,1,0:T(8,128)(2,1)} %param.6), channel_id=1, source_target_pairs={{1,0},{2,1},{3,2},{5,4},{6,5},{7,6},{9,8},{10,9},{11,10},{13,12},{... | collective-permute-start | bytes 1572872 | tf_op jit(solution)/shard_map/ppermute | solution.py:19
  10.6 53.3 %collective-permute-start.2 = (bf16[2,2,1,1,2,64,512]{6,5,4,3,2,1,0:T(8,128)(2,1)}, bf16[2,2,1,1,2,64,512]{6,5,4,3,2,1,0:T(8,128)(2,1)S(1)}, u32[]{:S(2)}, u32[]{:S(2)}) collective-permute-start(bf16[2,2,1,1,2,64,512]{6,5,4,3,2,1,0:T(8,128)(2,1)} %param.6), channel_id=1, source_target_pairs={{0,4},{4,8},{8,12},{1,5},{5,9},{9,13},{2,6},{6,10},{10,14},{3,7},{... | collective-permute-start | bytes 1572872 | tf_op jit(solution)/shard_map/ppermute | solution.py:19
  14.1 49.8 %collective-permute-start.3 = (bf16[2,2,1,1,2,64,512]{6,5,4,3,2,1,0:T(8,128)(2,1)}, bf16[2,2,1,1,2,64,512]{6,5,4,3,2,1,0:T(8,128)(2,1)S(1)}, u32[]{:S(2)}, u32[]{:S(2)}) collective-permute-start(bf16[2,2,1,1,2,64,512]{6,5,4,3,2,1,0:T(8,128)(2,1)} %param.6), channel_id=1, source_target_pairs={{4,0},{8,4},{12,8},{5,1},{9,5},{13,9},{6,2},{10,6},{14,10},{7,3},{... | collective-permute-start | bytes 1572872 | tf_op jit(solution)/shard_map/ppermute | solution.py:19
  63.9 9.2 %copy-start.3 = (bf16[2,2,1,1,2,64,512]{6,5,4,3,2,1,0:T(8,128)(2,1)}, bf16[2,2,1,1,2,64,512]{6,5,4,3,2,1,0:T(8,128)(2,1)S(1)}, u32[]{:S(2)}) copy-start(bf16[2,2,1,1,2,64,512]{6,5,4,3,2,1,0:T(8,128)(2,1)S(1)} %collective-permute-done.2) | copy-start | bytes 1572868
  63.9 9.2 %copy-start.5 = (bf16[2,2,1,1,2,64,512]{6,5,4,3,2,1,0:T(8,128)(2,1)}, bf16[2,2,1,1,2,64,512]{6,5,4,3,2,1,0:T(8,128)(2,1)S(1)}, u32[]{:S(2)}) copy-start(bf16[2,2,1,1,2,64,512]{6,5,4,3,2,1,0:T(8,128)(2,1)S(1)} %collective-permute-done.3) | copy-start | bytes 1572868
  65.7 25.9 %collective-permute-start.4 = (bf16[2,2,1,2,2,64,512]{6,5,4,3,2,1,0:T(8,128)(2,1)}, bf16[2,2,1,2,2,64,512]{6,5,4,3,2,1,0:T(8,128)(2,1)}, u32[]{:S(2)}, u32[]{:S(2)}) collective-permute-start(bf16[2,2,1,2,2,64,512]{6,5,4,3,2,1,0:T(8,128)(2,1)} %constant_dynamic-update-slice_fusion), channel_id=1, source_target_pairs={{0,4},{4,8},{8,12},{1,5},{5,9},{9,13},{2,6},{6,10},{10,14},{3,7},{... | collective-permute-start | bytes 3145736 | tf_op jit(solution)/shard_map/ppermute | solution.py:19
  71.1 26.5 %collective-permute-start.5 = (bf16[2,2,1,2,2,64,512]{6,5,4,3,2,1,0:T(8,128)(2,1)}, bf16[2,2,1,2,2,64,512]{6,5,4,3,2,1,0:T(8,128)(2,1)}, u32[]{:S(2)}, u32[]{:S(2)}) collective-permute-start(bf16[2,2,1,2,2,64,512]{6,5,4,3,2,1,0:T(8,128)(2,1)} %constant_dynamic-update-slice_fusion), channel_id=1, source_target_pairs={{4,0},{8,4},{12,8},{5,1},{9,5},{13,9},{6,2},{10,6},{14,10},{7,3},{... | collective-permute-start | bytes 3145736 | tf_op jit(solution)/shard_map/ppermute | solution.py:19
  73.7 25.2 %copy-start.2 = (bf16[2,2,1,1,2,64,512]{6,5,4,3,2,1,0:T(8,128)(2,1)S(1)}, bf16[2,2,1,1,2,64,512]{6,5,4,3,2,1,0:T(8,128)(2,1)}, u32[]{:S(2)}) copy-start(bf16[2,2,1,1,2,64,512]{6,5,4,3,2,1,0:T(8,128)(2,1)} %param.6) | copy-start | bytes 1572868
  73.7 25.2 %copy-start.4 = (bf16[2,2,1,1,2,64,512]{6,5,4,3,2,1,0:T(8,128)(2,1)S(1)}, bf16[2,2,1,1,2,64,512]{6,5,4,3,2,1,0:T(8,128)(2,1)}, u32[]{:S(2)}) copy-start(bf16[2,2,1,1,2,64,512]{6,5,4,3,2,1,0:T(8,128)(2,1)} %copy-done.3) | copy-start | bytes 1572868
  73.7 25.2 %copy-start.6 = (bf16[2,2,1,1,2,64,512]{6,5,4,3,2,1,0:T(8,128)(2,1)S(1)}, bf16[2,2,1,1,2,64,512]{6,5,4,3,2,1,0:T(8,128)(2,1)}, u32[]{:S(2)}) copy-start(bf16[2,2,1,1,2,64,512]{6,5,4,3,2,1,0:T(8,128)(2,1)} %copy-done.5) | copy-start | bytes 1572868
  107.4 76.5 %copy-start.7 = (bf16[512,512]{1,0:T(8,128)(2,1)S(1)}, bf16[512,512]{1,0:T(8,128)(2,1)}, u32[]{:S(2)}) copy-start(bf16[512,512]{1,0:T(8,128)(2,1)} %param.9) | copy-start | bytes 1572868
  126.7 4.2 %collective-permute-start.6 = (bf16[512,640]{1,0:T(8,128)(2,1)}, bf16[512,640]{1,0:T(8,128)(2,1)S(1)}, u32[]{:S(2)}, u32[]{:S(2)}) collective-permute-start(bf16[512,640]{1,0:T(8,128)(2,1)} %get-tuple-element.24), channel_id=1, source_target_pairs={{0,16},{16,0},{32,48},{48,32},{64,80},{80,64},{96,112},{112,96},{1... | collective-permute-start | bytes 1966088 | tf_op jit(solution)/shard_map/ppermute | solution.py:213
  130.8 0.8 copy-start.1
  135.5 11.8 %collective-permute-start.7 = (bf16[256,640]{1,0:T(8,128)(2,1)}, bf16[256,640]{1,0:T(8,128)(2,1)S(1)}, u32[]{:S(2)}, u32[]{:S(2)}) collective-permute-start(bf16[256,640]{1,0:T(8,128)(2,1)} %get-tuple-element.26), channel_id=1, source_target_pairs={{0,32},{16,48},{32,0},{48,16},{64,96},{80,112},{96,64},{112,80},{1... | collective-permute-start | bytes 983048 | tf_op jit(solution)/shard_map/ppermute | solution.py:213
  147.3 0.7 copy-start.8
  150.8 7.5 %collective-permute-start.8 = (bf16[128,640]{1,0:T(8,128)(2,1)}, bf16[128,640]{1,0:T(8,128)(2,1)S(1)}, u32[]{:S(2)}, u32[]{:S(2)}) collective-permute-start(bf16[128,640]{1,0:T(8,128)(2,1)} %get-tuple-element.28), channel_id=1, source_target_pairs={{0,128},{16,144},{32,160},{48,176},{64,192},{80,208},{96,224},{112... | collective-permute-start | bytes 491528 | tf_op jit(solution)/shard_map/ppermute | solution.py:213
  158.3 0.7 copy-start.9
  161.1 8.3 %collective-permute-start.9 = (bf16[64,640]{1,0:T(8,128)(2,1)}, bf16[64,640]{1,0:T(8,128)(2,1)S(1)}, u32[]{:S(2)}, u32[]{:S(2)}) collective-permute-start(bf16[64,640]{1,0:T(8,128)(2,1)} %get-tuple-element.30), channel_id=1, source_target_pairs={{0,64},{16,80},{32,96},{48,112},{64,0},{80,16},{96,32},{112,48},{1... | collective-permute-start | bytes 245768 | tf_op jit(solution)/shard_map/ppermute | solution.py:213
  169.4 0.6 copy-start.10
  172.0 7.6 %collective-permute-start.10 = (bf16[32,640]{1,0:T(8,128)(2,1)}, bf16[32,640]{1,0:T(8,128)(2,1)S(1)}, u32[]{:S(2)}, u32[]{:S(2)}) collective-permute-start(bf16[32,640]{1,0:T(8,128)(2,1)} %get-tuple-element.32), channel_id=1, source_target_pairs={{0,256},{16,272},{32,288},{48,304},{64,320},{80,336},{96,352},{112... | collective-permute-start | bytes 122888 | tf_op jit(solution)/shard_map/ppermute | solution.py:213
  179.6 0.6 copy-start.11

commit v6 on v4

--- a/solution.py
+++ b/solution.py
@@ -20,22 +20,15 @@
 
 
 def neighbourhood(kv_blocks):
+    left = shifted(kv_blocks, "width", True)
+    right = shifted(kv_blocks, "width", False)
     up_mid = shifted(kv_blocks, "height", True)
     down_mid = shifted(kv_blocks, "height", False)
-    frames = kv_blocks.shape[1]
-    rows = []
-    for f in range(frames):
-        own = kv_blocks[:, f : f + 1]
-        left = shifted(own, "width", True)
-        right = shifted(own, "width", False)
-        sides = jnp.concatenate([left, right], axis=3)
-        up_sides = shifted(sides, "height", True)
-        down_sides = shifted(sides, "height", False)
-        row = jnp.concatenate([left, own, right], axis=3)
-        rows.append((row, up_sides, down_sides))
-    row = jnp.concatenate([r[0] for r in rows], axis=1)
-    up_sides = jnp.concatenate([r[1] for r in rows], axis=1)
-    down_sides = jnp.concatenate([r[2] for r in rows], axis=1)
+    left, right, up_mid, down_mid = lax.optimization_barrier((left, right, up_mid, down_mid))
+    sides = jnp.concatenate([left, right], axis=3)
+    up_sides = shifted(sides, "height", True)
+    down_sides = shifted(sides, "height", False)
+    row = jnp.concatenate([left, kv_blocks, right], axis=3)
     up = jnp.concatenate([up_sides[:, :, :, :1], up_mid, up_sides[:, :, :, 1:]], axis=3)
     down = jnp.concatenate([down_sides[:, :, :, :1], down_mid, down_sides[:, :, :, 1:]], axis=3)
     return jnp.concatenate([up, row, down], axis=2)
@@ -167,14 +160,25 @@
     )(kept, got)
 
 
-def step_bits(nbits):
-    return [0, 1, 3, 2, 4] if nbits == 5 else list(range(nbits))
-
-
-def block_order(groups):
+def step_bits(nbits, core):
+    if nbits != 5:
+        return [jnp.int32(b) for b in range(nbits)]
+    first, second = [0, 1, 3, 2, 4], [0, 3, 1, 4, 2]
+    return [jnp.where(core == 0, a, b) for a, b in zip(first, second)]
+
+
+def step_pairs(nbits, step):
+    pairs = []
+    for t in range(1 << nbits):
+        bits = [0, 1, 3, 2, 4] if t % 2 == 0 else [0, 3, 1, 4, 2]
+        bit = bits[step] if nbits == 5 else step
+        pairs.append((t, t ^ (1 << bit)))
+    return pairs
+
+
+def block_order(groups, me):
     nbits = groups.bit_length() - 1
-    me = lax.axis_index("tm")
-    order = step_bits(nbits)
+    order = step_bits(nbits, me & 1)
     pos = jnp.arange(groups, dtype=jnp.int32)
     block = jnp.zeros_like(pos)
     for i, bit in enumerate(order):
@@ -186,11 +190,9 @@
 def tree_reduce(first, second):
     groups = lax.axis_size("tm")
     nbits = groups.bit_length() - 1
-    order = step_bits(nbits)
-    for i, bit in enumerate(order):
-        pairs = [(t, t ^ (1 << bit)) for t in range(groups)]
-        got = lax.ppermute(second, "tm", pairs)
-        last = i == len(order) - 1
+    for i in range(nbits):
+        got = lax.ppermute(second, "tm", step_pairs(nbits, i))
+        last = i == nbits - 1
         outs = merge(first, got, not last)
         if last:
             return outs[0]
@@ -214,7 +216,10 @@
     query_rows = queries[0, 0]
     qtok = query_rows.shape[0]
     groups = lax.axis_size("tm")
-    order = block_order(groups)
+    me = lax.axis_index("tm")
+    order = jnp.concatenate(
+        [block_order(groups, me)[: groups // 2], block_order(groups, me ^ 1)[: groups // 2]]
+    )
     query_rows = jnp.take(query_rows.reshape(groups, qtok // groups, width), order, axis=0)
     query_rows = query_rows.reshape(qtok, width)
     first, second = attention(query_rows, keys, values, keep)

time: 206 us -> 192 us (0.932)
  starting transfers between devices: 50.3 us -> 33 us
  waiting for transfers between devices: 95.6 us -> 101 us
  local copies, waits for them, and re-layouts: 19.1 us -> 16.2 us
    ppermute x10 -> x6, starting transfers between devices: 38.4 us -> 21.1 us  [shifted(): return lax.ppermute(array, axis, pairs)]
    ppermute x10 -> x6, waiting for transfers between devices: 53.3 us -> 68.3 us  [shifted(): return lax.ppermute(array, axis, pairs)]
    ppermute x5, waiting for transfers between devices: 42.3 us -> 32.7 us  [tree_reduce(): got = lax.ppermute(second, 'tm', step_pairs(nbits, i))]
    concatenate x2 -> x0, local copies, waits for them, and re-layouts: 2.17 us -> none  [the longest x1 1.08 us: neighbourhood(): down_sides = jnp.concatenate([r[2] for r in rows], axis=1)]
    unnamed x22 -> x25, local copies, waits for them, and re-layouts: 5.48 us -> 4.91 us
  transfers between devices with their start and end apart: 15 -> 11, of which waited for: 11 -> 9; matrix products, arithmetic and copies ran while one was open for 4% -> 3% of each run, Pallas kernels for 0% -> 0%
where the time goes in v6:
time: 192 us; the launch traced here: 191 us
  waiting for transfers between devices  101 us (53%)
  starting transfers between devices  33 us (17%)
  Pallas kernels  31.7 us (17%)
  local copies, waits for them, and re-layouts  16.2 us (8%)
  other arithmetic  7.55 us (4%)
    ppermute x6, waiting for transfers between devices, shifted(): return lax.ppermute(array, axis, pairs)  68.3 us
    ppermute x5, waiting for transfers between devices, tree_reduce(): got = lax.ppermute(second, 'tm', step_pairs(nbits, i))  32.7 us
    ppermute x6, starting transfers between devices, shifted(): return lax.ppermute(array, axis, pairs)  21.1 us
    pallas_call x1, Pallas kernels, attention(): pl.pallas_call(attention_kernel, grid=(tiles,), in_specs=[pl.BlockSpec((T...  19.1 us
    pallas_call x5, Pallas kernels, merge(): pl.pallas_call(merge_kernel, out_shape=[shape] * count, cost_estimate=pl....  12.5 us
    ppermute x5, starting transfers between devices, tree_reduce(): got = lax.ppermute(second, 'tm', step_pairs(nbits, i))  11.9 us
    unnamed x25, local copies, waits for them, and re-layouts  4.91 us
  transfers between devices with their start and end apart: 11, of which 9 were waited for; matrix products, arithmetic and copies ran while one was open for 3% of the time, Pallas kernels for 0%

profile of v6, /device:TPU:6, one launch (start us, length us, event | category | flops | bytes accessed | tf_op | source)
XLA Modules:
  0.0 191.4 jit_solution(1287694274747277788)
XLA Ops:
  0.0 9.2 %collective-permute-start = (bf16[2,2,1,1,2,64,512]{6,5,4,3,2,1,0:T(8,128)(2,1)}, bf16[2,2,1,1,2,64,512]{6,5,4,3,2,1,0:T(8,128)(2,1)S(1)}, u32[]{:S(2)}, u32[]{:S(2)}) collective-permute-start(bf16[2,2,1,1,2,64,512]{6,5,4,3,2,1,0:T(8,128)(2,1)} %param.6), channel_id=1, source_target_pairs={{0,1},{1,2},{2,3},{4,5},{5,6},{6,7},{8,9},{9,10},{10,11},{12,13},{... | collective-permute-start | bytes 1572872 | tf_op jit(solution)/shard_map/ppermute | solution.py:19
  9.3 1.3 collective-permute-start.1
  10.6 3.5 %collective-permute-start.2 = (bf16[2,2,1,1,2,64,512]{6,5,4,3,2,1,0:T(8,128)(2,1)}, bf16[2,2,1,1,2,64,512]{6,5,4,3,2,1,0:T(8,128)(2,1)S(1)}, u32[]{:S(2)}, u32[]{:S(2)}) collective-permute-start(bf16[2,2,1,1,2,64,512]{6,5,4,3,2,1,0:T(8,128)(2,1)} %param.6), channel_id=1, source_target_pairs={{0,4},{4,8},{8,12},{1,5},{5,9},{9,13},{2,6},{6,10},{10,14},{3,7},{... | collective-permute-start | bytes 1572872 | tf_op jit(solution)/shard_map/ppermute | solution.py:19
  14.1 1.3 collective-permute-start.3
  15.5 0.7 fusion.1
  16.2 4.7 %collective-permute-done = bf16[2,2,1,1,2,64,512]{6,5,4,3,2,1,0:T(8,128)(2,1)S(1)} collective-permute-done((bf16[2,2,1,1,2,64,512]{6,5,4,3,2,1,0:T(8,128)(2,1)}, bf16[2,2,1,1,2,64,512]{6,5,4,3,2,1,0:T(8,128)(2,1)S(1)}, u32[]{:S(2)}, u32[]{:S(2)}) %collective-permute-start) | collective-permute-done | bytes 524320 | tf_op jit(solution)/shard_map/ppermute | solution.py:19
  20.8 43.0 %collective-permute-done.1 = bf16[2,2,1,1,2,64,512]{6,5,4,3,2,1,0:T(8,128)(2,1)S(1)} collective-permute-done((bf16[2,2,1,1,2,64,512]{6,5,4,3,2,1,0:T(8,128)(2,1)}, bf16[2,2,1,1,2,64,512]{6,5,4,3,2,1,0:T(8,128)(2,1)S(1)}, u32[]{:S(2)}, u32[]{:S(2)}) %collective-permute-start.1) | collective-permute-done | bytes 524320 | tf_op jit(solution)/shard_map/ppermute | solution.py:19
  63.9 1.0 constant_dynamic-update-slice_fusion.1
  64.9 0.9 constant_dynamic-update-slice_fusion
  65.7 4.4 %collective-permute-start.4 = (bf16[2,2,1,2,2,64,512]{6,5,4,3,2,1,0:T(8,128)(2,1)}, bf16[2,2,1,2,2,64,512]{6,5,4,3,2,1,0:T(8,128)(2,1)}, u32[]{:S(2)}, u32[]{:S(2)}) collective-permute-start(bf16[2,2,1,2,2,64,512]{6,5,4,3,2,1,0:T(8,128)(2,1)} %constant_dynamic-update-slice_fusion), channel_id=1, source_target_pairs={{0,4},{4,8},{8,12},{1,5},{5,9},{9,13},{2,6},{6,10},{10,14},{3,7},{... | collective-permute-start | bytes 3145736 | tf_op jit(solution)/shard_map/ppermute | solution.py:19
  70.5 0.7 convert_element_type.12.keep_ref
  71.2 1.3 collective-permute-start.5
  72.5 0.7 fusion.3
  73.2 0.6 gather_fusion
  73.9 0.8 compare_and_fusion
  74.7 1.2 bitcast_select_fusion.q_ref
  75.9 15.7 %collective-permute-done.4 = bf16[2,2,1,2,2,64,512]{6,5,4,3,2,1,0:T(8,128)(2,1)} collective-permute-done((bf16[2,2,1,2,2,64,512]{6,5,4,3,2,1,0:T(8,128)(2,1)}, bf16[2,2,1,2,2,64,512]{6,5,4,3,2,1,0:T(8,128)(2,1)}, u32[]{:S(2)}, u32[]{:S(2)}) %collective-permute-start.4) | collective-permute-done | bytes 1048608 | tf_op jit(solution)/shard_map/ppermute | solution.py:19
  91.6 1.3 fusion.5
  92.9 4.9 %collective-permute-done.5 = bf16[2,2,1,2,2,64,512]{6,5,4,3,2,1,0:T(8,128)(2,1)} collective-permute-done((bf16[2,2,1,2,2,64,512]{6,5,4,3,2,1,0:T(8,128)(2,1)}, bf16[2,2,1,2,2,64,512]{6,5,4,3,2,1,0:T(8,128)(2,1)}, u32[]{:S(2)}, u32[]{:S(2)}) %collective-permute-start.5) | collective-permute-done | bytes 1048608 | tf_op jit(solution)/shard_map/ppermute | solution.py:19
  97.8 1.3 fusion.6
  99.1 2.8 %maximum_maximum_fusion = bf16[2,2,3,3,2,64,512]{6,5,4,3,2,1,0:T(8,128)(2,1)} fusion(bf16[2,2,1,1,2,64,512]{6,5,4,3,2,1,0:T(8,128)(2,1)S(1)} %get-tuple-element.38, bf16[2,2,1,1,2,64,512]{6,5,4,3,2,1,0:T(8,128)(2,1)S(1)} %copy-done.7, bf16[2,2,1,1,2,64,512]{6,5,4,3,2,1,0:T(8,128)(2,1)S(1)} %get-tuple-element.37, ...), kind=kLoop, calls=%fused_computation.2 | loop fusion | flops 18874368 | bytes 9437184 | tf_op jit(solution)/shard_map/concatenate | solution.py:34
  101.9 3.0 %gather_fusion.1 = bf16[8,2,2,64,512]{4,3,2,1,0:T(8,128)(2,1)S(1)} fusion(bf16[2,2,18,64,512]{4,3,2,1,0:T(8,128)(2,1)} %bitcast.26, s32[1024]{0:T(1024)S(1)} %get-tuple-element.43), kind=kCustom, calls=%fused_computation.1 | custom fusion | bytes 4194336 | tf_op jit(solution)/shard_map/jit(_take)/gather | solution.py:211
  105.3 1.1 copy.6
  106.4 1.1 copy.7
  107.5 19.1 %shard_map.55 = (f32[512,640]{1,0:T(8,128)}, f32[512,640]{1,0:T(8,128)}) custom-call(bf16[1024,512]{1,0:T(8,128)(2,1)} %bitcast_select_fusion.q_ref, bf16[1024,512]{1,0:T(8,128)(2,1)} %bitcast.27, bf16[1024,512]{1,0:T(8,128)(2,1)} %bitcast.28, s32[1,1024]{1,0:T(1,128)} %convert_element_type.12.keep_ref), custom_call_target="tpu_custom_call" | custom-call | flops 4294967296 | bytes 5242880 | tf_op jit(solution)/shard_map/pallas_call | solution.py:92
  126.6 2.0 %collective-permute-start.6 = (f32[512,640]{1,0:T(8,128)}, f32[512,640]{1,0:T(8,128)S(1)}, u32[]{:S(2)}, u32[]{:S(2)}) collective-permute-start(f32[512,640]{1,0:T(8,128)} %get-tuple-element.24), channel_id=1, source_target_pairs={{0,16},{16,0},{32,48},{48,32},{64,80},{80,64},{96,112},{112,96},{1... | collective-permute-start | bytes 3932168 | tf_op jit(solution)/shard_map/ppermute | solution.py:194
  128.7 3.2 %collective-permute-done.6.b_ref = f32[512,640]{1,0:T(8,128)S(1)} collective-permute-done((f32[512,640]{1,0:T(8,128)}, f32[512,640]{1,0:T(8,128)S(1)}, u32[]{:S(2)}, u32[]{:S(2)}) %collective-permute-start.6) | collective-permute-done | bytes 1310752 | tf_op jit(solution)/shard_map/ppermute | solution.py:194
  131.9 1.1 copy-done.1
  133.0 4.0 %shard_map.56 = (f32[256,640]{1,0:T(8,128)}, f32[256,640]{1,0:T(8,128)}) custom-call(f32[512,640]{1,0:T(8,128)} %get-tuple-element.23.a_ref, f32[512,640]{1,0:T(8,128)} %copy-done.1), custom_call_target="tpu_custom_call" | custom-call | flops 1310720 | bytes 3932160 | tf_op jit(solution)/shard_map/pallas_call | solution.py:154
  137.0 1.9 collective-permute-start.7
  138.9 10.8 %collective-permute-done.7.b_ref = f32[256,640]{1,0:T(8,128)S(1)} collective-permute-done((f32[256,640]{1,0:T(8,128)}, f32[256,640]{1,0:T(8,128)S(1)}, u32[]{:S(2)}, u32[]{:S(2)}) %collective-permute-start.7) | collective-permute-done | bytes 655392 | tf_op jit(solution)/shard_map/ppermute | solution.py:194
  149.6 0.8 copy-done.2
  150.5 2.8 %shard_map.57 = (f32[128,640]{1,0:T(8,128)}, f32[128,640]{1,0:T(8,128)}) custom-call(f32[256,640]{1,0:T(8,128)} %get-tuple-element.25.a_ref, f32[256,640]{1,0:T(8,128)} %copy-done.2), custom_call_target="tpu_custom_call" | custom-call | flops 655360 | bytes 1966080 | tf_op jit(solution)/shard_map/pallas_call | solution.py:154
  153.3 2.7 %collective-permute-start.8 = (f32[128,640]{1,0:T(8,128)}, f32[128,640]{1,0:T(8,128)S(1)}, u32[]{:S(2)}, u32[]{:S(2)}) collective-permute-start(f32[128,640]{1,0:T(8,128)} %get-tuple-element.28), channel_id=1, source_target_pairs={{0,128},{16,48},{32,160},{48,16},{64,192},{80,112},{96,224},{112,8... | collective-permute-start | bytes 983048 | tf_op jit(solution)/shard_map/ppermute | solution.py:194
  156.0 6.4 %collective-permute-done.8.b_ref = f32[128,640]{1,0:T(8,128)S(1)} collective-permute-done((f32[128,640]{1,0:T(8,128)}, f32[128,640]{1,0:T(8,128)S(1)}, u32[]{:S(2)}, u32[]{:S(2)}) %collective-permute-start.8) | collective-permute-done | bytes 327712 | tf_op jit(solution)/shard_map/ppermute | solution.py:194
  162.4 0.7 copy-done.9
  163.2 2.1 %shard_map.58 = (f32[64,640]{1,0:T(8,128)}, f32[64,640]{1,0:T(8,128)}) custom-call(f32[128,640]{1,0:T(8,128)} %get-tuple-element.27.a_ref, f32[128,640]{1,0:T(8,128)} %copy-done.9), custom_call_target="tpu_custom_call" | custom-call | flops 327680 | bytes 983040 | tf_op jit(solution)/shard_map/pallas_call | solution.py:154
  165.3 1.9 collective-permute-start.9
  167.2 7.6 %collective-permute-done.9.b_ref = f32[64,640]{1,0:T(8,128)S(1)} collective-permute-done((f32[64,640]{1,0:T(8,128)}, f32[64,640]{1,0:T(8,128)S(1)}, u32[]{:S(2)}, u32[]{:S(2)}) %collective-permute-start.9) | collective-permute-done | bytes 163872 | tf_op jit(solution)/shard_map/ppermute | solution.py:194
  174.8 0.7 copy-done.10
  175.5 1.9 shard_map.59
  177.4 3.3 %collective-permute-start.10 = (f32[32,640]{1,0:T(8,128)}, f32[32,640]{1,0:T(8,128)S(1)}, u32[]{:S(2)}, u32[]{:S(2)}) collective-permute-start(f32[32,640]{1,0:T(8,128)} %get-tuple-element.32), channel_id=1, source_target_pairs={{0,256},{16,80},{32,288},{48,112},{64,320},{80,16},{96,352},{112,4... | collective-permute-start | bytes 245768 | tf_op jit(solution)/shard_map/ppermute | solution.py:194
  180.7 4.7 %collective-permute-done.10.b_ref = f32[32,640]{1,0:T(8,128)S(1)} collective-permute-done((f32[32,640]{1,0:T(8,128)}, f32[32,640]{1,0:T(8,128)S(1)}, u32[]{:S(2)}, u32[]{:S(2)}) %collective-permute-start.10) | collective-permute-done | bytes 81952 | tf_op jit(solution)/shard_map/ppermute | solution.py:194
  185.4 0.6 copy-done.11
  186.0 1.7 shard_map.60
  187.7 0.8 slice.51
  188.7 1.0 multiply_reduce_fusion
  189.7 1.7 convolution_bitcast_fusion
  (36 shorter events, 1.1 us)
Async XLA Ops:
  0.0 73.2 %copy-start = (bf16[1,1,1024,512]{3,2,1,0:T(8,128)(2,1)S(1)}, bf16[1,1,1024,512]{3,2,1,0:T(8,128)(2,1)}, u32[]{:S(2)}) copy-start(bf16[1,1,1024,512]{3,2,1,0:T(8,128)(2,1)} %param.5) | copy-start | bytes 3145732
  0.0 20.8 %collective-permute-start = (bf16[2,2,1,1,2,64,512]{6,5,4,3,2,1,0:T(8,128)(2,1)}, bf16[2,2,1,1,2,64,512]{6,5,4,3,2,1,0:T(8,128)(2,1)S(1)}, u32[]{:S(2)}, u32[]{:S(2)}) collective-permute-start(bf16[2,2,1,1,2,64,512]{6,5,4,3,2,1,0:T(8,128)(2,1)} %param.6), channel_id=1, source_target_pairs={{0,1},{1,2},{2,3},{4,5},{5,6},{6,7},{8,9},{9,10},{10,11},{12,13},{... | collective-permute-start | bytes 1572872 | tf_op jit(solution)/shard_map/ppermute | solution.py:19
  9.3 54.6 %collective-permute-start.1 = (bf16[2,2,1,1,2,64,512]{6,5,4,3,2,1,0:T(8,128)(2,1)}, bf16[2,2,1,1,2,64,512]{6,5,4,3,2,1,0:T(8,128)(2,1)S(1)}, u32[]{:S(2)}, u32[]{:S(2)}) collective-permute-start(bf16[2,2,1,1,2,64,512]{6,5,4,3,2,1,0:T(8,128)(2,1)} %param.6), channel_id=1, source_target_pairs={{1,0},{2,1},{3,2},{5,4},{6,5},{7,6},{9,8},{10,9},{11,10},{13,12},{... | collective-permute-start | bytes 1572872 | tf_op jit(solution)/shard_map/ppermute | solution.py:19
  10.6 53.3 %collective-permute-start.2 = (bf16[2,2,1,1,2,64,512]{6,5,4,3,2,1,0:T(8,128)(2,1)}, bf16[2,2,1,1,2,64,512]{6,5,4,3,2,1,0:T(8,128)(2,1)S(1)}, u32[]{:S(2)}, u32[]{:S(2)}) collective-permute-start(bf16[2,2,1,1,2,64,512]{6,5,4,3,2,1,0:T(8,128)(2,1)} %param.6), channel_id=1, source_target_pairs={{0,4},{4,8},{8,12},{1,5},{5,9},{9,13},{2,6},{6,10},{10,14},{3,7},{... | collective-permute-start | bytes 1572872 | tf_op jit(solution)/shard_map/ppermute | solution.py:19
  14.1 49.8 %collective-permute-start.3 = (bf16[2,2,1,1,2,64,512]{6,5,4,3,2,1,0:T(8,128)(2,1)}, bf16[2,2,1,1,2,64,512]{6,5,4,3,2,1,0:T(8,128)(2,1)S(1)}, u32[]{:S(2)}, u32[]{:S(2)}) collective-permute-start(bf16[2,2,1,1,2,64,512]{6,5,4,3,2,1,0:T(8,128)(2,1)} %param.6), channel_id=1, source_target_pairs={{4,0},{8,4},{12,8},{5,1},{9,5},{13,9},{6,2},{10,6},{14,10},{7,3},{... | collective-permute-start | bytes 1572872 | tf_op jit(solution)/shard_map/ppermute | solution.py:19
  63.9 9.3 %copy-start.4 = (bf16[2,2,1,1,2,64,512]{6,5,4,3,2,1,0:T(8,128)(2,1)}, bf16[2,2,1,1,2,64,512]{6,5,4,3,2,1,0:T(8,128)(2,1)S(1)}, u32[]{:S(2)}) copy-start(bf16[2,2,1,1,2,64,512]{6,5,4,3,2,1,0:T(8,128)(2,1)S(1)} %collective-permute-done.2) | copy-start | bytes 1572868
  63.9 9.3 %copy-start.6 = (bf16[2,2,1,1,2,64,512]{6,5,4,3,2,1,0:T(8,128)(2,1)}, bf16[2,2,1,1,2,64,512]{6,5,4,3,2,1,0:T(8,128)(2,1)S(1)}, u32[]{:S(2)}) copy-start(bf16[2,2,1,1,2,64,512]{6,5,4,3,2,1,0:T(8,128)(2,1)S(1)} %collective-permute-done.3) | copy-start | bytes 1572868
  65.7 25.9 %collective-permute-start.4 = (bf16[2,2,1,2,2,64,512]{6,5,4,3,2,1,0:T(8,128)(2,1)}, bf16[2,2,1,2,2,64,512]{6,5,4,3,2,1,0:T(8,128)(2,1)}, u32[]{:S(2)}, u32[]{:S(2)}) collective-permute-start(bf16[2,2,1,2,2,64,512]{6,5,4,3,2,1,0:T(8,128)(2,1)} %constant_dynamic-update-slice_fusion), channel_id=1, source_target_pairs={{0,4},{4,8},{8,12},{1,5},{5,9},{9,13},{2,6},{6,10},{10,14},{3,7},{... | collective-permute-start | bytes 3145736 | tf_op jit(solution)/shard_map/ppermute | solution.py:19
  71.2 26.5 %collective-permute-start.5 = (bf16[2,2,1,2,2,64,512]{6,5,4,3,2,1,0:T(8,128)(2,1)}, bf16[2,2,1,2,2,64,512]{6,5,4,3,2,1,0:T(8,128)(2,1)}, u32[]{:S(2)}, u32[]{:S(2)}) collective-permute-start(bf16[2,2,1,2,2,64,512]{6,5,4,3,2,1,0:T(8,128)(2,1)} %constant_dynamic-update-slice_fusion), channel_id=1, source_target_pairs={{4,0},{8,4},{12,8},{5,1},{9,5},{13,9},{6,2},{10,6},{14,10},{7,3},{... | collective-permute-start | bytes 3145736 | tf_op jit(solution)/shard_map/ppermute | solution.py:19
  73.8 25.2 %copy-start.3 = (bf16[2,2,1,1,2,64,512]{6,5,4,3,2,1,0:T(8,128)(2,1)S(1)}, bf16[2,2,1,1,2,64,512]{6,5,4,3,2,1,0:T(8,128)(2,1)}, u32[]{:S(2)}) copy-start(bf16[2,2,1,1,2,64,512]{6,5,4,3,2,1,0:T(8,128)(2,1)} %param.6) | copy-start | bytes 1572868
  73.9 25.2 %copy-start.5 = (bf16[2,2,1,1,2,64,512]{6,5,4,3,2,1,0:T(8,128)(2,1)S(1)}, bf16[2,2,1,1,2,64,512]{6,5,4,3,2,1,0:T(8,128)(2,1)}, u32[]{:S(2)}) copy-start(bf16[2,2,1,1,2,64,512]{6,5,4,3,2,1,0:T(8,128)(2,1)} %copy-done.4) | copy-start | bytes 1572868
  73.9 25.2 %copy-start.7 = (bf16[2,2,1,1,2,64,512]{6,5,4,3,2,1,0:T(8,128)(2,1)S(1)}, bf16[2,2,1,1,2,64,512]{6,5,4,3,2,1,0:T(8,128)(2,1)}, u32[]{:S(2)}) copy-start(bf16[2,2,1,1,2,64,512]{6,5,4,3,2,1,0:T(8,128)(2,1)} %copy-done.6) | copy-start | bytes 1572868
  126.6 63.1 %copy-start.8 = (bf16[512,512]{1,0:T(8,128)(2,1)S(1)}, bf16[512,512]{1,0:T(8,128)(2,1)}, u32[]{:S(2)}) copy-start(bf16[512,512]{1,0:T(8,128)(2,1)} %param.9) | copy-start | bytes 1572868
  126.6 5.3 %collective-permute-start.6 = (f32[512,640]{1,0:T(8,128)}, f32[512,640]{1,0:T(8,128)S(1)}, u32[]{:S(2)}, u32[]{:S(2)}) collective-permute-start(f32[512,640]{1,0:T(8,128)} %get-tuple-element.24), channel_id=1, source_target_pairs={{0,16},{16,0},{32,48},{48,32},{64,80},{80,64},{96,112},{112,96},{1... | collective-permute-start | bytes 3932168 | tf_op jit(solution)/shard_map/ppermute | solution.py:194
  131.9 1.1 copy-start.1
  137.0 12.7 %collective-permute-start.7 = (f32[256,640]{1,0:T(8,128)}, f32[256,640]{1,0:T(8,128)S(1)}, u32[]{:S(2)}, u32[]{:S(2)}) collective-permute-start(f32[256,640]{1,0:T(8,128)} %get-tuple-element.26), channel_id=1, source_target_pairs={{0,32},{16,144},{32,0},{48,176},{64,96},{80,208},{96,64},{112,240}... | collective-permute-start | bytes 1966088 | tf_op jit(solution)/shard_map/ppermute | solution.py:194
  149.6 0.8 copy-start.2
  153.3 9.2 %collective-permute-start.8 = (f32[128,640]{1,0:T(8,128)}, f32[128,640]{1,0:T(8,128)S(1)}, u32[]{:S(2)}, u32[]{:S(2)}) collective-permute-start(f32[128,640]{1,0:T(8,128)} %get-tuple-element.28), channel_id=1, source_target_pairs={{0,128},{16,48},{32,160},{48,16},{64,192},{80,112},{96,224},{112,8... | collective-permute-start | bytes 983048 | tf_op jit(solution)/shard_map/ppermute | solution.py:194
  162.4 0.7 copy-start.9
  165.3 9.5 %collective-permute-start.9 = (f32[64,640]{1,0:T(8,128)}, f32[64,640]{1,0:T(8,128)S(1)}, u32[]{:S(2)}, u32[]{:S(2)}) collective-permute-start(f32[64,640]{1,0:T(8,128)} %get-tuple-element.30), channel_id=1, source_target_pairs={{0,64},{16,272},{32,96},{48,304},{64,0},{80,336},{96,32},{112,368}... | collective-permute-start | bytes 491528 | tf_op jit(solution)/shard_map/ppermute | solution.py:194
  174.8 0.7 copy-start.10
  177.4 8.0 %collective-permute-start.10 = (f32[32,640]{1,0:T(8,128)}, f32[32,640]{1,0:T(8,128)S(1)}, u32[]{:S(2)}, u32[]{:S(2)}) collective-permute-start(f32[32,640]{1,0:T(8,128)} %get-tuple-element.32), channel_id=1, source_target_pairs={{0,256},{16,80},{32,288},{48,112},{64,320},{80,16},{96,352},{112,4... | collective-permute-start | bytes 245768 | tf_op jit(solution)/shard_map/ppermute | solution.py:194
  185.4 0.6 copy-start.11

commit v7 on v6

--- a/solution.py
+++ b/solution.py
@@ -37,19 +37,18 @@
 PACK = 128
 
 
-def attention_kernel(q_ref, k_ref, v_ref, keep_ref, first_ref, second_ref):
+def attention_kernel(q_ref, k_ref, v_ref, keep_ref, out_ref):
     rows = q_ref.shape[0]
-    step = pl.program_id(0)
-    half = pl.num_programs(0) // 2
     keep = keep_ref[...] > 0
     lane = lax.broadcasted_iota(jnp.int32, (1, 2 * HD), 1)
     low = lane < HD
     stat_lane = lax.broadcasted_iota(jnp.int32, (1, PACK), 1)
     stats = jnp.zeros((rows, PACK), jnp.float32)
+    scale = jnp.asarray(1.0 / 8.0, jnp.bfloat16)
     blocks = []
     for pair in range(HEADS // 2):
         cols = pl.ds(pair * 2 * HD, 2 * HD)
-        q2 = q_ref[:, cols]
+        q2 = q_ref[:, cols] * scale
         k2 = k_ref[:, cols]
         v2 = v_ref[:, cols]
         outs = []
@@ -59,10 +58,9 @@
             scores = lax.dot_general(
                 qh, k2, (((1,), (1,)), ((), ())), preferred_element_type=jnp.float32
             )
-            scores = scores / jnp.float32(8.0)
             scores = jnp.where(keep, scores, jnp.float32(-1e30))
             top = jnp.max(scores, axis=1, keepdims=True)
-            probs = jnp.where(keep, jnp.exp(scores - top), jnp.float32(0.0))
+            probs = jnp.exp(scores - top)
             total = jnp.sum(probs, axis=1, keepdims=True)
             outs.append(
                 jnp.dot(probs.astype(jnp.bfloat16), v2, preferred_element_type=jnp.float32)
@@ -71,24 +69,14 @@
             stats = jnp.where(stat_lane == head, top, stats)
             stats = jnp.where(stat_lane == HEADS + head, total, stats)
         blocks.append(jnp.where(low, outs[0], outs[1]))
-    packed = jnp.concatenate(blocks + [stats], axis=1)
-
-    @pl.when(step < half)
-    def _():
-        first_ref[...] = packed
-
-    @pl.when(step >= half)
-    def _():
-        second_ref[...] = packed
+    out_ref[...] = jnp.concatenate(blocks + [stats], axis=1)
 
 
 def attention(query_rows, keys, values, keep):
     qtok, width = query_rows.shape
     count = keys.shape[0]
     tiles = qtok // TQ
-    half = tiles // 2
     flops = 2 * 2 * qtok * count * 2 * width
-    packed = jax.ShapeDtypeStruct((qtok // 2, width + PACK), jnp.float32)
     return pl.pallas_call(
         attention_kernel,
         grid=(tiles,),
@@ -98,11 +86,8 @@
             pl.BlockSpec((count, width), lambda i: (0, 0)),
             pl.BlockSpec((1, count), lambda i: (0, 0)),
         ],
-        out_specs=[
-            pl.BlockSpec((TQ, width + PACK), lambda i: (jnp.minimum(i, half - 1), 0)),
-            pl.BlockSpec((TQ, width + PACK), lambda i: (jnp.maximum(i - half, 0), 0)),
-        ],
-        out_shape=[packed, packed],
+        out_specs=pl.BlockSpec((TQ, width + PACK), lambda i: (i, 0)),
+        out_shape=jax.ShapeDtypeStruct((qtok, width + PACK), jnp.float32),
         cost_estimate=pl.CostEstimate(
             flops=flops,
             transcendentals=qtok * count * HEADS,
@@ -222,7 +207,8 @@
     )
     query_rows = jnp.take(query_rows.reshape(groups, qtok // groups, width), order, axis=0)
     query_rows = query_rows.reshape(qtok, width)
-    first, second = attention(query_rows, keys, values, keep)
+    second = attention(query_rows[qtok // 2 :], keys, values, keep)
+    first = attention(query_rows[: qtok // 2], keys, values, keep)
     final = tree_reduce(first, second)
     summed = final[:, :width]
     total = final[:, width + HEADS : width + 2 * HEADS]

time: 192 us -> 191 us (level)
  waiting for transfers between devices: 101 us -> 97.7 us
  Pallas kernels: 31.7 us -> 33.8 us
    ppermute x5, waiting for transfers between devices: 32.7 us -> 29.5 us  [tree_reduce(): got = lax.ppermute(second, 'tm', step_pairs(nbits, i))]
    pallas_call x1 -> x2, Pallas kernels: 19.1 us -> 21.3 us  [attention(): pl.pallas_call(attention_kernel, grid=(tiles,), in_specs=[pl.BlockSpec((T...]
  transfers between devices with their start and end apart: 11 -> 11, of which waited for: 9 -> 8; matrix products, arithmetic and copies ran while one was open for 3% -> 3% of each run, Pallas kernels for 0% -> 6%
where the time goes in v7:
time: 191 us; the launch traced here: 190 us
  waiting for transfers between devices  97.7 us (51%)
  Pallas kernels  33.8 us (18%)
  starting transfers between devices  32.8 us (17%)
  local copies, waits for them, and re-layouts  17 us (9%)
  other arithmetic  6.48 us (3%)
    ppermute x6, waiting for transfers between devices, shifted(): return lax.ppermute(array, axis, pairs)  68.1 us
    ppermute x5, waiting for transfers between devices, tree_reduce(): got = lax.ppermute(second, 'tm', step_pairs(nbits, i))  29.5 us
    pallas_call x2, Pallas kernels, attention(): pl.pallas_call(attention_kernel, grid=(tiles,), in_specs=[pl.BlockSpec((T...  21.3 us
    ppermute x6, starting transfers between devices, shifted(): return lax.ppermute(array, axis, pairs)  21.1 us
    pallas_call x5, Pallas kernels, merge(): pl.pallas_call(merge_kernel, out_shape=[shape] * count, cost_estimate=pl....  12.5 us
    ppermute x5, starting transfers between devices, tree_reduce(): got = lax.ppermute(second, 'tm', step_pairs(nbits, i))  11.7 us
    unnamed x25, local copies, waits for them, and re-layouts  4.91 us
  transfers between devices with their start and end apart: 11, of which 8 were waited for; matrix products, arithmetic and copies ran while one was open for 3% of the time, Pallas kernels for 6%

profile of v7, /device:TPU:6, one launch (start us, length us, event | category | flops | bytes accessed | tf_op | source)
XLA Modules:
  0.0 189.7 jit_solution(10234491234309904048)
XLA Ops:
  0.0 9.2 %collective-permute-start = (bf16[2,2,1,1,2,64,512]{6,5,4,3,2,1,0:T(8,128)(2,1)}, bf16[2,2,1,1,2,64,512]{6,5,4,3,2,1,0:T(8,128)(2,1)S(1)}, u32[]{:S(2)}, u32[]{:S(2)}) collective-permute-start(bf16[2,2,1,1,2,64,512]{6,5,4,3,2,1,0:T(8,128)(2,1)} %param.6), channel_id=1, source_target_pairs={{0,1},{1,2},{2,3},{4,5},{5,6},{6,7},{8,9},{9,10},{10,11},{12,13},{... | collective-permute-start | bytes 1572872 | tf_op jit(solution)/shard_map/ppermute | solution.py:19
  9.3 1.3 collective-permute-start.1
  10.6 3.5 %collective-permute-start.2 = (bf16[2,2,1,1,2,64,512]{6,5,4,3,2,1,0:T(8,128)(2,1)}, bf16[2,2,1,1,2,64,512]{6,5,4,3,2,1,0:T(8,128)(2,1)S(1)}, u32[]{:S(2)}, u32[]{:S(2)}) collective-permute-start(bf16[2,2,1,1,2,64,512]{6,5,4,3,2,1,0:T(8,128)(2,1)} %param.6), channel_id=1, source_target_pairs={{0,4},{4,8},{8,12},{1,5},{5,9},{9,13},{2,6},{6,10},{10,14},{3,7},{... | collective-permute-start | bytes 1572872 | tf_op jit(solution)/shard_map/ppermute | solution.py:19
  14.1 1.3 collective-permute-start.3
  15.6 0.7 fusion.3
  16.2 4.6 %collective-permute-done = bf16[2,2,1,1,2,64,512]{6,5,4,3,2,1,0:T(8,128)(2,1)S(1)} collective-permute-done((bf16[2,2,1,1,2,64,512]{6,5,4,3,2,1,0:T(8,128)(2,1)}, bf16[2,2,1,1,2,64,512]{6,5,4,3,2,1,0:T(8,128)(2,1)S(1)}, u32[]{:S(2)}, u32[]{:S(2)}) %collective-permute-start) | collective-permute-done | bytes 524320 | tf_op jit(solution)/shard_map/ppermute | solution.py:19
  20.8 43.0 %collective-permute-done.1 = bf16[2,2,1,1,2,64,512]{6,5,4,3,2,1,0:T(8,128)(2,1)S(1)} collective-permute-done((bf16[2,2,1,1,2,64,512]{6,5,4,3,2,1,0:T(8,128)(2,1)}, bf16[2,2,1,1,2,64,512]{6,5,4,3,2,1,0:T(8,128)(2,1)S(1)}, u32[]{:S(2)}, u32[]{:S(2)}) %collective-permute-start.1) | collective-permute-done | bytes 524320 | tf_op jit(solution)/shard_map/ppermute | solution.py:19
  63.9 1.0 constant_dynamic-update-slice_fusion.1
  64.9 0.8 constant_dynamic-update-slice_fusion
  65.7 4.4 %collective-permute-start.4 = (bf16[2,2,1,2,2,64,512]{6,5,4,3,2,1,0:T(8,128)(2,1)}, bf16[2,2,1,2,2,64,512]{6,5,4,3,2,1,0:T(8,128)(2,1)}, u32[]{:S(2)}, u32[]{:S(2)}) collective-permute-start(bf16[2,2,1,2,2,64,512]{6,5,4,3,2,1,0:T(8,128)(2,1)} %constant_dynamic-update-slice_fusion), channel_id=1, source_target_pairs={{0,4},{4,8},{8,12},{1,5},{5,9},{9,13},{2,6},{6,10},{10,14},{3,7},{... | collective-permute-start | bytes 3145736 | tf_op jit(solution)/shard_map/ppermute | solution.py:19
  70.1 0.7 fusion.1
  70.8 1.3 collective-permute-start.5
  72.2 0.7 convert_element_type.12.keep_ref
  72.9 0.6 gather_fusion
  73.6 0.8 compare_and_fusion
  74.5 1.1 fusion.5
  75.6 16.0 %collective-permute-done.4 = bf16[2,2,1,2,2,64,512]{6,5,4,3,2,1,0:T(8,128)(2,1)} collective-permute-done((bf16[2,2,1,2,2,64,512]{6,5,4,3,2,1,0:T(8,128)(2,1)}, bf16[2,2,1,2,2,64,512]{6,5,4,3,2,1,0:T(8,128)(2,1)}, u32[]{:S(2)}, u32[]{:S(2)}) %collective-permute-start.4) | collective-permute-done | bytes 1048608 | tf_op jit(solution)/shard_map/ppermute | solution.py:19
  91.6 1.3 fusion.6
  92.9 4.4 %collective-permute-done.5 = bf16[2,2,1,2,2,64,512]{6,5,4,3,2,1,0:T(8,128)(2,1)} collective-permute-done((bf16[2,2,1,2,2,64,512]{6,5,4,3,2,1,0:T(8,128)(2,1)}, bf16[2,2,1,2,2,64,512]{6,5,4,3,2,1,0:T(8,128)(2,1)}, u32[]{:S(2)}, u32[]{:S(2)}) %collective-permute-start.5) | collective-permute-done | bytes 1048608 | tf_op jit(solution)/shard_map/ppermute | solution.py:19
  97.3 1.3 fusion.7
  98.6 2.8 %maximum_maximum_fusion = bf16[2,2,3,3,2,64,512]{6,5,4,3,2,1,0:T(8,128)(2,1)} fusion(bf16[2,2,1,1,2,64,512]{6,5,4,3,2,1,0:T(8,128)(2,1)S(1)} %get-tuple-element.36, bf16[2,2,1,1,2,64,512]{6,5,4,3,2,1,0:T(8,128)(2,1)S(1)} %copy-done.7, bf16[2,2,1,1,2,64,512]{6,5,4,3,2,1,0:T(8,128)(2,1)S(1)} %get-tuple-element.35, ...), kind=kLoop, calls=%fused_computation.2 | loop fusion | flops 18874368 | bytes 9437184 | tf_op jit(solution)/shard_map/concatenate | solution.py:34
  101.4 3.0 %gather_fusion.1 = bf16[8,2,2,64,512]{4,3,2,1,0:T(8,128)(2,1)S(1)} fusion(bf16[2,2,18,64,512]{4,3,2,1,0:T(8,128)(2,1)} %bitcast.26, s32[1024]{0:T(1024)S(1)} %pad_clamp_fusion), kind=kCustom, calls=%fused_computation.1 | custom fusion | bytes 4194336 | tf_op jit(solution)/shard_map/jit(_take)/gather | solution.py:196
  104.9 1.1 copy.6
  106.0 1.1 copy.7
  107.1 10.6 %shard_map.56 = f32[512,640]{1,0:T(8,128)} custom-call(bf16[512,512]{1,0:T(8,128)(2,1)} %bitcast.32, bf16[1024,512]{1,0:T(8,128)(2,1)} %bitcast.27, bf16[1024,512]{1,0:T(8,128)(2,1)} %bitcast.29, s32[1,1024]{1,0:T(1,128)} %convert_element_type.12.keep_ref), custom_call_target="tpu_custom_call" | custom-call | flops 2147483648 | bytes 3670016 | tf_op jit(solution)/shard_map/pallas_call | solution.py:80
  117.7 1.9 %collective-permute-start.6 = (f32[512,640]{1,0:T(8,128)}, f32[512,640]{1,0:T(8,128)S(1)}, u32[]{:S(2)}, u32[]{:S(2)}) collective-permute-start(f32[512,640]{1,0:T(8,128)} %shard_map.56), channel_id=1, source_target_pairs={{0,16},{16,0},{32,48},{48,32},{64,80},{80,64},{96,112},{112,96},{1... | collective-permute-start | bytes 3932168 | tf_op jit(solution)/shard_map/ppermute | solution.py:179
  119.6 10.7 %shard_map.55.a_ref = f32[512,640]{1,0:T(8,128)} custom-call(bf16[512,512]{1,0:T(8,128)(2,1)} %bitcast.31, bf16[1024,512]{1,0:T(8,128)(2,1)} %bitcast.28, bf16[1024,512]{1,0:T(8,128)(2,1)} %bitcast.30, s32[1,1024]{1,0:T(1,128)} %convert_element_type.12.keep_ref), custom_call_target="tpu_custom_call" | custom-call | flops 2147483648 | bytes 3670016 | tf_op jit(solution)/shard_map/pallas_call | solution.py:80
  130.3 1.1 copy-done.1
  131.3 4.0 %shard_map.57 = (f32[256,640]{1,0:T(8,128)}, f32[256,640]{1,0:T(8,128)}) custom-call(f32[512,640]{1,0:T(8,128)} %shard_map.55.a_ref, f32[512,640]{1,0:T(8,128)} %copy-done.1), custom_call_target="tpu_custom_call" | custom-call | flops 1310720 | bytes 3932160 | tf_op jit(solution)/shard_map/pallas_call | solution.py:139
  135.3 1.9 %collective-permute-start.7 = (f32[256,640]{1,0:T(8,128)}, f32[256,640]{1,0:T(8,128)S(1)}, u32[]{:S(2)}, u32[]{:S(2)}) collective-permute-start(f32[256,640]{1,0:T(8,128)} %get-tuple-element.22), channel_id=1, source_target_pairs={{0,32},{16,144},{32,0},{48,176},{64,96},{80,208},{96,64},{112,240}... | collective-permute-start | bytes 1966088 | tf_op jit(solution)/shard_map/ppermute | solution.py:179
  137.2 10.8 %collective-permute-done.7.b_ref = f32[256,640]{1,0:T(8,128)S(1)} collective-permute-done((f32[256,640]{1,0:T(8,128)}, f32[256,640]{1,0:T(8,128)S(1)}, u32[]{:S(2)}, u32[]{:S(2)}) %collective-permute-start.7) | collective-permute-done | bytes 655392 | tf_op jit(solution)/shard_map/ppermute | solution.py:179
  148.0 0.8 copy-done.2
  148.8 2.8 %shard_map.58 = (f32[128,640]{1,0:T(8,128)}, f32[128,640]{1,0:T(8,128)}) custom-call(f32[256,640]{1,0:T(8,128)} %get-tuple-element.21.a_ref, f32[256,640]{1,0:T(8,128)} %copy-done.2), custom_call_target="tpu_custom_call" | custom-call | flops 655360 | bytes 1966080 | tf_op jit(solution)/shard_map/pallas_call | solution.py:139
  151.6 2.7 %collective-permute-start.8 = (f32[128,640]{1,0:T(8,128)}, f32[128,640]{1,0:T(8,128)S(1)}, u32[]{:S(2)}, u32[]{:S(2)}) collective-permute-start(f32[128,640]{1,0:T(8,128)} %get-tuple-element.24), channel_id=1, source_target_pairs={{0,128},{16,48},{32,160},{48,16},{64,192},{80,112},{96,224},{112,8... | collective-permute-start | bytes 983048 | tf_op jit(solution)/shard_map/ppermute | solution.py:179
  154.3 6.4 %collective-permute-done.8.b_ref = f32[128,640]{1,0:T(8,128)S(1)} collective-permute-done((f32[128,640]{1,0:T(8,128)}, f32[128,640]{1,0:T(8,128)S(1)}, u32[]{:S(2)}, u32[]{:S(2)}) %collective-permute-start.8) | collective-permute-done | bytes 327712 | tf_op jit(solution)/shard_map/ppermute | solution.py:179
  160.8 0.7 copy-done.9
  161.5 2.1 %shard_map.59 = (f32[64,640]{1,0:T(8,128)}, f32[64,640]{1,0:T(8,128)}) custom-call(f32[128,640]{1,0:T(8,128)} %get-tuple-element.23.a_ref, f32[128,640]{1,0:T(8,128)} %copy-done.9), custom_call_target="tpu_custom_call" | custom-call | flops 327680 | bytes 983040 | tf_op jit(solution)/shard_map/pallas_call | solution.py:139
  163.6 1.9 %collective-permute-start.9 = (f32[64,640]{1,0:T(8,128)}, f32[64,640]{1,0:T(8,128)S(1)}, u32[]{:S(2)}, u32[]{:S(2)}) collective-permute-start(f32[64,640]{1,0:T(8,128)} %get-tuple-element.26), channel_id=1, source_target_pairs={{0,64},{16,272},{32,96},{48,304},{64,0},{80,336},{96,32},{112,368}... | collective-permute-start | bytes 491528 | tf_op jit(solution)/shard_map/ppermute | solution.py:179
  165.6 7.6 %collective-permute-done.9.b_ref = f32[64,640]{1,0:T(8,128)S(1)} collective-permute-done((f32[64,640]{1,0:T(8,128)}, f32[64,640]{1,0:T(8,128)S(1)}, u32[]{:S(2)}, u32[]{:S(2)}) %collective-permute-start.9) | collective-permute-done | bytes 163872 | tf_op jit(solution)/shard_map/ppermute | solution.py:179
  173.2 0.7 copy-done.10
  173.8 1.9 shard_map.60
  175.7 3.3 %collective-permute-start.10 = (f32[32,640]{1,0:T(8,128)}, f32[32,640]{1,0:T(8,128)S(1)}, u32[]{:S(2)}, u32[]{:S(2)}) collective-permute-start(f32[32,640]{1,0:T(8,128)} %get-tuple-element.28), channel_id=1, source_target_pairs={{0,256},{16,80},{32,288},{48,112},{64,320},{80,16},{96,352},{112,4... | collective-permute-start | bytes 245768 | tf_op jit(solution)/shard_map/ppermute | solution.py:179
  179.0 4.7 %collective-permute-done.10.b_ref = f32[32,640]{1,0:T(8,128)S(1)} collective-permute-done((f32[32,640]{1,0:T(8,128)}, f32[32,640]{1,0:T(8,128)S(1)}, u32[]{:S(2)}, u32[]{:S(2)}) %collective-permute-start.10) | collective-permute-done | bytes 81952 | tf_op jit(solution)/shard_map/ppermute | solution.py:179
  183.7 0.6 copy-done.11
  184.4 1.7 shard_map.61
  186.1 0.8 slice.69
  187.0 1.0 multiply_reduce_fusion
  188.0 1.7 convolution_bitcast_fusion
  (36 shorter events, 1.1 us)
Async XLA Ops:
  0.0 72.9 %copy-start = (bf16[1,1,1024,512]{3,2,1,0:T(8,128)(2,1)S(1)}, bf16[1,1,1024,512]{3,2,1,0:T(8,128)(2,1)}, u32[]{:S(2)}) copy-start(bf16[1,1,1024,512]{3,2,1,0:T(8,128)(2,1)} %param.5) | copy-start | bytes 3145732
  0.0 20.8 %collective-permute-start = (bf16[2,2,1,1,2,64,512]{6,5,4,3,2,1,0:T(8,128)(2,1)}, bf16[2,2,1,1,2,64,512]{6,5,4,3,2,1,0:T(8,128)(2,1)S(1)}, u32[]{:S(2)}, u32[]{:S(2)}) collective-permute-start(bf16[2,2,1,1,2,64,512]{6,5,4,3,2,1,0:T(8,128)(2,1)} %param.6), channel_id=1, source_target_pairs={{0,1},{1,2},{2,3},{4,5},{5,6},{6,7},{8,9},{9,10},{10,11},{12,13},{... | collective-permute-start | bytes 1572872 | tf_op jit(solution)/shard_map/ppermute | solution.py:19
  9.3 54.6 %collective-permute-start.1 = (bf16[2,2,1,1,2,64,512]{6,5,4,3,2,1,0:T(8,128)(2,1)}, bf16[2,2,1,1,2,64,512]{6,5,4,3,2,1,0:T(8,128)(2,1)S(1)}, u32[]{:S(2)}, u32[]{:S(2)}) collective-permute-start(bf16[2,2,1,1,2,64,512]{6,5,4,3,2,1,0:T(8,128)(2,1)} %param.6), channel_id=1, source_target_pairs={{1,0},{2,1},{3,2},{5,4},{6,5},{7,6},{9,8},{10,9},{11,10},{13,12},{... | collective-permute-start | bytes 1572872 | tf_op jit(solution)/shard_map/ppermute | solution.py:19
  10.6 53.3 %collective-permute-start.2 = (bf16[2,2,1,1,2,64,512]{6,5,4,3,2,1,0:T(8,128)(2,1)}, bf16[2,2,1,1,2,64,512]{6,5,4,3,2,1,0:T(8,128)(2,1)S(1)}, u32[]{:S(2)}, u32[]{:S(2)}) collective-permute-start(bf16[2,2,1,1,2,64,512]{6,5,4,3,2,1,0:T(8,128)(2,1)} %param.6), channel_id=1, source_target_pairs={{0,4},{4,8},{8,12},{1,5},{5,9},{9,13},{2,6},{6,10},{10,14},{3,7},{... | collective-permute-start | bytes 1572872 | tf_op jit(solution)/shard_map/ppermute | solution.py:19
  14.1 49.8 %collective-permute-start.3 = (bf16[2,2,1,1,2,64,512]{6,5,4,3,2,1,0:T(8,128)(2,1)}, bf16[2,2,1,1,2,64,512]{6,5,4,3,2,1,0:T(8,128)(2,1)S(1)}, u32[]{:S(2)}, u32[]{:S(2)}) collective-permute-start(bf16[2,2,1,1,2,64,512]{6,5,4,3,2,1,0:T(8,128)(2,1)} %param.6), channel_id=1, source_target_pairs={{4,0},{8,4},{12,8},{5,1},{9,5},{13,9},{6,2},{10,6},{14,10},{7,3},{... | collective-permute-start | bytes 1572872 | tf_op jit(solution)/shard_map/ppermute | solution.py:19
  63.9 9.0 %copy-start.4 = (bf16[2,2,1,1,2,64,512]{6,5,4,3,2,1,0:T(8,128)(2,1)}, bf16[2,2,1,1,2,64,512]{6,5,4,3,2,1,0:T(8,128)(2,1)S(1)}, u32[]{:S(2)}) copy-start(bf16[2,2,1,1,2,64,512]{6,5,4,3,2,1,0:T(8,128)(2,1)S(1)} %collective-permute-done.2) | copy-start | bytes 1572868
  63.9 9.0 %copy-start.6 = (bf16[2,2,1,1,2,64,512]{6,5,4,3,2,1,0:T(8,128)(2,1)}, bf16[2,2,1,1,2,64,512]{6,5,4,3,2,1,0:T(8,128)(2,1)S(1)}, u32[]{:S(2)}) copy-start(bf16[2,2,1,1,2,64,512]{6,5,4,3,2,1,0:T(8,128)(2,1)S(1)} %collective-permute-done.3) | copy-start | bytes 1572868
  65.7 25.9 %collective-permute-start.4 = (bf16[2,2,1,2,2,64,512]{6,5,4,3,2,1,0:T(8,128)(2,1)}, bf16[2,2,1,2,2,64,512]{6,5,4,3,2,1,0:T(8,128)(2,1)}, u32[]{:S(2)}, u32[]{:S(2)}) collective-permute-start(bf16[2,2,1,2,2,64,512]{6,5,4,3,2,1,0:T(8,128)(2,1)} %constant_dynamic-update-slice_fusion), channel_id=1, source_target_pairs={{0,4},{4,8},{8,12},{1,5},{5,9},{9,13},{2,6},{6,10},{10,14},{3,7},{... | collective-permute-start | bytes 3145736 | tf_op jit(solution)/shard_map/ppermute | solution.py:19
  70.8 26.5 %collective-permute-start.5 = (bf16[2,2,1,2,2,64,512]{6,5,4,3,2,1,0:T(8,128)(2,1)}, bf16[2,2,1,2,2,64,512]{6,5,4,3,2,1,0:T(8,128)(2,1)}, u32[]{:S(2)}, u32[]{:S(2)}) collective-permute-start(bf16[2,2,1,2,2,64,512]{6,5,4,3,2,1,0:T(8,128)(2,1)} %constant_dynamic-update-slice_fusion), channel_id=1, source_target_pairs={{4,0},{8,4},{12,8},{5,1},{9,5},{13,9},{6,2},{10,6},{14,10},{7,3},{... | collective-permute-start | bytes 3145736 | tf_op jit(solution)/shard_map/ppermute | solution.py:19
  73.5 25.1 %copy-start.3 = (bf16[2,2,1,1,2,64,512]{6,5,4,3,2,1,0:T(8,128)(2,1)S(1)}, bf16[2,2,1,1,2,64,512]{6,5,4,3,2,1,0:T(8,128)(2,1)}, u32[]{:S(2)}) copy-start(bf16[2,2,1,1,2,64,512]{6,5,4,3,2,1,0:T(8,128)(2,1)} %param.6) | copy-start | bytes 1572868
  73.6 25.1 %copy-start.5 = (bf16[2,2,1,1,2,64,512]{6,5,4,3,2,1,0:T(8,128)(2,1)S(1)}, bf16[2,2,1,1,2,64,512]{6,5,4,3,2,1,0:T(8,128)(2,1)}, u32[]{:S(2)}) copy-start(bf16[2,2,1,1,2,64,512]{6,5,4,3,2,1,0:T(8,128)(2,1)} %copy-done.4) | copy-start | bytes 1572868
  73.6 25.1 %copy-start.7 = (bf16[2,2,1,1,2,64,512]{6,5,4,3,2,1,0:T(8,128)(2,1)S(1)}, bf16[2,2,1,1,2,64,512]{6,5,4,3,2,1,0:T(8,128)(2,1)}, u32[]{:S(2)}) copy-start(bf16[2,2,1,1,2,64,512]{6,5,4,3,2,1,0:T(8,128)(2,1)} %copy-done.6) | copy-start | bytes 1572868
  117.7 12.6 %collective-permute-start.6 = (f32[512,640]{1,0:T(8,128)}, f32[512,640]{1,0:T(8,128)S(1)}, u32[]{:S(2)}, u32[]{:S(2)}) collective-permute-start(f32[512,640]{1,0:T(8,128)} %shard_map.56), channel_id=1, source_target_pairs={{0,16},{16,0},{32,48},{48,32},{64,80},{80,64},{96,112},{112,96},{1... | collective-permute-start | bytes 3932168 | tf_op jit(solution)/shard_map/ppermute | solution.py:179
  130.2 57.8 %copy-start.8 = (bf16[512,512]{1,0:T(8,128)(2,1)S(1)}, bf16[512,512]{1,0:T(8,128)(2,1)}, u32[]{:S(2)}) copy-start(bf16[512,512]{1,0:T(8,128)(2,1)} %param.9) | copy-start | bytes 1572868
  130.2 1.1 copy-start.1
  135.3 12.7 %collective-permute-start.7 = (f32[256,640]{1,0:T(8,128)}, f32[256,640]{1,0:T(8,128)S(1)}, u32[]{:S(2)}, u32[]{:S(2)}) collective-permute-start(f32[256,640]{1,0:T(8,128)} %get-tuple-element.22), channel_id=1, source_target_pairs={{0,32},{16,144},{32,0},{48,176},{64,96},{80,208},{96,64},{112,240}... | collective-permute-start | bytes 1966088 | tf_op jit(solution)/shard_map/ppermute | solution.py:179
  148.0 0.8 copy-start.2
  151.6 9.2 %collective-permute-start.8 = (f32[128,640]{1,0:T(8,128)}, f32[128,640]{1,0:T(8,128)S(1)}, u32[]{:S(2)}, u32[]{:S(2)}) collective-permute-start(f32[128,640]{1,0:T(8,128)} %get-tuple-element.24), channel_id=1, source_target_pairs={{0,128},{16,48},{32,160},{48,16},{64,192},{80,112},{96,224},{112,8... | collective-permute-start | bytes 983048 | tf_op jit(solution)/shard_map/ppermute | solution.py:179
  160.8 0.7 copy-start.9
  163.6 9.5 %collective-permute-start.9 = (f32[64,640]{1,0:T(8,128)}, f32[64,640]{1,0:T(8,128)S(1)}, u32[]{:S(2)}, u32[]{:S(2)}) collective-permute-start(f32[64,640]{1,0:T(8,128)} %get-tuple-element.26), channel_id=1, source_target_pairs={{0,64},{16,272},{32,96},{48,304},{64,0},{80,336},{96,32},{112,368}... | collective-permute-start | bytes 491528 | tf_op jit(solution)/shard_map/ppermute | solution.py:179
  173.2 0.7 copy-start.10
  175.7 8.0 %collective-permute-start.10 = (f32[32,640]{1,0:T(8,128)}, f32[32,640]{1,0:T(8,128)S(1)}, u32[]{:S(2)}, u32[]{:S(2)}) collective-permute-start(f32[32,640]{1,0:T(8,128)} %get-tuple-element.28), channel_id=1, source_target_pairs={{0,256},{16,80},{32,288},{48,112},{64,320},{80,16},{96,352},{112,4... | collective-permute-start | bytes 245768 | tf_op jit(solution)/shard_map/ppermute | solution.py:179
  183.7 0.6 copy-start.11

commit v8 on v7

--- a/solution.py
+++ b/solution.py
@@ -37,63 +37,62 @@
 PACK = 128
 
 
-def attention_kernel(q_ref, k_ref, v_ref, keep_ref, out_ref):
-    rows = q_ref.shape[0]
+def attention_kernel(qt_ref, k_ref, vt_ref, keep_ref, out_ref):
+    rows = qt_ref.shape[1]
     keep = keep_ref[...] > 0
-    lane = lax.broadcasted_iota(jnp.int32, (1, 2 * HD), 1)
-    low = lane < HD
-    stat_lane = lax.broadcasted_iota(jnp.int32, (1, PACK), 1)
-    stats = jnp.zeros((rows, PACK), jnp.float32)
+    sub = lax.broadcasted_iota(jnp.int32, (2 * HD, 1), 0)
+    low = sub < HD
+    stat_row = lax.broadcasted_iota(jnp.int32, (PACK, 1), 0)
+    stats = jnp.zeros((PACK, rows), jnp.float32)
     scale = jnp.asarray(1.0 / 8.0, jnp.bfloat16)
     blocks = []
     for pair in range(HEADS // 2):
-        cols = pl.ds(pair * 2 * HD, 2 * HD)
-        q2 = q_ref[:, cols] * scale
-        k2 = k_ref[:, cols]
-        v2 = v_ref[:, cols]
+        dims = pl.ds(pair * 2 * HD, 2 * HD)
+        qt2 = qt_ref[dims, :] * scale
+        k2 = k_ref[:, dims]
+        vt2 = vt_ref[dims, :]
         outs = []
         for part in range(2):
             mine = low if part == 0 else jnp.logical_not(low)
-            qh = jnp.where(mine, q2, jnp.zeros_like(q2))
-            scores = lax.dot_general(
-                qh, k2, (((1,), (1,)), ((), ())), preferred_element_type=jnp.float32
-            )
+            qh = jnp.where(mine, qt2, jnp.zeros_like(qt2))
+            scores = jnp.dot(k2, qh, preferred_element_type=jnp.float32)
             scores = jnp.where(keep, scores, jnp.float32(-1e30))
-            top = jnp.max(scores, axis=1, keepdims=True)
+            top = jnp.max(scores, axis=0, keepdims=True)
             probs = jnp.exp(scores - top)
-            total = jnp.sum(probs, axis=1, keepdims=True)
+            total = jnp.sum(probs, axis=0, keepdims=True)
             outs.append(
-                jnp.dot(probs.astype(jnp.bfloat16), v2, preferred_element_type=jnp.float32)
+                jnp.dot(vt2, probs.astype(jnp.bfloat16), preferred_element_type=jnp.float32)
             )
             head = pair * 2 + part
-            stats = jnp.where(stat_lane == head, top, stats)
-            stats = jnp.where(stat_lane == HEADS + head, total, stats)
-        blocks.append(jnp.where(low, outs[0], outs[1]))
-    out_ref[...] = jnp.concatenate(blocks + [stats], axis=1)
-
-
-def attention(query_rows, keys, values, keep):
-    qtok, width = query_rows.shape
+            stats = jnp.where(stat_row == head, top, stats)
+            stats = jnp.where(stat_row == HEADS + head, total, stats)
+        blocks.append(jnp.where(low, outs[0], outs[1]).T)
+    out_ref[...] = jnp.concatenate(blocks + [stats.T], axis=1)
+
+
+def attention(query_t, keys, values_t, keep, first, count_rows):
+    width, qtok = query_t.shape
     count = keys.shape[0]
-    tiles = qtok // TQ
-    flops = 2 * 2 * qtok * count * 2 * width
+    tiles = count_rows // TQ
+    offset = first // TQ
+    flops = 2 * 2 * count_rows * count * 2 * width
     return pl.pallas_call(
         attention_kernel,
         grid=(tiles,),
         in_specs=[
-            pl.BlockSpec((TQ, width), lambda i: (i, 0)),
+            pl.BlockSpec((width, TQ), lambda i: (0, i + offset)),
             pl.BlockSpec((count, width), lambda i: (0, 0)),
-            pl.BlockSpec((count, width), lambda i: (0, 0)),
-            pl.BlockSpec((1, count), lambda i: (0, 0)),
+            pl.BlockSpec((width, count), lambda i: (0, 0)),
+            pl.BlockSpec((count, 1), lambda i: (0, 0)),
         ],
         out_specs=pl.BlockSpec((TQ, width + PACK), lambda i: (i, 0)),
-        out_shape=jax.ShapeDtypeStruct((qtok, width + PACK), jnp.float32),
+        out_shape=jax.ShapeDtypeStruct((count_rows, width + PACK), jnp.float32),
         cost_estimate=pl.CostEstimate(
             flops=flops,
-            transcendentals=qtok * count * HEADS,
-            bytes_accessed=qtok * width * 6 + count * width * 4,
+            transcendentals=count_rows * count * HEADS,
+            bytes_accessed=count_rows * width * 6 + count * width * 4,
         ),
-    )(query_rows, keys, values, keep)
+    )(query_t, keys, values_t, keep)
 
 
 def merge_kernel(a_ref, b_ref, *out_refs):
@@ -195,7 +194,7 @@
     nlist = listed.shape[0]
     chosen = jnp.take(hood, listed, axis=2)
     keep = jnp.broadcast_to((block_valid[0, 0] > 0)[None, :, None], (frames, nlist, blk))
-    keep = keep.reshape(1, -1).astype(jnp.int32)
+    keep = keep.reshape(-1, 1).astype(jnp.int32)
     keys = chosen[0].reshape(-1, width)
     values = chosen[1].reshape(-1, width)
     query_rows = queries[0, 0]
@@ -207,8 +206,10 @@
     )
     query_rows = jnp.take(query_rows.reshape(groups, qtok // groups, width), order, axis=0)
     query_rows = query_rows.reshape(qtok, width)
-    second = attention(query_rows[qtok // 2 :], keys, values, keep)
-    first = attention(query_rows[: qtok // 2], keys, values, keep)
+    query_t = query_rows.T
+    values_t = values.T
+    second = attention(query_t, keys, values_t, keep, qtok // 2, qtok // 2)
+    first = attention(query_t, keys, values_t, keep, 0, qtok // 2)
     final = tree_reduce(first, second)
     summed = final[:, :width]
     total = final[:, width + HEADS : width + 2 * HEADS]

time: 191 us -> 199 us (1.042)
  Pallas kernels: 33.8 us -> 41.1 us
    pallas_call x2, Pallas kernels: 21.3 us -> 28.6 us  [attention(): pl.pallas_call(attention_kernel, grid=(tiles,), in_specs=[pl.BlockSpec((w...]
    unnamed x25 -> x37, local copies, waits for them, and re-layouts: 4.91 us -> 4.96 us
  transfers between devices with their start and end apart: 11 -> 11, of which waited for: 8 -> 8; matrix products, arithmetic and copies ran while one was open for 3% -> 3% of each run, Pallas kernels for 6% -> 7%
where the time goes in v8:
time: 199 us; the launch traced here: 198 us
  waiting for transfers between devices  98.5 us (49%)
  Pallas kernels  41.1 us (21%)
  starting transfers between devices  33.1 us (17%)
  local copies, waits for them, and re-layouts  17.7 us (9%)
  other arithmetic  5.98 us (3%)
    ppermute x6, waiting for transfers between devices, shifted(): return lax.ppermute(array, axis, pairs)  68.9 us
    ppermute x5, waiting for transfers between devices, tree_reduce(): got = lax.ppermute(second, 'tm', step_pairs(nbits, i))  29.5 us
    pallas_call x2, Pallas kernels, attention(): pl.pallas_call(attention_kernel, grid=(tiles,), in_specs=[pl.BlockSpec((w...  28.6 us
    ppermute x6, starting transfers between devices, shifted(): return lax.ppermute(array, axis, pairs)  21.2 us
    pallas_call x5, Pallas kernels, merge(): pl.pallas_call(merge_kernel, out_shape=[shape] * count, cost_estimate=pl....  12.5 us
    ppermute x5, starting transfers between devices, tree_reduce(): got = lax.ppermute(second, 'tm', step_pairs(nbits, i))  11.9 us
    unnamed x37, local copies, waits for them, and re-layouts  4.96 us
  transfers between devices with their start and end apart: 11, of which 8 were waited for; matrix products, arithmetic and copies ran while one was open for 3% of the time, Pallas kernels for 7%

profile of v8, /device:TPU:6, one launch (start us, length us, event | category | flops | bytes accessed | tf_op | source)
XLA Modules:
  0.0 198.5 jit_solution(2933515565409038019)
XLA Ops:
  0.0 9.3 %collective-permute-start = (bf16[2,2,1,1,2,64,512]{6,5,4,3,2,1,0:T(8,128)(2,1)}, bf16[2,2,1,1,2,64,512]{6,5,4,3,2,1,0:T(8,128)(2,1)S(1)}, u32[]{:S(2)}, u32[]{:S(2)}) collective-permute-start(bf16[2,2,1,1,2,64,512]{6,5,4,3,2,1,0:T(8,128)(2,1)} %param.6), channel_id=1, source_target_pairs={{0,1},{1,2},{2,3},{4,5},{5,6},{6,7},{8,9},{9,10},{10,11},{12,13},{... | collective-permute-start | bytes 1572872 | tf_op jit(solution)/shard_map/ppermute | solution.py:19
  9.3 1.3 collective-permute-start.1
  10.6 3.5 %collective-permute-start.2 = (bf16[2,2,1,1,2,64,512]{6,5,4,3,2,1,0:T(8,128)(2,1)}, bf16[2,2,1,1,2,64,512]{6,5,4,3,2,1,0:T(8,128)(2,1)S(1)}, u32[]{:S(2)}, u32[]{:S(2)}) collective-permute-start(bf16[2,2,1,1,2,64,512]{6,5,4,3,2,1,0:T(8,128)(2,1)} %param.6), channel_id=1, source_target_pairs={{0,4},{4,8},{8,12},{1,5},{5,9},{9,13},{2,6},{6,10},{10,14},{3,7},{... | collective-permute-start | bytes 1572872 | tf_op jit(solution)/shard_map/ppermute | solution.py:19
  14.1 1.3 collective-permute-start.3
  15.5 0.7 fusion.3
  16.2 4.7 %collective-permute-done = bf16[2,2,1,1,2,64,512]{6,5,4,3,2,1,0:T(8,128)(2,1)S(1)} collective-permute-done((bf16[2,2,1,1,2,64,512]{6,5,4,3,2,1,0:T(8,128)(2,1)}, bf16[2,2,1,1,2,64,512]{6,5,4,3,2,1,0:T(8,128)(2,1)S(1)}, u32[]{:S(2)}, u32[]{:S(2)}) %collective-permute-start) | collective-permute-done | bytes 524320 | tf_op jit(solution)/shard_map/ppermute | solution.py:19
  20.9 43.0 %collective-permute-done.1 = bf16[2,2,1,1,2,64,512]{6,5,4,3,2,1,0:T(8,128)(2,1)S(1)} collective-permute-done((bf16[2,2,1,1,2,64,512]{6,5,4,3,2,1,0:T(8,128)(2,1)}, bf16[2,2,1,1,2,64,512]{6,5,4,3,2,1,0:T(8,128)(2,1)S(1)}, u32[]{:S(2)}, u32[]{:S(2)}) %collective-permute-start.1) | collective-permute-done | bytes 524320 | tf_op jit(solution)/shard_map/ppermute | solution.py:19
  63.9 1.0 constant_dynamic-update-slice_fusion.1
  64.9 0.9 constant_dynamic-update-slice_fusion
  65.8 4.4 %collective-permute-start.4 = (bf16[2,2,1,2,2,64,512]{6,5,4,3,2,1,0:T(8,128)(2,1)}, bf16[2,2,1,2,2,64,512]{6,5,4,3,2,1,0:T(8,128)(2,1)}, u32[]{:S(2)}, u32[]{:S(2)}) collective-permute-start(bf16[2,2,1,2,2,64,512]{6,5,4,3,2,1,0:T(8,128)(2,1)} %constant_dynamic-update-slice_fusion), channel_id=1, source_target_pairs={{0,4},{4,8},{8,12},{1,5},{5,9},{9,13},{2,6},{6,10},{10,14},{3,7},{... | collective-permute-start | bytes 3145736 | tf_op jit(solution)/shard_map/ppermute | solution.py:19
  70.3 0.6 gather_fusion
  70.9 0.5 copy.7
  71.5 1.4 collective-permute-start.5
  73.3 1.3 convert_element_type.15.keep_ref
  74.6 1.1 select_bitcast_fusion.1.qt_ref
  75.7 16.0 %collective-permute-done.4 = bf16[2,2,1,2,2,64,512]{6,5,4,3,2,1,0:T(8,128)(2,1)} collective-permute-done((bf16[2,2,1,2,2,64,512]{6,5,4,3,2,1,0:T(8,128)(2,1)}, bf16[2,2,1,2,2,64,512]{6,5,4,3,2,1,0:T(8,128)(2,1)}, u32[]{:S(2)}, u32[]{:S(2)}) %collective-permute-start.4) | collective-permute-done | bytes 1048608 | tf_op jit(solution)/shard_map/ppermute | solution.py:19
  91.7 1.3 fusion.5
  92.9 5.2 %collective-permute-done.5 = bf16[2,2,1,2,2,64,512]{6,5,4,3,2,1,0:T(8,128)(2,1)} collective-permute-done((bf16[2,2,1,2,2,64,512]{6,5,4,3,2,1,0:T(8,128)(2,1)}, bf16[2,2,1,2,2,64,512]{6,5,4,3,2,1,0:T(8,128)(2,1)}, u32[]{:S(2)}, u32[]{:S(2)}) %collective-permute-start.5) | collective-permute-done | bytes 1048608 | tf_op jit(solution)/shard_map/ppermute | solution.py:19
  98.2 1.3 fusion.6
  99.5 2.8 %maximum_maximum_fusion = bf16[2,2,3,3,2,64,512]{6,5,4,3,2,1,0:T(8,128)(2,1)} fusion(bf16[2,2,1,1,2,64,512]{6,5,4,3,2,1,0:T(8,128)(2,1)S(1)} %get-tuple-element.34, bf16[2,2,1,1,2,64,512]{6,5,4,3,2,1,0:T(8,128)(2,1)S(1)} %copy-done.11, bf16[2,2,1,1,2,64,512]{6,5,4,3,2,1,0:T(8,128)(2,1)S(1)} %get-tuple-element.33, ...), kind=kLoop, calls=%fused_computation.2 | loop fusion | flops 18874368 | bytes 9437184 | tf_op jit(solution)/shard_map/concatenate | solution.py:34
  102.3 3.0 %gather_fusion.1 = bf16[8,2,2,64,512]{4,3,2,1,0:T(8,128)(2,1)S(1)} fusion(bf16[2,2,18,64,512]{4,3,2,1,0:T(8,128)(2,1)} %bitcast.28, s32[1024]{0:T(1024)S(1)} %get-tuple-element.39), kind=kCustom, calls=%fused_computation.1 | custom fusion | bytes 4194336 | tf_op jit(solution)/shard_map/jit(_take)/gather | solution.py:195
  105.3 0.3 select_bitcast_fusion
  105.8 1.3 copy.10
  107.2 1.1 copy.8
  108.3 14.3 %shard_map.56 = f32[512,640]{1,0:T(8,128)} custom-call(bf16[512,1024]{1,0:T(8,128)(2,1)} %select_bitcast_fusion.1.qt_ref, bf16[1024,512]{1,0:T(8,128)(2,1)} %bitcast.33, bf16[512,1024]{1,0:T(8,128)(2,1)} %bitcast.31, s32[1024,1]{1,0:T(8,128)} %convert_element_type.15.keep_ref), custom_call_target="tpu_custom_call" | custom-call | flops 2147483648 | bytes 3670016 | tf_op jit(solution)/shard_map/pallas_call | solution.py:79
  122.5 2.1 %collective-permute-start.6 = (f32[512,640]{1,0:T(8,128)}, f32[512,640]{1,0:T(8,128)S(1)}, u32[]{:S(2)}, u32[]{:S(2)}) collective-permute-start(f32[512,640]{1,0:T(8,128)} %shard_map.56), channel_id=1, source_target_pairs={{0,16},{16,0},{32,48},{48,32},{64,80},{80,64},{96,112},{112,96},{1... | collective-permute-start | bytes 3932168 | tf_op jit(solution)/shard_map/ppermute | solution.py:178
  124.6 14.3 %shard_map.55.a_ref = f32[512,640]{1,0:T(8,128)} custom-call(bf16[512,1024]{1,0:T(8,128)(2,1)} %select_bitcast_fusion.1.qt_ref, bf16[1024,512]{1,0:T(8,128)(2,1)} %bitcast.34, bf16[512,1024]{1,0:T(8,128)(2,1)} %bitcast.32, s32[1024,1]{1,0:T(8,128)} %convert_element_type.15.keep_ref), custom_call_target="tpu_custom_call" | custom-call | flops 2147483648 | bytes 3670016 | tf_op jit(solution)/shard_map/pallas_call | solution.py:79
  138.9 1.1 copy-done.5
  140.0 4.0 %shard_map.57 = (f32[256,640]{1,0:T(8,128)}, f32[256,640]{1,0:T(8,128)}) custom-call(f32[512,640]{1,0:T(8,128)} %shard_map.55.a_ref, f32[512,640]{1,0:T(8,128)} %copy-done.5), custom_call_target="tpu_custom_call" | custom-call | flops 1310720 | bytes 3932160 | tf_op jit(solution)/shard_map/pallas_call | solution.py:138
  144.0 1.9 collective-permute-start.7
  145.9 10.8 %collective-permute-done.7.b_ref = f32[256,640]{1,0:T(8,128)S(1)} collective-permute-done((f32[256,640]{1,0:T(8,128)}, f32[256,640]{1,0:T(8,128)S(1)}, u32[]{:S(2)}, u32[]{:S(2)}) %collective-permute-start.7) | collective-permute-done | bytes 655392 | tf_op jit(solution)/shard_map/ppermute | solution.py:178
  156.7 0.8 copy-done.6
  157.5 2.8 %shard_map.58 = (f32[128,640]{1,0:T(8,128)}, f32[128,640]{1,0:T(8,128)}) custom-call(f32[256,640]{1,0:T(8,128)} %get-tuple-element.21.a_ref, f32[256,640]{1,0:T(8,128)} %copy-done.6), custom_call_target="tpu_custom_call" | custom-call | flops 655360 | bytes 1966080 | tf_op jit(solution)/shard_map/pallas_call | solution.py:138
  160.3 2.7 %collective-permute-start.8 = (f32[128,640]{1,0:T(8,128)}, f32[128,640]{1,0:T(8,128)S(1)}, u32[]{:S(2)}, u32[]{:S(2)}) collective-permute-start(f32[128,640]{1,0:T(8,128)} %get-tuple-element.24), channel_id=1, source_target_pairs={{0,128},{16,48},{32,160},{48,16},{64,192},{80,112},{96,224},{112,8... | collective-permute-start | bytes 983048 | tf_op jit(solution)/shard_map/ppermute | solution.py:178
  163.0 6.4 %collective-permute-done.8.b_ref = f32[128,640]{1,0:T(8,128)S(1)} collective-permute-done((f32[128,640]{1,0:T(8,128)}, f32[128,640]{1,0:T(8,128)S(1)}, u32[]{:S(2)}, u32[]{:S(2)}) %collective-permute-start.8) | collective-permute-done | bytes 327712 | tf_op jit(solution)/shard_map/ppermute | solution.py:178
  169.5 0.7 copy-done.13
  170.2 2.2 %shard_map.59 = (f32[64,640]{1,0:T(8,128)}, f32[64,640]{1,0:T(8,128)}) custom-call(f32[128,640]{1,0:T(8,128)} %get-tuple-element.23.a_ref, f32[128,640]{1,0:T(8,128)} %copy-done.13), custom_call_target="tpu_custom_call" | custom-call | flops 327680 | bytes 983040 | tf_op jit(solution)/shard_map/pallas_call | solution.py:138
  172.4 1.9 collective-permute-start.9
  174.3 7.6 %collective-permute-done.9.b_ref = f32[64,640]{1,0:T(8,128)S(1)} collective-permute-done((f32[64,640]{1,0:T(8,128)}, f32[64,640]{1,0:T(8,128)S(1)}, u32[]{:S(2)}, u32[]{:S(2)}) %collective-permute-start.9) | collective-permute-done | bytes 163872 | tf_op jit(solution)/shard_map/ppermute | solution.py:178
  181.9 0.7 copy-done.14
  182.5 1.9 shard_map.60
  184.4 3.3 %collective-permute-start.10 = (f32[32,640]{1,0:T(8,128)}, f32[32,640]{1,0:T(8,128)S(1)}, u32[]{:S(2)}, u32[]{:S(2)}) collective-permute-start(f32[32,640]{1,0:T(8,128)} %get-tuple-element.28), channel_id=1, source_target_pairs={{0,256},{16,80},{32,288},{48,112},{64,320},{80,16},{96,352},{112,4... | collective-permute-start | bytes 245768 | tf_op jit(solution)/shard_map/ppermute | solution.py:178
  187.7 4.7 %collective-permute-done.10.b_ref = f32[32,640]{1,0:T(8,128)S(1)} collective-permute-done((f32[32,640]{1,0:T(8,128)}, f32[32,640]{1,0:T(8,128)S(1)}, u32[]{:S(2)}, u32[]{:S(2)}) %collective-permute-start.10) | collective-permute-done | bytes 81952 | tf_op jit(solution)/shard_map/ppermute | solution.py:178
  192.5 0.6 copy-done.15
  193.1 1.7 shard_map.61
  194.8 0.8 slice.51
  195.8 1.0 multiply_reduce_fusion
  196.8 1.7 convolution_bitcast_fusion
  (51 shorter events, 1.0 us)
Async XLA Ops:
  0.0 70.3 %copy-start = (bf16[1,1,1024,512]{3,2,1,0:T(8,128)(2,1)S(1)}, bf16[1,1,1024,512]{3,2,1,0:T(8,128)(2,1)}, u32[]{:S(2)}) copy-start(bf16[1,1,1024,512]{3,2,1,0:T(8,128)(2,1)} %param.5) | copy-start | bytes 3145732
  0.0 74.5 %copy-start.17 = (s32[1,1,8]{2,1,0:T(1,128)S(1)}, s32[1,1,8]{2,1,0:T(1,128)}, u32[]{:S(2)}) copy-start(s32[1,1,8]{2,1,0:T(1,128)} %param.7) | copy-start | bytes 100
  0.0 73.2 %copy-start.16 = (s32[1,1,8]{2,1,0:T(1,128)S(1)}, s32[1,1,8]{2,1,0:T(1,128)}, u32[]{:S(2)}) copy-start(s32[1,1,8]{2,1,0:T(1,128)} %param.8) | copy-start | bytes 100
  0.0 20.8 %collective-permute-start = (bf16[2,2,1,1,2,64,512]{6,5,4,3,2,1,0:T(8,128)(2,1)}, bf16[2,2,1,1,2,64,512]{6,5,4,3,2,1,0:T(8,128)(2,1)S(1)}, u32[]{:S(2)}, u32[]{:S(2)}) collective-permute-start(bf16[2,2,1,1,2,64,512]{6,5,4,3,2,1,0:T(8,128)(2,1)} %param.6), channel_id=1, source_target_pairs={{0,1},{1,2},{2,3},{4,5},{5,6},{6,7},{8,9},{9,10},{10,11},{12,13},{... | collective-permute-start | bytes 1572872 | tf_op jit(solution)/shard_map/ppermute | solution.py:19
  9.3 54.6 %collective-permute-start.1 = (bf16[2,2,1,1,2,64,512]{6,5,4,3,2,1,0:T(8,128)(2,1)}, bf16[2,2,1,1,2,64,512]{6,5,4,3,2,1,0:T(8,128)(2,1)S(1)}, u32[]{:S(2)}, u32[]{:S(2)}) collective-permute-start(bf16[2,2,1,1,2,64,512]{6,5,4,3,2,1,0:T(8,128)(2,1)} %param.6), channel_id=1, source_target_pairs={{1,0},{2,1},{3,2},{5,4},{6,5},{7,6},{9,8},{10,9},{11,10},{13,12},{... | collective-permute-start | bytes 1572872 | tf_op jit(solution)/shard_map/ppermute | solution.py:19
  10.6 53.3 %collective-permute-start.2 = (bf16[2,2,1,1,2,64,512]{6,5,4,3,2,1,0:T(8,128)(2,1)}, bf16[2,2,1,1,2,64,512]{6,5,4,3,2,1,0:T(8,128)(2,1)S(1)}, u32[]{:S(2)}, u32[]{:S(2)}) collective-permute-start(bf16[2,2,1,1,2,64,512]{6,5,4,3,2,1,0:T(8,128)(2,1)} %param.6), channel_id=1, source_target_pairs={{0,4},{4,8},{8,12},{1,5},{5,9},{9,13},{2,6},{6,10},{10,14},{3,7},{... | collective-permute-start | bytes 1572872 | tf_op jit(solution)/shard_map/ppermute | solution.py:19
  14.1 49.8 %collective-permute-start.3 = (bf16[2,2,1,1,2,64,512]{6,5,4,3,2,1,0:T(8,128)(2,1)}, bf16[2,2,1,1,2,64,512]{6,5,4,3,2,1,0:T(8,128)(2,1)S(1)}, u32[]{:S(2)}, u32[]{:S(2)}) collective-permute-start(bf16[2,2,1,1,2,64,512]{6,5,4,3,2,1,0:T(8,128)(2,1)} %param.6), channel_id=1, source_target_pairs={{4,0},{8,4},{12,8},{5,1},{9,5},{13,9},{6,2},{10,6},{14,10},{7,3},{... | collective-permute-start | bytes 1572872 | tf_op jit(solution)/shard_map/ppermute | solution.py:19
  20.9 49.4 %copy-start.1 = (bf16[2,2,1,1,2,64,512]{6,5,4,3,2,1,0:T(8,128)(2,1)}, bf16[2,2,1,1,2,64,512]{6,5,4,3,2,1,0:T(8,128)(2,1)S(1)}, u32[]{:S(2)}) copy-start(bf16[2,2,1,1,2,64,512]{6,5,4,3,2,1,0:T(8,128)(2,1)S(1)} %collective-permute-done) | copy-start | bytes 1572868
  63.9 6.4 %copy-start.3 = (bf16[2,2,1,1,2,64,512]{6,5,4,3,2,1,0:T(8,128)(2,1)}, bf16[2,2,1,1,2,64,512]{6,5,4,3,2,1,0:T(8,128)(2,1)S(1)}, u32[]{:S(2)}) copy-start(bf16[2,2,1,1,2,64,512]{6,5,4,3,2,1,0:T(8,128)(2,1)S(1)} %collective-permute-done.1) | copy-start | bytes 1572868
  63.9 7.0 %copy-start.8 = (bf16[2,2,1,1,2,64,512]{6,5,4,3,2,1,0:T(8,128)(2,1)}, bf16[2,2,1,1,2,64,512]{6,5,4,3,2,1,0:T(8,128)(2,1)S(1)}, u32[]{:S(2)}) copy-start(bf16[2,2,1,1,2,64,512]{6,5,4,3,2,1,0:T(8,128)(2,1)S(1)} %collective-permute-done.2) | copy-start | bytes 1572868
  63.9 7.0 %copy-start.10 = (bf16[2,2,1,1,2,64,512]{6,5,4,3,2,1,0:T(8,128)(2,1)}, bf16[2,2,1,1,2,64,512]{6,5,4,3,2,1,0:T(8,128)(2,1)S(1)}, u32[]{:S(2)}) copy-start(bf16[2,2,1,1,2,64,512]{6,5,4,3,2,1,0:T(8,128)(2,1)S(1)} %collective-permute-done.3) | copy-start | bytes 1572868
  65.8 25.9 %collective-permute-start.4 = (bf16[2,2,1,2,2,64,512]{6,5,4,3,2,1,0:T(8,128)(2,1)}, bf16[2,2,1,2,2,64,512]{6,5,4,3,2,1,0:T(8,128)(2,1)}, u32[]{:S(2)}, u32[]{:S(2)}) collective-permute-start(bf16[2,2,1,2,2,64,512]{6,5,4,3,2,1,0:T(8,128)(2,1)} %constant_dynamic-update-slice_fusion), channel_id=1, source_target_pairs={{0,4},{4,8},{8,12},{1,5},{5,9},{9,13},{2,6},{6,10},{10,14},{3,7},{... | collective-permute-start | bytes 3145736 | tf_op jit(solution)/shard_map/ppermute | solution.py:19
  71.5 28.0 %copy-start.2 = (bf16[2,2,1,1,2,64,512]{6,5,4,3,2,1,0:T(8,128)(2,1)S(1)}, bf16[2,2,1,1,2,64,512]{6,5,4,3,2,1,0:T(8,128)(2,1)}, u32[]{:S(2)}) copy-start(bf16[2,2,1,1,2,64,512]{6,5,4,3,2,1,0:T(8,128)(2,1)} %copy-done.1) | copy-start | bytes 1572868
  71.5 28.0 %copy-start.4 = (bf16[2,2,1,1,2,64,512]{6,5,4,3,2,1,0:T(8,128)(2,1)S(1)}, bf16[2,2,1,1,2,64,512]{6,5,4,3,2,1,0:T(8,128)(2,1)}, u32[]{:S(2)}) copy-start(bf16[2,2,1,1,2,64,512]{6,5,4,3,2,1,0:T(8,128)(2,1)} %copy-done.3) | copy-start | bytes 1572868
  71.5 26.7 %collective-permute-start.5 = (bf16[2,2,1,2,2,64,512]{6,5,4,3,2,1,0:T(8,128)(2,1)}, bf16[2,2,1,2,2,64,512]{6,5,4,3,2,1,0:T(8,128)(2,1)}, u32[]{:S(2)}, u32[]{:S(2)}) collective-permute-start(bf16[2,2,1,2,2,64,512]{6,5,4,3,2,1,0:T(8,128)(2,1)} %constant_dynamic-update-slice_fusion), channel_id=1, source_target_pairs={{4,0},{8,4},{12,8},{5,1},{9,5},{13,9},{6,2},{10,6},{14,10},{7,3},{... | collective-permute-start | bytes 3145736 | tf_op jit(solution)/shard_map/ppermute | solution.py:19
  74.5 24.9 %copy-start.7 = (bf16[2,2,1,1,2,64,512]{6,5,4,3,2,1,0:T(8,128)(2,1)S(1)}, bf16[2,2,1,1,2,64,512]{6,5,4,3,2,1,0:T(8,128)(2,1)}, u32[]{:S(2)}) copy-start(bf16[2,2,1,1,2,64,512]{6,5,4,3,2,1,0:T(8,128)(2,1)} %param.6) | copy-start | bytes 1572868
  74.6 24.9 %copy-start.9 = (bf16[2,2,1,1,2,64,512]{6,5,4,3,2,1,0:T(8,128)(2,1)S(1)}, bf16[2,2,1,1,2,64,512]{6,5,4,3,2,1,0:T(8,128)(2,1)}, u32[]{:S(2)}) copy-start(bf16[2,2,1,1,2,64,512]{6,5,4,3,2,1,0:T(8,128)(2,1)} %copy-done.8) | copy-start | bytes 1572868
  74.6 24.9 %copy-start.11 = (bf16[2,2,1,1,2,64,512]{6,5,4,3,2,1,0:T(8,128)(2,1)S(1)}, bf16[2,2,1,1,2,64,512]{6,5,4,3,2,1,0:T(8,128)(2,1)}, u32[]{:S(2)}) copy-start(bf16[2,2,1,1,2,64,512]{6,5,4,3,2,1,0:T(8,128)(2,1)} %copy-done.10) | copy-start | bytes 1572868
  122.5 16.4 %collective-permute-start.6 = (f32[512,640]{1,0:T(8,128)}, f32[512,640]{1,0:T(8,128)S(1)}, u32[]{:S(2)}, u32[]{:S(2)}) collective-permute-start(f32[512,640]{1,0:T(8,128)} %shard_map.56), channel_id=1, source_target_pairs={{0,16},{16,0},{32,48},{48,32},{64,80},{80,64},{96,112},{112,96},{1... | collective-permute-start | bytes 3932168 | tf_op jit(solution)/shard_map/ppermute | solution.py:178
  138.9 57.8 %copy-start.12 = (bf16[512,512]{1,0:T(8,128)(2,1)S(1)}, bf16[512,512]{1,0:T(8,128)(2,1)}, u32[]{:S(2)}) copy-start(bf16[512,512]{1,0:T(8,128)(2,1)} %param.9) | copy-start | bytes 1572868
  138.9 1.1 copy-start.5
  144.0 12.7 %collective-permute-start.7 = (f32[256,640]{1,0:T(8,128)}, f32[256,640]{1,0:T(8,128)S(1)}, u32[]{:S(2)}, u32[]{:S(2)}) collective-permute-start(f32[256,640]{1,0:T(8,128)} %get-tuple-element.22), channel_id=1, source_target_pairs={{0,32},{16,144},{32,0},{48,176},{64,96},{80,208},{96,64},{112,240}... | collective-permute-start | bytes 1966088 | tf_op jit(solution)/shard_map/ppermute | solution.py:178
  156.7 0.9 copy-start.6
  160.3 9.2 %collective-permute-start.8 = (f32[128,640]{1,0:T(8,128)}, f32[128,640]{1,0:T(8,128)S(1)}, u32[]{:S(2)}, u32[]{:S(2)}) collective-permute-start(f32[128,640]{1,0:T(8,128)} %get-tuple-element.24), channel_id=1, source_target_pairs={{0,128},{16,48},{32,160},{48,16},{64,192},{80,112},{96,224},{112,8... | collective-permute-start | bytes 983048 | tf_op jit(solution)/shard_map/ppermute | solution.py:178
  169.5 0.7 copy-start.13
  172.4 9.5 %collective-permute-start.9 = (f32[64,640]{1,0:T(8,128)}, f32[64,640]{1,0:T(8,128)S(1)}, u32[]{:S(2)}, u32[]{:S(2)}) collective-permute-start(f32[64,640]{1,0:T(8,128)} %get-tuple-element.26), channel_id=1, source_target_pairs={{0,64},{16,272},{32,96},{48,304},{64,0},{80,336},{96,32},{112,368}... | collective-permute-start | bytes 491528 | tf_op jit(solution)/shard_map/ppermute | solution.py:178
  181.9 0.7 copy-start.14
  184.4 8.0 %collective-permute-start.10 = (f32[32,640]{1,0:T(8,128)}, f32[32,640]{1,0:T(8,128)S(1)}, u32[]{:S(2)}, u32[]{:S(2)}) collective-permute-start(f32[32,640]{1,0:T(8,128)} %get-tuple-element.28), channel_id=1, source_target_pairs={{0,256},{16,80},{32,288},{48,112},{64,320},{80,16},{96,352},{112,4... | collective-permute-start | bytes 245768 | tf_op jit(solution)/shard_map/ppermute | solution.py:178
  192.5 0.6 copy-start.15

commit v9 on v7

--- a/solution.py
+++ b/solution.py
@@ -37,8 +37,12 @@
 PACK = 128
 
 
-def attention_kernel(q_ref, k_ref, v_ref, keep_ref, out_ref):
+def attention_kernel(listed_ref, q_ref, *refs):
+    nlist = (len(refs) - 2) // 2
+    key_refs, value_refs = refs[:nlist], refs[nlist : 2 * nlist]
+    keep_ref, out_ref = refs[2 * nlist], refs[2 * nlist + 1]
     rows = q_ref.shape[0]
+    frames = key_refs[0].shape[1]
     keep = keep_ref[...] > 0
     lane = lax.broadcasted_iota(jnp.int32, (1, 2 * HD), 1)
     low = lane < HD
@@ -49,8 +53,12 @@
     for pair in range(HEADS // 2):
         cols = pl.ds(pair * 2 * HD, 2 * HD)
         q2 = q_ref[:, cols] * scale
-        k2 = k_ref[:, cols]
-        v2 = v_ref[:, cols]
+        k2 = jnp.concatenate(
+            [r[0, f, 0, :, cols] for r in key_refs for f in range(frames)], axis=0
+        )
+        v2 = jnp.concatenate(
+            [r[0, f, 0, :, cols] for r in value_refs for f in range(frames)], axis=0
+        )
         outs = []
         for part in range(2):
             mine = low if part == 0 else jnp.logical_not(low)
@@ -72,28 +80,37 @@
     out_ref[...] = jnp.concatenate(blocks + [stats], axis=1)
 
 
-def attention(query_rows, keys, values, keep):
+def attention(query_rows, hood, listed, keep):
     qtok, width = query_rows.shape
-    count = keys.shape[0]
+    _, frames, _, blk, _ = hood.shape
+    nlist = listed.shape[0]
+    count = nlist * frames * blk
     tiles = qtok // TQ
     flops = 2 * 2 * qtok * count * 2 * width
+    block = (1, frames, 1, blk, width)
+
+    def entry_spec(kind, e):
+        return pl.BlockSpec(block, lambda i, lst: (kind, 0, lst[e], 0, 0))
+
+    grid_spec = pltpu.PrefetchScalarGridSpec(
+        num_scalar_prefetch=1,
+        grid=(tiles,),
+        in_specs=[pl.BlockSpec((TQ, width), lambda i, lst: (i, 0))]
+        + [entry_spec(0, e) for e in range(nlist)]
+        + [entry_spec(1, e) for e in range(nlist)]
+        + [pl.BlockSpec((1, count), lambda i, lst: (0, 0))],
+        out_specs=pl.BlockSpec((TQ, width + PACK), lambda i, lst: (i, 0)),
+    )
     return pl.pallas_call(
         attention_kernel,
-        grid=(tiles,),
-        in_specs=[
-            pl.BlockSpec((TQ, width), lambda i: (i, 0)),
-            pl.BlockSpec((count, width), lambda i: (0, 0)),
-            pl.BlockSpec((count, width), lambda i: (0, 0)),
-            pl.BlockSpec((1, count), lambda i: (0, 0)),
-        ],
-        out_specs=pl.BlockSpec((TQ, width + PACK), lambda i: (i, 0)),
+        grid_spec=grid_spec,
         out_shape=jax.ShapeDtypeStruct((qtok, width + PACK), jnp.float32),
         cost_estimate=pl.CostEstimate(
             flops=flops,
             transcendentals=qtok * count * HEADS,
             bytes_accessed=qtok * width * 6 + count * width * 4,
         ),
-    )(query_rows, keys, values, keep)
+    )(listed, query_rows, *([hood] * (2 * nlist)), keep)
 
 
 def merge_kernel(a_ref, b_ref, *out_refs):
@@ -193,11 +210,8 @@
     hood = hood.reshape(2, frames, 9 * nblk, blk, width)
     listed = block_list[0, 0]
     nlist = listed.shape[0]
-    chosen = jnp.take(hood, listed, axis=2)
-    keep = jnp.broadcast_to((block_valid[0, 0] > 0)[None, :, None], (frames, nlist, blk))
+    keep = jnp.broadcast_to((block_valid[0, 0] > 0)[:, None, None], (nlist, frames, blk))
     keep = keep.reshape(1, -1).astype(jnp.int32)
-    keys = chosen[0].reshape(-1, width)
-    values = chosen[1].reshape(-1, width)
     query_rows = queries[0, 0]
     qtok = query_rows.shape[0]
     groups = lax.axis_size("tm")
@@ -207,8 +221,8 @@
     )
     query_rows = jnp.take(query_rows.reshape(groups, qtok // groups, width), order, axis=0)
     query_rows = query_rows.reshape(qtok, width)
-    second = attention(query_rows[qtok // 2 :], keys, values, keep)
-    first = attention(query_rows[: qtok // 2], keys, values, keep)
+    second = attention(query_rows[qtok // 2 :], hood, listed, keep)
+    first = attention(query_rows[: qtok // 2], hood, listed, keep)
     final = tree_reduce(first, second)
     summed = final[:, :width]
     total = final[:, width + HEADS : width + 2 * HEADS]

time: 191 us -> 187 us (0.979)
  local copies, waits for them, and re-layouts: 17 us -> 11.6 us
    gather x1 -> x0, local copies, waits for them, and re-layouts: 3.02 us -> none  [local(): chosen = jnp.take(hood, listed, axis=2)]
    slice x4 -> x1, local copies, waits for them, and re-layouts: 3.39 us -> 1.04 us  [local(): second = attention(query_rows[qtok // 2:], hood, listed, keep)]
    pallas_call x2, Pallas kernels: 21.3 us -> 23.2 us  [attention(): pl.pallas_call(attention_kernel, grid_spec=grid_spec, out_shape=jax.Shape...]
    unnamed x25 -> x23, local copies, waits for them, and re-layouts: 4.91 us -> 4.83 us
where the time goes in v9:
time: 187 us; the launch traced here: 186 us
  waiting for transfers between devices  99.1 us (53%)
  Pallas kernels  35.7 us (19%)
  starting transfers between devices  32.8 us (18%)
  local copies, waits for them, and re-layouts  11.6 us (6%)
  other arithmetic  4.78 us (3%)
  matrix products  1.96 us (1%)
    ppermute x6, waiting for transfers between devices, shifted(): return lax.ppermute(array, axis, pairs)  69.6 us
    ppermute x5, waiting for transfers between devices, tree_reduce(): got = lax.ppermute(second, 'tm', step_pairs(nbits, i))  29.5 us
    pallas_call x2, Pallas kernels, attention(): pl.pallas_call(attention_kernel, grid_spec=grid_spec, out_shape=jax.Shape...  23.2 us
    ppermute x6, starting transfers between devices, shifted(): return lax.ppermute(array, axis, pairs)  21.1 us
    pallas_call x5, Pallas kernels, merge(): pl.pallas_call(merge_kernel, out_shape=[shape] * count, cost_estimate=pl....  12.5 us
    ppermute x5, starting transfers between devices, tree_reduce(): got = lax.ppermute(second, 'tm', step_pairs(nbits, i))  11.8 us
    unnamed x23, local copies, waits for them, and re-layouts  4.83 us
  transfers between devices with their start and end apart: 11, of which 8 were waited for; matrix products, arithmetic and copies ran while one was open for 3% of the time, Pallas kernels for 6%

profile of v9, /device:TPU:6, one launch (start us, length us, event | category | flops | bytes accessed | tf_op | source)
XLA Modules:
  0.0 186.2 jit_solution(13330075156733274611)
XLA Ops:
  0.0 9.2 %collective-permute-start = (bf16[2,2,1,1,2,64,512]{6,5,4,3,2,1,0:T(8,128)(2,1)}, bf16[2,2,1,1,2,64,512]{6,5,4,3,2,1,0:T(8,128)(2,1)S(1)}, u32[]{:S(2)}, u32[]{:S(2)}) collective-permute-start(bf16[2,2,1,1,2,64,512]{6,5,4,3,2,1,0:T(8,128)(2,1)} %param.6), channel_id=1, source_target_pairs={{0,1},{1,2},{2,3},{4,5},{5,6},{6,7},{8,9},{9,10},{10,11},{12,13},{... | collective-permute-start | bytes 1572872 | tf_op jit(solution)/shard_map/ppermute | solution.py:19
  9.3 1.3 collective-permute-start.1
  10.6 3.5 %collective-permute-start.2 = (bf16[2,2,1,1,2,64,512]{6,5,4,3,2,1,0:T(8,128)(2,1)}, bf16[2,2,1,1,2,64,512]{6,5,4,3,2,1,0:T(8,128)(2,1)S(1)}, u32[]{:S(2)}, u32[]{:S(2)}) collective-permute-start(bf16[2,2,1,1,2,64,512]{6,5,4,3,2,1,0:T(8,128)(2,1)} %param.6), channel_id=1, source_target_pairs={{0,4},{4,8},{8,12},{1,5},{5,9},{9,13},{2,6},{6,10},{10,14},{3,7},{... | collective-permute-start | bytes 1572872 | tf_op jit(solution)/shard_map/ppermute | solution.py:19
  14.1 1.3 collective-permute-start.3
  15.5 5.4 %collective-permute-done = bf16[2,2,1,1,2,64,512]{6,5,4,3,2,1,0:T(8,128)(2,1)S(1)} collective-permute-done((bf16[2,2,1,1,2,64,512]{6,5,4,3,2,1,0:T(8,128)(2,1)}, bf16[2,2,1,1,2,64,512]{6,5,4,3,2,1,0:T(8,128)(2,1)S(1)}, u32[]{:S(2)}, u32[]{:S(2)}) %collective-permute-start) | collective-permute-done | bytes 524320 | tf_op jit(solution)/shard_map/ppermute | solution.py:19
  20.8 43.0 %collective-permute-done.1 = bf16[2,2,1,1,2,64,512]{6,5,4,3,2,1,0:T(8,128)(2,1)S(1)} collective-permute-done((bf16[2,2,1,1,2,64,512]{6,5,4,3,2,1,0:T(8,128)(2,1)}, bf16[2,2,1,1,2,64,512]{6,5,4,3,2,1,0:T(8,128)(2,1)S(1)}, u32[]{:S(2)}, u32[]{:S(2)}) %collective-permute-start.1) | collective-permute-done | bytes 524320 | tf_op jit(solution)/shard_map/ppermute | solution.py:19
  63.9 0.9 constant_dynamic-update-slice_fusion.1
  64.8 0.8 constant_dynamic-update-slice_fusion
  65.6 4.4 %collective-permute-start.4 = (bf16[2,2,1,2,2,64,512]{6,5,4,3,2,1,0:T(8,128)(2,1)}, bf16[2,2,1,2,2,64,512]{6,5,4,3,2,1,0:T(8,128)(2,1)}, u32[]{:S(2)}, u32[]{:S(2)}) collective-permute-start(bf16[2,2,1,2,2,64,512]{6,5,4,3,2,1,0:T(8,128)(2,1)} %constant_dynamic-update-slice_fusion), channel_id=1, source_target_pairs={{0,4},{4,8},{8,12},{1,5},{5,9},{9,13},{2,6},{6,10},{10,14},{3,7},{... | collective-permute-start | bytes 3145736 | tf_op jit(solution)/shard_map/ppermute | solution.py:19
  70.0 0.7 fusion.1
  70.7 1.3 collective-permute-start.5
  72.0 0.1 fusion.2
  72.1 0.7 convert_element_type.12.refs_16_
  72.9 0.6 gather_fusion
  73.5 0.1 compare_and_fusion
  73.6 0.2 broadcast_select_fusion
  73.8 1.0 fusion.3
  74.8 16.7 %collective-permute-done.4 = bf16[2,2,1,2,2,64,512]{6,5,4,3,2,1,0:T(8,128)(2,1)} collective-permute-done((bf16[2,2,1,2,2,64,512]{6,5,4,3,2,1,0:T(8,128)(2,1)}, bf16[2,2,1,2,2,64,512]{6,5,4,3,2,1,0:T(8,128)(2,1)}, u32[]{:S(2)}, u32[]{:S(2)}) %collective-permute-start.4) | collective-permute-done | bytes 1048608 | tf_op jit(solution)/shard_map/ppermute | solution.py:19
  91.5 1.3 fusion.4
  92.8 4.4 %collective-permute-done.5 = bf16[2,2,1,2,2,64,512]{6,5,4,3,2,1,0:T(8,128)(2,1)} collective-permute-done((bf16[2,2,1,2,2,64,512]{6,5,4,3,2,1,0:T(8,128)(2,1)}, bf16[2,2,1,2,2,64,512]{6,5,4,3,2,1,0:T(8,128)(2,1)}, u32[]{:S(2)}, u32[]{:S(2)}) %collective-permute-start.5) | collective-permute-done | bytes 1048608 | tf_op jit(solution)/shard_map/ppermute | solution.py:19
  97.2 1.3 fusion.5
  98.5 2.8 %maximum_maximum_fusion = bf16[2,2,3,3,2,64,512]{6,5,4,3,2,1,0:T(8,128)(2,1)} fusion(bf16[2,2,1,1,2,64,512]{6,5,4,3,2,1,0:T(8,128)(2,1)S(1)} %get-tuple-element.34, bf16[2,2,1,1,2,64,512]{6,5,4,3,2,1,0:T(8,128)(2,1)S(1)} %copy-done.7, bf16[2,2,1,1,2,64,512]{6,5,4,3,2,1,0:T(8,128)(2,1)S(1)} %get-tuple-element.33, ...), kind=kLoop, calls=%fused_computation.1 | loop fusion | flops 18874368 | bytes 9437184 | tf_op jit(solution)/shard_map/concatenate | solution.py:34
  101.3 11.6 %shard_map.56 = f32[512,640]{1,0:T(8,128)} custom-call(s32[8]{0:T(128)} %bitcast.51, bf16[512,512]{1,0:T(8,128)(2,1)} %bitcast.50, bf16[2,2,18,64,512]{4,3,2,1,0:T(8,128)(2,1)} %bitcast.32, bf16[2,2,18,64,512]{4,3,2,1,0:T(8,128)(2,1)} %bitcast.18, bf16[2,2,18,64,512]{4,3,2,1,0:T(8,128)(2,1)} %bitcast.19, bf16[2,2,18,64,512]{4,3,2,1,0:T(8,128)(2,1)} %bitcast.20, ...), custom_call_target="tpu_custom_call" | custom-call | flops 2147483648 | bytes 3670016 | tf_op jit(solution)/shard_map/pallas_call | solution.py:104
  112.9 1.9 %collective-permute-start.6 = (f32[512,640]{1,0:T(8,128)}, f32[512,640]{1,0:T(8,128)S(1)}, u32[]{:S(2)}, u32[]{:S(2)}) collective-permute-start(f32[512,640]{1,0:T(8,128)} %shard_map.56), channel_id=1, source_target_pairs={{0,16},{16,0},{32,48},{48,32},{64,80},{80,64},{96,112},{112,96},{1... | collective-permute-start | bytes 3932168 | tf_op jit(solution)/shard_map/ppermute | solution.py:196
  114.8 11.6 %shard_map.55.a_ref = f32[512,640]{1,0:T(8,128)} custom-call(s32[8]{0:T(128)} %bitcast.52, bf16[512,512]{1,0:T(8,128)(2,1)} %bitcast.49, bf16[2,2,18,64,512]{4,3,2,1,0:T(8,128)(2,1)} %bitcast.33, bf16[2,2,18,64,512]{4,3,2,1,0:T(8,128)(2,1)} %bitcast.34, bf16[2,2,18,64,512]{4,3,2,1,0:T(8,128)(2,1)} %bitcast.35, bf16[2,2,18,64,512]{4,3,2,1,0:T(8,128)(2,1)} %bitcast.36, ...), custom_call_target="tpu_custom_call" | custom-call | flops 2147483648 | bytes 3670016 | tf_op jit(solution)/shard_map/pallas_call | solution.py:104
  126.4 1.1 copy-done.1
  127.5 4.0 %shard_map.57 = (f32[256,640]{1,0:T(8,128)}, f32[256,640]{1,0:T(8,128)}) custom-call(f32[512,640]{1,0:T(8,128)} %shard_map.55.a_ref, f32[512,640]{1,0:T(8,128)} %copy-done.1), custom_call_target="tpu_custom_call" | custom-call | flops 1310720 | bytes 3932160 | tf_op jit(solution)/shard_map/pallas_call | solution.py:156
  131.5 1.9 %collective-permute-start.7 = (f32[256,640]{1,0:T(8,128)}, f32[256,640]{1,0:T(8,128)S(1)}, u32[]{:S(2)}, u32[]{:S(2)}) collective-permute-start(f32[256,640]{1,0:T(8,128)} %get-tuple-element.22), channel_id=1, source_target_pairs={{0,32},{16,144},{32,0},{48,176},{64,96},{80,208},{96,64},{112,240}... | collective-permute-start | bytes 1966088 | tf_op jit(solution)/shard_map/ppermute | solution.py:196
  133.4 10.8 %collective-permute-done.7.b_ref = f32[256,640]{1,0:T(8,128)S(1)} collective-permute-done((f32[256,640]{1,0:T(8,128)}, f32[256,640]{1,0:T(8,128)S(1)}, u32[]{:S(2)}, u32[]{:S(2)}) %collective-permute-start.7) | collective-permute-done | bytes 655392 | tf_op jit(solution)/shard_map/ppermute | solution.py:196
  144.2 0.8 copy-done.2
  145.0 2.8 %shard_map.58 = (f32[128,640]{1,0:T(8,128)}, f32[128,640]{1,0:T(8,128)}) custom-call(f32[256,640]{1,0:T(8,128)} %get-tuple-element.21.a_ref, f32[256,640]{1,0:T(8,128)} %copy-done.2), custom_call_target="tpu_custom_call" | custom-call | flops 655360 | bytes 1966080 | tf_op jit(solution)/shard_map/pallas_call | solution.py:156
  147.8 2.7 %collective-permute-start.8 = (f32[128,640]{1,0:T(8,128)}, f32[128,640]{1,0:T(8,128)S(1)}, u32[]{:S(2)}, u32[]{:S(2)}) collective-permute-start(f32[128,640]{1,0:T(8,128)} %get-tuple-element.24), channel_id=1, source_target_pairs={{0,128},{16,48},{32,160},{48,16},{64,192},{80,112},{96,224},{112,8... | collective-permute-start | bytes 983048 | tf_op jit(solution)/shard_map/ppermute | solution.py:196
  150.5 6.4 %collective-permute-done.8.b_ref = f32[128,640]{1,0:T(8,128)S(1)} collective-permute-done((f32[128,640]{1,0:T(8,128)}, f32[128,640]{1,0:T(8,128)S(1)}, u32[]{:S(2)}, u32[]{:S(2)}) %collective-permute-start.8) | collective-permute-done | bytes 327712 | tf_op jit(solution)/shard_map/ppermute | solution.py:196
  157.0 0.7 copy-done.8
  157.7 2.1 %shard_map.59 = (f32[64,640]{1,0:T(8,128)}, f32[64,640]{1,0:T(8,128)}) custom-call(f32[128,640]{1,0:T(8,128)} %get-tuple-element.23.a_ref, f32[128,640]{1,0:T(8,128)} %copy-done.8), custom_call_target="tpu_custom_call" | custom-call | flops 327680 | bytes 983040 | tf_op jit(solution)/shard_map/pallas_call | solution.py:156
  159.8 1.9 %collective-permute-start.9 = (f32[64,640]{1,0:T(8,128)}, f32[64,640]{1,0:T(8,128)S(1)}, u32[]{:S(2)}, u32[]{:S(2)}) collective-permute-start(f32[64,640]{1,0:T(8,128)} %get-tuple-element.26), channel_id=1, source_target_pairs={{0,64},{16,272},{32,96},{48,304},{64,0},{80,336},{96,32},{112,368}... | collective-permute-start | bytes 491528 | tf_op jit(solution)/shard_map/ppermute | solution.py:196
  161.7 7.6 %collective-permute-done.9.b_ref = f32[64,640]{1,0:T(8,128)S(1)} collective-permute-done((f32[64,640]{1,0:T(8,128)}, f32[64,640]{1,0:T(8,128)S(1)}, u32[]{:S(2)}, u32[]{:S(2)}) %collective-permute-start.9) | collective-permute-done | bytes 163872 | tf_op jit(solution)/shard_map/ppermute | solution.py:196
  169.3 0.7 copy-done.9
  170.0 1.9 %shard_map.60 = (f32[32,640]{1,0:T(8,128)}, f32[32,640]{1,0:T(8,128)}) custom-call(f32[64,640]{1,0:T(8,128)} %get-tuple-element.25.a_ref, f32[64,640]{1,0:T(8,128)} %copy-done.9), custom_call_target="tpu_custom_call" | custom-call | flops 163840 | bytes 491520 | tf_op jit(solution)/shard_map/pallas_call | solution.py:156
  171.9 3.3 %collective-permute-start.10 = (f32[32,640]{1,0:T(8,128)}, f32[32,640]{1,0:T(8,128)S(1)}, u32[]{:S(2)}, u32[]{:S(2)}) collective-permute-start(f32[32,640]{1,0:T(8,128)} %get-tuple-element.28), channel_id=1, source_target_pairs={{0,256},{16,80},{32,288},{48,112},{64,320},{80,16},{96,352},{112,4... | collective-permute-start | bytes 245768 | tf_op jit(solution)/shard_map/ppermute | solution.py:196
  175.2 4.7 %collective-permute-done.10.b_ref = f32[32,640]{1,0:T(8,128)S(1)} collective-permute-done((f32[32,640]{1,0:T(8,128)}, f32[32,640]{1,0:T(8,128)S(1)}, u32[]{:S(2)}, u32[]{:S(2)}) %collective-permute-start.10) | collective-permute-done | bytes 81952 | tf_op jit(solution)/shard_map/ppermute | solution.py:196
  179.9 0.6 copy-done.10
  180.5 1.7 shard_map.61
  182.2 0.8 slice.57
  183.0 0.1 broadcast_in_dim.23
  183.1 0.1 reshape.137
  183.2 1.0 multiply_reduce_fusion
  184.2 2.0 %convolution_bitcast_fusion = f32[1,1,32,512]{3,2,1,0:T(8,128)} fusion(bf16[512,512]{1,0:T(8,128)(2,1)} %param.9, f32[32]{0:T(128)S(1)} %add_rsqrt_fusion, f32[32,512]{1,0:T(8,128)S(1)} %reshape.137, f32[32,640]{1,0:T(8,128)} %shard_map.61), kind=kOutput, calls=%fused_computation.2 | convolution fusion | flops 16826368 | bytes 721024 | tf_op jit(solution)/shard_map/dot_general | solution.py:233
  (26 shorter events, 0.2 us)
Async XLA Ops:
  0.0 72.8 %copy-start = (bf16[1,1,1024,512]{3,2,1,0:T(8,128)(2,1)S(1)}, bf16[1,1,1024,512]{3,2,1,0:T(8,128)(2,1)}, u32[]{:S(2)}) copy-start(bf16[1,1,1024,512]{3,2,1,0:T(8,128)(2,1)} %param.5) | copy-start | bytes 3145732
  0.0 20.8 %collective-permute-start = (bf16[2,2,1,1,2,64,512]{6,5,4,3,2,1,0:T(8,128)(2,1)}, bf16[2,2,1,1,2,64,512]{6,5,4,3,2,1,0:T(8,128)(2,1)S(1)}, u32[]{:S(2)}, u32[]{:S(2)}) collective-permute-start(bf16[2,2,1,1,2,64,512]{6,5,4,3,2,1,0:T(8,128)(2,1)} %param.6), channel_id=1, source_target_pairs={{0,1},{1,2},{2,3},{4,5},{5,6},{6,7},{8,9},{9,10},{10,11},{12,13},{... | collective-permute-start | bytes 1572872 | tf_op jit(solution)/shard_map/ppermute | solution.py:19
  9.3 54.6 %collective-permute-start.1 = (bf16[2,2,1,1,2,64,512]{6,5,4,3,2,1,0:T(8,128)(2,1)}, bf16[2,2,1,1,2,64,512]{6,5,4,3,2,1,0:T(8,128)(2,1)S(1)}, u32[]{:S(2)}, u32[]{:S(2)}) collective-permute-start(bf16[2,2,1,1,2,64,512]{6,5,4,3,2,1,0:T(8,128)(2,1)} %param.6), channel_id=1, source_target_pairs={{1,0},{2,1},{3,2},{5,4},{6,5},{7,6},{9,8},{10,9},{11,10},{13,12},{... | collective-permute-start | bytes 1572872 | tf_op jit(solution)/shard_map/ppermute | solution.py:19
  10.6 53.3 %collective-permute-start.2 = (bf16[2,2,1,1,2,64,512]{6,5,4,3,2,1,0:T(8,128)(2,1)}, bf16[2,2,1,1,2,64,512]{6,5,4,3,2,1,0:T(8,128)(2,1)S(1)}, u32[]{:S(2)}, u32[]{:S(2)}) collective-permute-start(bf16[2,2,1,1,2,64,512]{6,5,4,3,2,1,0:T(8,128)(2,1)} %param.6), channel_id=1, source_target_pairs={{0,4},{4,8},{8,12},{1,5},{5,9},{9,13},{2,6},{6,10},{10,14},{3,7},{... | collective-permute-start | bytes 1572872 | tf_op jit(solution)/shard_map/ppermute | solution.py:19
  14.1 49.8 %collective-permute-start.3 = (bf16[2,2,1,1,2,64,512]{6,5,4,3,2,1,0:T(8,128)(2,1)}, bf16[2,2,1,1,2,64,512]{6,5,4,3,2,1,0:T(8,128)(2,1)S(1)}, u32[]{:S(2)}, u32[]{:S(2)}) collective-permute-start(bf16[2,2,1,1,2,64,512]{6,5,4,3,2,1,0:T(8,128)(2,1)} %param.6), channel_id=1, source_target_pairs={{4,0},{8,4},{12,8},{5,1},{9,5},{13,9},{6,2},{10,6},{14,10},{7,3},{... | collective-permute-start | bytes 1572872 | tf_op jit(solution)/shard_map/ppermute | solution.py:19
  63.9 8.9 %copy-start.4 = (bf16[2,2,1,1,2,64,512]{6,5,4,3,2,1,0:T(8,128)(2,1)}, bf16[2,2,1,1,2,64,512]{6,5,4,3,2,1,0:T(8,128)(2,1)S(1)}, u32[]{:S(2)}) copy-start(bf16[2,2,1,1,2,64,512]{6,5,4,3,2,1,0:T(8,128)(2,1)S(1)} %collective-permute-done.2) | copy-start | bytes 1572868
  63.9 8.9 %copy-start.6 = (bf16[2,2,1,1,2,64,512]{6,5,4,3,2,1,0:T(8,128)(2,1)}, bf16[2,2,1,1,2,64,512]{6,5,4,3,2,1,0:T(8,128)(2,1)S(1)}, u32[]{:S(2)}) copy-start(bf16[2,2,1,1,2,64,512]{6,5,4,3,2,1,0:T(8,128)(2,1)S(1)} %collective-permute-done.3) | copy-start | bytes 1572868
  65.6 25.9 %collective-permute-start.4 = (bf16[2,2,1,2,2,64,512]{6,5,4,3,2,1,0:T(8,128)(2,1)}, bf16[2,2,1,2,2,64,512]{6,5,4,3,2,1,0:T(8,128)(2,1)}, u32[]{:S(2)}, u32[]{:S(2)}) collective-permute-start(bf16[2,2,1,2,2,64,512]{6,5,4,3,2,1,0:T(8,128)(2,1)} %constant_dynamic-update-slice_fusion), channel_id=1, source_target_pairs={{0,4},{4,8},{8,12},{1,5},{5,9},{9,13},{2,6},{6,10},{10,14},{3,7},{... | collective-permute-start | bytes 3145736 | tf_op jit(solution)/shard_map/ppermute | solution.py:19
  70.7 26.5 %collective-permute-start.5 = (bf16[2,2,1,2,2,64,512]{6,5,4,3,2,1,0:T(8,128)(2,1)}, bf16[2,2,1,2,2,64,512]{6,5,4,3,2,1,0:T(8,128)(2,1)}, u32[]{:S(2)}, u32[]{:S(2)}) collective-permute-start(bf16[2,2,1,2,2,64,512]{6,5,4,3,2,1,0:T(8,128)(2,1)} %constant_dynamic-update-slice_fusion), channel_id=1, source_target_pairs={{4,0},{8,4},{12,8},{5,1},{9,5},{13,9},{6,2},{10,6},{14,10},{7,3},{... | collective-permute-start | bytes 3145736 | tf_op jit(solution)/shard_map/ppermute | solution.py:19
  73.5 25.0 %copy-start.3 = (bf16[2,2,1,1,2,64,512]{6,5,4,3,2,1,0:T(8,128)(2,1)S(1)}, bf16[2,2,1,1,2,64,512]{6,5,4,3,2,1,0:T(8,128)(2,1)}, u32[]{:S(2)}) copy-start(bf16[2,2,1,1,2,64,512]{6,5,4,3,2,1,0:T(8,128)(2,1)} %param.6) | copy-start | bytes 1572868
  73.5 25.0 %copy-start.5 = (bf16[2,2,1,1,2,64,512]{6,5,4,3,2,1,0:T(8,128)(2,1)S(1)}, bf16[2,2,1,1,2,64,512]{6,5,4,3,2,1,0:T(8,128)(2,1)}, u32[]{:S(2)}) copy-start(bf16[2,2,1,1,2,64,512]{6,5,4,3,2,1,0:T(8,128)(2,1)} %copy-done.4) | copy-start | bytes 1572868
  73.5 25.0 %copy-start.7 = (bf16[2,2,1,1,2,64,512]{6,5,4,3,2,1,0:T(8,128)(2,1)S(1)}, bf16[2,2,1,1,2,64,512]{6,5,4,3,2,1,0:T(8,128)(2,1)}, u32[]{:S(2)}) copy-start(bf16[2,2,1,1,2,64,512]{6,5,4,3,2,1,0:T(8,128)(2,1)} %copy-done.6) | copy-start | bytes 1572868
  112.9 13.5 %collective-permute-start.6 = (f32[512,640]{1,0:T(8,128)}, f32[512,640]{1,0:T(8,128)S(1)}, u32[]{:S(2)}, u32[]{:S(2)}) collective-permute-start(f32[512,640]{1,0:T(8,128)} %shard_map.56), channel_id=1, source_target_pairs={{0,16},{16,0},{32,48},{48,32},{64,80},{80,64},{96,112},{112,96},{1... | collective-permute-start | bytes 3932168 | tf_op jit(solution)/shard_map/ppermute | solution.py:196
  126.4 1.1 copy-start.1
  131.5 12.7 %collective-permute-start.7 = (f32[256,640]{1,0:T(8,128)}, f32[256,640]{1,0:T(8,128)S(1)}, u32[]{:S(2)}, u32[]{:S(2)}) collective-permute-start(f32[256,640]{1,0:T(8,128)} %get-tuple-element.22), channel_id=1, source_target_pairs={{0,32},{16,144},{32,0},{48,176},{64,96},{80,208},{96,64},{112,240}... | collective-permute-start | bytes 1966088 | tf_op jit(solution)/shard_map/ppermute | solution.py:196
  144.2 0.8 copy-start.2
  147.8 9.2 %collective-permute-start.8 = (f32[128,640]{1,0:T(8,128)}, f32[128,640]{1,0:T(8,128)S(1)}, u32[]{:S(2)}, u32[]{:S(2)}) collective-permute-start(f32[128,640]{1,0:T(8,128)} %get-tuple-element.24), channel_id=1, source_target_pairs={{0,128},{16,48},{32,160},{48,16},{64,192},{80,112},{96,224},{112,8... | collective-permute-start | bytes 983048 | tf_op jit(solution)/shard_map/ppermute | solution.py:196
  157.0 0.7 copy-start.8
  159.8 9.5 %collective-permute-start.9 = (f32[64,640]{1,0:T(8,128)}, f32[64,640]{1,0:T(8,128)S(1)}, u32[]{:S(2)}, u32[]{:S(2)}) collective-permute-start(f32[64,640]{1,0:T(8,128)} %get-tuple-element.26), channel_id=1, source_target_pairs={{0,64},{16,272},{32,96},{48,304},{64,0},{80,336},{96,32},{112,368}... | collective-permute-start | bytes 491528 | tf_op jit(solution)/shard_map/ppermute | solution.py:196
  169.3 0.7 copy-start.9
  171.9 8.0 %collective-permute-start.10 = (f32[32,640]{1,0:T(8,128)}, f32[32,640]{1,0:T(8,128)S(1)}, u32[]{:S(2)}, u32[]{:S(2)}) collective-permute-start(f32[32,640]{1,0:T(8,128)} %get-tuple-element.28), channel_id=1, source_target_pairs={{0,256},{16,80},{32,288},{48,112},{64,320},{80,16},{96,352},{112,4... | collective-permute-start | bytes 245768 | tf_op jit(solution)/shard_map/ppermute | solution.py:196
  179.9 0.6 copy-start.10

commit v10 on v9

--- a/solution.py
+++ b/solution.py
@@ -7,7 +7,7 @@
 
 HEADS = 8
 HD = 64
-TQ = 256
+TQ = 512
 
 
 def shifted(array, axis, forward):

time: 187 us -> 184 us (0.984)
  Pallas kernels: 35.7 us -> 32.3 us
    pallas_call x2, Pallas kernels: 23.2 us -> 19.8 us  [attention(): pl.pallas_call(attention_kernel, grid_spec=grid_spec, out_shape=jax.Shape...]
  transfers between devices with their start and end apart: 11 -> 11, of which waited for: 8 -> 8; matrix products, arithmetic and copies ran while one was open for 3% -> 3% of each run, Pallas kernels for 6% -> 5%
where the time goes in v10:
time: 184 us; the launch traced here: 183 us
  waiting for transfers between devices  99.1 us (54%)
  starting transfers between devices  33 us (18%)
  Pallas kernels  32.3 us (18%)
  local copies, waits for them, and re-layouts  11.6 us (6%)
  other arithmetic  4.78 us (3%)
  matrix products  1.96 us (1%)
    ppermute x6, waiting for transfers between devices, shifted(): return lax.ppermute(array, axis, pairs)  69.6 us
    ppermute x5, waiting for transfers between devices, tree_reduce(): got = lax.ppermute(second, 'tm', step_pairs(nbits, i))  29.5 us
    ppermute x6, starting transfers between devices, shifted(): return lax.ppermute(array, axis, pairs)  21.1 us
    pallas_call x2, Pallas kernels, attention(): pl.pallas_call(attention_kernel, grid_spec=grid_spec, out_shape=jax.Shape...  19.8 us
    pallas_call x5, Pallas kernels, merge(): pl.pallas_call(merge_kernel, out_shape=[shape] * count, cost_estimate=pl....  12.5 us
    ppermute x5, starting transfers between devices, tree_reduce(): got = lax.ppermute(second, 'tm', step_pairs(nbits, i))  11.9 us
    unnamed x23, local copies, waits for them, and re-layouts  4.83 us
  transfers between devices with their start and end apart: 11, of which 8 were waited for; matrix products, arithmetic and copies ran while one was open for 3% of the time, Pallas kernels for 5%

profile of v10, /device:TPU:6, one launch (start us, length us, event | category | flops | bytes accessed | tf_op | source)
XLA Modules:
  0.0 183.0 jit_solution(8239175608247833732)
XLA Ops:
  0.0 9.2 %collective-permute-start = (bf16[2,2,1,1,2,64,512]{6,5,4,3,2,1,0:T(8,128)(2,1)}, bf16[2,2,1,1,2,64,512]{6,5,4,3,2,1,0:T(8,128)(2,1)S(1)}, u32[]{:S(2)}, u32[]{:S(2)}) collective-permute-start(bf16[2,2,1,1,2,64,512]{6,5,4,3,2,1,0:T(8,128)(2,1)} %param.6), channel_id=1, source_target_pairs={{0,1},{1,2},{2,3},{4,5},{5,6},{6,7},{8,9},{9,10},{10,11},{12,13},{... | collective-permute-start | bytes 1572872 | tf_op jit(solution)/shard_map/ppermute | solution.py:19
  9.3 1.3 collective-permute-start.1
  10.6 3.5 %collective-permute-start.2 = (bf16[2,2,1,1,2,64,512]{6,5,4,3,2,1,0:T(8,128)(2,1)}, bf16[2,2,1,1,2,64,512]{6,5,4,3,2,1,0:T(8,128)(2,1)S(1)}, u32[]{:S(2)}, u32[]{:S(2)}) collective-permute-start(bf16[2,2,1,1,2,64,512]{6,5,4,3,2,1,0:T(8,128)(2,1)} %param.6), channel_id=1, source_target_pairs={{0,4},{4,8},{8,12},{1,5},{5,9},{9,13},{2,6},{6,10},{10,14},{3,7},{... | collective-permute-start | bytes 1572872 | tf_op jit(solution)/shard_map/ppermute | solution.py:19
  14.1 1.3 collective-permute-start.3
  15.5 5.4 %collective-permute-done = bf16[2,2,1,1,2,64,512]{6,5,4,3,2,1,0:T(8,128)(2,1)S(1)} collective-permute-done((bf16[2,2,1,1,2,64,512]{6,5,4,3,2,1,0:T(8,128)(2,1)}, bf16[2,2,1,1,2,64,512]{6,5,4,3,2,1,0:T(8,128)(2,1)S(1)}, u32[]{:S(2)}, u32[]{:S(2)}) %collective-permute-start) | collective-permute-done | bytes 524320 | tf_op jit(solution)/shard_map/ppermute | solution.py:19
  20.8 43.0 %collective-permute-done.1 = bf16[2,2,1,1,2,64,512]{6,5,4,3,2,1,0:T(8,128)(2,1)S(1)} collective-permute-done((bf16[2,2,1,1,2,64,512]{6,5,4,3,2,1,0:T(8,128)(2,1)}, bf16[2,2,1,1,2,64,512]{6,5,4,3,2,1,0:T(8,128)(2,1)S(1)}, u32[]{:S(2)}, u32[]{:S(2)}) %collective-permute-start.1) | collective-permute-done | bytes 524320 | tf_op jit(solution)/shard_map/ppermute | solution.py:19
  63.9 0.9 constant_dynamic-update-slice_fusion.1
  64.8 0.8 constant_dynamic-update-slice_fusion
  65.6 4.4 %collective-permute-start.4 = (bf16[2,2,1,2,2,64,512]{6,5,4,3,2,1,0:T(8,128)(2,1)}, bf16[2,2,1,2,2,64,512]{6,5,4,3,2,1,0:T(8,128)(2,1)}, u32[]{:S(2)}, u32[]{:S(2)}) collective-permute-start(bf16[2,2,1,2,2,64,512]{6,5,4,3,2,1,0:T(8,128)(2,1)} %constant_dynamic-update-slice_fusion), channel_id=1, source_target_pairs={{0,4},{4,8},{8,12},{1,5},{5,9},{9,13},{2,6},{6,10},{10,14},{3,7},{... | collective-permute-start | bytes 3145736 | tf_op jit(solution)/shard_map/ppermute | solution.py:19
  70.0 0.7 fusion.1
  70.7 1.3 collective-permute-start.5
  72.0 0.1 fusion.2
  72.1 0.7 convert_element_type.12.refs_16_
  72.9 0.6 gather_fusion
  73.5 0.1 compare_and_fusion
  73.6 0.2 broadcast_select_fusion
  73.8 1.0 fusion.3
  74.8 16.7 %collective-permute-done.4 = bf16[2,2,1,2,2,64,512]{6,5,4,3,2,1,0:T(8,128)(2,1)} collective-permute-done((bf16[2,2,1,2,2,64,512]{6,5,4,3,2,1,0:T(8,128)(2,1)}, bf16[2,2,1,2,2,64,512]{6,5,4,3,2,1,0:T(8,128)(2,1)}, u32[]{:S(2)}, u32[]{:S(2)}) %collective-permute-start.4) | collective-permute-done | bytes 1048608 | tf_op jit(solution)/shard_map/ppermute | solution.py:19
  91.5 1.3 fusion.4
  92.8 4.4 %collective-permute-done.5 = bf16[2,2,1,2,2,64,512]{6,5,4,3,2,1,0:T(8,128)(2,1)} collective-permute-done((bf16[2,2,1,2,2,64,512]{6,5,4,3,2,1,0:T(8,128)(2,1)}, bf16[2,2,1,2,2,64,512]{6,5,4,3,2,1,0:T(8,128)(2,1)}, u32[]{:S(2)}, u32[]{:S(2)}) %collective-permute-start.5) | collective-permute-done | bytes 1048608 | tf_op jit(solution)/shard_map/ppermute | solution.py:19
  97.2 1.3 fusion.5
  98.5 2.8 %maximum_maximum_fusion = bf16[2,2,3,3,2,64,512]{6,5,4,3,2,1,0:T(8,128)(2,1)} fusion(bf16[2,2,1,1,2,64,512]{6,5,4,3,2,1,0:T(8,128)(2,1)S(1)} %get-tuple-element.34, bf16[2,2,1,1,2,64,512]{6,5,4,3,2,1,0:T(8,128)(2,1)S(1)} %copy-done.7, bf16[2,2,1,1,2,64,512]{6,5,4,3,2,1,0:T(8,128)(2,1)S(1)} %get-tuple-element.33, ...), kind=kLoop, calls=%fused_computation.1 | loop fusion | flops 18874368 | bytes 9437184 | tf_op jit(solution)/shard_map/concatenate | solution.py:34
  101.3 9.9 %shard_map.56 = f32[512,640]{1,0:T(8,128)} custom-call(s32[8]{0:T(128)} %bitcast.51, bf16[512,512]{1,0:T(8,128)(2,1)} %bitcast.50, bf16[2,2,18,64,512]{4,3,2,1,0:T(8,128)(2,1)} %bitcast.32, bf16[2,2,18,64,512]{4,3,2,1,0:T(8,128)(2,1)} %bitcast.18, bf16[2,2,18,64,512]{4,3,2,1,0:T(8,128)(2,1)} %bitcast.19, bf16[2,2,18,64,512]{4,3,2,1,0:T(8,128)(2,1)} %bitcast.20, ...), custom_call_target="tpu_custom_call" | custom-call | flops 2147483648 | bytes 3670016 | tf_op jit(solution)/shard_map/pallas_call | solution.py:104
  111.2 2.1 %collective-permute-start.6 = (f32[512,640]{1,0:T(8,128)}, f32[512,640]{1,0:T(8,128)S(1)}, u32[]{:S(2)}, u32[]{:S(2)}) collective-permute-start(f32[512,640]{1,0:T(8,128)} %shard_map.56), channel_id=1, source_target_pairs={{0,16},{16,0},{32,48},{48,32},{64,80},{80,64},{96,112},{112,96},{1... | collective-permute-start | bytes 3932168 | tf_op jit(solution)/shard_map/ppermute | solution.py:196
  113.3 9.9 %shard_map.55.a_ref = f32[512,640]{1,0:T(8,128)} custom-call(s32[8]{0:T(128)} %bitcast.52, bf16[512,512]{1,0:T(8,128)(2,1)} %bitcast.49, bf16[2,2,18,64,512]{4,3,2,1,0:T(8,128)(2,1)} %bitcast.33, bf16[2,2,18,64,512]{4,3,2,1,0:T(8,128)(2,1)} %bitcast.34, bf16[2,2,18,64,512]{4,3,2,1,0:T(8,128)(2,1)} %bitcast.35, bf16[2,2,18,64,512]{4,3,2,1,0:T(8,128)(2,1)} %bitcast.36, ...), custom_call_target="tpu_custom_call" | custom-call | flops 2147483648 | bytes 3670016 | tf_op jit(solution)/shard_map/pallas_call | solution.py:104
  123.3 1.1 copy-done.1
  124.3 4.0 %shard_map.57 = (f32[256,640]{1,0:T(8,128)}, f32[256,640]{1,0:T(8,128)}) custom-call(f32[512,640]{1,0:T(8,128)} %shard_map.55.a_ref, f32[512,640]{1,0:T(8,128)} %copy-done.1), custom_call_target="tpu_custom_call" | custom-call | flops 1310720 | bytes 3932160 | tf_op jit(solution)/shard_map/pallas_call | solution.py:156
  128.3 1.9 %collective-permute-start.7 = (f32[256,640]{1,0:T(8,128)}, f32[256,640]{1,0:T(8,128)S(1)}, u32[]{:S(2)}, u32[]{:S(2)}) collective-permute-start(f32[256,640]{1,0:T(8,128)} %get-tuple-element.22), channel_id=1, source_target_pairs={{0,32},{16,144},{32,0},{48,176},{64,96},{80,208},{96,64},{112,240}... | collective-permute-start | bytes 1966088 | tf_op jit(solution)/shard_map/ppermute | solution.py:196
  130.2 10.8 %collective-permute-done.7.b_ref = f32[256,640]{1,0:T(8,128)S(1)} collective-permute-done((f32[256,640]{1,0:T(8,128)}, f32[256,640]{1,0:T(8,128)S(1)}, u32[]{:S(2)}, u32[]{:S(2)}) %collective-permute-start.7) | collective-permute-done | bytes 655392 | tf_op jit(solution)/shard_map/ppermute | solution.py:196
  141.0 0.8 copy-done.2
  141.8 2.8 %shard_map.58 = (f32[128,640]{1,0:T(8,128)}, f32[128,640]{1,0:T(8,128)}) custom-call(f32[256,640]{1,0:T(8,128)} %get-tuple-element.21.a_ref, f32[256,640]{1,0:T(8,128)} %copy-done.2), custom_call_target="tpu_custom_call" | custom-call | flops 655360 | bytes 1966080 | tf_op jit(solution)/shard_map/pallas_call | solution.py:156
  144.6 2.7 %collective-permute-start.8 = (f32[128,640]{1,0:T(8,128)}, f32[128,640]{1,0:T(8,128)S(1)}, u32[]{:S(2)}, u32[]{:S(2)}) collective-permute-start(f32[128,640]{1,0:T(8,128)} %get-tuple-element.24), channel_id=1, source_target_pairs={{0,128},{16,48},{32,160},{48,16},{64,192},{80,112},{96,224},{112,8... | collective-permute-start | bytes 983048 | tf_op jit(solution)/shard_map/ppermute | solution.py:196
  147.3 6.4 %collective-permute-done.8.b_ref = f32[128,640]{1,0:T(8,128)S(1)} collective-permute-done((f32[128,640]{1,0:T(8,128)}, f32[128,640]{1,0:T(8,128)S(1)}, u32[]{:S(2)}, u32[]{:S(2)}) %collective-permute-start.8) | collective-permute-done | bytes 327712 | tf_op jit(solution)/shard_map/ppermute | solution.py:196
  153.8 0.7 copy-done.8
  154.5 2.1 %shard_map.59 = (f32[64,640]{1,0:T(8,128)}, f32[64,640]{1,0:T(8,128)}) custom-call(f32[128,640]{1,0:T(8,128)} %get-tuple-element.23.a_ref, f32[128,640]{1,0:T(8,128)} %copy-done.8), custom_call_target="tpu_custom_call" | custom-call | flops 327680 | bytes 983040 | tf_op jit(solution)/shard_map/pallas_call | solution.py:156
  156.6 1.9 %collective-permute-start.9 = (f32[64,640]{1,0:T(8,128)}, f32[64,640]{1,0:T(8,128)S(1)}, u32[]{:S(2)}, u32[]{:S(2)}) collective-permute-start(f32[64,640]{1,0:T(8,128)} %get-tuple-element.26), channel_id=1, source_target_pairs={{0,64},{16,272},{32,96},{48,304},{64,0},{80,336},{96,32},{112,368}... | collective-permute-start | bytes 491528 | tf_op jit(solution)/shard_map/ppermute | solution.py:196
  158.5 7.6 %collective-permute-done.9.b_ref = f32[64,640]{1,0:T(8,128)S(1)} collective-permute-done((f32[64,640]{1,0:T(8,128)}, f32[64,640]{1,0:T(8,128)S(1)}, u32[]{:S(2)}, u32[]{:S(2)}) %collective-permute-start.9) | collective-permute-done | bytes 163872 | tf_op jit(solution)/shard_map/ppermute | solution.py:196
  166.2 0.7 copy-done.9
  166.8 1.9 %shard_map.60 = (f32[32,640]{1,0:T(8,128)}, f32[32,640]{1,0:T(8,128)}) custom-call(f32[64,640]{1,0:T(8,128)} %get-tuple-element.25.a_ref, f32[64,640]{1,0:T(8,128)} %copy-done.9), custom_call_target="tpu_custom_call" | custom-call | flops 163840 | bytes 491520 | tf_op jit(solution)/shard_map/pallas_call | solution.py:156
  168.7 3.3 %collective-permute-start.10 = (f32[32,640]{1,0:T(8,128)}, f32[32,640]{1,0:T(8,128)S(1)}, u32[]{:S(2)}, u32[]{:S(2)}) collective-permute-start(f32[32,640]{1,0:T(8,128)} %get-tuple-element.28), channel_id=1, source_target_pairs={{0,256},{16,80},{32,288},{48,112},{64,320},{80,16},{96,352},{112,4... | collective-permute-start | bytes 245768 | tf_op jit(solution)/shard_map/ppermute | solution.py:196
  172.0 4.7 %collective-permute-done.10.b_ref = f32[32,640]{1,0:T(8,128)S(1)} collective-permute-done((f32[32,640]{1,0:T(8,128)}, f32[32,640]{1,0:T(8,128)S(1)}, u32[]{:S(2)}, u32[]{:S(2)}) %collective-permute-start.10) | collective-permute-done | bytes 81952 | tf_op jit(solution)/shard_map/ppermute | solution.py:196
  176.7 0.6 copy-done.10
  177.3 1.7 shard_map.61
  179.1 0.8 slice.57
  179.8 0.1 broadcast_in_dim.23
  179.9 0.1 reshape.137
  180.0 1.0 multiply_reduce_fusion
  181.0 2.0 %convolution_bitcast_fusion = f32[1,1,32,512]{3,2,1,0:T(8,128)} fusion(bf16[512,512]{1,0:T(8,128)(2,1)} %param.9, f32[32]{0:T(128)S(1)} %add_rsqrt_fusion, f32[32,512]{1,0:T(8,128)S(1)} %reshape.137, f32[32,640]{1,0:T(8,128)} %shard_map.61), kind=kOutput, calls=%fused_computation.2 | convolution fusion | flops 16826368 | bytes 721024 | tf_op jit(solution)/shard_map/dot_general | solution.py:233
  (26 shorter events, 0.2 us)
Async XLA Ops:
  0.0 72.8 %copy-start = (bf16[1,1,1024,512]{3,2,1,0:T(8,128)(2,1)S(1)}, bf16[1,1,1024,512]{3,2,1,0:T(8,128)(2,1)}, u32[]{:S(2)}) copy-start(bf16[1,1,1024,512]{3,2,1,0:T(8,128)(2,1)} %param.5) | copy-start | bytes 3145732
  0.0 20.8 %collective-permute-start = (bf16[2,2,1,1,2,64,512]{6,5,4,3,2,1,0:T(8,128)(2,1)}, bf16[2,2,1,1,2,64,512]{6,5,4,3,2,1,0:T(8,128)(2,1)S(1)}, u32[]{:S(2)}, u32[]{:S(2)}) collective-permute-start(bf16[2,2,1,1,2,64,512]{6,5,4,3,2,1,0:T(8,128)(2,1)} %param.6), channel_id=1, source_target_pairs={{0,1},{1,2},{2,3},{4,5},{5,6},{6,7},{8,9},{9,10},{10,11},{12,13},{... | collective-permute-start | bytes 1572872 | tf_op jit(solution)/shard_map/ppermute | solution.py:19
  9.3 54.6 %collective-permute-start.1 = (bf16[2,2,1,1,2,64,512]{6,5,4,3,2,1,0:T(8,128)(2,1)}, bf16[2,2,1,1,2,64,512]{6,5,4,3,2,1,0:T(8,128)(2,1)S(1)}, u32[]{:S(2)}, u32[]{:S(2)}) collective-permute-start(bf16[2,2,1,1,2,64,512]{6,5,4,3,2,1,0:T(8,128)(2,1)} %param.6), channel_id=1, source_target_pairs={{1,0},{2,1},{3,2},{5,4},{6,5},{7,6},{9,8},{10,9},{11,10},{13,12},{... | collective-permute-start | bytes 1572872 | tf_op jit(solution)/shard_map/ppermute | solution.py:19
  10.6 53.3 %collective-permute-start.2 = (bf16[2,2,1,1,2,64,512]{6,5,4,3,2,1,0:T(8,128)(2,1)}, bf16[2,2,1,1,2,64,512]{6,5,4,3,2,1,0:T(8,128)(2,1)S(1)}, u32[]{:S(2)}, u32[]{:S(2)}) collective-permute-start(bf16[2,2,1,1,2,64,512]{6,5,4,3,2,1,0:T(8,128)(2,1)} %param.6), channel_id=1, source_target_pairs={{0,4},{4,8},{8,12},{1,5},{5,9},{9,13},{2,6},{6,10},{10,14},{3,7},{... | collective-permute-start | bytes 1572872 | tf_op jit(solution)/shard_map/ppermute | solution.py:19
  14.1 49.8 %collective-permute-start.3 = (bf16[2,2,1,1,2,64,512]{6,5,4,3,2,1,0:T(8,128)(2,1)}, bf16[2,2,1,1,2,64,512]{6,5,4,3,2,1,0:T(8,128)(2,1)S(1)}, u32[]{:S(2)}, u32[]{:S(2)}) collective-permute-start(bf16[2,2,1,1,2,64,512]{6,5,4,3,2,1,0:T(8,128)(2,1)} %param.6), channel_id=1, source_target_pairs={{4,0},{8,4},{12,8},{5,1},{9,5},{13,9},{6,2},{10,6},{14,10},{7,3},{... | collective-permute-start | bytes 1572872 | tf_op jit(solution)/shard_map/ppermute | solution.py:19
  63.9 8.9 %copy-start.4 = (bf16[2,2,1,1,2,64,512]{6,5,4,3,2,1,0:T(8,128)(2,1)}, bf16[2,2,1,1,2,64,512]{6,5,4,3,2,1,0:T(8,128)(2,1)S(1)}, u32[]{:S(2)}) copy-start(bf16[2,2,1,1,2,64,512]{6,5,4,3,2,1,0:T(8,128)(2,1)S(1)} %collective-permute-done.2) | copy-start | bytes 1572868
  63.9 8.9 %copy-start.6 = (bf16[2,2,1,1,2,64,512]{6,5,4,3,2,1,0:T(8,128)(2,1)}, bf16[2,2,1,1,2,64,512]{6,5,4,3,2,1,0:T(8,128)(2,1)S(1)}, u32[]{:S(2)}) copy-start(bf16[2,2,1,1,2,64,512]{6,5,4,3,2,1,0:T(8,128)(2,1)S(1)} %collective-permute-done.3) | copy-start | bytes 1572868
  65.6 25.9 %collective-permute-start.4 = (bf16[2,2,1,2,2,64,512]{6,5,4,3,2,1,0:T(8,128)(2,1)}, bf16[2,2,1,2,2,64,512]{6,5,4,3,2,1,0:T(8,128)(2,1)}, u32[]{:S(2)}, u32[]{:S(2)}) collective-permute-start(bf16[2,2,1,2,2,64,512]{6,5,4,3,2,1,0:T(8,128)(2,1)} %constant_dynamic-update-slice_fusion), channel_id=1, source_target_pairs={{0,4},{4,8},{8,12},{1,5},{5,9},{9,13},{2,6},{6,10},{10,14},{3,7},{... | collective-permute-start | bytes 3145736 | tf_op jit(solution)/shard_map/ppermute | solution.py:19
  70.7 26.5 %collective-permute-start.5 = (bf16[2,2,1,2,2,64,512]{6,5,4,3,2,1,0:T(8,128)(2,1)}, bf16[2,2,1,2,2,64,512]{6,5,4,3,2,1,0:T(8,128)(2,1)}, u32[]{:S(2)}, u32[]{:S(2)}) collective-permute-start(bf16[2,2,1,2,2,64,512]{6,5,4,3,2,1,0:T(8,128)(2,1)} %constant_dynamic-update-slice_fusion), channel_id=1, source_target_pairs={{4,0},{8,4},{12,8},{5,1},{9,5},{13,9},{6,2},{10,6},{14,10},{7,3},{... | collective-permute-start | bytes 3145736 | tf_op jit(solution)/shard_map/ppermute | solution.py:19
  73.5 25.0 %copy-start.3 = (bf16[2,2,1,1,2,64,512]{6,5,4,3,2,1,0:T(8,128)(2,1)S(1)}, bf16[2,2,1,1,2,64,512]{6,5,4,3,2,1,0:T(8,128)(2,1)}, u32[]{:S(2)}) copy-start(bf16[2,2,1,1,2,64,512]{6,5,4,3,2,1,0:T(8,128)(2,1)} %param.6) | copy-start | bytes 1572868
  73.5 25.0 %copy-start.5 = (bf16[2,2,1,1,2,64,512]{6,5,4,3,2,1,0:T(8,128)(2,1)S(1)}, bf16[2,2,1,1,2,64,512]{6,5,4,3,2,1,0:T(8,128)(2,1)}, u32[]{:S(2)}) copy-start(bf16[2,2,1,1,2,64,512]{6,5,4,3,2,1,0:T(8,128)(2,1)} %copy-done.4) | copy-start | bytes 1572868
  73.5 25.0 %copy-start.7 = (bf16[2,2,1,1,2,64,512]{6,5,4,3,2,1,0:T(8,128)(2,1)S(1)}, bf16[2,2,1,1,2,64,512]{6,5,4,3,2,1,0:T(8,128)(2,1)}, u32[]{:S(2)}) copy-start(bf16[2,2,1,1,2,64,512]{6,5,4,3,2,1,0:T(8,128)(2,1)} %copy-done.6) | copy-start | bytes 1572868
  111.2 12.0 %collective-permute-start.6 = (f32[512,640]{1,0:T(8,128)}, f32[512,640]{1,0:T(8,128)S(1)}, u32[]{:S(2)}, u32[]{:S(2)}) collective-permute-start(f32[512,640]{1,0:T(8,128)} %shard_map.56), channel_id=1, source_target_pairs={{0,16},{16,0},{32,48},{48,32},{64,80},{80,64},{96,112},{112,96},{1... | collective-permute-start | bytes 3932168 | tf_op jit(solution)/shard_map/ppermute | solution.py:196
  123.2 1.1 copy-start.1
  128.3 12.7 %collective-permute-start.7 = (f32[256,640]{1,0:T(8,128)}, f32[256,640]{1,0:T(8,128)S(1)}, u32[]{:S(2)}, u32[]{:S(2)}) collective-permute-start(f32[256,640]{1,0:T(8,128)} %get-tuple-element.22), channel_id=1, source_target_pairs={{0,32},{16,144},{32,0},{48,176},{64,96},{80,208},{96,64},{112,240}... | collective-permute-start | bytes 1966088 | tf_op jit(solution)/shard_map/ppermute | solution.py:196
  141.0 0.8 copy-start.2
  144.6 9.2 %collective-permute-start.8 = (f32[128,640]{1,0:T(8,128)}, f32[128,640]{1,0:T(8,128)S(1)}, u32[]{:S(2)}, u32[]{:S(2)}) collective-permute-start(f32[128,640]{1,0:T(8,128)} %get-tuple-element.24), channel_id=1, source_target_pairs={{0,128},{16,48},{32,160},{48,16},{64,192},{80,112},{96,224},{112,8... | collective-permute-start | bytes 983048 | tf_op jit(solution)/shard_map/ppermute | solution.py:196
  153.8 0.7 copy-start.8
  156.6 9.5 %collective-permute-start.9 = (f32[64,640]{1,0:T(8,128)}, f32[64,640]{1,0:T(8,128)S(1)}, u32[]{:S(2)}, u32[]{:S(2)}) collective-permute-start(f32[64,640]{1,0:T(8,128)} %get-tuple-element.26), channel_id=1, source_target_pairs={{0,64},{16,272},{32,96},{48,304},{64,0},{80,336},{96,32},{112,368}... | collective-permute-start | bytes 491528 | tf_op jit(solution)/shard_map/ppermute | solution.py:196
  166.1 0.7 copy-start.9
  168.7 8.0 %collective-permute-start.10 = (f32[32,640]{1,0:T(8,128)}, f32[32,640]{1,0:T(8,128)S(1)}, u32[]{:S(2)}, u32[]{:S(2)}) collective-permute-start(f32[32,640]{1,0:T(8,128)} %get-tuple-element.28), channel_id=1, source_target_pairs={{0,256},{16,80},{32,288},{48,112},{64,320},{80,16},{96,352},{112,4... | collective-permute-start | bytes 245768 | tf_op jit(solution)/shard_map/ppermute | solution.py:196
  176.7 0.6 copy-start.10

commit v11 on v10

--- a/solution.py
+++ b/solution.py
@@ -85,7 +85,8 @@
     _, frames, _, blk, _ = hood.shape
     nlist = listed.shape[0]
     count = nlist * frames * blk
-    tiles = qtok // TQ
+    tq = min(TQ, qtok)
+    tiles = qtok // tq
     flops = 2 * 2 * qtok * count * 2 * width
     block = (1, frames, 1, blk, width)
 
@@ -95,11 +96,11 @@
     grid_spec = pltpu.PrefetchScalarGridSpec(
         num_scalar_prefetch=1,
         grid=(tiles,),
-        in_specs=[pl.BlockSpec((TQ, width), lambda i, lst: (i, 0))]
+        in_specs=[pl.BlockSpec((tq, width), lambda i, lst: (i, 0))]
         + [entry_spec(0, e) for e in range(nlist)]
         + [entry_spec(1, e) for e in range(nlist)]
         + [pl.BlockSpec((1, count), lambda i, lst: (0, 0))],
-        out_specs=pl.BlockSpec((TQ, width + PACK), lambda i, lst: (i, 0)),
+        out_specs=pl.BlockSpec((tq, width + PACK), lambda i, lst: (i, 0)),
     )
     return pl.pallas_call(
         attention_kernel,
@@ -149,12 +150,22 @@
         out_refs[1][...] = merged[half:]
 
 
-def merge(kept, got, split):
+def merge(kept, got, split, offset=0):
     rows, cols = kept.shape
     count = 2 if split else 1
     shape = jax.ShapeDtypeStruct((rows // count, cols), jnp.float32)
+    if split:
+        out_specs = [pl.BlockSpec((rows // 2, cols), lambda i: (0, 0))] * 2
+    else:
+        out_specs = [pl.BlockSpec((rows, cols), lambda i: (0, 0))]
     return pl.pallas_call(
         merge_kernel,
+        grid=(1,),
+        in_specs=[
+            pl.BlockSpec((rows, cols), lambda i: (0, 0)),
+            pl.BlockSpec((rows, cols), lambda i: (offset // rows, 0)),
+        ],
+        out_specs=out_specs,
         out_shape=[shape] * count,
         cost_estimate=pl.CostEstimate(
             flops=4 * rows * cols, transcendentals=2 * rows * PACK, bytes_accessed=12 * rows * cols
@@ -189,16 +200,25 @@
     return block
 
 
-def tree_reduce(first, second):
+def tree_reduce(query_rows, hood, listed, keep):
     groups = lax.axis_size("tm")
     nbits = groups.bit_length() - 1
-    for i in range(nbits):
-        got = lax.ppermute(second, "tm", step_pairs(nbits, i))
+    qtok = query_rows.shape[0]
+    half, quarter = qtok // 2, qtok // 4
+    second = attention(query_rows[half:], hood, listed, keep)
+    got_first = lax.ppermute(second, "tm", step_pairs(nbits, 0))
+    sent = attention(query_rows[quarter:half], hood, listed, keep)
+    (sent,) = merge(sent, got_first, False, quarter)
+    second = lax.ppermute(sent, "tm", step_pairs(nbits, 1))
+    first = attention(query_rows[:quarter], hood, listed, keep)
+    (first,) = merge(first, got_first, False, 0)
+    for i in range(1, nbits):
         last = i == nbits - 1
-        outs = merge(first, got, not last)
+        outs = merge(first, second, not last)
         if last:
             return outs[0]
         first, second = outs
+        second = lax.ppermute(second, "tm", step_pairs(nbits, i + 1))
 
 
 def local(queries, kv_blocks, block_list, block_valid, w_out):
@@ -221,9 +241,7 @@
     )
     query_rows = jnp.take(query_rows.reshape(groups, qtok // groups, width), order, axis=0)
     query_rows = query_rows.reshape(qtok, width)
-    second = attention(query_rows[qtok // 2 :], hood, listed, keep)
-    first = attention(query_rows[: qtok // 2], hood, listed, keep)
-    final = tree_reduce(first, second)
+    final = tree_reduce(query_rows, hood, listed, keep)
     summed = final[:, :width]
     total = final[:, width + HEADS : width + 2 * HEADS]
     own_rows = summed.shape[0]

time: 184 us -> 176 us (0.957)
  waiting for transfers between devices: 99.1 us -> 75.4 us
  starting transfers between devices: 33 us -> 40.2 us
  Pallas kernels: 32.3 us -> 38.4 us
    ppermute x5, waiting for transfers between devices: 29.5 us -> 17.1 us  [the longest x3 16.4 us: tree_reduce(): second = lax.ppermute(second, 'tm', step_pairs(nbits, i + 1))]
    ppermute x6, waiting for transfers between devices: 69.6 us -> 58.3 us  [shifted(): return lax.ppermute(array, axis, pairs)]
    ppermute x5, starting transfers between devices: 11.9 us -> 17.4 us  [the longest x3 13.4 us: tree_reduce(): second = lax.ppermute(second, 'tm', step_pairs(nbits, i + 1))]
    pallas_call x2 -> x3, Pallas kernels: 19.8 us -> 24.4 us  [attention(): pl.pallas_call(attention_kernel, grid_spec=grid_spec, out_shape=jax.Shape...]
    pallas_call x5 -> x6, Pallas kernels: 12.5 us -> 14 us  [merge(): pl.pallas_call(merge_kernel, grid=(1,), in_specs=[pl.BlockSpec((rows, col...]
    unnamed x23 -> x33, local copies, waits for them, and re-layouts: 4.83 us -> 5.01 us
  transfers between devices with their start and end apart: 11 -> 11, of which waited for: 8 -> 6; matrix products, arithmetic and copies ran while one was open for 3% -> 3% of each run, Pallas kernels for 5% -> 10%
where the time goes in v11:
time: 176 us; the launch traced here: 173 us
  waiting for transfers between devices  75.4 us (43%)
  starting transfers between devices  40.2 us (23%)
  Pallas kernels  38.4 us (22%)
  local copies, waits for them, and re-layouts  12.5 us (7%)
  other arithmetic  4.78 us (3%)
    ppermute x6, waiting for transfers between devices, shifted(): return lax.ppermute(array, axis, pairs)  58.3 us
    pallas_call x3, Pallas kernels, attention(): pl.pallas_call(attention_kernel, grid_spec=grid_spec, out_shape=jax.Shape...  24.4 us
    ppermute x6, starting transfers between devices, shifted(): return lax.ppermute(array, axis, pairs)  22.8 us
    ppermute x3, waiting for transfers between devices, tree_reduce(): second = lax.ppermute(second, 'tm', step_pairs(nbits, i + 1))  16.4 us
    pallas_call x6, Pallas kernels, merge(): pl.pallas_call(merge_kernel, grid=(1,), in_specs=[pl.BlockSpec((rows, col...  14 us
    ppermute x3, starting transfers between devices, tree_reduce(): second = lax.ppermute(second, 'tm', step_pairs(nbits, i + 1))  13.4 us
    unnamed x33, local copies, waits for them, and re-layouts  5.01 us
  transfers between devices with their start and end apart: 11, of which 6 were waited for; matrix products, arithmetic and copies ran while one was open for 3% of the time, Pallas kernels for 10%

profile of v11, /device:TPU:6, one launch (start us, length us, event | category | flops | bytes accessed | tf_op | source)
XLA Modules:
  0.0 173.3 jit_solution(6504590103157236401)
XLA Ops:
  0.0 3.6 %collective-permute-start.2 = (bf16[2,2,1,1,2,64,512]{6,5,4,3,2,1,0:T(8,128)(2,1)}, bf16[2,2,1,1,2,64,512]{6,5,4,3,2,1,0:T(8,128)(2,1)S(1)}, u32[]{:S(2)}, u32[]{:S(2)}) collective-permute-start(bf16[2,2,1,1,2,64,512]{6,5,4,3,2,1,0:T(8,128)(2,1)} %param.6), channel_id=1, source_target_pairs={{0,4},{4,8},{8,12},{1,5},{5,9},{9,13},{2,6},{6,10},{10,14},{3,7},{... | collective-permute-start | bytes 1572872 | tf_op jit(solution)/shard_map/ppermute | solution.py:19
  3.6 1.3 collective-permute-start.1
  4.9 9.8 %collective-permute-start = (bf16[2,2,1,1,2,64,512]{6,5,4,3,2,1,0:T(8,128)(2,1)}, bf16[2,2,1,1,2,64,512]{6,5,4,3,2,1,0:T(8,128)(2,1)S(1)}, u32[]{:S(2)}, u32[]{:S(2)}) collective-permute-start(bf16[2,2,1,1,2,64,512]{6,5,4,3,2,1,0:T(8,128)(2,1)} %param.6), channel_id=1, source_target_pairs={{0,1},{1,2},{2,3},{4,5},{5,6},{6,7},{8,9},{9,10},{10,11},{12,13},{... | collective-permute-start | bytes 1572872 | tf_op jit(solution)/shard_map/ppermute | solution.py:19
  14.7 1.3 collective-permute-start.3
  16.1 0.7 fusion.1
  16.8 0.7 convert_element_type.12.refs_16_
  17.5 40.8 %collective-permute-done.1 = bf16[2,2,1,1,2,64,512]{6,5,4,3,2,1,0:T(8,128)(2,1)S(1)} collective-permute-done((bf16[2,2,1,1,2,64,512]{6,5,4,3,2,1,0:T(8,128)(2,1)}, bf16[2,2,1,1,2,64,512]{6,5,4,3,2,1,0:T(8,128)(2,1)S(1)}, u32[]{:S(2)}, u32[]{:S(2)}) %collective-permute-start.1) | collective-permute-done | bytes 524320 | tf_op jit(solution)/shard_map/ppermute | solution.py:19
  58.3 1.0 constant_dynamic-update-slice_fusion.1
  59.3 0.9 constant_dynamic-update-slice_fusion
  60.2 1.3 collective-permute-start.5
  61.5 5.5 %collective-permute-start.4 = (bf16[2,2,1,2,2,64,512]{6,5,4,3,2,1,0:T(8,128)(2,1)}, bf16[2,2,1,2,2,64,512]{6,5,4,3,2,1,0:T(8,128)(2,1)}, u32[]{:S(2)}, u32[]{:S(2)}) collective-permute-start(bf16[2,2,1,2,2,64,512]{6,5,4,3,2,1,0:T(8,128)(2,1)} %constant_dynamic-update-slice_fusion), channel_id=1, source_target_pairs={{0,4},{4,8},{8,12},{1,5},{5,9},{9,13},{2,6},{6,10},{10,14},{3,7},{... | collective-permute-start | bytes 3145736 | tf_op jit(solution)/shard_map/ppermute | solution.py:19
  67.2 0.6 gather_fusion
  67.8 0.1 compare_and_fusion
  67.9 0.2 broadcast_select_fusion
  68.1 0.8 slice.63
  68.9 17.4 %collective-permute-done.5 = bf16[2,2,1,2,2,64,512]{6,5,4,3,2,1,0:T(8,128)(2,1)} collective-permute-done((bf16[2,2,1,2,2,64,512]{6,5,4,3,2,1,0:T(8,128)(2,1)}, bf16[2,2,1,2,2,64,512]{6,5,4,3,2,1,0:T(8,128)(2,1)}, u32[]{:S(2)}, u32[]{:S(2)}) %collective-permute-start.5) | collective-permute-done | bytes 1048608 | tf_op jit(solution)/shard_map/ppermute | solution.py:19
  86.4 1.3 fusion.5
  87.7 1.3 fusion.4
  89.0 2.8 %maximum_maximum_fusion = bf16[2,2,3,3,2,64,512]{6,5,4,3,2,1,0:T(8,128)(2,1)} fusion(bf16[2,2,1,1,2,64,512]{6,5,4,3,2,1,0:T(8,128)(2,1)S(1)} %get-tuple-element.30, bf16[2,2,1,1,2,64,512]{6,5,4,3,2,1,0:T(8,128)(2,1)S(1)} %copy-done.11, bf16[2,2,1,1,2,64,512]{6,5,4,3,2,1,0:T(8,128)(2,1)S(1)} %get-tuple-element.29, ...), kind=kLoop, calls=%fused_computation.1 | loop fusion | flops 18874368 | bytes 9437184 | tf_op jit(solution)/shard_map/concatenate | solution.py:34
  91.8 9.9 %shard_map.56 = f32[512,640]{1,0:T(8,128)} custom-call(s32[8]{0:T(128)} %bitcast.69, bf16[512,512]{1,0:T(8,128)(2,1)} %bitcast.66, bf16[2,2,18,64,512]{4,3,2,1,0:T(8,128)(2,1)} %bitcast.18, bf16[2,2,18,64,512]{4,3,2,1,0:T(8,128)(2,1)} %bitcast.19, bf16[2,2,18,64,512]{4,3,2,1,0:T(8,128)(2,1)} %bitcast.20, bf16[2,2,18,64,512]{4,3,2,1,0:T(8,128)(2,1)} %bitcast.21, ...), custom_call_target="tpu_custom_call" | custom-call | flops 2147483648 | bytes 3670016 | tf_op jit(solution)/shard_map/pallas_call | solution.py:105
  101.7 2.1 %collective-permute-start.6 = (f32[512,640]{1,0:T(8,128)}, f32[512,640]{1,0:T(8,128)S(1)}, u32[]{:S(2)}, u32[]{:S(2)}) collective-permute-start(f32[512,640]{1,0:T(8,128)} %shard_map.56), channel_id=1, source_target_pairs={{0,16},{16,0},{32,48},{48,32},{64,80},{80,64},{96,112},{112,96},{1... | collective-permute-start | bytes 3932168 | tf_op jit(solution)/shard_map/ppermute | solution.py:209
  103.8 0.9 fusion.3
  104.7 7.2 %shard_map.58.a_ref = f32[256,640]{1,0:T(8,128)} custom-call(s32[8]{0:T(128)} %bitcast.70, bf16[256,512]{1,0:T(8,128)(2,1)} %bitcast.68, bf16[2,2,18,64,512]{4,3,2,1,0:T(8,128)(2,1)} %bitcast.41, bf16[2,2,18,64,512]{4,3,2,1,0:T(8,128)(2,1)} %bitcast.35, bf16[2,2,18,64,512]{4,3,2,1,0:T(8,128)(2,1)} %bitcast.36, bf16[2,2,18,64,512]{4,3,2,1,0:T(8,128)(2,1)} %bitcast.37, ...), custom_call_target="tpu_custom_call" | custom-call | flops 1073741824 | bytes 2883584 | tf_op jit(solution)/shard_map/pallas_call | solution.py:105
  111.9 1.1 copy-done.1
  113.0 2.8 %shard_map.59 = f32[256,640]{1,0:T(8,128)} custom-call(f32[256,640]{1,0:T(8,128)} %shard_map.58.a_ref, f32[512,640]{1,0:T(8,128)} %copy-done.1), custom_call_target="tpu_custom_call" | custom-call | flops 655360 | bytes 1966080 | tf_op jit(solution)/shard_map/pallas_call | solution.py:161
  115.7 1.9 %collective-permute-start.7 = (f32[256,640]{1,0:T(8,128)}, f32[256,640]{1,0:T(8,128)S(1)}, u32[]{:S(2)}, u32[]{:S(2)}) collective-permute-start(f32[256,640]{1,0:T(8,128)} %shard_map.59), channel_id=1, source_target_pairs={{0,32},{16,144},{32,0},{48,176},{64,96},{80,208},{96,64},{112,240}... | collective-permute-start | bytes 1966088 | tf_op jit(solution)/shard_map/ppermute | solution.py:212
  117.7 7.2 %shard_map.55.a_ref = f32[256,640]{1,0:T(8,128)} custom-call(s32[8]{0:T(128)} %bitcast.71, bf16[256,512]{1,0:T(8,128)(2,1)} %bitcast.67, bf16[2,2,18,64,512]{4,3,2,1,0:T(8,128)(2,1)} %bitcast.50, bf16[2,2,18,64,512]{4,3,2,1,0:T(8,128)(2,1)} %bitcast.51, bf16[2,2,18,64,512]{4,3,2,1,0:T(8,128)(2,1)} %bitcast.52, bf16[2,2,18,64,512]{4,3,2,1,0:T(8,128)(2,1)} %bitcast.53, ...), custom_call_target="tpu_custom_call" | custom-call | flops 1073741824 | bytes 2883584 | tf_op jit(solution)/shard_map/pallas_call | solution.py:105
  124.9 2.8 %shard_map.57.a_ref = f32[256,640]{1,0:T(8,128)} custom-call(f32[256,640]{1,0:T(8,128)} %shard_map.55.a_ref, f32[512,640]{1,0:T(8,128)} %copy-done.1), custom_call_target="tpu_custom_call" | custom-call | flops 655360 | bytes 1966080 | tf_op jit(solution)/shard_map/pallas_call | solution.py:161
  127.7 0.7 collective-permute-done.7.b_ref
  128.4 0.9 copy-done.6
  129.3 2.8 %shard_map.60 = (f32[128,640]{1,0:T(8,128)}, f32[128,640]{1,0:T(8,128)}) custom-call(f32[256,640]{1,0:T(8,128)} %shard_map.57.a_ref, f32[256,640]{1,0:T(8,128)} %copy-done.6), custom_call_target="tpu_custom_call" | custom-call | flops 655360 | bytes 1966080 | tf_op jit(solution)/shard_map/pallas_call | solution.py:161
  132.1 2.7 %collective-permute-start.8 = (f32[128,640]{1,0:T(8,128)}, f32[128,640]{1,0:T(8,128)S(1)}, u32[]{:S(2)}, u32[]{:S(2)}) collective-permute-start(f32[128,640]{1,0:T(8,128)} %get-tuple-element.20), channel_id=1, source_target_pairs={{0,128},{16,48},{32,160},{48,16},{64,192},{80,112},{96,224},{112,8... | collective-permute-start | bytes 983048 | tf_op jit(solution)/shard_map/ppermute | solution.py:221
  134.8 6.4 %collective-permute-done.8.b_ref = f32[128,640]{1,0:T(8,128)S(1)} collective-permute-done((f32[128,640]{1,0:T(8,128)}, f32[128,640]{1,0:T(8,128)S(1)}, u32[]{:S(2)}, u32[]{:S(2)}) %collective-permute-start.8) | collective-permute-done | bytes 327712 | tf_op jit(solution)/shard_map/ppermute | solution.py:221
  141.2 0.7 copy-done.13
  142.0 2.1 %shard_map.61 = (f32[64,640]{1,0:T(8,128)}, f32[64,640]{1,0:T(8,128)}) custom-call(f32[128,640]{1,0:T(8,128)} %get-tuple-element.19.a_ref, f32[128,640]{1,0:T(8,128)} %copy-done.13), custom_call_target="tpu_custom_call" | custom-call | flops 327680 | bytes 983040 | tf_op jit(solution)/shard_map/pallas_call | solution.py:161
  144.1 7.3 %collective-permute-start.9 = (f32[64,640]{1,0:T(8,128)}, f32[64,640]{1,0:T(8,128)S(1)}, u32[]{:S(2)}, u32[]{:S(2)}) collective-permute-start(f32[64,640]{1,0:T(8,128)} %get-tuple-element.22), channel_id=1, source_target_pairs={{0,64},{16,272},{32,96},{48,304},{64,0},{80,336},{96,32},{112,368}... | collective-permute-start | bytes 491528 | tf_op jit(solution)/shard_map/ppermute | solution.py:221
  151.4 5.2 %collective-permute-done.9.b_ref = f32[64,640]{1,0:T(8,128)S(1)} collective-permute-done((f32[64,640]{1,0:T(8,128)}, f32[64,640]{1,0:T(8,128)S(1)}, u32[]{:S(2)}, u32[]{:S(2)}) %collective-permute-start.9) | collective-permute-done | bytes 163872 | tf_op jit(solution)/shard_map/ppermute | solution.py:221
  156.7 0.7 copy-done.14
  157.4 1.9 %shard_map.62 = (f32[32,640]{1,0:T(8,128)}, f32[32,640]{1,0:T(8,128)}) custom-call(f32[64,640]{1,0:T(8,128)} %get-tuple-element.21.a_ref, f32[64,640]{1,0:T(8,128)} %copy-done.14), custom_call_target="tpu_custom_call" | custom-call | flops 163840 | bytes 491520 | tf_op jit(solution)/shard_map/pallas_call | solution.py:161
  159.2 3.3 %collective-permute-start.10 = (f32[32,640]{1,0:T(8,128)}, f32[32,640]{1,0:T(8,128)S(1)}, u32[]{:S(2)}, u32[]{:S(2)}) collective-permute-start(f32[32,640]{1,0:T(8,128)} %get-tuple-element.24), channel_id=1, source_target_pairs={{0,256},{16,80},{32,288},{48,112},{64,320},{80,16},{96,352},{112,4... | collective-permute-start | bytes 245768 | tf_op jit(solution)/shard_map/ppermute | solution.py:221
  162.6 4.7 %collective-permute-done.10.b_ref = f32[32,640]{1,0:T(8,128)S(1)} collective-permute-done((f32[32,640]{1,0:T(8,128)}, f32[32,640]{1,0:T(8,128)S(1)}, u32[]{:S(2)}, u32[]{:S(2)}) %collective-permute-start.10) | collective-permute-done | bytes 81952 | tf_op jit(solution)/shard_map/ppermute | solution.py:221
  167.3 0.6 copy-done.15
  167.9 1.7 shard_map.63
  169.6 0.8 slice.66
  170.4 0.1 broadcast_in_dim.23
  170.5 0.1 reshape.138
  170.6 1.0 multiply_reduce_fusion
  171.6 1.7 convolution_bitcast_fusion
  (39 shorter events, 0.3 us)
Async XLA Ops:
  0.0 67.1 %copy-start = (bf16[1,1,1024,512]{3,2,1,0:T(8,128)(2,1)S(1)}, bf16[1,1,1024,512]{3,2,1,0:T(8,128)(2,1)}, u32[]{:S(2)}) copy-start(bf16[1,1,1024,512]{3,2,1,0:T(8,128)(2,1)} %param.5) | copy-start | bytes 3145732
  0.0 17.5 %collective-permute-start.2 = (bf16[2,2,1,1,2,64,512]{6,5,4,3,2,1,0:T(8,128)(2,1)}, bf16[2,2,1,1,2,64,512]{6,5,4,3,2,1,0:T(8,128)(2,1)S(1)}, u32[]{:S(2)}, u32[]{:S(2)}) collective-permute-start(bf16[2,2,1,1,2,64,512]{6,5,4,3,2,1,0:T(8,128)(2,1)} %param.6), channel_id=1, source_target_pairs={{0,4},{4,8},{8,12},{1,5},{5,9},{9,13},{2,6},{6,10},{10,14},{3,7},{... | collective-permute-start | bytes 1572872 | tf_op jit(solution)/shard_map/ppermute | solution.py:19
  3.6 54.7 %collective-permute-start.1 = (bf16[2,2,1,1,2,64,512]{6,5,4,3,2,1,0:T(8,128)(2,1)}, bf16[2,2,1,1,2,64,512]{6,5,4,3,2,1,0:T(8,128)(2,1)S(1)}, u32[]{:S(2)}, u32[]{:S(2)}) collective-permute-start(bf16[2,2,1,1,2,64,512]{6,5,4,3,2,1,0:T(8,128)(2,1)} %param.6), channel_id=1, source_target_pairs={{1,0},{2,1},{3,2},{5,4},{6,5},{7,6},{9,8},{10,9},{11,10},{13,12},{... | collective-permute-start | bytes 1572872 | tf_op jit(solution)/shard_map/ppermute | solution.py:19
  4.9 53.4 %collective-permute-start = (bf16[2,2,1,1,2,64,512]{6,5,4,3,2,1,0:T(8,128)(2,1)}, bf16[2,2,1,1,2,64,512]{6,5,4,3,2,1,0:T(8,128)(2,1)S(1)}, u32[]{:S(2)}, u32[]{:S(2)}) collective-permute-start(bf16[2,2,1,1,2,64,512]{6,5,4,3,2,1,0:T(8,128)(2,1)} %param.6), channel_id=1, source_target_pairs={{0,1},{1,2},{2,3},{4,5},{5,6},{6,7},{8,9},{9,10},{10,11},{12,13},{... | collective-permute-start | bytes 1572872 | tf_op jit(solution)/shard_map/ppermute | solution.py:19
  14.7 43.6 %collective-permute-start.3 = (bf16[2,2,1,1,2,64,512]{6,5,4,3,2,1,0:T(8,128)(2,1)}, bf16[2,2,1,1,2,64,512]{6,5,4,3,2,1,0:T(8,128)(2,1)S(1)}, u32[]{:S(2)}, u32[]{:S(2)}) collective-permute-start(bf16[2,2,1,1,2,64,512]{6,5,4,3,2,1,0:T(8,128)(2,1)} %param.6), channel_id=1, source_target_pairs={{4,0},{8,4},{12,8},{5,1},{9,5},{13,9},{6,2},{10,6},{14,10},{7,3},{... | collective-permute-start | bytes 1572872 | tf_op jit(solution)/shard_map/ppermute | solution.py:19
  17.5 49.6 %copy-start.8 = (bf16[2,2,1,1,2,64,512]{6,5,4,3,2,1,0:T(8,128)(2,1)}, bf16[2,2,1,1,2,64,512]{6,5,4,3,2,1,0:T(8,128)(2,1)S(1)}, u32[]{:S(2)}) copy-start(bf16[2,2,1,1,2,64,512]{6,5,4,3,2,1,0:T(8,128)(2,1)S(1)} %collective-permute-done.2) | copy-start | bytes 1572868
  58.3 8.8 %copy-start.2 = (bf16[2,2,1,1,2,64,512]{6,5,4,3,2,1,0:T(8,128)(2,1)}, bf16[2,2,1,1,2,64,512]{6,5,4,3,2,1,0:T(8,128)(2,1)S(1)}, u32[]{:S(2)}) copy-start(bf16[2,2,1,1,2,64,512]{6,5,4,3,2,1,0:T(8,128)(2,1)S(1)} %collective-permute-done.1) | copy-start | bytes 1572868
  58.3 8.8 %copy-start.4 = (bf16[2,2,1,1,2,64,512]{6,5,4,3,2,1,0:T(8,128)(2,1)}, bf16[2,2,1,1,2,64,512]{6,5,4,3,2,1,0:T(8,128)(2,1)S(1)}, u32[]{:S(2)}) copy-start(bf16[2,2,1,1,2,64,512]{6,5,4,3,2,1,0:T(8,128)(2,1)S(1)} %collective-permute-done) | copy-start | bytes 1572868
  58.3 8.8 %copy-start.10 = (bf16[2,2,1,1,2,64,512]{6,5,4,3,2,1,0:T(8,128)(2,1)}, bf16[2,2,1,1,2,64,512]{6,5,4,3,2,1,0:T(8,128)(2,1)S(1)}, u32[]{:S(2)}) copy-start(bf16[2,2,1,1,2,64,512]{6,5,4,3,2,1,0:T(8,128)(2,1)S(1)} %collective-permute-done.3) | copy-start | bytes 1572868
  60.2 26.2 %collective-permute-start.5 = (bf16[2,2,1,2,2,64,512]{6,5,4,3,2,1,0:T(8,128)(2,1)}, bf16[2,2,1,2,2,64,512]{6,5,4,3,2,1,0:T(8,128)(2,1)}, u32[]{:S(2)}, u32[]{:S(2)}) collective-permute-start(bf16[2,2,1,2,2,64,512]{6,5,4,3,2,1,0:T(8,128)(2,1)} %constant_dynamic-update-slice_fusion), channel_id=1, source_target_pairs={{4,0},{8,4},{12,8},{5,1},{9,5},{13,9},{6,2},{10,6},{14,10},{7,3},{... | collective-permute-start | bytes 3145736 | tf_op jit(solution)/shard_map/ppermute | solution.py:19
  61.5 26.2 %collective-permute-start.4 = (bf16[2,2,1,2,2,64,512]{6,5,4,3,2,1,0:T(8,128)(2,1)}, bf16[2,2,1,2,2,64,512]{6,5,4,3,2,1,0:T(8,128)(2,1)}, u32[]{:S(2)}, u32[]{:S(2)}) collective-permute-start(bf16[2,2,1,2,2,64,512]{6,5,4,3,2,1,0:T(8,128)(2,1)} %constant_dynamic-update-slice_fusion), channel_id=1, source_target_pairs={{0,4},{4,8},{8,12},{1,5},{5,9},{9,13},{2,6},{6,10},{10,14},{3,7},{... | collective-permute-start | bytes 3145736 | tf_op jit(solution)/shard_map/ppermute | solution.py:19
  67.8 21.2 %copy-start.3 = (bf16[2,2,1,1,2,64,512]{6,5,4,3,2,1,0:T(8,128)(2,1)S(1)}, bf16[2,2,1,1,2,64,512]{6,5,4,3,2,1,0:T(8,128)(2,1)}, u32[]{:S(2)}) copy-start(bf16[2,2,1,1,2,64,512]{6,5,4,3,2,1,0:T(8,128)(2,1)} %copy-done.2) | copy-start | bytes 1572868
  67.8 21.2 %copy-start.5 = (bf16[2,2,1,1,2,64,512]{6,5,4,3,2,1,0:T(8,128)(2,1)S(1)}, bf16[2,2,1,1,2,64,512]{6,5,4,3,2,1,0:T(8,128)(2,1)}, u32[]{:S(2)}) copy-start(bf16[2,2,1,1,2,64,512]{6,5,4,3,2,1,0:T(8,128)(2,1)} %copy-done.4) | copy-start | bytes 1572868
  67.8 21.2 %copy-start.7 = (bf16[2,2,1,1,2,64,512]{6,5,4,3,2,1,0:T(8,128)(2,1)S(1)}, bf16[2,2,1,1,2,64,512]{6,5,4,3,2,1,0:T(8,128)(2,1)}, u32[]{:S(2)}) copy-start(bf16[2,2,1,1,2,64,512]{6,5,4,3,2,1,0:T(8,128)(2,1)} %param.6) | copy-start | bytes 1572868
  67.8 21.2 %copy-start.9 = (bf16[2,2,1,1,2,64,512]{6,5,4,3,2,1,0:T(8,128)(2,1)S(1)}, bf16[2,2,1,1,2,64,512]{6,5,4,3,2,1,0:T(8,128)(2,1)}, u32[]{:S(2)}) copy-start(bf16[2,2,1,1,2,64,512]{6,5,4,3,2,1,0:T(8,128)(2,1)} %copy-done.8) | copy-start | bytes 1572868
  67.8 21.2 %copy-start.11 = (bf16[2,2,1,1,2,64,512]{6,5,4,3,2,1,0:T(8,128)(2,1)S(1)}, bf16[2,2,1,1,2,64,512]{6,5,4,3,2,1,0:T(8,128)(2,1)}, u32[]{:S(2)}) copy-start(bf16[2,2,1,1,2,64,512]{6,5,4,3,2,1,0:T(8,128)(2,1)} %copy-done.10) | copy-start | bytes 1572868
  101.7 10.2 %collective-permute-start.6 = (f32[512,640]{1,0:T(8,128)}, f32[512,640]{1,0:T(8,128)S(1)}, u32[]{:S(2)}, u32[]{:S(2)}) collective-permute-start(f32[512,640]{1,0:T(8,128)} %shard_map.56), channel_id=1, source_target_pairs={{0,16},{16,0},{32,48},{48,32},{64,80},{80,64},{96,112},{112,96},{1... | collective-permute-start | bytes 3932168 | tf_op jit(solution)/shard_map/ppermute | solution.py:209
  111.9 1.1 copy-start.1
  115.7 12.7 %collective-permute-start.7 = (f32[256,640]{1,0:T(8,128)}, f32[256,640]{1,0:T(8,128)S(1)}, u32[]{:S(2)}, u32[]{:S(2)}) collective-permute-start(f32[256,640]{1,0:T(8,128)} %shard_map.59), channel_id=1, source_target_pairs={{0,32},{16,144},{32,0},{48,176},{64,96},{80,208},{96,64},{112,240}... | collective-permute-start | bytes 1966088 | tf_op jit(solution)/shard_map/ppermute | solution.py:212
  124.9 46.7 %copy-start.12 = (bf16[512,512]{1,0:T(8,128)(2,1)S(1)}, bf16[512,512]{1,0:T(8,128)(2,1)}, u32[]{:S(2)}) copy-start(bf16[512,512]{1,0:T(8,128)(2,1)} %param.9) | copy-start | bytes 1572868
  128.4 0.9 copy-start.6
  132.1 9.2 %collective-permute-start.8 = (f32[128,640]{1,0:T(8,128)}, f32[128,640]{1,0:T(8,128)S(1)}, u32[]{:S(2)}, u32[]{:S(2)}) collective-permute-start(f32[128,640]{1,0:T(8,128)} %get-tuple-element.20), channel_id=1, source_target_pairs={{0,128},{16,48},{32,160},{48,16},{64,192},{80,112},{96,224},{112,8... | collective-permute-start | bytes 983048 | tf_op jit(solution)/shard_map/ppermute | solution.py:221
  141.2 0.7 copy-start.13
  144.1 12.6 %collective-permute-start.9 = (f32[64,640]{1,0:T(8,128)}, f32[64,640]{1,0:T(8,128)S(1)}, u32[]{:S(2)}, u32[]{:S(2)}) collective-permute-start(f32[64,640]{1,0:T(8,128)} %get-tuple-element.22), channel_id=1, source_target_pairs={{0,64},{16,272},{32,96},{48,304},{64,0},{80,336},{96,32},{112,368}... | collective-permute-start | bytes 491528 | tf_op jit(solution)/shard_map/ppermute | solution.py:221
  156.7 0.7 copy-start.14
  159.2 8.0 %collective-permute-start.10 = (f32[32,640]{1,0:T(8,128)}, f32[32,640]{1,0:T(8,128)S(1)}, u32[]{:S(2)}, u32[]{:S(2)}) collective-permute-start(f32[32,640]{1,0:T(8,128)} %get-tuple-element.24), channel_id=1, source_target_pairs={{0,256},{16,80},{32,288},{48,112},{64,320},{80,16},{96,352},{112,4... | collective-permute-start | bytes 245768 | tf_op jit(solution)/shard_map/ppermute | solution.py:221
  167.3 0.6 copy-start.15

commit v12 on v11

--- a/solution.py
+++ b/solution.py
@@ -204,15 +204,20 @@
     groups = lax.axis_size("tm")
     nbits = groups.bit_length() - 1
     qtok = query_rows.shape[0]
-    half, quarter = qtok // 2, qtok // 4
+    half, quarter, eighth = qtok // 2, qtok // 4, qtok // 8
     second = attention(query_rows[half:], hood, listed, keep)
-    got_first = lax.ppermute(second, "tm", step_pairs(nbits, 0))
+    got_1 = lax.ppermute(second, "tm", step_pairs(nbits, 0))
     sent = attention(query_rows[quarter:half], hood, listed, keep)
-    (sent,) = merge(sent, got_first, False, quarter)
-    second = lax.ppermute(sent, "tm", step_pairs(nbits, 1))
-    first = attention(query_rows[:quarter], hood, listed, keep)
-    (first,) = merge(first, got_first, False, 0)
-    for i in range(1, nbits):
+    (sent,) = merge(sent, got_1, False, quarter)
+    got_2 = lax.ppermute(sent, "tm", step_pairs(nbits, 1))
+    sent = attention(query_rows[eighth:quarter], hood, listed, keep)
+    (sent,) = merge(sent, got_1, False, eighth)
+    (sent,) = merge(sent, got_2, False, eighth)
+    second = lax.ppermute(sent, "tm", step_pairs(nbits, 2))
+    first = attention(query_rows[:eighth], hood, listed, keep)
+    (first,) = merge(first, got_1, False, 0)
+    (first,) = merge(first, got_2, False, 0)
+    for i in range(2, nbits):
         last = i == nbits - 1
         outs = merge(first, second, not last)
         if last:

time: 176 us -> 179 us (1.017)
  the two profiles are of different devices: /device:TPU:6 before, /device:TPU:408 now
where the time goes in v12:
time: 179 us; the launch traced here: 178 us
  waiting for transfers between devices  78.6 us (44%)
  Pallas kernels  46.3 us (26%)
  starting transfers between devices  33.7 us (19%)
  local copies, waits for them, and re-layouts  13 us (7%)
  other arithmetic  4.79 us (3%)
    ppermute x6, waiting for transfers between devices, shifted(): return lax.ppermute(array, axis, pairs)  66.1 us
    pallas_call x4, Pallas kernels, attention(): pl.pallas_call(attention_kernel, grid_spec=grid_spec, out_shape=jax.Shape...  29.1 us
    ppermute x6, starting transfers between devices, shifted(): return lax.ppermute(array, axis, pairs)  19.3 us
    pallas_call x8, Pallas kernels, merge(): pl.pallas_call(merge_kernel, grid=(1,), in_specs=[pl.BlockSpec((rows, col...  17.2 us
    ppermute x2, waiting for transfers between devices, tree_reduce(): second = lax.ppermute(second, 'tm', step_pairs(nbits, i + 1))  10.6 us
    ppermute x2, starting transfers between devices, tree_reduce(): second = lax.ppermute(second, 'tm', step_pairs(nbits, i + 1))  7.02 us
    unnamed x33, local copies, waits for them, and re-layouts  4.97 us
  transfers between devices with their start and end apart: 11, of which 8 were waited for; matrix products, arithmetic and copies ran while one was open for 3% of the time, Pallas kernels for 14%

profile of v12, /device:TPU:408, one launch (start us, length us, event | category | flops | bytes accessed | tf_op | source)
XLA Modules:
  0.0 178.4 jit_solution(15119860689988992591)
XLA Ops:
  0.0 1.4 collective-permute-start.2
  1.4 5.5 %collective-permute-start.1 = (bf16[2,2,1,1,2,64,512]{6,5,4,3,2,1,0:T(8,128)(2,1)}, bf16[2,2,1,1,2,64,512]{6,5,4,3,2,1,0:T(8,128)(2,1)S(1)}, u32[]{:S(2)}, u32[]{:S(2)}) collective-permute-start(bf16[2,2,1,1,2,64,512]{6,5,4,3,2,1,0:T(8,128)(2,1)} %param.6), channel_id=1, source_target_pairs={{1,0},{2,1},{3,2},{5,4},{6,5},{7,6},{9,8},{10,9},{11,10},{13,12},{... | collective-permute-start | bytes 1572872 | tf_op jit(solution)/shard_map/ppermute | solution.py:19
  6.9 1.3 collective-permute-start
  8.2 4.6 %collective-permute-start.3 = (bf16[2,2,1,1,2,64,512]{6,5,4,3,2,1,0:T(8,128)(2,1)}, bf16[2,2,1,1,2,64,512]{6,5,4,3,2,1,0:T(8,128)(2,1)S(1)}, u32[]{:S(2)}, u32[]{:S(2)}) collective-permute-start(bf16[2,2,1,1,2,64,512]{6,5,4,3,2,1,0:T(8,128)(2,1)} %param.6), channel_id=1, source_target_pairs={{4,0},{8,4},{12,8},{5,1},{9,5},{13,9},{6,2},{10,6},{14,10},{7,3},{... | collective-permute-start | bytes 1572872 | tf_op jit(solution)/shard_map/ppermute | solution.py:19
  12.9 0.7 fusion.1
  13.6 0.7 convert_element_type.12.refs_16_
  14.3 1.6 collective-permute-done.2
  15.9 36.2 %collective-permute-done.1 = bf16[2,2,1,1,2,64,512]{6,5,4,3,2,1,0:T(8,128)(2,1)S(1)} collective-permute-done((bf16[2,2,1,1,2,64,512]{6,5,4,3,2,1,0:T(8,128)(2,1)}, bf16[2,2,1,1,2,64,512]{6,5,4,3,2,1,0:T(8,128)(2,1)S(1)}, u32[]{:S(2)}, u32[]{:S(2)}) %collective-permute-start.1) | collective-permute-done | bytes 524320 | tf_op jit(solution)/shard_map/ppermute | solution.py:19
  52.1 7.3 %collective-permute-done = bf16[2,2,1,1,2,64,512]{6,5,4,3,2,1,0:T(8,128)(2,1)S(1)} collective-permute-done((bf16[2,2,1,1,2,64,512]{6,5,4,3,2,1,0:T(8,128)(2,1)}, bf16[2,2,1,1,2,64,512]{6,5,4,3,2,1,0:T(8,128)(2,1)S(1)}, u32[]{:S(2)}, u32[]{:S(2)}) %collective-permute-start) | collective-permute-done | bytes 524320 | tf_op jit(solution)/shard_map/ppermute | solution.py:19
  59.4 1.0 constant_dynamic-update-slice_fusion.1
  60.4 0.9 constant_dynamic-update-slice_fusion
  61.2 5.2 %collective-permute-start.5 = (bf16[2,2,1,2,2,64,512]{6,5,4,3,2,1,0:T(8,128)(2,1)}, bf16[2,2,1,2,2,64,512]{6,5,4,3,2,1,0:T(8,128)(2,1)}, u32[]{:S(2)}, u32[]{:S(2)}) collective-permute-start(bf16[2,2,1,2,2,64,512]{6,5,4,3,2,1,0:T(8,128)(2,1)} %constant_dynamic-update-slice_fusion), channel_id=1, source_target_pairs={{4,0},{8,4},{12,8},{5,1},{9,5},{13,9},{6,2},{10,6},{14,10},{7,3},{... | collective-permute-start | bytes 3145736 | tf_op jit(solution)/shard_map/ppermute | solution.py:19
  66.5 1.3 collective-permute-start.4
  68.9 0.8 slice.71
  69.7 17.1 %collective-permute-done.5 = bf16[2,2,1,2,2,64,512]{6,5,4,3,2,1,0:T(8,128)(2,1)} collective-permute-done((bf16[2,2,1,2,2,64,512]{6,5,4,3,2,1,0:T(8,128)(2,1)}, bf16[2,2,1,2,2,64,512]{6,5,4,3,2,1,0:T(8,128)(2,1)}, u32[]{:S(2)}, u32[]{:S(2)}) %collective-permute-start.5) | collective-permute-done | bytes 1048608 | tf_op jit(solution)/shard_map/ppermute | solution.py:19
  86.8 1.3 fusion.5
  88.1 3.8 %collective-permute-done.4 = bf16[2,2,1,2,2,64,512]{6,5,4,3,2,1,0:T(8,128)(2,1)} collective-permute-done((bf16[2,2,1,2,2,64,512]{6,5,4,3,2,1,0:T(8,128)(2,1)}, bf16[2,2,1,2,2,64,512]{6,5,4,3,2,1,0:T(8,128)(2,1)}, u32[]{:S(2)}, u32[]{:S(2)}) %collective-permute-start.4) | collective-permute-done | bytes 1048608 | tf_op jit(solution)/shard_map/ppermute | solution.py:19
  91.9 1.3 fusion.4
  93.2 2.8 %maximum_maximum_fusion = bf16[2,2,3,3,2,64,512]{6,5,4,3,2,1,0:T(8,128)(2,1)} fusion(bf16[2,2,1,1,2,64,512]{6,5,4,3,2,1,0:T(8,128)(2,1)S(1)} %get-tuple-element.26, bf16[2,2,1,1,2,64,512]{6,5,4,3,2,1,0:T(8,128)(2,1)S(1)} %copy-done.11, bf16[2,2,1,1,2,64,512]{6,5,4,3,2,1,0:T(8,128)(2,1)S(1)} %get-tuple-element.25, ...), kind=kLoop, calls=%fused_computation.1 | loop fusion | flops 18874368 | bytes 9437184 | tf_op jit(solution)/shard_map/concatenate | solution.py:34
  96.0 9.9 %shard_map.56 = f32[512,640]{1,0:T(8,128)} custom-call(s32[8]{0:T(128)} %bitcast.87, bf16[512,512]{1,0:T(8,128)(2,1)} %bitcast.83, bf16[2,2,18,64,512]{4,3,2,1,0:T(8,128)(2,1)} %bitcast.19, bf16[2,2,18,64,512]{4,3,2,1,0:T(8,128)(2,1)} %bitcast.20, bf16[2,2,18,64,512]{4,3,2,1,0:T(8,128)(2,1)} %bitcast.21, bf16[2,2,18,64,512]{4,3,2,1,0:T(8,128)(2,1)} %bitcast.22, ...), custom_call_target="tpu_custom_call" | custom-call | flops 2147483648 | bytes 3670016 | tf_op jit(solution)/shard_map/pallas_call | solution.py:105
  106.0 2.1 %collective-permute-start.6 = (f32[512,640]{1,0:T(8,128)}, f32[512,640]{1,0:T(8,128)S(1)}, u32[]{:S(2)}, u32[]{:S(2)}) collective-permute-start(f32[512,640]{1,0:T(8,128)} %shard_map.56), channel_id=1, source_target_pairs={{0,16},{16,0},{32,48},{48,32},{64,80},{80,64},{96,112},{112,96},{1... | collective-permute-start | bytes 3932168 | tf_op jit(solution)/shard_map/ppermute | solution.py:209
  108.1 0.7 slice.72
  108.8 7.2 %shard_map.58.a_ref = f32[256,640]{1,0:T(8,128)} custom-call(s32[8]{0:T(128)} %bitcast.88, bf16[256,512]{1,0:T(8,128)(2,1)} %bitcast.84, bf16[2,2,18,64,512]{4,3,2,1,0:T(8,128)(2,1)} %bitcast.50, bf16[2,2,18,64,512]{4,3,2,1,0:T(8,128)(2,1)} %bitcast.36, bf16[2,2,18,64,512]{4,3,2,1,0:T(8,128)(2,1)} %bitcast.37, bf16[2,2,18,64,512]{4,3,2,1,0:T(8,128)(2,1)} %bitcast.38, ...), custom_call_target="tpu_custom_call" | custom-call | flops 1073741824 | bytes 2883584 | tf_op jit(solution)/shard_map/pallas_call | solution.py:105
  116.0 1.1 copy-done.1
  117.1 2.8 %shard_map.59 = f32[256,640]{1,0:T(8,128)} custom-call(f32[256,640]{1,0:T(8,128)} %shard_map.58.a_ref, f32[512,640]{1,0:T(8,128)} %copy-done.1), custom_call_target="tpu_custom_call" | custom-call | flops 655360 | bytes 1966080 | tf_op jit(solution)/shard_map/pallas_call | solution.py:161
  119.9 1.9 %collective-permute-start.7 = (f32[256,640]{1,0:T(8,128)}, f32[256,640]{1,0:T(8,128)S(1)}, u32[]{:S(2)}, u32[]{:S(2)}) collective-permute-start(f32[256,640]{1,0:T(8,128)} %shard_map.59), channel_id=1, source_target_pairs={{0,32},{16,144},{32,0},{48,176},{64,96},{80,208},{96,64},{112,240}... | collective-permute-start | bytes 1966088 | tf_op jit(solution)/shard_map/ppermute | solution.py:212
  121.8 0.7 fusion.3
  122.5 6.0 %shard_map.61.a_ref = f32[128,640]{1,0:T(8,128)} custom-call(s32[8]{0:T(128)} %bitcast.89, bf16[128,512]{1,0:T(8,128)(2,1)} %bitcast.86, bf16[2,2,18,64,512]{4,3,2,1,0:T(8,128)(2,1)} %bitcast.59, bf16[2,2,18,64,512]{4,3,2,1,0:T(8,128)(2,1)} %bitcast.52, bf16[2,2,18,64,512]{4,3,2,1,0:T(8,128)(2,1)} %bitcast.53, bf16[2,2,18,64,512]{4,3,2,1,0:T(8,128)(2,1)} %bitcast.54, ...), custom_call_target="tpu_custom_call" | custom-call | flops 536870912 | bytes 2490368 | tf_op jit(solution)/shard_map/pallas_call | solution.py:105
  128.5 2.2 %shard_map.62.a_ref = f32[128,640]{1,0:T(8,128)} custom-call(f32[128,640]{1,0:T(8,128)} %shard_map.61.a_ref, f32[512,640]{1,0:T(8,128)} %copy-done.1), custom_call_target="tpu_custom_call" | custom-call | flops 327680 | bytes 983040 | tf_op jit(solution)/shard_map/pallas_call | solution.py:161
  130.6 1.9 %collective-permute-done.7.b_ref = f32[256,640]{1,0:T(8,128)S(1)} collective-permute-done((f32[256,640]{1,0:T(8,128)}, f32[256,640]{1,0:T(8,128)S(1)}, u32[]{:S(2)}, u32[]{:S(2)}) %collective-permute-start.7) | collective-permute-done | bytes 655392 | tf_op jit(solution)/shard_map/ppermute | solution.py:212
  132.5 0.8 copy-done.2
  133.4 2.2 %shard_map.63 = f32[128,640]{1,0:T(8,128)} custom-call(f32[128,640]{1,0:T(8,128)} %shard_map.62.a_ref, f32[256,640]{1,0:T(8,128)} %copy-done.2), custom_call_target="tpu_custom_call" | custom-call | flops 327680 | bytes 983040 | tf_op jit(solution)/shard_map/pallas_call | solution.py:161
  135.6 3.4 %collective-permute-start.8 = (f32[128,640]{1,0:T(8,128)}, f32[128,640]{1,0:T(8,128)S(1)}, u32[]{:S(2)}, u32[]{:S(2)}) collective-permute-start(f32[128,640]{1,0:T(8,128)} %shard_map.63), channel_id=1, source_target_pairs={{0,128},{16,48},{32,160},{48,16},{64,192},{80,112},{96,224},{112,8... | collective-permute-start | bytes 983048 | tf_op jit(solution)/shard_map/ppermute | solution.py:216
  138.9 6.0 %shard_map.55.a_ref = f32[128,640]{1,0:T(8,128)} custom-call(s32[8]{0:T(128)} %bitcast.90, bf16[128,512]{1,0:T(8,128)(2,1)} %bitcast.85, bf16[2,2,18,64,512]{4,3,2,1,0:T(8,128)(2,1)} %bitcast.67, bf16[2,2,18,64,512]{4,3,2,1,0:T(8,128)(2,1)} %bitcast.68, bf16[2,2,18,64,512]{4,3,2,1,0:T(8,128)(2,1)} %bitcast.69, bf16[2,2,18,64,512]{4,3,2,1,0:T(8,128)(2,1)} %bitcast.70, ...), custom_call_target="tpu_custom_call" | custom-call | flops 536870912 | bytes 2490368 | tf_op jit(solution)/shard_map/pallas_call | solution.py:105
  144.9 2.2 %shard_map.57.a_ref = f32[128,640]{1,0:T(8,128)} custom-call(f32[128,640]{1,0:T(8,128)} %shard_map.55.a_ref, f32[512,640]{1,0:T(8,128)} %copy-done.1), custom_call_target="tpu_custom_call" | custom-call | flops 327680 | bytes 983040 | tf_op jit(solution)/shard_map/pallas_call | solution.py:161
  147.2 2.2 %shard_map.60.a_ref = f32[128,640]{1,0:T(8,128)} custom-call(f32[128,640]{1,0:T(8,128)} %shard_map.57.a_ref, f32[256,640]{1,0:T(8,128)} %copy-done.2), custom_call_target="tpu_custom_call" | custom-call | flops 327680 | bytes 983040 | tf_op jit(solution)/shard_map/pallas_call | solution.py:161
  149.3 0.7 copy-done.13
  150.1 2.2 %shard_map.64 = (f32[64,640]{1,0:T(8,128)}, f32[64,640]{1,0:T(8,128)}) custom-call(f32[128,640]{1,0:T(8,128)} %shard_map.60.a_ref, f32[128,640]{1,0:T(8,128)} %copy-done.13), custom_call_target="tpu_custom_call" | custom-call | flops 327680 | bytes 983040 | tf_op jit(solution)/shard_map/pallas_call | solution.py:161
  152.2 2.4 %collective-permute-start.9 = (f32[64,640]{1,0:T(8,128)}, f32[64,640]{1,0:T(8,128)S(1)}, u32[]{:S(2)}, u32[]{:S(2)}) collective-permute-start(f32[64,640]{1,0:T(8,128)} %get-tuple-element.18), channel_id=1, source_target_pairs={{0,64},{16,272},{32,96},{48,304},{64,0},{80,336},{96,32},{112,368}... | collective-permute-start | bytes 491528 | tf_op jit(solution)/shard_map/ppermute | solution.py:226
  154.6 7.2 %collective-permute-done.9.b_ref = f32[64,640]{1,0:T(8,128)S(1)} collective-permute-done((f32[64,640]{1,0:T(8,128)}, f32[64,640]{1,0:T(8,128)S(1)}, u32[]{:S(2)}, u32[]{:S(2)}) %collective-permute-start.9) | collective-permute-done | bytes 163872 | tf_op jit(solution)/shard_map/ppermute | solution.py:226
  161.8 0.7 copy-done.14
  162.5 1.9 %shard_map.65 = (f32[32,640]{1,0:T(8,128)}, f32[32,640]{1,0:T(8,128)}) custom-call(f32[64,640]{1,0:T(8,128)} %get-tuple-element.17.a_ref, f32[64,640]{1,0:T(8,128)} %copy-done.14), custom_call_target="tpu_custom_call" | custom-call | flops 163840 | bytes 491520 | tf_op jit(solution)/shard_map/pallas_call | solution.py:161
  164.4 4.6 %collective-permute-start.10 = (f32[32,640]{1,0:T(8,128)}, f32[32,640]{1,0:T(8,128)S(1)}, u32[]{:S(2)}, u32[]{:S(2)}) collective-permute-start(f32[32,640]{1,0:T(8,128)} %get-tuple-element.20), channel_id=1, source_target_pairs={{0,256},{16,80},{32,288},{48,112},{64,320},{80,16},{96,352},{112,4... | collective-permute-start | bytes 245768 | tf_op jit(solution)/shard_map/ppermute | solution.py:226
  169.0 3.4 %collective-permute-done.10.b_ref = f32[32,640]{1,0:T(8,128)S(1)} collective-permute-done((f32[32,640]{1,0:T(8,128)}, f32[32,640]{1,0:T(8,128)S(1)}, u32[]{:S(2)}, u32[]{:S(2)}) %collective-permute-start.10) | collective-permute-done | bytes 81952 | tf_op jit(solution)/shard_map/ppermute | solution.py:226
  173.0 1.7 shard_map.66
  174.8 0.8 slice.75
  175.7 1.0 multiply_reduce_fusion
  176.7 1.7 convolution_bitcast_fusion
  (43 shorter events, 1.9 us)
Async XLA Ops:
  0.0 67.9 %copy-start = (bf16[1,1,1024,512]{3,2,1,0:T(8,128)(2,1)S(1)}, bf16[1,1,1024,512]{3,2,1,0:T(8,128)(2,1)}, u32[]{:S(2)}) copy-start(bf16[1,1,1024,512]{3,2,1,0:T(8,128)(2,1)} %param.5) | copy-start | bytes 3145732
  0.0 15.9 %collective-permute-start.2 = (bf16[2,2,1,1,2,64,512]{6,5,4,3,2,1,0:T(8,128)(2,1)}, bf16[2,2,1,1,2,64,512]{6,5,4,3,2,1,0:T(8,128)(2,1)S(1)}, u32[]{:S(2)}, u32[]{:S(2)}) collective-permute-start(bf16[2,2,1,1,2,64,512]{6,5,4,3,2,1,0:T(8,128)(2,1)} %param.6), channel_id=1, source_target_pairs={{0,4},{4,8},{8,12},{1,5},{5,9},{9,13},{2,6},{6,10},{10,14},{3,7},{... | collective-permute-start | bytes 1572872 | tf_op jit(solution)/shard_map/ppermute | solution.py:19
  1.4 50.7 %collective-permute-start.1 = (bf16[2,2,1,1,2,64,512]{6,5,4,3,2,1,0:T(8,128)(2,1)}, bf16[2,2,1,1,2,64,512]{6,5,4,3,2,1,0:T(8,128)(2,1)S(1)}, u32[]{:S(2)}, u32[]{:S(2)}) collective-permute-start(bf16[2,2,1,1,2,64,512]{6,5,4,3,2,1,0:T(8,128)(2,1)} %param.6), channel_id=1, source_target_pairs={{1,0},{2,1},{3,2},{5,4},{6,5},{7,6},{9,8},{10,9},{11,10},{13,12},{... | collective-permute-start | bytes 1572872 | tf_op jit(solution)/shard_map/ppermute | solution.py:19
  6.9 52.5 %collective-permute-start = (bf16[2,2,1,1,2,64,512]{6,5,4,3,2,1,0:T(8,128)(2,1)}, bf16[2,2,1,1,2,64,512]{6,5,4,3,2,1,0:T(8,128)(2,1)S(1)}, u32[]{:S(2)}, u32[]{:S(2)}) collective-permute-start(bf16[2,2,1,1,2,64,512]{6,5,4,3,2,1,0:T(8,128)(2,1)} %param.6), channel_id=1, source_target_pairs={{0,1},{1,2},{2,3},{4,5},{5,6},{6,7},{8,9},{9,10},{10,11},{12,13},{... | collective-permute-start | bytes 1572872 | tf_op jit(solution)/shard_map/ppermute | solution.py:19
  8.2 51.2 %collective-permute-start.3 = (bf16[2,2,1,1,2,64,512]{6,5,4,3,2,1,0:T(8,128)(2,1)}, bf16[2,2,1,1,2,64,512]{6,5,4,3,2,1,0:T(8,128)(2,1)S(1)}, u32[]{:S(2)}, u32[]{:S(2)}) collective-permute-start(bf16[2,2,1,1,2,64,512]{6,5,4,3,2,1,0:T(8,128)(2,1)} %param.6), channel_id=1, source_target_pairs={{4,0},{8,4},{12,8},{5,1},{9,5},{13,9},{6,2},{10,6},{14,10},{7,3},{... | collective-permute-start | bytes 1572872 | tf_op jit(solution)/shard_map/ppermute | solution.py:19
  15.9 52.0 %copy-start.8 = (bf16[2,2,1,1,2,64,512]{6,5,4,3,2,1,0:T(8,128)(2,1)}, bf16[2,2,1,1,2,64,512]{6,5,4,3,2,1,0:T(8,128)(2,1)S(1)}, u32[]{:S(2)}) copy-start(bf16[2,2,1,1,2,64,512]{6,5,4,3,2,1,0:T(8,128)(2,1)S(1)} %collective-permute-done.2) | copy-start | bytes 1572868
  52.1 15.8 %copy-start.3 = (bf16[2,2,1,1,2,64,512]{6,5,4,3,2,1,0:T(8,128)(2,1)}, bf16[2,2,1,1,2,64,512]{6,5,4,3,2,1,0:T(8,128)(2,1)S(1)}, u32[]{:S(2)}) copy-start(bf16[2,2,1,1,2,64,512]{6,5,4,3,2,1,0:T(8,128)(2,1)S(1)} %collective-permute-done.1) | copy-start | bytes 1572868
  59.4 8.5 %copy-start.5 = (bf16[2,2,1,1,2,64,512]{6,5,4,3,2,1,0:T(8,128)(2,1)}, bf16[2,2,1,1,2,64,512]{6,5,4,3,2,1,0:T(8,128)(2,1)S(1)}, u32[]{:S(2)}) copy-start(bf16[2,2,1,1,2,64,512]{6,5,4,3,2,1,0:T(8,128)(2,1)S(1)} %collective-permute-done) | copy-start | bytes 1572868
  59.4 8.5 %copy-start.10 = (bf16[2,2,1,1,2,64,512]{6,5,4,3,2,1,0:T(8,128)(2,1)}, bf16[2,2,1,1,2,64,512]{6,5,4,3,2,1,0:T(8,128)(2,1)S(1)}, u32[]{:S(2)}) copy-start(bf16[2,2,1,1,2,64,512]{6,5,4,3,2,1,0:T(8,128)(2,1)S(1)} %collective-permute-done.3) | copy-start | bytes 1572868
  61.2 25.6 %collective-permute-start.5 = (bf16[2,2,1,2,2,64,512]{6,5,4,3,2,1,0:T(8,128)(2,1)}, bf16[2,2,1,2,2,64,512]{6,5,4,3,2,1,0:T(8,128)(2,1)}, u32[]{:S(2)}, u32[]{:S(2)}) collective-permute-start(bf16[2,2,1,2,2,64,512]{6,5,4,3,2,1,0:T(8,128)(2,1)} %constant_dynamic-update-slice_fusion), channel_id=1, source_target_pairs={{4,0},{8,4},{12,8},{5,1},{9,5},{13,9},{6,2},{10,6},{14,10},{7,3},{... | collective-permute-start | bytes 3145736 | tf_op jit(solution)/shard_map/ppermute | solution.py:19
  66.5 25.4 %collective-permute-start.4 = (bf16[2,2,1,2,2,64,512]{6,5,4,3,2,1,0:T(8,128)(2,1)}, bf16[2,2,1,2,2,64,512]{6,5,4,3,2,1,0:T(8,128)(2,1)}, u32[]{:S(2)}, u32[]{:S(2)}) collective-permute-start(bf16[2,2,1,2,2,64,512]{6,5,4,3,2,1,0:T(8,128)(2,1)} %constant_dynamic-update-slice_fusion), channel_id=1, source_target_pairs={{0,4},{4,8},{8,12},{1,5},{5,9},{9,13},{2,6},{6,10},{10,14},{3,7},{... | collective-permute-start | bytes 3145736 | tf_op jit(solution)/shard_map/ppermute | solution.py:19
  68.5 24.6 %copy-start.4 = (bf16[2,2,1,1,2,64,512]{6,5,4,3,2,1,0:T(8,128)(2,1)S(1)}, bf16[2,2,1,1,2,64,512]{6,5,4,3,2,1,0:T(8,128)(2,1)}, u32[]{:S(2)}) copy-start(bf16[2,2,1,1,2,64,512]{6,5,4,3,2,1,0:T(8,128)(2,1)} %copy-done.3) | copy-start | bytes 1572868
  68.6 24.6 %copy-start.6 = (bf16[2,2,1,1,2,64,512]{6,5,4,3,2,1,0:T(8,128)(2,1)S(1)}, bf16[2,2,1,1,2,64,512]{6,5,4,3,2,1,0:T(8,128)(2,1)}, u32[]{:S(2)}) copy-start(bf16[2,2,1,1,2,64,512]{6,5,4,3,2,1,0:T(8,128)(2,1)} %copy-done.5) | copy-start | bytes 1572868
  68.6 24.6 %copy-start.7 = (bf16[2,2,1,1,2,64,512]{6,5,4,3,2,1,0:T(8,128)(2,1)S(1)}, bf16[2,2,1,1,2,64,512]{6,5,4,3,2,1,0:T(8,128)(2,1)}, u32[]{:S(2)}) copy-start(bf16[2,2,1,1,2,64,512]{6,5,4,3,2,1,0:T(8,128)(2,1)} %param.6) | copy-start | bytes 1572868
  68.6 24.6 %copy-start.9 = (bf16[2,2,1,1,2,64,512]{6,5,4,3,2,1,0:T(8,128)(2,1)S(1)}, bf16[2,2,1,1,2,64,512]{6,5,4,3,2,1,0:T(8,128)(2,1)}, u32[]{:S(2)}) copy-start(bf16[2,2,1,1,2,64,512]{6,5,4,3,2,1,0:T(8,128)(2,1)} %copy-done.8) | copy-start | bytes 1572868
  68.6 24.6 %copy-start.11 = (bf16[2,2,1,1,2,64,512]{6,5,4,3,2,1,0:T(8,128)(2,1)S(1)}, bf16[2,2,1,1,2,64,512]{6,5,4,3,2,1,0:T(8,128)(2,1)}, u32[]{:S(2)}) copy-start(bf16[2,2,1,1,2,64,512]{6,5,4,3,2,1,0:T(8,128)(2,1)} %copy-done.10) | copy-start | bytes 1572868
  106.0 10.0 %collective-permute-start.6 = (f32[512,640]{1,0:T(8,128)}, f32[512,640]{1,0:T(8,128)S(1)}, u32[]{:S(2)}, u32[]{:S(2)}) collective-permute-start(f32[512,640]{1,0:T(8,128)} %shard_map.56), channel_id=1, source_target_pairs={{0,16},{16,0},{32,48},{48,32},{64,80},{80,64},{96,112},{112,96},{1... | collective-permute-start | bytes 3932168 | tf_op jit(solution)/shard_map/ppermute | solution.py:209
  116.0 1.1 copy-start.1
  119.9 12.7 %collective-permute-start.7 = (f32[256,640]{1,0:T(8,128)}, f32[256,640]{1,0:T(8,128)S(1)}, u32[]{:S(2)}, u32[]{:S(2)}) collective-permute-start(f32[256,640]{1,0:T(8,128)} %shard_map.59), channel_id=1, source_target_pairs={{0,32},{16,144},{32,0},{48,176},{64,96},{80,208},{96,64},{112,240}... | collective-permute-start | bytes 1966088 | tf_op jit(solution)/shard_map/ppermute | solution.py:212
  132.5 0.8 copy-start.2
  135.6 13.8 %collective-permute-start.8 = (f32[128,640]{1,0:T(8,128)}, f32[128,640]{1,0:T(8,128)S(1)}, u32[]{:S(2)}, u32[]{:S(2)}) collective-permute-start(f32[128,640]{1,0:T(8,128)} %shard_map.63), channel_id=1, source_target_pairs={{0,128},{16,48},{32,160},{48,16},{64,192},{80,112},{96,224},{112,8... | collective-permute-start | bytes 983048 | tf_op jit(solution)/shard_map/ppermute | solution.py:216
  144.9 31.8 %copy-start.12 = (bf16[512,512]{1,0:T(8,128)(2,1)S(1)}, bf16[512,512]{1,0:T(8,128)(2,1)}, u32[]{:S(2)}) copy-start(bf16[512,512]{1,0:T(8,128)(2,1)} %param.9) | copy-start | bytes 1572868
  149.3 0.7 copy-start.13
  152.2 9.6 %collective-permute-start.9 = (f32[64,640]{1,0:T(8,128)}, f32[64,640]{1,0:T(8,128)S(1)}, u32[]{:S(2)}, u32[]{:S(2)}) collective-permute-start(f32[64,640]{1,0:T(8,128)} %get-tuple-element.18), channel_id=1, source_target_pairs={{0,64},{16,272},{32,96},{48,304},{64,0},{80,336},{96,32},{112,368}... | collective-permute-start | bytes 491528 | tf_op jit(solution)/shard_map/ppermute | solution.py:226
  161.8 0.7 copy-start.14
  164.4 8.0 %collective-permute-start.10 = (f32[32,640]{1,0:T(8,128)}, f32[32,640]{1,0:T(8,128)S(1)}, u32[]{:S(2)}, u32[]{:S(2)}) collective-permute-start(f32[32,640]{1,0:T(8,128)} %get-tuple-element.20), channel_id=1, source_target_pairs={{0,256},{16,80},{32,288},{48,112},{64,320},{80,16},{96,352},{112,4... | collective-permute-start | bytes 245768 | tf_op jit(solution)/shard_map/ppermute | solution.py:226
  172.4 0.6 copy-start.15

commit v13 on v11

--- a/solution.py
+++ b/solution.py
@@ -173,6 +173,51 @@
     )(kept, got)
 
 
+def finish_kernel(a_ref, b_ref, w_ref, out_ref):
+    tmp = a_ref.shape
+    merge_kernel(a_ref, b_ref, _Sink(tmp))
+    merged = _Sink.value
+    width = tmp[1] - PACK
+    stats = merged[:, width:]
+    stat_lane = lax.broadcasted_iota(jnp.int32, (1, PACK), 1)
+    totals = [
+        jnp.sum(jnp.where(stat_lane == HEADS + h, stats, 0.0), axis=1, keepdims=True)
+        for h in range(HEADS)
+    ]
+    lane = lax.broadcasted_iota(jnp.int32, (1, 2 * HD), 1)
+    low = lane < HD
+    blocks = []
+    for pair in range(HEADS // 2):
+        block = merged[:, pair * 2 * HD : (pair + 1) * 2 * HD]
+        blocks.append(block / jnp.where(low, totals[2 * pair], totals[2 * pair + 1]))
+    attended = jnp.concatenate(blocks, axis=1)
+    square = jnp.mean(attended * attended, axis=1, keepdims=True)
+    normed = (attended * lax.rsqrt(square + 1e-06)).astype(jnp.bfloat16)
+    out_ref[...] = jnp.dot(normed, w_ref[...], preferred_element_type=jnp.float32)
+
+
+class _Sink:
+    value = None
+
+    def __init__(self, shape):
+        self.shape = shape
+
+    def __setitem__(self, index, value):
+        _Sink.value = value
+
+
+def finish(kept, got, w_out):
+    rows, cols = kept.shape
+    width = w_out.shape[1]
+    return pl.pallas_call(
+        finish_kernel,
+        out_shape=jax.ShapeDtypeStruct((rows, width), jnp.float32),
+        cost_estimate=pl.CostEstimate(
+            flops=2 * rows * cols * width, transcendentals=rows, bytes_accessed=2 * cols * width
+        ),
+    )(kept, got, w_out)
+
+
 def step_bits(nbits, core):
     if nbits != 5:
         return [jnp.int32(b) for b in range(nbits)]
@@ -200,7 +245,7 @@
     return block
 
 
-def tree_reduce(query_rows, hood, listed, keep):
+def tree_reduce(query_rows, hood, listed, keep, w_out):
     groups = lax.axis_size("tm")
     nbits = groups.bit_length() - 1
     qtok = query_rows.shape[0]
@@ -213,10 +258,9 @@
     first = attention(query_rows[:quarter], hood, listed, keep)
     (first,) = merge(first, got_first, False, 0)
     for i in range(1, nbits):
-        last = i == nbits - 1
-        outs = merge(first, second, not last)
-        if last:
-            return outs[0]
+        if i == nbits - 1:
+            return finish(first, second, w_out)
+        outs = merge(first, second, True)
         first, second = outs
         second = lax.ppermute(second, "tm", step_pairs(nbits, i + 1))
 
@@ -241,15 +285,8 @@
     )
     query_rows = jnp.take(query_rows.reshape(groups, qtok // groups, width), order, axis=0)
     query_rows = query_rows.reshape(qtok, width)
-    final = tree_reduce(query_rows, hood, listed, keep)
-    summed = final[:, :width]
-    total = final[:, width + HEADS : width + 2 * HEADS]
-    own_rows = summed.shape[0]
-    attended = summed / jnp.repeat(total, HD, axis=1)
-    normed = attended * lax.rsqrt(jnp.mean(attended * attended, axis=1, keepdims=True) + 1e-06)
-    normed = normed.astype(jnp.bfloat16)
-    joined = jnp.dot(normed, w_out, preferred_element_type=jnp.float32)
-    return joined.reshape(1, 1, own_rows, width)
+    joined = tree_reduce(query_rows, hood, listed, keep, w_out)
+    return joined.reshape(1, 1, joined.shape[0], width)
 
 
 def solution(mesh):

time: 176 us -> 173 us (0.983)
    pallas_call x0 -> x1, Pallas kernels: none -> 2.22 us  [finish(): pl.pallas_call(finish_kernel, out_shape=jax.ShapeDtypeStruct((rows, width...]
    pallas_call x6 -> x5, Pallas kernels: 14 us -> 12.3 us  [merge(): pl.pallas_call(merge_kernel, grid=(1,), in_specs=[pl.BlockSpec((rows, col...]
    unnamed x33 -> x31, local copies, waits for them, and re-layouts: 5.01 us -> 5.02 us
where the time goes in v13:
time: 173 us; the launch traced here: 170 us
  waiting for transfers between devices  75.4 us (44%)
  starting transfers between devices  40.1 us (23%)
  Pallas kernels  38.9 us (22%)
  local copies, waits for them, and re-layouts  11.5 us (7%)
  other arithmetic  3.8 us (2%)
    ppermute x6, waiting for transfers between devices, shifted(): return lax.ppermute(array, axis, pairs)  58.3 us
    pallas_call x3, Pallas kernels, attention(): pl.pallas_call(attention_kernel, grid_spec=grid_spec, out_shape=jax.Shape...  24.4 us
    ppermute x6, starting transfers between devices, shifted(): return lax.ppermute(array, axis, pairs)  22.8 us
    ppermute x3, waiting for transfers between devices, tree_reduce(): second = lax.ppermute(second, 'tm', step_pairs(nbits, i + 1))  16.4 us
    ppermute x3, starting transfers between devices, tree_reduce(): second = lax.ppermute(second, 'tm', step_pairs(nbits, i + 1))  13.3 us
    pallas_call x5, Pallas kernels, merge(): pl.pallas_call(merge_kernel, grid=(1,), in_specs=[pl.BlockSpec((rows, col...  12.3 us
    unnamed x31, local copies, waits for them, and re-layouts  5.02 us
  transfers between devices with their start and end apart: 11, of which 6 were waited for; matrix products, arithmetic and copies ran while one was open for 3% of the time, Pallas kernels for 10%

profile of v13, /device:TPU:6, one launch (start us, length us, event | category | flops | bytes accessed | tf_op | source)
XLA Modules:
  0.0 170.1 jit_solution(4729860175310965964)
XLA Ops:
  0.0 3.6 %collective-permute-start.2 = (bf16[2,2,1,1,2,64,512]{6,5,4,3,2,1,0:T(8,128)(2,1)}, bf16[2,2,1,1,2,64,512]{6,5,4,3,2,1,0:T(8,128)(2,1)S(1)}, u32[]{:S(2)}, u32[]{:S(2)}) collective-permute-start(bf16[2,2,1,1,2,64,512]{6,5,4,3,2,1,0:T(8,128)(2,1)} %param.6), channel_id=1, source_target_pairs={{0,4},{4,8},{8,12},{1,5},{5,9},{9,13},{2,6},{6,10},{10,14},{3,7},{... | collective-permute-start | bytes 1572872 | tf_op jit(solution)/shard_map/ppermute | solution.py:19
  3.6 1.3 collective-permute-start.1
  4.9 9.8 %collective-permute-start = (bf16[2,2,1,1,2,64,512]{6,5,4,3,2,1,0:T(8,128)(2,1)}, bf16[2,2,1,1,2,64,512]{6,5,4,3,2,1,0:T(8,128)(2,1)S(1)}, u32[]{:S(2)}, u32[]{:S(2)}) collective-permute-start(bf16[2,2,1,1,2,64,512]{6,5,4,3,2,1,0:T(8,128)(2,1)} %param.6), channel_id=1, source_target_pairs={{0,1},{1,2},{2,3},{4,5},{5,6},{6,7},{8,9},{9,10},{10,11},{12,13},{... | collective-permute-start | bytes 1572872 | tf_op jit(solution)/shard_map/ppermute | solution.py:19
  14.7 1.3 collective-permute-start.3
  16.1 0.7 fusion
  16.7 0.1 broadcast_in_dim.18
  16.8 0.7 convert_element_type.9.refs_16_
  17.5 0.0 collective-permute-done.2
  17.5 40.8 %collective-permute-done.1 = bf16[2,2,1,1,2,64,512]{6,5,4,3,2,1,0:T(8,128)(2,1)S(1)} collective-permute-done((bf16[2,2,1,1,2,64,512]{6,5,4,3,2,1,0:T(8,128)(2,1)}, bf16[2,2,1,1,2,64,512]{6,5,4,3,2,1,0:T(8,128)(2,1)S(1)}, u32[]{:S(2)}, u32[]{:S(2)}) %collective-permute-start.1) | collective-permute-done | bytes 524320 | tf_op jit(solution)/shard_map/ppermute | solution.py:19
  58.3 0.0 collective-permute-done
  58.3 1.0 constant_dynamic-update-slice_fusion.1
  59.3 0.9 constant_dynamic-update-slice_fusion
  60.2 1.3 collective-permute-start.5
  61.5 5.5 %collective-permute-start.4 = (bf16[2,2,1,2,2,64,512]{6,5,4,3,2,1,0:T(8,128)(2,1)}, bf16[2,2,1,2,2,64,512]{6,5,4,3,2,1,0:T(8,128)(2,1)}, u32[]{:S(2)}, u32[]{:S(2)}) collective-permute-start(bf16[2,2,1,2,2,64,512]{6,5,4,3,2,1,0:T(8,128)(2,1)} %constant_dynamic-update-slice_fusion), channel_id=1, source_target_pairs={{0,4},{4,8},{8,12},{1,5},{5,9},{9,13},{2,6},{6,10},{10,14},{3,7},{... | collective-permute-start | bytes 3145736 | tf_op jit(solution)/shard_map/ppermute | solution.py:19
  67.0 0.1 fusion.1
  67.2 0.6 gather_fusion
  67.8 0.0 copy-start.7
  67.8 0.1 compare_and_fusion
  67.9 0.2 broadcast_select_fusion
  68.1 0.9 slice.55
  68.9 17.5 %collective-permute-done.5 = bf16[2,2,1,2,2,64,512]{6,5,4,3,2,1,0:T(8,128)(2,1)} collective-permute-done((bf16[2,2,1,2,2,64,512]{6,5,4,3,2,1,0:T(8,128)(2,1)}, bf16[2,2,1,2,2,64,512]{6,5,4,3,2,1,0:T(8,128)(2,1)}, u32[]{:S(2)}, u32[]{:S(2)}) %collective-permute-start.5) | collective-permute-done | bytes 1048608 | tf_op jit(solution)/shard_map/ppermute | solution.py:19
  86.4 1.3 fusion.4
  87.7 1.3 fusion.3
  89.0 2.8 %maximum_maximum_fusion = bf16[2,2,3,3,2,64,512]{6,5,4,3,2,1,0:T(8,128)(2,1)} fusion(bf16[2,2,1,1,2,64,512]{6,5,4,3,2,1,0:T(8,128)(2,1)S(1)} %get-tuple-element.30, bf16[2,2,1,1,2,64,512]{6,5,4,3,2,1,0:T(8,128)(2,1)S(1)} %copy-done.11, bf16[2,2,1,1,2,64,512]{6,5,4,3,2,1,0:T(8,128)(2,1)S(1)} %get-tuple-element.29, ...), kind=kLoop, calls=%fused_computation.1 | loop fusion | flops 18874368 | bytes 9437184 | tf_op jit(solution)/shard_map/concatenate | solution.py:34
  91.8 9.9 %shard_map.56 = f32[512,640]{1,0:T(8,128)} custom-call(s32[8]{0:T(128)} %bitcast.67, bf16[512,512]{1,0:T(8,128)(2,1)} %bitcast.64, bf16[2,2,18,64,512]{4,3,2,1,0:T(8,128)(2,1)} %bitcast.16, bf16[2,2,18,64,512]{4,3,2,1,0:T(8,128)(2,1)} %bitcast.17, bf16[2,2,18,64,512]{4,3,2,1,0:T(8,128)(2,1)} %bitcast.18, bf16[2,2,18,64,512]{4,3,2,1,0:T(8,128)(2,1)} %bitcast.19, ...), custom_call_target="tpu_custom_call" | custom-call | flops 2147483648 | bytes 3670016 | tf_op jit(solution)/shard_map/pallas_call | solution.py:105
  101.7 2.1 %collective-permute-start.6 = (f32[512,640]{1,0:T(8,128)}, f32[512,640]{1,0:T(8,128)S(1)}, u32[]{:S(2)}, u32[]{:S(2)}) collective-permute-start(f32[512,640]{1,0:T(8,128)} %shard_map.56), channel_id=1, source_target_pairs={{0,16},{16,0},{32,48},{48,32},{64,80},{80,64},{96,112},{112,96},{1... | collective-permute-start | bytes 3932168 | tf_op jit(solution)/shard_map/ppermute | solution.py:254
  103.8 0.9 fusion.2
  104.7 7.2 %shard_map.58.a_ref = f32[256,640]{1,0:T(8,128)} custom-call(s32[8]{0:T(128)} %bitcast.68, bf16[256,512]{1,0:T(8,128)(2,1)} %bitcast.66, bf16[2,2,18,64,512]{4,3,2,1,0:T(8,128)(2,1)} %bitcast.39, bf16[2,2,18,64,512]{4,3,2,1,0:T(8,128)(2,1)} %bitcast.33, bf16[2,2,18,64,512]{4,3,2,1,0:T(8,128)(2,1)} %bitcast.34, bf16[2,2,18,64,512]{4,3,2,1,0:T(8,128)(2,1)} %bitcast.35, ...), custom_call_target="tpu_custom_call" | custom-call | flops 1073741824 | bytes 2883584 | tf_op jit(solution)/shard_map/pallas_call | solution.py:105
  111.9 1.1 copy-done.1
  113.0 2.8 %shard_map.59 = f32[256,640]{1,0:T(8,128)} custom-call(f32[256,640]{1,0:T(8,128)} %shard_map.58.a_ref, f32[512,640]{1,0:T(8,128)} %copy-done.1), custom_call_target="tpu_custom_call" | custom-call | flops 655360 | bytes 1966080 | tf_op jit(solution)/shard_map/pallas_call | solution.py:161
  115.8 1.9 %collective-permute-start.7 = (f32[256,640]{1,0:T(8,128)}, f32[256,640]{1,0:T(8,128)S(1)}, u32[]{:S(2)}, u32[]{:S(2)}) collective-permute-start(f32[256,640]{1,0:T(8,128)} %shard_map.59), channel_id=1, source_target_pairs={{0,32},{16,144},{32,0},{48,176},{64,96},{80,208},{96,64},{112,240}... | collective-permute-start | bytes 1966088 | tf_op jit(solution)/shard_map/ppermute | solution.py:257
  117.7 7.2 %shard_map.55.a_ref = f32[256,640]{1,0:T(8,128)} custom-call(s32[8]{0:T(128)} %bitcast.69, bf16[256,512]{1,0:T(8,128)(2,1)} %bitcast.65, bf16[2,2,18,64,512]{4,3,2,1,0:T(8,128)(2,1)} %bitcast.48, bf16[2,2,18,64,512]{4,3,2,1,0:T(8,128)(2,1)} %bitcast.49, bf16[2,2,18,64,512]{4,3,2,1,0:T(8,128)(2,1)} %bitcast.50, bf16[2,2,18,64,512]{4,3,2,1,0:T(8,128)(2,1)} %bitcast.51, ...), custom_call_target="tpu_custom_call" | custom-call | flops 1073741824 | bytes 2883584 | tf_op jit(solution)/shard_map/pallas_call | solution.py:105
  125.0 2.8 %shard_map.57.a_ref = f32[256,640]{1,0:T(8,128)} custom-call(f32[256,640]{1,0:T(8,128)} %shard_map.55.a_ref, f32[512,640]{1,0:T(8,128)} %copy-done.1), custom_call_target="tpu_custom_call" | custom-call | flops 655360 | bytes 1966080 | tf_op jit(solution)/shard_map/pallas_call | solution.py:161
  127.7 0.8 collective-permute-done.7.b_ref
  128.5 0.9 copy-done.6
  129.4 2.7 %shard_map.60 = (f32[128,640]{1,0:T(8,128)}, f32[128,640]{1,0:T(8,128)}) custom-call(f32[256,640]{1,0:T(8,128)} %shard_map.57.a_ref, f32[256,640]{1,0:T(8,128)} %copy-done.6), custom_call_target="tpu_custom_call" | custom-call | flops 655360 | bytes 1966080 | tf_op jit(solution)/shard_map/pallas_call | solution.py:161
  132.1 2.7 %collective-permute-start.8 = (f32[128,640]{1,0:T(8,128)}, f32[128,640]{1,0:T(8,128)S(1)}, u32[]{:S(2)}, u32[]{:S(2)}) collective-permute-start(f32[128,640]{1,0:T(8,128)} %get-tuple-element.20), channel_id=1, source_target_pairs={{0,128},{16,48},{32,160},{48,16},{64,192},{80,112},{96,224},{112,8... | collective-permute-start | bytes 983048 | tf_op jit(solution)/shard_map/ppermute | solution.py:265
  134.8 6.4 %collective-permute-done.8.b_ref = f32[128,640]{1,0:T(8,128)S(1)} collective-permute-done((f32[128,640]{1,0:T(8,128)}, f32[128,640]{1,0:T(8,128)S(1)}, u32[]{:S(2)}, u32[]{:S(2)}) %collective-permute-start.8) | collective-permute-done | bytes 327712 | tf_op jit(solution)/shard_map/ppermute | solution.py:265
  141.3 0.7 copy-done.12
  142.0 2.1 %shard_map.61 = (f32[64,640]{1,0:T(8,128)}, f32[64,640]{1,0:T(8,128)}) custom-call(f32[128,640]{1,0:T(8,128)} %get-tuple-element.19.a_ref, f32[128,640]{1,0:T(8,128)} %copy-done.12), custom_call_target="tpu_custom_call" | custom-call | flops 327680 | bytes 983040 | tf_op jit(solution)/shard_map/pallas_call | solution.py:161
  144.1 7.3 %collective-permute-start.9 = (f32[64,640]{1,0:T(8,128)}, f32[64,640]{1,0:T(8,128)S(1)}, u32[]{:S(2)}, u32[]{:S(2)}) collective-permute-start(f32[64,640]{1,0:T(8,128)} %get-tuple-element.22), channel_id=1, source_target_pairs={{0,64},{16,272},{32,96},{48,304},{64,0},{80,336},{96,32},{112,368}... | collective-permute-start | bytes 491528 | tf_op jit(solution)/shard_map/ppermute | solution.py:265
  151.5 5.2 %collective-permute-done.9.b_ref = f32[64,640]{1,0:T(8,128)S(1)} collective-permute-done((f32[64,640]{1,0:T(8,128)}, f32[64,640]{1,0:T(8,128)S(1)}, u32[]{:S(2)}, u32[]{:S(2)}) %collective-permute-start.9) | collective-permute-done | bytes 163872 | tf_op jit(solution)/shard_map/ppermute | solution.py:265
  156.7 0.7 copy-done.13
  157.4 1.9 %shard_map.62 = (f32[32,640]{1,0:T(8,128)}, f32[32,640]{1,0:T(8,128)}) custom-call(f32[64,640]{1,0:T(8,128)} %get-tuple-element.21.a_ref, f32[64,640]{1,0:T(8,128)} %copy-done.13), custom_call_target="tpu_custom_call" | custom-call | flops 163840 | bytes 491520 | tf_op jit(solution)/shard_map/pallas_call | solution.py:161
  159.2 3.3 %collective-permute-start.10 = (f32[32,640]{1,0:T(8,128)}, f32[32,640]{1,0:T(8,128)S(1)}, u32[]{:S(2)}, u32[]{:S(2)}) collective-permute-start(f32[32,640]{1,0:T(8,128)} %get-tuple-element.24), channel_id=1, source_target_pairs={{0,256},{16,80},{32,288},{48,112},{64,320},{80,16},{96,352},{112,4... | collective-permute-start | bytes 245768 | tf_op jit(solution)/shard_map/ppermute | solution.py:265
  162.5 4.7 %collective-permute-done.10.b_ref = f32[32,640]{1,0:T(8,128)S(1)} collective-permute-done((f32[32,640]{1,0:T(8,128)}, f32[32,640]{1,0:T(8,128)S(1)}, u32[]{:S(2)}, u32[]{:S(2)}) %collective-permute-start.10) | collective-permute-done | bytes 81952 | tf_op jit(solution)/shard_map/ppermute | solution.py:265
  167.3 0.6 copy-done.14
  167.9 2.2 %shard_map.63 = f32[32,512]{1,0:T(8,128)} custom-call(f32[32,640]{1,0:T(8,128)} %get-tuple-element.23.a_ref, f32[32,640]{1,0:T(8,128)} %copy-done.14, bf16[512,512]{1,0:T(8,128)(2,1)} %w_ref.1), custom_call_target="tpu_custom_call" | custom-call | flops 20971520 | bytes 655360 | tf_op jit(solution)/shard_map/pallas_call | solution.py:212
  (31 shorter events, 0.1 us)
Async XLA Ops:
  0.0 67.1 %copy-start = (bf16[1,1,1024,512]{3,2,1,0:T(8,128)(2,1)S(1)}, bf16[1,1,1024,512]{3,2,1,0:T(8,128)(2,1)}, u32[]{:S(2)}) copy-start(bf16[1,1,1024,512]{3,2,1,0:T(8,128)(2,1)} %param.5) | copy-start | bytes 3145732
  0.0 17.5 %collective-permute-start.2 = (bf16[2,2,1,1,2,64,512]{6,5,4,3,2,1,0:T(8,128)(2,1)}, bf16[2,2,1,1,2,64,512]{6,5,4,3,2,1,0:T(8,128)(2,1)S(1)}, u32[]{:S(2)}, u32[]{:S(2)}) collective-permute-start(bf16[2,2,1,1,2,64,512]{6,5,4,3,2,1,0:T(8,128)(2,1)} %param.6), channel_id=1, source_target_pairs={{0,4},{4,8},{8,12},{1,5},{5,9},{9,13},{2,6},{6,10},{10,14},{3,7},{... | collective-permute-start | bytes 1572872 | tf_op jit(solution)/shard_map/ppermute | solution.py:19
  3.6 54.7 %collective-permute-start.1 = (bf16[2,2,1,1,2,64,512]{6,5,4,3,2,1,0:T(8,128)(2,1)}, bf16[2,2,1,1,2,64,512]{6,5,4,3,2,1,0:T(8,128)(2,1)S(1)}, u32[]{:S(2)}, u32[]{:S(2)}) collective-permute-start(bf16[2,2,1,1,2,64,512]{6,5,4,3,2,1,0:T(8,128)(2,1)} %param.6), channel_id=1, source_target_pairs={{1,0},{2,1},{3,2},{5,4},{6,5},{7,6},{9,8},{10,9},{11,10},{13,12},{... | collective-permute-start | bytes 1572872 | tf_op jit(solution)/shard_map/ppermute | solution.py:19
  4.9 53.4 %collective-permute-start = (bf16[2,2,1,1,2,64,512]{6,5,4,3,2,1,0:T(8,128)(2,1)}, bf16[2,2,1,1,2,64,512]{6,5,4,3,2,1,0:T(8,128)(2,1)S(1)}, u32[]{:S(2)}, u32[]{:S(2)}) collective-permute-start(bf16[2,2,1,1,2,64,512]{6,5,4,3,2,1,0:T(8,128)(2,1)} %param.6), channel_id=1, source_target_pairs={{0,1},{1,2},{2,3},{4,5},{5,6},{6,7},{8,9},{9,10},{10,11},{12,13},{... | collective-permute-start | bytes 1572872 | tf_op jit(solution)/shard_map/ppermute | solution.py:19
  14.7 43.6 %collective-permute-start.3 = (bf16[2,2,1,1,2,64,512]{6,5,4,3,2,1,0:T(8,128)(2,1)}, bf16[2,2,1,1,2,64,512]{6,5,4,3,2,1,0:T(8,128)(2,1)S(1)}, u32[]{:S(2)}, u32[]{:S(2)}) collective-permute-start(bf16[2,2,1,1,2,64,512]{6,5,4,3,2,1,0:T(8,128)(2,1)} %param.6), channel_id=1, source_target_pairs={{4,0},{8,4},{12,8},{5,1},{9,5},{13,9},{6,2},{10,6},{14,10},{7,3},{... | collective-permute-start | bytes 1572872 | tf_op jit(solution)/shard_map/ppermute | solution.py:19
  17.5 49.6 %copy-start.8 = (bf16[2,2,1,1,2,64,512]{6,5,4,3,2,1,0:T(8,128)(2,1)}, bf16[2,2,1,1,2,64,512]{6,5,4,3,2,1,0:T(8,128)(2,1)S(1)}, u32[]{:S(2)}) copy-start(bf16[2,2,1,1,2,64,512]{6,5,4,3,2,1,0:T(8,128)(2,1)S(1)} %collective-permute-done.2) | copy-start | bytes 1572868
  58.3 8.8 %copy-start.2 = (bf16[2,2,1,1,2,64,512]{6,5,4,3,2,1,0:T(8,128)(2,1)}, bf16[2,2,1,1,2,64,512]{6,5,4,3,2,1,0:T(8,128)(2,1)S(1)}, u32[]{:S(2)}) copy-start(bf16[2,2,1,1,2,64,512]{6,5,4,3,2,1,0:T(8,128)(2,1)S(1)} %collective-permute-done.1) | copy-start | bytes 1572868
  58.3 8.8 %copy-start.4 = (bf16[2,2,1,1,2,64,512]{6,5,4,3,2,1,0:T(8,128)(2,1)}, bf16[2,2,1,1,2,64,512]{6,5,4,3,2,1,0:T(8,128)(2,1)S(1)}, u32[]{:S(2)}) copy-start(bf16[2,2,1,1,2,64,512]{6,5,4,3,2,1,0:T(8,128)(2,1)S(1)} %collective-permute-done) | copy-start | bytes 1572868
  58.3 8.8 %copy-start.10 = (bf16[2,2,1,1,2,64,512]{6,5,4,3,2,1,0:T(8,128)(2,1)}, bf16[2,2,1,1,2,64,512]{6,5,4,3,2,1,0:T(8,128)(2,1)S(1)}, u32[]{:S(2)}) copy-start(bf16[2,2,1,1,2,64,512]{6,5,4,3,2,1,0:T(8,128)(2,1)S(1)} %collective-permute-done.3) | copy-start | bytes 1572868
  60.2 26.2 %collective-permute-start.5 = (bf16[2,2,1,2,2,64,512]{6,5,4,3,2,1,0:T(8,128)(2,1)}, bf16[2,2,1,2,2,64,512]{6,5,4,3,2,1,0:T(8,128)(2,1)}, u32[]{:S(2)}, u32[]{:S(2)}) collective-permute-start(bf16[2,2,1,2,2,64,512]{6,5,4,3,2,1,0:T(8,128)(2,1)} %constant_dynamic-update-slice_fusion), channel_id=1, source_target_pairs={{4,0},{8,4},{12,8},{5,1},{9,5},{13,9},{6,2},{10,6},{14,10},{7,3},{... | collective-permute-start | bytes 3145736 | tf_op jit(solution)/shard_map/ppermute | solution.py:19
  61.5 26.2 %collective-permute-start.4 = (bf16[2,2,1,2,2,64,512]{6,5,4,3,2,1,0:T(8,128)(2,1)}, bf16[2,2,1,2,2,64,512]{6,5,4,3,2,1,0:T(8,128)(2,1)}, u32[]{:S(2)}, u32[]{:S(2)}) collective-permute-start(bf16[2,2,1,2,2,64,512]{6,5,4,3,2,1,0:T(8,128)(2,1)} %constant_dynamic-update-slice_fusion), channel_id=1, source_target_pairs={{0,4},{4,8},{8,12},{1,5},{5,9},{9,13},{2,6},{6,10},{10,14},{3,7},{... | collective-permute-start | bytes 3145736 | tf_op jit(solution)/shard_map/ppermute | solution.py:19
  67.8 21.2 %copy-start.3 = (bf16[2,2,1,1,2,64,512]{6,5,4,3,2,1,0:T(8,128)(2,1)S(1)}, bf16[2,2,1,1,2,64,512]{6,5,4,3,2,1,0:T(8,128)(2,1)}, u32[]{:S(2)}) copy-start(bf16[2,2,1,1,2,64,512]{6,5,4,3,2,1,0:T(8,128)(2,1)} %copy-done.2) | copy-start | bytes 1572868
  67.8 21.2 %copy-start.5 = (bf16[2,2,1,1,2,64,512]{6,5,4,3,2,1,0:T(8,128)(2,1)S(1)}, bf16[2,2,1,1,2,64,512]{6,5,4,3,2,1,0:T(8,128)(2,1)}, u32[]{:S(2)}) copy-start(bf16[2,2,1,1,2,64,512]{6,5,4,3,2,1,0:T(8,128)(2,1)} %copy-done.4) | copy-start | bytes 1572868
  67.8 21.2 %copy-start.7 = (bf16[2,2,1,1,2,64,512]{6,5,4,3,2,1,0:T(8,128)(2,1)S(1)}, bf16[2,2,1,1,2,64,512]{6,5,4,3,2,1,0:T(8,128)(2,1)}, u32[]{:S(2)}) copy-start(bf16[2,2,1,1,2,64,512]{6,5,4,3,2,1,0:T(8,128)(2,1)} %param.6) | copy-start | bytes 1572868
  67.8 21.2 %copy-start.9 = (bf16[2,2,1,1,2,64,512]{6,5,4,3,2,1,0:T(8,128)(2,1)S(1)}, bf16[2,2,1,1,2,64,512]{6,5,4,3,2,1,0:T(8,128)(2,1)}, u32[]{:S(2)}) copy-start(bf16[2,2,1,1,2,64,512]{6,5,4,3,2,1,0:T(8,128)(2,1)} %copy-done.8) | copy-start | bytes 1572868
  67.8 21.2 %copy-start.11 = (bf16[2,2,1,1,2,64,512]{6,5,4,3,2,1,0:T(8,128)(2,1)S(1)}, bf16[2,2,1,1,2,64,512]{6,5,4,3,2,1,0:T(8,128)(2,1)}, u32[]{:S(2)}) copy-start(bf16[2,2,1,1,2,64,512]{6,5,4,3,2,1,0:T(8,128)(2,1)} %copy-done.10) | copy-start | bytes 1572868
  101.7 10.2 %collective-permute-start.6 = (f32[512,640]{1,0:T(8,128)}, f32[512,640]{1,0:T(8,128)S(1)}, u32[]{:S(2)}, u32[]{:S(2)}) collective-permute-start(f32[512,640]{1,0:T(8,128)} %shard_map.56), channel_id=1, source_target_pairs={{0,16},{16,0},{32,48},{48,32},{64,80},{80,64},{96,112},{112,96},{1... | collective-permute-start | bytes 3932168 | tf_op jit(solution)/shard_map/ppermute | solution.py:254
  111.9 1.1 copy-start.1
  115.8 12.7 %collective-permute-start.7 = (f32[256,640]{1,0:T(8,128)}, f32[256,640]{1,0:T(8,128)S(1)}, u32[]{:S(2)}, u32[]{:S(2)}) collective-permute-start(f32[256,640]{1,0:T(8,128)} %shard_map.59), channel_id=1, source_target_pairs={{0,32},{16,144},{32,0},{48,176},{64,96},{80,208},{96,64},{112,240}... | collective-permute-start | bytes 1966088 | tf_op jit(solution)/shard_map/ppermute | solution.py:257
  128.5 0.9 copy-start.6
  132.1 9.2 %collective-permute-start.8 = (f32[128,640]{1,0:T(8,128)}, f32[128,640]{1,0:T(8,128)S(1)}, u32[]{:S(2)}, u32[]{:S(2)}) collective-permute-start(f32[128,640]{1,0:T(8,128)} %get-tuple-element.20), channel_id=1, source_target_pairs={{0,128},{16,48},{32,160},{48,16},{64,192},{80,112},{96,224},{112,8... | collective-permute-start | bytes 983048 | tf_op jit(solution)/shard_map/ppermute | solution.py:265
  141.3 0.7 copy-start.12
  144.1 12.6 %collective-permute-start.9 = (f32[64,640]{1,0:T(8,128)}, f32[64,640]{1,0:T(8,128)S(1)}, u32[]{:S(2)}, u32[]{:S(2)}) collective-permute-start(f32[64,640]{1,0:T(8,128)} %get-tuple-element.22), channel_id=1, source_target_pairs={{0,64},{16,272},{32,96},{48,304},{64,0},{80,336},{96,32},{112,368}... | collective-permute-start | bytes 491528 | tf_op jit(solution)/shard_map/ppermute | solution.py:265
  156.7 0.7 copy-start.13
  159.2 8.0 %collective-permute-start.10 = (f32[32,640]{1,0:T(8,128)}, f32[32,640]{1,0:T(8,128)S(1)}, u32[]{:S(2)}, u32[]{:S(2)}) collective-permute-start(f32[32,640]{1,0:T(8,128)} %get-tuple-element.24), channel_id=1, source_target_pairs={{0,256},{16,80},{32,288},{48,112},{64,320},{80,16},{96,352},{112,4... | collective-permute-start | bytes 245768 | tf_op jit(solution)/shard_map/ppermute | solution.py:265
  167.3 0.6 copy-start.14

commit v14 on v13

--- a/solution.py
+++ b/solution.py
@@ -1,3 +1,5 @@
+import functools
+
 import jax
 import jax.numpy as jnp
 from jax import lax
@@ -37,12 +39,17 @@
 PACK = 128
 
 
-def attention_kernel(listed_ref, q_ref, *refs):
-    nlist = (len(refs) - 2) // 2
-    key_refs, value_refs = refs[:nlist], refs[nlist : 2 * nlist]
-    keep_ref, out_ref = refs[2 * nlist], refs[2 * nlist + 1]
+def attention_kernel(gather, *refs):
+    if gather:
+        listed_ref, q_ref = refs[0], refs[1]
+        refs = refs[2:]
+        nlist = (len(refs) - 4) // 2
+        key_refs, value_refs = refs[:nlist], refs[nlist : 2 * nlist]
+        keep_ref, out_ref, keys_out, values_out = refs[2 * nlist :]
+        frames = key_refs[0].shape[1]
+    else:
+        q_ref, keys_ref, values_ref, keep_ref, out_ref = refs
     rows = q_ref.shape[0]
-    frames = key_refs[0].shape[1]
     keep = keep_ref[...] > 0
     lane = lax.broadcasted_iota(jnp.int32, (1, 2 * HD), 1)
     low = lane < HD
@@ -53,12 +60,18 @@
     for pair in range(HEADS // 2):
         cols = pl.ds(pair * 2 * HD, 2 * HD)
         q2 = q_ref[:, cols] * scale
-        k2 = jnp.concatenate(
-            [r[0, f, 0, :, cols] for r in key_refs for f in range(frames)], axis=0
-        )
-        v2 = jnp.concatenate(
-            [r[0, f, 0, :, cols] for r in value_refs for f in range(frames)], axis=0
-        )
+        if gather:
+            k2 = jnp.concatenate(
+                [r[0, f, 0, :, cols] for r in key_refs for f in range(frames)], axis=0
+            )
+            v2 = jnp.concatenate(
+                [r[0, f, 0, :, cols] for r in value_refs for f in range(frames)], axis=0
+            )
+            keys_out[:, cols] = k2
+            values_out[:, cols] = v2
+        else:
+            k2 = keys_ref[:, cols]
+            v2 = values_ref[:, cols]
         outs = []
         for part in range(2):
             mine = low if part == 0 else jnp.logical_not(low)
@@ -85,33 +98,51 @@
     _, frames, _, blk, _ = hood.shape
     nlist = listed.shape[0]
     count = nlist * frames * blk
-    tq = min(TQ, qtok)
-    tiles = qtok // tq
     flops = 2 * 2 * qtok * count * 2 * width
     block = (1, frames, 1, blk, width)
 
     def entry_spec(kind, e):
         return pl.BlockSpec(block, lambda i, lst: (kind, 0, lst[e], 0, 0))
 
+    whole = pl.BlockSpec((count, width), lambda i, lst: (0, 0))
     grid_spec = pltpu.PrefetchScalarGridSpec(
         num_scalar_prefetch=1,
-        grid=(tiles,),
-        in_specs=[pl.BlockSpec((tq, width), lambda i, lst: (i, 0))]
+        grid=(1,),
+        in_specs=[pl.BlockSpec((qtok, width), lambda i, lst: (0, 0))]
         + [entry_spec(0, e) for e in range(nlist)]
         + [entry_spec(1, e) for e in range(nlist)]
         + [pl.BlockSpec((1, count), lambda i, lst: (0, 0))],
-        out_specs=pl.BlockSpec((tq, width + PACK), lambda i, lst: (i, 0)),
+        out_specs=[pl.BlockSpec((qtok, width + PACK), lambda i, lst: (0, 0)), whole, whole],
     )
     return pl.pallas_call(
-        attention_kernel,
+        functools.partial(attention_kernel, True),
         grid_spec=grid_spec,
+        out_shape=[
+            jax.ShapeDtypeStruct((qtok, width + PACK), jnp.float32),
+            jax.ShapeDtypeStruct((count, width), hood.dtype),
+            jax.ShapeDtypeStruct((count, width), hood.dtype),
+        ],
+        cost_estimate=pl.CostEstimate(
+            flops=flops,
+            transcendentals=qtok * count * HEADS,
+            bytes_accessed=qtok * width * 6 + count * width * 8,
+        ),
+    )(listed, query_rows, *([hood] * (2 * nlist)), keep)
+
+
+def attention_again(query_rows, keys, values, keep):
+    qtok, width = query_rows.shape
+    count = keys.shape[0]
+    flops = 2 * 2 * qtok * count * 2 * width
+    return pl.pallas_call(
+        functools.partial(attention_kernel, False),
         out_shape=jax.ShapeDtypeStruct((qtok, width + PACK), jnp.float32),
         cost_estimate=pl.CostEstimate(
             flops=flops,
             transcendentals=qtok * count * HEADS,
             bytes_accessed=qtok * width * 6 + count * width * 4,
         ),
-    )(listed, query_rows, *([hood] * (2 * nlist)), keep)
+    )(query_rows, keys, values, keep)
 
 
 def merge_kernel(a_ref, b_ref, *out_refs):
@@ -250,12 +281,12 @@
     nbits = groups.bit_length() - 1
     qtok = query_rows.shape[0]
     half, quarter = qtok // 2, qtok // 4
-    second = attention(query_rows[half:], hood, listed, keep)
+    second, keys, values = attention(query_rows[half:], hood, listed, keep)
     got_first = lax.ppermute(second, "tm", step_pairs(nbits, 0))
-    sent = attention(query_rows[quarter:half], hood, listed, keep)
+    sent = attention_again(query_rows[quarter:half], keys, values, keep)
     (sent,) = merge(sent, got_first, False, quarter)
     second = lax.ppermute(sent, "tm", step_pairs(nbits, 1))
-    first = attention(query_rows[:quarter], hood, listed, keep)
+    first = attention_again(query_rows[:quarter], keys, values, keep)
     (first,) = merge(first, got_first, False, 0)
     for i in range(1, nbits):
         if i == nbits - 1:

time: 173 us -> 177 us (1.023)
  waiting for transfers between devices: 75.4 us -> 86.5 us
  starting transfers between devices: 40.1 us -> 34.1 us
    ppermute x6, waiting for transfers between devices: 58.3 us -> 65.7 us  [shifted(): return lax.ppermute(array, axis, pairs)]
    ppermute x3, starting transfers between devices: 13.3 us -> 7.92 us  [tree_reduce(): second = lax.ppermute(second, 'tm', step_pairs(nbits, i + 1))]
    ppermute x3, waiting for transfers between devices: 16.4 us -> 19.3 us  [tree_reduce(): second = lax.ppermute(second, 'tm', step_pairs(nbits, i + 1))]
    unnamed x31 -> x27, local copies, waits for them, and re-layouts: 5.02 us -> 4.91 us
  transfers between devices with their start and end apart: 11 -> 11, of which waited for: 6 -> 7; matrix products, arithmetic and copies ran while one was open for 3% -> 3% of each run, Pallas kernels for 10% -> 9%
where the time goes in v14:
time: 177 us; the launch traced here: 175 us
  waiting for transfers between devices  86.5 us (49%)
  Pallas kernels  37.6 us (21%)
  starting transfers between devices  34.1 us (19%)
  local copies, waits for them, and re-layouts  11.4 us (6%)
  other arithmetic  4.78 us (3%)
    ppermute x6, waiting for transfers between devices, shifted(): return lax.ppermute(array, axis, pairs)  65.7 us
    ppermute x6, starting transfers between devices, shifted(): return lax.ppermute(array, axis, pairs)  22.2 us
    ppermute x3, waiting for transfers between devices, tree_reduce(): second = lax.ppermute(second, 'tm', step_pairs(nbits, i + 1))  19.3 us
    pallas_call x2, Pallas kernels, attention_again(): pl.pallas_call(functools.partial(attention_kernel, False), out_shape=jax....  13.1 us
    pallas_call x5, Pallas kernels, merge(): pl.pallas_call(merge_kernel, grid=(1,), in_specs=[pl.BlockSpec((rows, col...  12.3 us
    pallas_call x1, Pallas kernels, attention(): pl.pallas_call(functools.partial(attention_kernel, True), grid_spec=grid_...  10 us
    ppermute x3, starting transfers between devices, tree_reduce(): second = lax.ppermute(second, 'tm', step_pairs(nbits, i + 1))  7.92 us
    unnamed x27, local copies, waits for them, and re-layouts  4.91 us
  transfers between devices with their start and end apart: 11, of which 7 were waited for; matrix products, arithmetic and copies ran while one was open for 3% of the time, Pallas kernels for 9%

profile of v14, /device:TPU:6, one launch (start us, length us, event | category | flops | bytes accessed | tf_op | source)
XLA Modules:
  0.0 174.7 jit_solution(7405628744797390191)
XLA Ops:
  0.0 9.2 %collective-permute-start = (bf16[2,2,1,1,2,64,512]{6,5,4,3,2,1,0:T(8,128)(2,1)}, bf16[2,2,1,1,2,64,512]{6,5,4,3,2,1,0:T(8,128)(2,1)S(1)}, u32[]{:S(2)}, u32[]{:S(2)}) collective-permute-start(bf16[2,2,1,1,2,64,512]{6,5,4,3,2,1,0:T(8,128)(2,1)} %param.6), channel_id=1, source_target_pairs={{0,1},{1,2},{2,3},{4,5},{5,6},{6,7},{8,9},{9,10},{10,11},{12,13},{... | collective-permute-start | bytes 1572872 | tf_op jit(solution)/shard_map/ppermute | solution.py:21
  9.3 1.3 collective-permute-start.1
  10.6 3.5 %collective-permute-start.2 = (bf16[2,2,1,1,2,64,512]{6,5,4,3,2,1,0:T(8,128)(2,1)}, bf16[2,2,1,1,2,64,512]{6,5,4,3,2,1,0:T(8,128)(2,1)S(1)}, u32[]{:S(2)}, u32[]{:S(2)}) collective-permute-start(bf16[2,2,1,1,2,64,512]{6,5,4,3,2,1,0:T(8,128)(2,1)} %param.6), channel_id=1, source_target_pairs={{0,4},{4,8},{8,12},{1,5},{5,9},{9,13},{2,6},{6,10},{10,14},{3,7},{... | collective-permute-start | bytes 1572872 | tf_op jit(solution)/shard_map/ppermute | solution.py:21
  14.1 1.3 collective-permute-start.3
  15.5 5.4 %collective-permute-done = bf16[2,2,1,1,2,64,512]{6,5,4,3,2,1,0:T(8,128)(2,1)S(1)} collective-permute-done((bf16[2,2,1,1,2,64,512]{6,5,4,3,2,1,0:T(8,128)(2,1)}, bf16[2,2,1,1,2,64,512]{6,5,4,3,2,1,0:T(8,128)(2,1)S(1)}, u32[]{:S(2)}, u32[]{:S(2)}) %collective-permute-start) | collective-permute-done | bytes 524320 | tf_op jit(solution)/shard_map/ppermute | solution.py:21
  20.8 43.0 %collective-permute-done.1 = bf16[2,2,1,1,2,64,512]{6,5,4,3,2,1,0:T(8,128)(2,1)S(1)} collective-permute-done((bf16[2,2,1,1,2,64,512]{6,5,4,3,2,1,0:T(8,128)(2,1)}, bf16[2,2,1,1,2,64,512]{6,5,4,3,2,1,0:T(8,128)(2,1)S(1)}, u32[]{:S(2)}, u32[]{:S(2)}) %collective-permute-start.1) | collective-permute-done | bytes 524320 | tf_op jit(solution)/shard_map/ppermute | solution.py:21
  63.9 0.0 collective-permute-done.2
  63.9 0.0 collective-permute-done.3
  63.9 0.9 constant_dynamic-update-slice_fusion.1
  64.8 0.9 constant_dynamic-update-slice_fusion
  65.7 1.3 collective-permute-start.5
  67.0 5.5 %collective-permute-start.4 = (bf16[2,2,1,2,2,64,512]{6,5,4,3,2,1,0:T(8,128)(2,1)}, bf16[2,2,1,2,2,64,512]{6,5,4,3,2,1,0:T(8,128)(2,1)}, u32[]{:S(2)}, u32[]{:S(2)}) collective-permute-start(bf16[2,2,1,2,2,64,512]{6,5,4,3,2,1,0:T(8,128)(2,1)} %constant_dynamic-update-slice_fusion), channel_id=1, source_target_pairs={{0,4},{4,8},{8,12},{1,5},{5,9},{9,13},{2,6},{6,10},{10,14},{3,7},{... | collective-permute-start | bytes 3145736 | tf_op jit(solution)/shard_map/ppermute | solution.py:21
  72.6 0.1 fusion.1
  72.7 0.6 gather_fusion
  73.3 0.1 compare_and_fusion
  73.4 0.2 broadcast_select_fusion
  73.6 0.9 slice.51
  74.5 0.1 broadcast_in_dim.18
  74.5 0.7 convert_element_type.9.refs_18_.refs_3_
  75.2 17.3 %collective-permute-done.5 = bf16[2,2,1,2,2,64,512]{6,5,4,3,2,1,0:T(8,128)(2,1)} collective-permute-done((bf16[2,2,1,2,2,64,512]{6,5,4,3,2,1,0:T(8,128)(2,1)}, bf16[2,2,1,2,2,64,512]{6,5,4,3,2,1,0:T(8,128)(2,1)}, u32[]{:S(2)}, u32[]{:S(2)}) %collective-permute-start.5) | collective-permute-done | bytes 1048608 | tf_op jit(solution)/shard_map/ppermute | solution.py:21
  92.5 1.3 fusion.4
  93.8 0.0 collective-permute-done.4
  93.8 1.3 fusion.3
  95.1 4.4 %maximum_maximum_fusion = bf16[2,2,3,3,2,64,512]{6,5,4,3,2,1,0:T(8,128)(2,1)} fusion(bf16[2,2,1,1,2,64,512]{6,5,4,3,2,1,0:T(8,128)(2,1)S(1)} %get-tuple-element.36, bf16[2,2,1,1,2,64,512]{6,5,4,3,2,1,0:T(8,128)(2,1)} %copy-done.8, bf16[2,2,1,1,2,64,512]{6,5,4,3,2,1,0:T(8,128)(2,1)S(1)} %get-tuple-element.35, ...), kind=kLoop, calls=%fused_computation.1 | loop fusion | flops 18874368 | bytes 9437184 | tf_op jit(solution)/shard_map/concatenate | solution.py:36
  99.5 10.0 %shard_map.55 = (f32[512,640]{1,0:T(8,128)}, bf16[1024,512]{1,0:T(8,128)(2,1)}, bf16[1024,512]{1,0:T(8,128)(2,1)}) custom-call(s32[8]{0:T(128)} %bitcast.35, bf16[512,512]{1,0:T(8,128)(2,1)} %bitcast.32, bf16[2,2,18,64,512]{4,3,2,1,0:T(8,128)(2,1)} %bitcast.16, bf16[2,2,18,64,512]{4,3,2,1,0:T(8,128)(2,1)} %bitcast.17, bf16[2,2,18,64,512]{4,3,2,1,0:T(8,128)(2,1)} %bitcast.18, ...), custom_call_target="tpu_custom_call" | custom-call | flops 2147483648 | bytes 5767168 | tf_op jit(solution)/shard_map/pallas_call | solution.py:117
  109.5 2.1 %collective-permute-start.6 = (f32[512,640]{1,0:T(8,128)}, f32[512,640]{1,0:T(8,128)S(1)}, u32[]{:S(2)}, u32[]{:S(2)}) collective-permute-start(f32[512,640]{1,0:T(8,128)} %get-tuple-element.24), channel_id=1, source_target_pairs={{0,16},{16,0},{32,48},{48,32},{64,80},{80,64},{96,112},{112,96},{1... | collective-permute-start | bytes 3932168 | tf_op jit(solution)/shard_map/ppermute | solution.py:285
  111.6 0.9 fusion.2
  112.5 6.5 %shard_map.58.a_ref = f32[256,640]{1,0:T(8,128)} custom-call(bf16[256,512]{1,0:T(8,128)(2,1)} %bitcast.34, bf16[1024,512]{1,0:T(8,128)(2,1)} %get-tuple-element.22.refs_1_, bf16[1024,512]{1,0:T(8,128)(2,1)} %get-tuple-element.23.refs_2_, s32[1,1024]{1,0:T(1,128)} %convert_element_type.9.refs_18_.refs_3_), custom_call_target="tpu_custom_call" | custom-call | flops 1073741824 | bytes 2883584 | tf_op jit(solution)/shard_map/pallas_call | solution.py:137
  119.0 1.1 copy-done.1
  120.1 2.8 %shard_map.59 = f32[256,640]{1,0:T(8,128)} custom-call(f32[256,640]{1,0:T(8,128)} %shard_map.58.a_ref, f32[512,640]{1,0:T(8,128)} %copy-done.1), custom_call_target="tpu_custom_call" | custom-call | flops 655360 | bytes 1966080 | tf_op jit(solution)/shard_map/pallas_call | solution.py:192
  122.9 1.9 %collective-permute-start.7 = (f32[256,640]{1,0:T(8,128)}, f32[256,640]{1,0:T(8,128)S(1)}, u32[]{:S(2)}, u32[]{:S(2)}) collective-permute-start(f32[256,640]{1,0:T(8,128)} %shard_map.59), channel_id=1, source_target_pairs={{0,32},{16,144},{32,0},{48,176},{64,96},{80,208},{96,64},{112,240}... | collective-permute-start | bytes 1966088 | tf_op jit(solution)/shard_map/ppermute | solution.py:288
  124.8 6.5 %shard_map.56.a_ref = f32[256,640]{1,0:T(8,128)} custom-call(bf16[256,512]{1,0:T(8,128)(2,1)} %bitcast.33, bf16[1024,512]{1,0:T(8,128)(2,1)} %get-tuple-element.22.refs_1_, bf16[1024,512]{1,0:T(8,128)(2,1)} %get-tuple-element.23.refs_2_, s32[1,1024]{1,0:T(1,128)} %convert_element_type.9.refs_18_.refs_3_), custom_call_target="tpu_custom_call" | custom-call | flops 1073741824 | bytes 2883584 | tf_op jit(solution)/shard_map/pallas_call | solution.py:137
  131.3 2.8 %shard_map.57.a_ref = f32[256,640]{1,0:T(8,128)} custom-call(f32[256,640]{1,0:T(8,128)} %shard_map.56.a_ref, f32[512,640]{1,0:T(8,128)} %copy-done.1), custom_call_target="tpu_custom_call" | custom-call | flops 655360 | bytes 1966080 | tf_op jit(solution)/shard_map/pallas_call | solution.py:192
  134.1 1.5 collective-permute-done.7.b_ref
  135.6 0.8 copy-done.6
  136.4 2.8 %shard_map.60 = (f32[128,640]{1,0:T(8,128)}, f32[128,640]{1,0:T(8,128)}) custom-call(f32[256,640]{1,0:T(8,128)} %shard_map.57.a_ref, f32[256,640]{1,0:T(8,128)} %copy-done.6), custom_call_target="tpu_custom_call" | custom-call | flops 655360 | bytes 1966080 | tf_op jit(solution)/shard_map/pallas_call | solution.py:192
  139.2 2.7 %collective-permute-start.8 = (f32[128,640]{1,0:T(8,128)}, f32[128,640]{1,0:T(8,128)S(1)}, u32[]{:S(2)}, u32[]{:S(2)}) collective-permute-start(f32[128,640]{1,0:T(8,128)} %get-tuple-element.26), channel_id=1, source_target_pairs={{0,128},{16,48},{32,160},{48,16},{64,192},{80,112},{96,224},{112,8... | collective-permute-start | bytes 983048 | tf_op jit(solution)/shard_map/ppermute | solution.py:296
  141.9 6.4 %collective-permute-done.8.b_ref = f32[128,640]{1,0:T(8,128)S(1)} collective-permute-done((f32[128,640]{1,0:T(8,128)}, f32[128,640]{1,0:T(8,128)S(1)}, u32[]{:S(2)}, u32[]{:S(2)}) %collective-permute-start.8) | collective-permute-done | bytes 327712 | tf_op jit(solution)/shard_map/ppermute | solution.py:296
  148.4 0.7 copy-done.9
  149.1 2.1 %shard_map.61 = (f32[64,640]{1,0:T(8,128)}, f32[64,640]{1,0:T(8,128)}) custom-call(f32[128,640]{1,0:T(8,128)} %get-tuple-element.25.a_ref, f32[128,640]{1,0:T(8,128)} %copy-done.9), custom_call_target="tpu_custom_call" | custom-call | flops 327680 | bytes 983040 | tf_op jit(solution)/shard_map/pallas_call | solution.py:192
  151.2 1.9 %collective-permute-start.9 = (f32[64,640]{1,0:T(8,128)}, f32[64,640]{1,0:T(8,128)S(1)}, u32[]{:S(2)}, u32[]{:S(2)}) collective-permute-start(f32[64,640]{1,0:T(8,128)} %get-tuple-element.28), channel_id=1, source_target_pairs={{0,64},{16,272},{32,96},{48,304},{64,0},{80,336},{96,32},{112,368}... | collective-permute-start | bytes 491528 | tf_op jit(solution)/shard_map/ppermute | solution.py:296
  153.1 8.1 %collective-permute-done.9.b_ref = f32[64,640]{1,0:T(8,128)S(1)} collective-permute-done((f32[64,640]{1,0:T(8,128)}, f32[64,640]{1,0:T(8,128)S(1)}, u32[]{:S(2)}, u32[]{:S(2)}) %collective-permute-start.9) | collective-permute-done | bytes 163872 | tf_op jit(solution)/shard_map/ppermute | solution.py:296
  161.3 0.7 copy-done.10
  161.9 1.9 %shard_map.62 = (f32[32,640]{1,0:T(8,128)}, f32[32,640]{1,0:T(8,128)}) custom-call(f32[64,640]{1,0:T(8,128)} %get-tuple-element.27.a_ref, f32[64,640]{1,0:T(8,128)} %copy-done.10), custom_call_target="tpu_custom_call" | custom-call | flops 163840 | bytes 491520 | tf_op jit(solution)/shard_map/pallas_call | solution.py:192
  163.8 3.3 %collective-permute-start.10 = (f32[32,640]{1,0:T(8,128)}, f32[32,640]{1,0:T(8,128)S(1)}, u32[]{:S(2)}, u32[]{:S(2)}) collective-permute-start(f32[32,640]{1,0:T(8,128)} %get-tuple-element.30), channel_id=1, source_target_pairs={{0,256},{16,80},{32,288},{48,112},{64,320},{80,16},{96,352},{112,4... | collective-permute-start | bytes 245768 | tf_op jit(solution)/shard_map/ppermute | solution.py:296
  167.1 4.7 %collective-permute-done.10.b_ref = f32[32,640]{1,0:T(8,128)S(1)} collective-permute-done((f32[32,640]{1,0:T(8,128)}, f32[32,640]{1,0:T(8,128)S(1)}, u32[]{:S(2)}, u32[]{:S(2)}) %collective-permute-start.10) | collective-permute-done | bytes 81952 | tf_op jit(solution)/shard_map/ppermute | solution.py:296
  171.8 0.6 copy-done.11
  172.5 2.2 %shard_map.63 = f32[32,512]{1,0:T(8,128)} custom-call(f32[32,640]{1,0:T(8,128)} %get-tuple-element.29.a_ref, f32[32,640]{1,0:T(8,128)} %copy-done.11, bf16[512,512]{1,0:T(8,128)(2,1)} %w_ref.1), custom_call_target="tpu_custom_call" | custom-call | flops 20971520 | bytes 655360 | tf_op jit(solution)/shard_map/pallas_call | solution.py:243
  (27 shorter events, 0.1 us)
Async XLA Ops:
  0.0 72.7 %copy-start = (bf16[1,1,1024,512]{3,2,1,0:T(8,128)(2,1)S(1)}, bf16[1,1,1024,512]{3,2,1,0:T(8,128)(2,1)}, u32[]{:S(2)}) copy-start(bf16[1,1,1024,512]{3,2,1,0:T(8,128)(2,1)} %param.5) | copy-start | bytes 3145732
  0.0 74.5 %copy-start.12 = (s32[1,1,8]{2,1,0:T(1,128)S(1)}, s32[1,1,8]{2,1,0:T(1,128)}, u32[]{:S(2)}) copy-start(s32[1,1,8]{2,1,0:T(1,128)} %param.8) | copy-start | bytes 100
  0.0 20.8 %collective-permute-start = (bf16[2,2,1,1,2,64,512]{6,5,4,3,2,1,0:T(8,128)(2,1)}, bf16[2,2,1,1,2,64,512]{6,5,4,3,2,1,0:T(8,128)(2,1)S(1)}, u32[]{:S(2)}, u32[]{:S(2)}) collective-permute-start(bf16[2,2,1,1,2,64,512]{6,5,4,3,2,1,0:T(8,128)(2,1)} %param.6), channel_id=1, source_target_pairs={{0,1},{1,2},{2,3},{4,5},{5,6},{6,7},{8,9},{9,10},{10,11},{12,13},{... | collective-permute-start | bytes 1572872 | tf_op jit(solution)/shard_map/ppermute | solution.py:21
  9.3 54.6 %collective-permute-start.1 = (bf16[2,2,1,1,2,64,512]{6,5,4,3,2,1,0:T(8,128)(2,1)}, bf16[2,2,1,1,2,64,512]{6,5,4,3,2,1,0:T(8,128)(2,1)S(1)}, u32[]{:S(2)}, u32[]{:S(2)}) collective-permute-start(bf16[2,2,1,1,2,64,512]{6,5,4,3,2,1,0:T(8,128)(2,1)} %param.6), channel_id=1, source_target_pairs={{1,0},{2,1},{3,2},{5,4},{6,5},{7,6},{9,8},{10,9},{11,10},{13,12},{... | collective-permute-start | bytes 1572872 | tf_op jit(solution)/shard_map/ppermute | solution.py:21
  10.6 53.3 %collective-permute-start.2 = (bf16[2,2,1,1,2,64,512]{6,5,4,3,2,1,0:T(8,128)(2,1)}, bf16[2,2,1,1,2,64,512]{6,5,4,3,2,1,0:T(8,128)(2,1)S(1)}, u32[]{:S(2)}, u32[]{:S(2)}) collective-permute-start(bf16[2,2,1,1,2,64,512]{6,5,4,3,2,1,0:T(8,128)(2,1)} %param.6), channel_id=1, source_target_pairs={{0,4},{4,8},{8,12},{1,5},{5,9},{9,13},{2,6},{6,10},{10,14},{3,7},{... | collective-permute-start | bytes 1572872 | tf_op jit(solution)/shard_map/ppermute | solution.py:21
  14.1 49.8 %collective-permute-start.3 = (bf16[2,2,1,1,2,64,512]{6,5,4,3,2,1,0:T(8,128)(2,1)}, bf16[2,2,1,1,2,64,512]{6,5,4,3,2,1,0:T(8,128)(2,1)S(1)}, u32[]{:S(2)}, u32[]{:S(2)}) collective-permute-start(bf16[2,2,1,1,2,64,512]{6,5,4,3,2,1,0:T(8,128)(2,1)} %param.6), channel_id=1, source_target_pairs={{4,0},{8,4},{12,8},{5,1},{9,5},{13,9},{6,2},{10,6},{14,10},{7,3},{... | collective-permute-start | bytes 1572872 | tf_op jit(solution)/shard_map/ppermute | solution.py:21
  20.8 51.8 %copy-start.2 = (bf16[2,2,1,1,2,64,512]{6,5,4,3,2,1,0:T(8,128)(2,1)}, bf16[2,2,1,1,2,64,512]{6,5,4,3,2,1,0:T(8,128)(2,1)S(1)}, u32[]{:S(2)}) copy-start(bf16[2,2,1,1,2,64,512]{6,5,4,3,2,1,0:T(8,128)(2,1)S(1)} %collective-permute-done) | copy-start | bytes 1572868
  63.9 8.8 %copy-start.4 = (bf16[2,2,1,1,2,64,512]{6,5,4,3,2,1,0:T(8,128)(2,1)}, bf16[2,2,1,1,2,64,512]{6,5,4,3,2,1,0:T(8,128)(2,1)S(1)}, u32[]{:S(2)}) copy-start(bf16[2,2,1,1,2,64,512]{6,5,4,3,2,1,0:T(8,128)(2,1)S(1)} %collective-permute-done.1) | copy-start | bytes 1572868
  63.9 8.8 %copy-start.7 = (bf16[2,2,1,1,2,64,512]{6,5,4,3,2,1,0:T(8,128)(2,1)}, bf16[2,2,1,1,2,64,512]{6,5,4,3,2,1,0:T(8,128)(2,1)S(1)}, u32[]{:S(2)}) copy-start(bf16[2,2,1,1,2,64,512]{6,5,4,3,2,1,0:T(8,128)(2,1)S(1)} %collective-permute-done.2) | copy-start | bytes 1572868
  63.9 8.8 %copy-start.8 = (bf16[2,2,1,1,2,64,512]{6,5,4,3,2,1,0:T(8,128)(2,1)}, bf16[2,2,1,1,2,64,512]{6,5,4,3,2,1,0:T(8,128)(2,1)S(1)}, u32[]{:S(2)}) copy-start(bf16[2,2,1,1,2,64,512]{6,5,4,3,2,1,0:T(8,128)(2,1)S(1)} %collective-permute-done.3) | copy-start | bytes 1572868
  65.7 26.8 %collective-permute-start.5 = (bf16[2,2,1,2,2,64,512]{6,5,4,3,2,1,0:T(8,128)(2,1)}, bf16[2,2,1,2,2,64,512]{6,5,4,3,2,1,0:T(8,128)(2,1)}, u32[]{:S(2)}, u32[]{:S(2)}) collective-permute-start(bf16[2,2,1,2,2,64,512]{6,5,4,3,2,1,0:T(8,128)(2,1)} %constant_dynamic-update-slice_fusion), channel_id=1, source_target_pairs={{4,0},{8,4},{12,8},{5,1},{9,5},{13,9},{6,2},{10,6},{14,10},{7,3},{... | collective-permute-start | bytes 3145736 | tf_op jit(solution)/shard_map/ppermute | solution.py:21
  67.0 26.8 %collective-permute-start.4 = (bf16[2,2,1,2,2,64,512]{6,5,4,3,2,1,0:T(8,128)(2,1)}, bf16[2,2,1,2,2,64,512]{6,5,4,3,2,1,0:T(8,128)(2,1)}, u32[]{:S(2)}, u32[]{:S(2)}) collective-permute-start(bf16[2,2,1,2,2,64,512]{6,5,4,3,2,1,0:T(8,128)(2,1)} %constant_dynamic-update-slice_fusion), channel_id=1, source_target_pairs={{0,4},{4,8},{8,12},{1,5},{5,9},{9,13},{2,6},{6,10},{10,14},{3,7},{... | collective-permute-start | bytes 3145736 | tf_op jit(solution)/shard_map/ppermute | solution.py:21
  73.6 21.5 %copy-start.3 = (bf16[2,2,1,1,2,64,512]{6,5,4,3,2,1,0:T(8,128)(2,1)S(1)}, bf16[2,2,1,1,2,64,512]{6,5,4,3,2,1,0:T(8,128)(2,1)}, u32[]{:S(2)}) copy-start(bf16[2,2,1,1,2,64,512]{6,5,4,3,2,1,0:T(8,128)(2,1)} %copy-done.2) | copy-start | bytes 1572868
  73.6 21.5 %copy-start.5 = (bf16[2,2,1,1,2,64,512]{6,5,4,3,2,1,0:T(8,128)(2,1)S(1)}, bf16[2,2,1,1,2,64,512]{6,5,4,3,2,1,0:T(8,128)(2,1)}, u32[]{:S(2)}) copy-start(bf16[2,2,1,1,2,64,512]{6,5,4,3,2,1,0:T(8,128)(2,1)} %copy-done.4) | copy-start | bytes 1572868
  109.5 9.5 %collective-permute-start.6 = (f32[512,640]{1,0:T(8,128)}, f32[512,640]{1,0:T(8,128)S(1)}, u32[]{:S(2)}, u32[]{:S(2)}) collective-permute-start(f32[512,640]{1,0:T(8,128)} %get-tuple-element.24), channel_id=1, source_target_pairs={{0,16},{16,0},{32,48},{48,32},{64,80},{80,64},{96,112},{112,96},{1... | collective-permute-start | bytes 3932168 | tf_op jit(solution)/shard_map/ppermute | solution.py:285
  119.0 1.1 copy-start.1
  122.9 12.7 %collective-permute-start.7 = (f32[256,640]{1,0:T(8,128)}, f32[256,640]{1,0:T(8,128)S(1)}, u32[]{:S(2)}, u32[]{:S(2)}) collective-permute-start(f32[256,640]{1,0:T(8,128)} %shard_map.59), channel_id=1, source_target_pairs={{0,32},{16,144},{32,0},{48,176},{64,96},{80,208},{96,64},{112,240}... | collective-permute-start | bytes 1966088 | tf_op jit(solution)/shard_map/ppermute | solution.py:288
  135.6 0.8 copy-start.6
  139.2 9.2 %collective-permute-start.8 = (f32[128,640]{1,0:T(8,128)}, f32[128,640]{1,0:T(8,128)S(1)}, u32[]{:S(2)}, u32[]{:S(2)}) collective-permute-start(f32[128,640]{1,0:T(8,128)} %get-tuple-element.26), channel_id=1, source_target_pairs={{0,128},{16,48},{32,160},{48,16},{64,192},{80,112},{96,224},{112,8... | collective-permute-start | bytes 983048 | tf_op jit(solution)/shard_map/ppermute | solution.py:296
  148.4 0.7 copy-start.9
  151.2 10.0 %collective-permute-start.9 = (f32[64,640]{1,0:T(8,128)}, f32[64,640]{1,0:T(8,128)S(1)}, u32[]{:S(2)}, u32[]{:S(2)}) collective-permute-start(f32[64,640]{1,0:T(8,128)} %get-tuple-element.28), channel_id=1, source_target_pairs={{0,64},{16,272},{32,96},{48,304},{64,0},{80,336},{96,32},{112,368}... | collective-permute-start | bytes 491528 | tf_op jit(solution)/shard_map/ppermute | solution.py:296
  161.3 0.7 copy-start.10
  163.8 8.0 %collective-permute-start.10 = (f32[32,640]{1,0:T(8,128)}, f32[32,640]{1,0:T(8,128)S(1)}, u32[]{:S(2)}, u32[]{:S(2)}) collective-permute-start(f32[32,640]{1,0:T(8,128)} %get-tuple-element.30), channel_id=1, source_target_pairs={{0,256},{16,80},{32,288},{48,112},{64,320},{80,16},{96,352},{112,4... | collective-permute-start | bytes 245768 | tf_op jit(solution)/shard_map/ppermute | solution.py:296
  171.8 0.6 copy-start.11

commit v15 on v13

--- a/solution.py
+++ b/solution.py
@@ -150,6 +150,21 @@
         out_refs[1][...] = merged[half:]
 
 
+def merge_part(kept, got, start, rows):
+    cols = kept.shape[1]
+    spec = pl.BlockSpec((rows, cols), lambda i: (start // rows, 0))
+    return pl.pallas_call(
+        merge_kernel,
+        grid=(1,),
+        in_specs=[spec, spec],
+        out_specs=[pl.BlockSpec((rows, cols), lambda i: (0, 0))],
+        out_shape=[jax.ShapeDtypeStruct((rows, cols), jnp.float32)],
+        cost_estimate=pl.CostEstimate(
+            flops=4 * rows * cols, transcendentals=2 * rows * PACK, bytes_accessed=12 * rows * cols
+        ),
+    )(kept, got)[0]
+
+
 def merge(kept, got, split, offset=0):
     rows, cols = kept.shape
     count = 2 if split else 1
@@ -260,9 +275,10 @@
     for i in range(1, nbits):
         if i == nbits - 1:
             return finish(first, second, w_out)
-        outs = merge(first, second, True)
-        first, second = outs
-        second = lax.ppermute(second, "tm", step_pairs(nbits, i + 1))
+        rows = first.shape[0] // 2
+        sent = merge_part(first, second, rows, rows)
+        first = merge_part(first, second, 0, rows)
+        second = lax.ppermute(sent, "tm", step_pairs(nbits, i + 1))
 
 
 def local(queries, kv_blocks, block_list, block_valid, w_out):

time: 173 us -> 172 us (level)
  waiting for transfers between devices: 75.4 us -> 69.7 us
  Pallas kernels: 38.9 us -> 43.6 us
    pallas_call x0 -> x6, Pallas kernels: none -> 11.5 us  [merge_part(): pl.pallas_call(merge_kernel, grid=(1,), in_specs=[spec, spec], out_specs=...]
    pallas_call x5 -> x2, Pallas kernels: 12.3 us -> 5.52 us  [merge(): pl.pallas_call(merge_kernel, grid=(1,), in_specs=[pl.BlockSpec((rows, col...]
    ppermute x3, waiting for transfers between devices: 16.4 us -> 10.7 us  [tree_reduce(): second = lax.ppermute(sent, 'tm', step_pairs(nbits, i + 1))]
  transfers between devices with their start and end apart: 11 -> 11, of which waited for: 6 -> 6; matrix products, arithmetic and copies ran while one was open for 3% -> 3% of each run, Pallas kernels for 10% -> 14%
where the time goes in v15:
time: 172 us; the launch traced here: 169 us
  waiting for transfers between devices  69.7 us (41%)
  Pallas kernels  43.6 us (25%)
  starting transfers between devices  40.1 us (23%)
  local copies, waits for them, and re-layouts  11.5 us (7%)
  other arithmetic  3.8 us (2%)
    ppermute x6, waiting for transfers between devices, shifted(): return lax.ppermute(array, axis, pairs)  58.3 us
    pallas_call x3, Pallas kernels, attention(): pl.pallas_call(attention_kernel, grid_spec=grid_spec, out_shape=jax.Shape...  24.4 us
    ppermute x6, starting transfers between devices, shifted(): return lax.ppermute(array, axis, pairs)  22.8 us
    ppermute x3, starting transfers between devices, tree_reduce(): second = lax.ppermute(sent, 'tm', step_pairs(nbits, i + 1))  13.3 us
    pallas_call x6, Pallas kernels, merge_part(): pl.pallas_call(merge_kernel, grid=(1,), in_specs=[spec, spec], out_specs=...  11.5 us
    ppermute x3, waiting for transfers between devices, tree_reduce(): second = lax.ppermute(sent, 'tm', step_pairs(nbits, i + 1))  10.7 us
    pallas_call x2, Pallas kernels, merge(): pl.pallas_call(merge_kernel, grid=(1,), in_specs=[pl.BlockSpec((rows, col...  5.52 us
    unnamed x31, local copies, waits for them, and re-layouts  4.98 us
  transfers between devices with their start and end apart: 11, of which 6 were waited for; matrix products, arithmetic and copies ran while one was open for 3% of the time, Pallas kernels for 14%

profile of v15, /device:TPU:6, one launch (start us, length us, event | category | flops | bytes accessed | tf_op | source)
XLA Modules:
  0.0 169.1 jit_solution(8090887377731188035)
XLA Ops:
  0.0 3.6 %collective-permute-start.2 = (bf16[2,2,1,1,2,64,512]{6,5,4,3,2,1,0:T(8,128)(2,1)}, bf16[2,2,1,1,2,64,512]{6,5,4,3,2,1,0:T(8,128)(2,1)S(1)}, u32[]{:S(2)}, u32[]{:S(2)}) collective-permute-start(bf16[2,2,1,1,2,64,512]{6,5,4,3,2,1,0:T(8,128)(2,1)} %param.6), channel_id=1, source_target_pairs={{0,4},{4,8},{8,12},{1,5},{5,9},{9,13},{2,6},{6,10},{10,14},{3,7},{... | collective-permute-start | bytes 1572872 | tf_op jit(solution)/shard_map/ppermute | solution.py:19
  3.6 1.3 collective-permute-start.1
  4.9 9.8 %collective-permute-start = (bf16[2,2,1,1,2,64,512]{6,5,4,3,2,1,0:T(8,128)(2,1)}, bf16[2,2,1,1,2,64,512]{6,5,4,3,2,1,0:T(8,128)(2,1)S(1)}, u32[]{:S(2)}, u32[]{:S(2)}) collective-permute-start(bf16[2,2,1,1,2,64,512]{6,5,4,3,2,1,0:T(8,128)(2,1)} %param.6), channel_id=1, source_target_pairs={{0,1},{1,2},{2,3},{4,5},{5,6},{6,7},{8,9},{9,10},{10,11},{12,13},{... | collective-permute-start | bytes 1572872 | tf_op jit(solution)/shard_map/ppermute | solution.py:19
  14.7 1.3 collective-permute-start.3
  16.1 0.7 fusion
  16.7 0.1 broadcast_in_dim.18
  16.8 0.7 convert_element_type.9.refs_16_
  17.5 40.8 %collective-permute-done.1 = bf16[2,2,1,1,2,64,512]{6,5,4,3,2,1,0:T(8,128)(2,1)S(1)} collective-permute-done((bf16[2,2,1,1,2,64,512]{6,5,4,3,2,1,0:T(8,128)(2,1)}, bf16[2,2,1,1,2,64,512]{6,5,4,3,2,1,0:T(8,128)(2,1)S(1)}, u32[]{:S(2)}, u32[]{:S(2)}) %collective-permute-start.1) | collective-permute-done | bytes 524320 | tf_op jit(solution)/shard_map/ppermute | solution.py:19
  58.3 1.0 constant_dynamic-update-slice_fusion.1
  59.3 0.8 constant_dynamic-update-slice_fusion
  60.1 1.3 collective-permute-start.5
  61.5 5.5 %collective-permute-start.4 = (bf16[2,2,1,2,2,64,512]{6,5,4,3,2,1,0:T(8,128)(2,1)}, bf16[2,2,1,2,2,64,512]{6,5,4,3,2,1,0:T(8,128)(2,1)}, u32[]{:S(2)}, u32[]{:S(2)}) collective-permute-start(bf16[2,2,1,2,2,64,512]{6,5,4,3,2,1,0:T(8,128)(2,1)} %constant_dynamic-update-slice_fusion), channel_id=1, source_target_pairs={{0,4},{4,8},{8,12},{1,5},{5,9},{9,13},{2,6},{6,10},{10,14},{3,7},{... | collective-permute-start | bytes 3145736 | tf_op jit(solution)/shard_map/ppermute | solution.py:19
  67.0 0.1 fusion.1
  67.1 0.6 gather_fusion
  67.8 0.1 compare_and_fusion
  67.9 0.2 broadcast_select_fusion
  68.1 0.8 slice.55
  68.9 17.5 %collective-permute-done.5 = bf16[2,2,1,2,2,64,512]{6,5,4,3,2,1,0:T(8,128)(2,1)} collective-permute-done((bf16[2,2,1,2,2,64,512]{6,5,4,3,2,1,0:T(8,128)(2,1)}, bf16[2,2,1,2,2,64,512]{6,5,4,3,2,1,0:T(8,128)(2,1)}, u32[]{:S(2)}, u32[]{:S(2)}) %collective-permute-start.5) | collective-permute-done | bytes 1048608 | tf_op jit(solution)/shard_map/ppermute | solution.py:19
  86.4 1.3 fusion.4
  87.7 1.3 fusion.3
  89.0 2.8 %maximum_maximum_fusion = bf16[2,2,3,3,2,64,512]{6,5,4,3,2,1,0:T(8,128)(2,1)} fusion(bf16[2,2,1,1,2,64,512]{6,5,4,3,2,1,0:T(8,128)(2,1)S(1)} %get-tuple-element.18, bf16[2,2,1,1,2,64,512]{6,5,4,3,2,1,0:T(8,128)(2,1)S(1)} %copy-done.13, bf16[2,2,1,1,2,64,512]{6,5,4,3,2,1,0:T(8,128)(2,1)S(1)} %get-tuple-element.17, ...), kind=kLoop, calls=%fused_computation.1 | loop fusion | flops 18874368 | bytes 9437184 | tf_op jit(solution)/shard_map/concatenate | solution.py:34
  91.8 9.9 %shard_map.56 = f32[512,640]{1,0:T(8,128)} custom-call(s32[8]{0:T(128)} %bitcast.67, bf16[512,512]{1,0:T(8,128)(2,1)} %bitcast.64, bf16[2,2,18,64,512]{4,3,2,1,0:T(8,128)(2,1)} %bitcast.16, bf16[2,2,18,64,512]{4,3,2,1,0:T(8,128)(2,1)} %bitcast.17, bf16[2,2,18,64,512]{4,3,2,1,0:T(8,128)(2,1)} %bitcast.18, bf16[2,2,18,64,512]{4,3,2,1,0:T(8,128)(2,1)} %bitcast.19, ...), custom_call_target="tpu_custom_call" | custom-call | flops 2147483648 | bytes 3670016 | tf_op jit(solution)/shard_map/pallas_call | solution.py:105
  101.7 2.1 %collective-permute-start.6 = (f32[512,640]{1,0:T(8,128)}, f32[512,640]{1,0:T(8,128)S(1)}, u32[]{:S(2)}, u32[]{:S(2)}) collective-permute-start(f32[512,640]{1,0:T(8,128)} %shard_map.56), channel_id=1, source_target_pairs={{0,16},{16,0},{32,48},{48,32},{64,80},{80,64},{96,112},{112,96},{1... | collective-permute-start | bytes 3932168 | tf_op jit(solution)/shard_map/ppermute | solution.py:269
  103.8 0.8 fusion.2
  104.6 7.2 %shard_map.58.a_ref = f32[256,640]{1,0:T(8,128)} custom-call(s32[8]{0:T(128)} %bitcast.68, bf16[256,512]{1,0:T(8,128)(2,1)} %bitcast.66, bf16[2,2,18,64,512]{4,3,2,1,0:T(8,128)(2,1)} %bitcast.39, bf16[2,2,18,64,512]{4,3,2,1,0:T(8,128)(2,1)} %bitcast.33, bf16[2,2,18,64,512]{4,3,2,1,0:T(8,128)(2,1)} %bitcast.34, bf16[2,2,18,64,512]{4,3,2,1,0:T(8,128)(2,1)} %bitcast.35, ...), custom_call_target="tpu_custom_call" | custom-call | flops 1073741824 | bytes 2883584 | tf_op jit(solution)/shard_map/pallas_call | solution.py:105
  111.9 1.1 copy-done.1
  113.0 2.8 %shard_map.59 = f32[256,640]{1,0:T(8,128)} custom-call(f32[256,640]{1,0:T(8,128)} %shard_map.58.a_ref, f32[512,640]{1,0:T(8,128)} %copy-done.1), custom_call_target="tpu_custom_call" | custom-call | flops 655360 | bytes 1966080 | tf_op jit(solution)/shard_map/pallas_call | solution.py:176
  115.7 1.9 %collective-permute-start.7 = (f32[256,640]{1,0:T(8,128)}, f32[256,640]{1,0:T(8,128)S(1)}, u32[]{:S(2)}, u32[]{:S(2)}) collective-permute-start(f32[256,640]{1,0:T(8,128)} %shard_map.59), channel_id=1, source_target_pairs={{0,32},{16,144},{32,0},{48,176},{64,96},{80,208},{96,64},{112,240}... | collective-permute-start | bytes 1966088 | tf_op jit(solution)/shard_map/ppermute | solution.py:272
  117.6 7.2 %shard_map.55.a_ref = f32[256,640]{1,0:T(8,128)} custom-call(s32[8]{0:T(128)} %bitcast.69, bf16[256,512]{1,0:T(8,128)(2,1)} %bitcast.65, bf16[2,2,18,64,512]{4,3,2,1,0:T(8,128)(2,1)} %bitcast.48, bf16[2,2,18,64,512]{4,3,2,1,0:T(8,128)(2,1)} %bitcast.49, bf16[2,2,18,64,512]{4,3,2,1,0:T(8,128)(2,1)} %bitcast.50, bf16[2,2,18,64,512]{4,3,2,1,0:T(8,128)(2,1)} %bitcast.51, ...), custom_call_target="tpu_custom_call" | custom-call | flops 1073741824 | bytes 2883584 | tf_op jit(solution)/shard_map/pallas_call | solution.py:105
  124.9 2.8 %shard_map.57.a_ref = f32[256,640]{1,0:T(8,128)} custom-call(f32[256,640]{1,0:T(8,128)} %shard_map.55.a_ref, f32[512,640]{1,0:T(8,128)} %copy-done.1), custom_call_target="tpu_custom_call" | custom-call | flops 655360 | bytes 1966080 | tf_op jit(solution)/shard_map/pallas_call | solution.py:176
  127.6 0.8 collective-permute-done.7.b_ref
  128.4 0.9 copy-done.2
  129.3 2.2 %shard_map.61 = f32[128,640]{1,0:T(8,128)} custom-call(f32[256,640]{1,0:T(8,128)} %shard_map.57.a_ref, f32[256,640]{1,0:T(8,128)} %copy-done.2), custom_call_target="tpu_custom_call" | custom-call | flops 327680 | bytes 983040 | tf_op jit(solution)/shard_map/pallas_call | solution.py:156
  131.5 2.7 %collective-permute-start.8 = (f32[128,640]{1,0:T(8,128)}, f32[128,640]{1,0:T(8,128)S(1)}, u32[]{:S(2)}, u32[]{:S(2)}) collective-permute-start(f32[128,640]{1,0:T(8,128)} %shard_map.61), channel_id=1, source_target_pairs={{0,128},{16,48},{32,160},{48,16},{64,192},{80,112},{96,224},{112,8... | collective-permute-start | bytes 983048 | tf_op jit(solution)/shard_map/ppermute | solution.py:281
  134.2 2.2 %shard_map.60.a_ref = f32[128,640]{1,0:T(8,128)} custom-call(f32[256,640]{1,0:T(8,128)} %shard_map.57.a_ref, f32[256,640]{1,0:T(8,128)} %copy-done.2), custom_call_target="tpu_custom_call" | custom-call | flops 327680 | bytes 983040 | tf_op jit(solution)/shard_map/pallas_call | solution.py:156
  136.4 4.3 %collective-permute-done.8.b_ref = f32[128,640]{1,0:T(8,128)S(1)} collective-permute-done((f32[128,640]{1,0:T(8,128)}, f32[128,640]{1,0:T(8,128)S(1)}, u32[]{:S(2)}, u32[]{:S(2)}) %collective-permute-start.8) | collective-permute-done | bytes 327712 | tf_op jit(solution)/shard_map/ppermute | solution.py:281
  140.6 0.7 copy-done.7
  141.4 1.9 %shard_map.63 = f32[64,640]{1,0:T(8,128)} custom-call(f32[128,640]{1,0:T(8,128)} %shard_map.60.a_ref, f32[128,640]{1,0:T(8,128)} %copy-done.7), custom_call_target="tpu_custom_call" | custom-call | flops 163840 | bytes 491520 | tf_op jit(solution)/shard_map/pallas_call | solution.py:156
  143.2 7.3 %collective-permute-start.9 = (f32[64,640]{1,0:T(8,128)}, f32[64,640]{1,0:T(8,128)S(1)}, u32[]{:S(2)}, u32[]{:S(2)}) collective-permute-start(f32[64,640]{1,0:T(8,128)} %shard_map.63), channel_id=1, source_target_pairs={{0,64},{16,272},{32,96},{48,304},{64,0},{80,336},{96,32},{112,368}... | collective-permute-start | bytes 491528 | tf_op jit(solution)/shard_map/ppermute | solution.py:281
  150.5 1.9 %shard_map.62.a_ref = f32[64,640]{1,0:T(8,128)} custom-call(f32[128,640]{1,0:T(8,128)} %shard_map.60.a_ref, f32[128,640]{1,0:T(8,128)} %copy-done.7), custom_call_target="tpu_custom_call" | custom-call | flops 163840 | bytes 491520 | tf_op jit(solution)/shard_map/pallas_call | solution.py:156
  152.4 3.4 %collective-permute-done.9.b_ref = f32[64,640]{1,0:T(8,128)S(1)} collective-permute-done((f32[64,640]{1,0:T(8,128)}, f32[64,640]{1,0:T(8,128)S(1)}, u32[]{:S(2)}, u32[]{:S(2)}) %collective-permute-start.9) | collective-permute-done | bytes 163872 | tf_op jit(solution)/shard_map/ppermute | solution.py:281
  155.8 0.7 copy-done.8
  156.5 1.7 %shard_map.65 = f32[32,640]{1,0:T(8,128)} custom-call(f32[64,640]{1,0:T(8,128)} %shard_map.62.a_ref, f32[64,640]{1,0:T(8,128)} %copy-done.8), custom_call_target="tpu_custom_call" | custom-call | flops 81920 | bytes 245760 | tf_op jit(solution)/shard_map/pallas_call | solution.py:156
  158.2 3.3 %collective-permute-start.10 = (f32[32,640]{1,0:T(8,128)}, f32[32,640]{1,0:T(8,128)S(1)}, u32[]{:S(2)}, u32[]{:S(2)}) collective-permute-start(f32[32,640]{1,0:T(8,128)} %shard_map.65), channel_id=1, source_target_pairs={{0,256},{16,80},{32,288},{48,112},{64,320},{80,16},{96,352},{112,4... | collective-permute-start | bytes 245768 | tf_op jit(solution)/shard_map/ppermute | solution.py:281
  161.5 1.7 %shard_map.64.a_ref = f32[32,640]{1,0:T(8,128)} custom-call(f32[64,640]{1,0:T(8,128)} %shard_map.62.a_ref, f32[64,640]{1,0:T(8,128)} %copy-done.8), custom_call_target="tpu_custom_call" | custom-call | flops 81920 | bytes 245760 | tf_op jit(solution)/shard_map/pallas_call | solution.py:156
  163.2 3.0 %collective-permute-done.10.b_ref = f32[32,640]{1,0:T(8,128)S(1)} collective-permute-done((f32[32,640]{1,0:T(8,128)}, f32[32,640]{1,0:T(8,128)S(1)}, u32[]{:S(2)}, u32[]{:S(2)}) %collective-permute-start.10) | collective-permute-done | bytes 81952 | tf_op jit(solution)/shard_map/ppermute | solution.py:281
  166.2 0.6 copy-done.14
  166.8 2.2 %shard_map.66 = f32[32,512]{1,0:T(8,128)} custom-call(f32[32,640]{1,0:T(8,128)} %shard_map.64.a_ref, f32[32,640]{1,0:T(8,128)} %copy-done.14, bf16[512,512]{1,0:T(8,128)(2,1)} %w_ref.1), custom_call_target="tpu_custom_call" | custom-call | flops 20971520 | bytes 655360 | tf_op jit(solution)/shard_map/pallas_call | solution.py:227
  (34 shorter events, 0.1 us)
Async XLA Ops:
  0.0 67.1 %copy-start = (bf16[1,1,1024,512]{3,2,1,0:T(8,128)(2,1)S(1)}, bf16[1,1,1024,512]{3,2,1,0:T(8,128)(2,1)}, u32[]{:S(2)}) copy-start(bf16[1,1,1024,512]{3,2,1,0:T(8,128)(2,1)} %param.5) | copy-start | bytes 3145732
  0.0 17.5 %collective-permute-start.2 = (bf16[2,2,1,1,2,64,512]{6,5,4,3,2,1,0:T(8,128)(2,1)}, bf16[2,2,1,1,2,64,512]{6,5,4,3,2,1,0:T(8,128)(2,1)S(1)}, u32[]{:S(2)}, u32[]{:S(2)}) collective-permute-start(bf16[2,2,1,1,2,64,512]{6,5,4,3,2,1,0:T(8,128)(2,1)} %param.6), channel_id=1, source_target_pairs={{0,4},{4,8},{8,12},{1,5},{5,9},{9,13},{2,6},{6,10},{10,14},{3,7},{... | collective-permute-start | bytes 1572872 | tf_op jit(solution)/shard_map/ppermute | solution.py:19
  3.6 54.7 %collective-permute-start.1 = (bf16[2,2,1,1,2,64,512]{6,5,4,3,2,1,0:T(8,128)(2,1)}, bf16[2,2,1,1,2,64,512]{6,5,4,3,2,1,0:T(8,128)(2,1)S(1)}, u32[]{:S(2)}, u32[]{:S(2)}) collective-permute-start(bf16[2,2,1,1,2,64,512]{6,5,4,3,2,1,0:T(8,128)(2,1)} %param.6), channel_id=1, source_target_pairs={{1,0},{2,1},{3,2},{5,4},{6,5},{7,6},{9,8},{10,9},{11,10},{13,12},{... | collective-permute-start | bytes 1572872 | tf_op jit(solution)/shard_map/ppermute | solution.py:19
  4.9 53.4 %collective-permute-start = (bf16[2,2,1,1,2,64,512]{6,5,4,3,2,1,0:T(8,128)(2,1)}, bf16[2,2,1,1,2,64,512]{6,5,4,3,2,1,0:T(8,128)(2,1)S(1)}, u32[]{:S(2)}, u32[]{:S(2)}) collective-permute-start(bf16[2,2,1,1,2,64,512]{6,5,4,3,2,1,0:T(8,128)(2,1)} %param.6), channel_id=1, source_target_pairs={{0,1},{1,2},{2,3},{4,5},{5,6},{6,7},{8,9},{9,10},{10,11},{12,13},{... | collective-permute-start | bytes 1572872 | tf_op jit(solution)/shard_map/ppermute | solution.py:19
  14.7 43.6 %collective-permute-start.3 = (bf16[2,2,1,1,2,64,512]{6,5,4,3,2,1,0:T(8,128)(2,1)}, bf16[2,2,1,1,2,64,512]{6,5,4,3,2,1,0:T(8,128)(2,1)S(1)}, u32[]{:S(2)}, u32[]{:S(2)}) collective-permute-start(bf16[2,2,1,1,2,64,512]{6,5,4,3,2,1,0:T(8,128)(2,1)} %param.6), channel_id=1, source_target_pairs={{4,0},{8,4},{12,8},{5,1},{9,5},{13,9},{6,2},{10,6},{14,10},{7,3},{... | collective-permute-start | bytes 1572872 | tf_op jit(solution)/shard_map/ppermute | solution.py:19
  17.5 50.3 %copy-start.10 = (bf16[2,2,1,1,2,64,512]{6,5,4,3,2,1,0:T(8,128)(2,1)}, bf16[2,2,1,1,2,64,512]{6,5,4,3,2,1,0:T(8,128)(2,1)S(1)}, u32[]{:S(2)}) copy-start(bf16[2,2,1,1,2,64,512]{6,5,4,3,2,1,0:T(8,128)(2,1)S(1)} %collective-permute-done.2) | copy-start | bytes 1572868
  58.3 8.8 %copy-start.3 = (bf16[2,2,1,1,2,64,512]{6,5,4,3,2,1,0:T(8,128)(2,1)}, bf16[2,2,1,1,2,64,512]{6,5,4,3,2,1,0:T(8,128)(2,1)S(1)}, u32[]{:S(2)}) copy-start(bf16[2,2,1,1,2,64,512]{6,5,4,3,2,1,0:T(8,128)(2,1)S(1)} %collective-permute-done.1) | copy-start | bytes 1572868
  58.3 8.8 %copy-start.5 = (bf16[2,2,1,1,2,64,512]{6,5,4,3,2,1,0:T(8,128)(2,1)}, bf16[2,2,1,1,2,64,512]{6,5,4,3,2,1,0:T(8,128)(2,1)S(1)}, u32[]{:S(2)}) copy-start(bf16[2,2,1,1,2,64,512]{6,5,4,3,2,1,0:T(8,128)(2,1)S(1)} %collective-permute-done) | copy-start | bytes 1572868
  58.3 9.5 %copy-start.12 = (bf16[2,2,1,1,2,64,512]{6,5,4,3,2,1,0:T(8,128)(2,1)}, bf16[2,2,1,1,2,64,512]{6,5,4,3,2,1,0:T(8,128)(2,1)S(1)}, u32[]{:S(2)}) copy-start(bf16[2,2,1,1,2,64,512]{6,5,4,3,2,1,0:T(8,128)(2,1)S(1)} %collective-permute-done.3) | copy-start | bytes 1572868
  60.1 26.2 %collective-permute-start.5 = (bf16[2,2,1,2,2,64,512]{6,5,4,3,2,1,0:T(8,128)(2,1)}, bf16[2,2,1,2,2,64,512]{6,5,4,3,2,1,0:T(8,128)(2,1)}, u32[]{:S(2)}, u32[]{:S(2)}) collective-permute-start(bf16[2,2,1,2,2,64,512]{6,5,4,3,2,1,0:T(8,128)(2,1)} %constant_dynamic-update-slice_fusion), channel_id=1, source_target_pairs={{4,0},{8,4},{12,8},{5,1},{9,5},{13,9},{6,2},{10,6},{14,10},{7,3},{... | collective-permute-start | bytes 3145736 | tf_op jit(solution)/shard_map/ppermute | solution.py:19
  61.5 26.2 %collective-permute-start.4 = (bf16[2,2,1,2,2,64,512]{6,5,4,3,2,1,0:T(8,128)(2,1)}, bf16[2,2,1,2,2,64,512]{6,5,4,3,2,1,0:T(8,128)(2,1)}, u32[]{:S(2)}, u32[]{:S(2)}) collective-permute-start(bf16[2,2,1,2,2,64,512]{6,5,4,3,2,1,0:T(8,128)(2,1)} %constant_dynamic-update-slice_fusion), channel_id=1, source_target_pairs={{0,4},{4,8},{8,12},{1,5},{5,9},{9,13},{2,6},{6,10},{10,14},{3,7},{... | collective-permute-start | bytes 3145736 | tf_op jit(solution)/shard_map/ppermute | solution.py:19
  67.7 21.2 %copy-start.4 = (bf16[2,2,1,1,2,64,512]{6,5,4,3,2,1,0:T(8,128)(2,1)S(1)}, bf16[2,2,1,1,2,64,512]{6,5,4,3,2,1,0:T(8,128)(2,1)}, u32[]{:S(2)}) copy-start(bf16[2,2,1,1,2,64,512]{6,5,4,3,2,1,0:T(8,128)(2,1)} %copy-done.3) | copy-start | bytes 1572868
  67.8 21.2 %copy-start.6 = (bf16[2,2,1,1,2,64,512]{6,5,4,3,2,1,0:T(8,128)(2,1)S(1)}, bf16[2,2,1,1,2,64,512]{6,5,4,3,2,1,0:T(8,128)(2,1)}, u32[]{:S(2)}) copy-start(bf16[2,2,1,1,2,64,512]{6,5,4,3,2,1,0:T(8,128)(2,1)} %copy-done.5) | copy-start | bytes 1572868
  67.8 21.2 %copy-start.9 = (bf16[2,2,1,1,2,64,512]{6,5,4,3,2,1,0:T(8,128)(2,1)S(1)}, bf16[2,2,1,1,2,64,512]{6,5,4,3,2,1,0:T(8,128)(2,1)}, u32[]{:S(2)}) copy-start(bf16[2,2,1,1,2,64,512]{6,5,4,3,2,1,0:T(8,128)(2,1)} %param.6) | copy-start | bytes 1572868
  67.9 21.1 %copy-start.11 = (bf16[2,2,1,1,2,64,512]{6,5,4,3,2,1,0:T(8,128)(2,1)S(1)}, bf16[2,2,1,1,2,64,512]{6,5,4,3,2,1,0:T(8,128)(2,1)}, u32[]{:S(2)}) copy-start(bf16[2,2,1,1,2,64,512]{6,5,4,3,2,1,0:T(8,128)(2,1)} %copy-done.10) | copy-start | bytes 1572868
  67.9 21.1 %copy-start.13 = (bf16[2,2,1,1,2,64,512]{6,5,4,3,2,1,0:T(8,128)(2,1)S(1)}, bf16[2,2,1,1,2,64,512]{6,5,4,3,2,1,0:T(8,128)(2,1)}, u32[]{:S(2)}) copy-start(bf16[2,2,1,1,2,64,512]{6,5,4,3,2,1,0:T(8,128)(2,1)} %copy-done.12) | copy-start | bytes 1572868
  101.7 10.2 %collective-permute-start.6 = (f32[512,640]{1,0:T(8,128)}, f32[512,640]{1,0:T(8,128)S(1)}, u32[]{:S(2)}, u32[]{:S(2)}) collective-permute-start(f32[512,640]{1,0:T(8,128)} %shard_map.56), channel_id=1, source_target_pairs={{0,16},{16,0},{32,48},{48,32},{64,80},{80,64},{96,112},{112,96},{1... | collective-permute-start | bytes 3932168 | tf_op jit(solution)/shard_map/ppermute | solution.py:269
  111.9 1.1 copy-start.1
  115.7 12.7 %collective-permute-start.7 = (f32[256,640]{1,0:T(8,128)}, f32[256,640]{1,0:T(8,128)S(1)}, u32[]{:S(2)}, u32[]{:S(2)}) collective-permute-start(f32[256,640]{1,0:T(8,128)} %shard_map.59), channel_id=1, source_target_pairs={{0,32},{16,144},{32,0},{48,176},{64,96},{80,208},{96,64},{112,240}... | collective-permute-start | bytes 1966088 | tf_op jit(solution)/shard_map/ppermute | solution.py:272
  128.4 0.9 copy-start.2
  131.5 9.2 %collective-permute-start.8 = (f32[128,640]{1,0:T(8,128)}, f32[128,640]{1,0:T(8,128)S(1)}, u32[]{:S(2)}, u32[]{:S(2)}) collective-permute-start(f32[128,640]{1,0:T(8,128)} %shard_map.61), channel_id=1, source_target_pairs={{0,128},{16,48},{32,160},{48,16},{64,192},{80,112},{96,224},{112,8... | collective-permute-start | bytes 983048 | tf_op jit(solution)/shard_map/ppermute | solution.py:281
  140.6 0.7 copy-start.7
  143.2 12.5 %collective-permute-start.9 = (f32[64,640]{1,0:T(8,128)}, f32[64,640]{1,0:T(8,128)S(1)}, u32[]{:S(2)}, u32[]{:S(2)}) collective-permute-start(f32[64,640]{1,0:T(8,128)} %shard_map.63), channel_id=1, source_target_pairs={{0,64},{16,272},{32,96},{48,304},{64,0},{80,336},{96,32},{112,368}... | collective-permute-start | bytes 491528 | tf_op jit(solution)/shard_map/ppermute | solution.py:281
  155.8 0.7 copy-start.8
  158.2 8.0 %collective-permute-start.10 = (f32[32,640]{1,0:T(8,128)}, f32[32,640]{1,0:T(8,128)S(1)}, u32[]{:S(2)}, u32[]{:S(2)}) collective-permute-start(f32[32,640]{1,0:T(8,128)} %shard_map.65), channel_id=1, source_target_pairs={{0,256},{16,80},{32,288},{48,112},{64,320},{80,16},{96,352},{112,4... | collective-permute-start | bytes 245768 | tf_op jit(solution)/shard_map/ppermute | solution.py:281
  166.2 0.6 copy-start.14
